TPU v7x, 32 devices: a whole 2x2x4 slice. The times are simulated.
32 devices in a mesh: dp: 2 (over y), expert: 16 (over z, x, core).
Axes of the slice: x: 2, y: 2, z: 4, core: 2. Of those that a mesh axis runs over, the one named last changes fastest.
Arguments:
- tokens: bfloat16 [4096, 1024], P(('dp', 'expert')), may hold values from -6 to 6
- masked: int32 [4096], P(('dp', 'expert')), may hold values 0 or 1
- importance: float32 [4096], P(('dp', 'expert')), may hold values from 1 to 10
- routes: int32 [4096, 8], P(('dp', 'expert')), may hold values from 0 to 15, all different within a row; in each aligned block of 128 rows (0 to 127, 128 to 255, ...) at most 96 rows name the same one
- gates: float32 [4096, 8], P(('dp', 'expert')), may hold values from 0.05 to 0.3
- cotangent: bfloat16 [4096, 1024], P(('dp', 'expert')), may hold values from -6 to 6
- w_gate: bfloat16 [16, 512, 1024], P('expert'), may hold values from -0.1875 to 0.1875
- w_up: bfloat16 [16, 512, 1024], P('expert'), may hold values from -0.1875 to 0.1875
- w_down: bfloat16 [16, 512, 1024], P('expert'), may hold values from -0.25 to 0.25
Outputs:
- mixed: bfloat16 [4096, 1024], P(('dp', 'expert'))
- weight_grads: float32 [16, 512, 3, 1024], P('expert', 'dp')
Inputs may be any that keep to these rules, and one draw needn't show every extreme that they name: `routes`: among the 128 rows of one device (aligned blocks of rows), no expert is named by more than 96 rows, a bound that some block reaches; a row names 8 different experts.
All inputs are finite; a program needn't handle non-finite values. No bound on the sum of `masked` on one device may be relied on, other than what follows from the above.
Results may differ from a plain program's by a relative error of at most 0.0057.
Values may be sent and summed in bfloat16 or wider, within the bound.
No kernel may reach another device: no remote copies, remote signals or barrier semaphores. Data moves between devices by JAX's collectives and lax.ppermute only.
A program may use at most 64 MiB of HBM per device.

v0:
```python
import jax
import jax.numpy as jnp
from jax import lax
from jax.sharding import PartitionSpec as P


def contract_rows(left, right):
    return lax.dot_general(
        left, right, (((0,), (0,)), ((), ())), preferred_element_type=jnp.float32
    )


def contract_cols(left, right):
    return lax.dot_general(
        left, right, (((1,), (1,)), ((), ())), preferred_element_type=jnp.float32
    )


def local(tokens, masked, importance, routes, gates, cotangent, w_gate, w_up, w_down):
    tok_rows = tokens.shape[0]
    width = tokens.shape[1]
    topk = routes.shape[1]
    experts = lax.axis_size("expert")
    capacity = min(tok_rows, 3 * tok_rows * topk // (2 * experts))
    flat = routes.reshape(-1)
    onehot = (flat[:, None] == jnp.arange(experts, dtype=jnp.int32)[None, :]).astype(jnp.int32)
    before = jnp.cumsum(onehot, axis=0) - onehot
    slots = jnp.sum(before * onehot, axis=1)
    target = flat * capacity + slots
    owner = jnp.arange(tok_rows * topk, dtype=jnp.int32) // topk
    coef = importance * masked.astype(jnp.float32)
    factor = (coef[:, None] * gates).reshape(-1)
    sent_x = jnp.zeros((experts * capacity, width), jnp.bfloat16).at[target].set(tokens[owner])
    scaled = (factor[:, None] * cotangent[owner].astype(jnp.float32)).astype(jnp.bfloat16)
    sent_q = jnp.zeros((experts * capacity, width), jnp.bfloat16).at[target].set(scaled)
    layout = (experts, capacity, width)
    wgate = w_gate[0]
    wup = w_up[0]
    wdown = w_down[0]
    recv_x, recv_q = (
        lax.all_to_all(sent_x.reshape(layout), "expert", split_axis=0, concat_axis=0, tiled=True),
        lax.all_to_all(sent_q.reshape(layout), "expert", split_axis=0, concat_axis=0, tiled=True),
    )
    forward_rows_x = recv_x.reshape(-1, width)
    forward_gate_pre = contract_cols(forward_rows_x, wgate)
    forward_up_pre = contract_cols(forward_rows_x, wup)
    forward_sig = jax.nn.sigmoid(forward_gate_pre)
    forward_act = forward_gate_pre * forward_sig
    forward_hidden = (forward_act * forward_up_pre).astype(jnp.bfloat16)
    expert_out = jnp.dot(forward_hidden, wdown, preferred_element_type=jnp.float32).astype(
        jnp.bfloat16
    )
    rows_x, gate_pre, up_pre, sig, act, hidden, expert_out = (
        forward_rows_x,
        forward_gate_pre,
        forward_up_pre,
        forward_sig,
        forward_act,
        forward_hidden,
        expert_out,
    )
    returned = lax.all_to_all(
        expert_out.reshape(layout), "expert", split_axis=0, concat_axis=0, tiled=True
    )
    picked = returned.reshape(-1, width)[target].astype(jnp.float32)
    summed = jnp.sum(picked.reshape(tok_rows, topk, width) * gates[:, :, None], axis=1)
    mixed = summed.astype(jnp.bfloat16)
    rows_q = recv_q.reshape(-1, width)
    back = contract_cols(rows_q, wdown)
    d_gate = (back * up_pre * sig * (1.0 + gate_pre * (1.0 - sig))).astype(jnp.bfloat16)
    d_up = (back * act).astype(jnp.bfloat16)
    share = wgate.shape[0] // lax.axis_size("dp")
    grad_gate = contract_rows(d_gate, rows_x)
    grad_up = contract_rows(d_up, rows_x)
    grad_down = contract_rows(hidden, rows_q)
    summed = lax.psum_scatter(
        jnp.stack([grad_gate, grad_up, grad_down], axis=1), "dp", scatter_dimension=0, tiled=True
    )
    weight_grads = summed.reshape(1, share, 3, width)
    return (mixed, weight_grads)


def solution(mesh):
    in_specs = (
        P(("dp", "expert"), None),
        P(("dp", "expert")),
        P(("dp", "expert")),
        P(("dp", "expert"), None),
        P(("dp", "expert"), None),
        P(("dp", "expert"), None),
        P("expert", None, None),
        P("expert", None, None),
        P("expert", None, None),
    )
    out_specs = (P(("dp", "expert"), None), P("expert", "dp", None, None))
    return jax.shard_map(local, mesh=mesh, in_specs=in_specs, out_specs=out_specs, check_vma=False)
```

profile of v0, /device:TPU:15, one launch (start us, length us, event | category | flops | bytes accessed | tf_op | source)
XLA Modules:
  0.0 296.5 jit_solution(6712441092233542278)
XLA Ops:
  7.2 0.8 broadcast_multiply_fusion.1
  8.0 0.8 copy.15
  9.2 4.5 %reduce-window.6 = s32[16,8,128]{2,1,0:T(8,128)S(1)} reduce-window(s32[16,8,128]{2,1,0:T(8,128)S(1)} %fusion.19, s32[]{:T(128)} %constant.27.clone.1), window={size=1x1x128 pad=0_0x0_0x127_0}, to_apply=%region_0.0 | reduce-window | flops 2080768 | bytes 131076 | tf_op jit(solution)/shard_map/reduce-window
  13.8 0.1 copy.17
  14.2 16.7 %scatter_custom_fusion = bf16[1536,1024]{1,0:T(8,128)(2,1)} fusion(s32[1024]{0:T(1024)S(1)} %bitcast.64, bf16[128,1024]{1,0:T(8,128)(2,1)} %param.9, s32[1024]{0:T(1024)S(1)} %broadcast_clamp_fusion.1, bf16[]{:T(256)} %constant.25.clone.1), kind=kCustom, calls=%fused_computation.16 | custom fusion | bytes 3146240 | tf_op jit(solution)/shard_map/scatter | solution.py:33
  30.8 6.7 %all-to-all-start = ((bf16[16,96,1024]{2,1,0:T(8,128)(2,1)}), bf16[16,96,1024]{2,1,0:T(8,128)(2,1)}, u32[]{:S(2)}, u32[]{:S(2)}) async-start(bf16[16,96,1024]{2,1,0:T(8,128)(2,1)} %bitcast.59), calls=%async_computation | async-start | bytes 6291456 | tf_op jit(solution)/shard_map/all_to_all | solution.py:41
  37.8 15.1 %scatter_custom_fusion.1 = bf16[1536,1024]{1,0:T(8,128)(2,1)} fusion(s32[1024]{0:T(1024)S(1)} %bitcast.65, f32[1024]{0:T(1024)S(1)} %mul.80, bf16[]{:T(256)} %constant.25.clone.1, bf16[128,1024]{1,0:T(8,128)(2,1)S(1)} %copy-done.1, s32[1024]{0:T(1024)S(1)} %broadcast_clamp_fusion.1), kind=kCustom, calls=%fused_computation.15 | custom fusion | flops 3145728 | bytes 3416066 | tf_op jit(solution)/shard_map/scatter | solution.py:35
  52.9 54.6 %all-to-all-done = bf16[16,96,1024]{2,1,0:T(8,128)(2,1)} async-done(((bf16[16,96,1024]{2,1,0:T(8,128)(2,1)}), bf16[16,96,1024]{2,1,0:T(8,128)(2,1)}, u32[]{:S(2)}, u32[]{:S(2)}) %all-to-all-start) | async-done | bytes 3145760 | tf_op jit(solution)/shard_map/all_to_all | solution.py:41
  107.5 5.0 %all-to-all-start.2 = ((bf16[16,96,1024]{2,1,0:T(8,128)(2,1)}), bf16[16,96,1024]{2,1,0:T(8,128)(2,1)}, u32[]{:S(2)}, u32[]{:S(2)}) async-start(bf16[16,96,1024]{2,1,0:T(8,128)(2,1)} %bitcast.58), calls=%async_computation.2 | async-start | bytes 6291456 | tf_op jit(solution)/shard_map/all_to_all | solution.py:42
  112.6 0.3 reduce-scatter.2.cloned.1.call-start
  112.8 3.9 %fusion.13 = f32[1536,512]{1,0:T(8,128)S(1)} fusion(bf16[1536,1024]{1,0:T(8,128)(2,1)} %bitcast.6, bf16[1,512,1024]{2,1,0:T(8,128)(2,1)S(1)} %copy-done.3), kind=kOutput, calls=%fused_computation.29 | convolution fusion | flops 1610612736 | bytes 7340032 | tf_op jit(solution)/shard_map/dot_general | solution.py:14
  116.8 1.6 copy-done.7
  118.4 5.8 %multiply_convert_fusion.3 = (bf16[1536,512]{1,0:T(8,128)(2,1)S(1)}, f32[1536,512]{1,0:T(8,128)}) fusion(f32[1536,512]{1,0:T(8,128)S(1)} %fusion.13, bf16[1536,1024]{1,0:T(8,128)(2,1)} %bitcast.6, bf16[1,512,1024]{2,1,0:T(8,128)(2,1)S(1)} %copy-done.4), kind=kOutput, calls=%fused_computation.12 | convolution fusion | flops 1615331328 | bytes 12058624 | tf_op jit(solution)/shard_map/dot_general | solution.py:14
  124.2 58.4 %all-to-all-done.2 = bf16[16,96,1024]{2,1,0:T(8,128)(2,1)} async-done(((bf16[16,96,1024]{2,1,0:T(8,128)(2,1)}), bf16[16,96,1024]{2,1,0:T(8,128)(2,1)}, u32[]{:S(2)}, u32[]{:S(2)}) %all-to-all-start.2) | async-done | bytes 3145760 | tf_op jit(solution)/shard_map/all_to_all | solution.py:42
  182.6 3.7 %convolution_bitcast_fusion = f32[512,1,1024]{2,0,1:T(8,128)S(1)} fusion(bf16[1536,512]{1,0:T(8,128)(2,1)S(1)} %get-tuple-element.2, bf16[1536,1024]{1,0:T(8,128)(2,1)} %bitcast.14), kind=kOutput, calls=%fused_computation.19 | convolution fusion | flops 1610612736 | bytes 6815744 | tf_op jit(solution)/shard_map/dot_general | solution.py:8
  186.3 3.9 %fusion.8 = f32[1536,512]{1,0:T(8,128)S(1)} fusion(bf16[1536,1024]{1,0:T(8,128)(2,1)} %bitcast.14, bf16[1,512,1024]{2,1,0:T(8,128)(2,1)S(1)} %copy-done), kind=kOutput, calls=%fused_computation.24 | convolution fusion | flops 1610612736 | bytes 7340032 | tf_op jit(solution)/shard_map/dot_general | solution.py:14
  190.2 3.9 %convolution_bitcast_fusion.1 = f32[512,1,1024]{2,0,1:T(8,128)S(1)} fusion(bf16[1536,1024]{1,0:T(8,128)(2,1)} %bitcast.6, f32[1536,512]{1,0:T(8,128)S(1)} %fusion.8, f32[1536,512]{1,0:T(8,128)S(1)} %copy-done.8), kind=kOutput, calls=%fused_computation.20 | convolution fusion | flops 1615331328 | bytes 11534336 | tf_op jit(solution)/shard_map/dot_general | solution.py:8
  194.1 4.4 %convolution_bitcast_fusion.2 = f32[512,1,1024]{2,0,1:T(8,128)S(1)} fusion(bf16[1536,1024]{1,0:T(8,128)(2,1)} %bitcast.6, f32[1536,512]{1,0:T(8,128)S(1)} %copy-done.8, f32[1536,512]{1,0:T(8,128)S(1)} %fusion.8, f32[1536,512]{1,0:T(8,128)S(1)} %copy-done.9), kind=kOutput, calls=%fused_computation.21 | convolution fusion | flops 1618477056 | bytes 14680064 | tf_op jit(solution)/shard_map/dot_general | solution.py:8
  198.5 3.2 %pad_maximum_fusion = f32[512,3,1024]{2,0,1:T(8,128)} fusion(f32[512,1,1024]{2,0,1:T(8,128)S(1)} %convolution_bitcast_fusion, f32[512,1,1024]{2,0,1:T(8,128)S(1)} %convolution_bitcast_fusion.1, f32[512,1,1024]{2,0,1:T(8,128)S(1)} %convolution_bitcast_fusion.2), kind=kLoop, calls=%fused_computation.5 | loop fusion | flops 3145728 | bytes 12582912 | tf_op jit(solution)/shard_map/stack | solution.py:77
  201.7 3.7 %convolution_convert_fusion = bf16[1536,1024]{1,0:T(8,128)(2,1)} fusion(bf16[1536,512]{1,0:T(8,128)(2,1)S(1)} %get-tuple-element.2, bf16[1,512,1024]{2,1,0:T(8,128)(2,1)S(1)} %copy-done), kind=kOutput, calls=%fused_computation.9 | convolution fusion | flops 1612185600 | bytes 5767168 | tf_op jit(solution)/shard_map/dot_general | solution.py:50
  205.4 4.9 %all-to-all-start.1 = ((bf16[16,96,1024]{2,1,0:T(8,128)(2,1)}), bf16[16,96,1024]{2,1,0:T(8,128)(2,1)}, u32[]{:S(2)}, u32[]{:S(2)}) async-start(bf16[16,96,1024]{2,1,0:T(8,128)(2,1)} %bitcast.60), calls=%async_computation.1 | async-start | bytes 6291456 | tf_op jit(solution)/shard_map/all_to_all | solution.py:62
  210.5 69.9 %all-to-all-done.1 = bf16[16,96,1024]{2,1,0:T(8,128)(2,1)} async-done(((bf16[16,96,1024]{2,1,0:T(8,128)(2,1)}), bf16[16,96,1024]{2,1,0:T(8,128)(2,1)}, u32[]{:S(2)}, u32[]{:S(2)}) %all-to-all-start.1) | async-done | bytes 3145760 | tf_op jit(solution)/shard_map/all_to_all | solution.py:62
  280.4 7.3 %gather_fusion = bf16[1024,1024]{1,0:T(8,128)(2,1)S(1)} fusion(bf16[1536,1024]{1,0:T(8,128)(2,1)} %bitcast.11, s32[1024]{0:T(1024)S(1)} %broadcast_clamp_fusion), kind=kCustom, calls=%fused_computation.1 | custom fusion | bytes 4198400 | tf_op jit(solution)/shard_map/gather | solution.py:65
  287.6 2.0 fusion
  (41 shorter events, 1.1 us)
Async XLA Ops:
  7.2 179.1 %copy-start = (bf16[1,512,1024]{2,1,0:T(8,128)(2,1)S(1)}, bf16[1,512,1024]{2,1,0:T(8,128)(2,1)}, u32[]{:S(2)}) copy-start(bf16[1,512,1024]{2,1,0:T(8,128)(2,1)} %param.17) | copy-start | bytes 3145732
  30.8 6.7 %copy-start.5 = (f32[128]{0:T(128)S(1)}, f32[128]{0:T(128)}, u32[]{:S(2)}) copy-start(f32[128]{0:T(128)} %param.11) | copy-start | bytes 1540
  30.8 6.7 %copy-start.6 = (s32[128]{0:T(128)S(1)}, s32[128]{0:T(128)}, u32[]{:S(2)}) copy-start(s32[128]{0:T(128)} %param.10) | copy-start | bytes 1540
  30.8 6.7 %copy-start.2 = (f32[128,8]{0,1:T(8,128)S(1)}, f32[128,8]{0,1:T(8,128)}, u32[]{:S(2)}) copy-start(f32[128,8]{0,1:T(8,128)} %param.13) | copy-start | bytes 12292
  30.8 7.0 %copy-start.1 = (bf16[128,1024]{1,0:T(8,128)(2,1)S(1)}, bf16[128,1024]{1,0:T(8,128)(2,1)}, u32[]{:S(2)}) copy-start(bf16[128,1024]{1,0:T(8,128)(2,1)} %param.14) | copy-start | bytes 786436
  30.8 76.7 %all-to-all-start = ((bf16[16,96,1024]{2,1,0:T(8,128)(2,1)}), bf16[16,96,1024]{2,1,0:T(8,128)(2,1)}, u32[]{:S(2)}, u32[]{:S(2)}) async-start(bf16[16,96,1024]{2,1,0:T(8,128)(2,1)} %bitcast.59), calls=%async_computation | async-start | bytes 6291456 | tf_op jit(solution)/shard_map/all_to_all | solution.py:41
  107.5 5.3 %copy-start.3 = (bf16[1,512,1024]{2,1,0:T(8,128)(2,1)S(1)}, bf16[1,512,1024]{2,1,0:T(8,128)(2,1)}, u32[]{:S(2)}) copy-start(bf16[1,512,1024]{2,1,0:T(8,128)(2,1)} %param.15) | copy-start | bytes 3145732
  107.5 75.0 %all-to-all-start.2 = ((bf16[16,96,1024]{2,1,0:T(8,128)(2,1)}), bf16[16,96,1024]{2,1,0:T(8,128)(2,1)}, u32[]{:S(2)}, u32[]{:S(2)}) async-start(bf16[16,96,1024]{2,1,0:T(8,128)(2,1)} %bitcast.58), calls=%async_computation.2 | async-start | bytes 6291456 | tf_op jit(solution)/shard_map/all_to_all | solution.py:42
  112.6 177.1 %reduce-scatter.2.cloned.1.call-start = ((), (), s32[]{:S(2)}) async-start(), calls=%async_computation.4 | async-start | bytes 9437184 | tf_op jit(solution)/shard_map/reduce_scatter | solution.py:76
  112.8 5.5 %copy-start.4 = (bf16[1,512,1024]{2,1,0:T(8,128)(2,1)S(1)}, bf16[1,512,1024]{2,1,0:T(8,128)(2,1)}, u32[]{:S(2)}) copy-start(bf16[1,512,1024]{2,1,0:T(8,128)(2,1)} %param.16) | copy-start | bytes 3145732
  116.7 1.6 copy-start.7
  186.3 3.9 %copy-start.8 = (f32[1536,512]{1,0:T(8,128)S(1)}, f32[1536,512]{1,0:T(8,128)}, u32[]{:S(2)}) copy-start(f32[1536,512]{1,0:T(8,128)} %copy-done.7) | copy-start | bytes 9437188
  190.2 3.9 %copy-start.9 = (f32[1536,512]{1,0:T(8,128)S(1)}, f32[1536,512]{1,0:T(8,128)}, u32[]{:S(2)}) copy-start(f32[1536,512]{1,0:T(8,128)} %get-tuple-element.3) | copy-start | bytes 9437188
  205.4 74.9 %all-to-all-start.1 = ((bf16[16,96,1024]{2,1,0:T(8,128)(2,1)}), bf16[16,96,1024]{2,1,0:T(8,128)(2,1)}, u32[]{:S(2)}, u32[]{:S(2)}) async-start(bf16[16,96,1024]{2,1,0:T(8,128)(2,1)} %bitcast.60), calls=%async_computation.1 | async-start | bytes 6291456 | tf_op jit(solution)/shard_map/all_to_all | solution.py:62
Sparse Core Ops, SparseCore 0:
  201.9 75.5 reduce-scatter.1
where the time goes:
time: 297 us
  waiting for transfers between devices  183 us (62%)
  matrix products  29.3 us (10%)
  local copies, waits for them, and re-layouts  27.3 us (9%)
  other arithmetic  25.8 us (9%)
  starting transfers between devices  16.9 us (6%)
  between operations  14.2 us (5%)
    all_to_all x1, waiting for transfers between devices, local(): lax.all_to_all(expert_out.reshape(layout), 'expert', split_axis=0, concat...  69.9 us
    all_to_all x1, waiting for transfers between devices, local(): lax.all_to_all(sent_q.reshape(layout), 'expert', split_axis=0, concat_axi...  58.4 us
    all_to_all x1, waiting for transfers between devices, local(): lax.all_to_all(sent_x.reshape(layout), 'expert', split_axis=0, concat_axi...  54.6 us
    scatter x1, local copies, waits for them, and re-layouts, local(): jnp.zeros((experts * capacity, width), jnp.bfloat16).at[target]  16.7 us
    scatter x1, other arithmetic, local(): jnp.zeros((experts * capacity, width), jnp.bfloat16).at[target].set(scaled)  15.1 us
    dot_general x3, matrix products, contract_cols(): lax.dot_general(left, right, (((1,), (1,)), ((), ())), preferred_element_...  13.6 us
    dot_general x3, matrix products, contract_rows(): lax.dot_general(left, right, (((0,), (0,)), ((), ())), preferred_element_...  12 us
    gather x1, local copies, waits for them, and re-layouts, local(): picked = returned.reshape(-1, width)[target].astype(jnp.float32)  7.27 us
  transfers between devices with their start and end apart: 4, of which 3 were waited for; matrix products, arithmetic and copies ran while one was open for 13% of the time, Pallas kernels for 0%

commit v1 on v0

v1 whole, which is shorter than its diff:
```python
import jax
import jax.numpy as jnp
from jax import lax
from jax.sharding import PartitionSpec as P

GATHER_ROWS = 2048
RETURN = "a2a"


def contract_rows(left, right):
    return lax.dot_general(
        left, right, (((0,), (0,)), ((), ())), preferred_element_type=jnp.float32
    )


def contract_cols(left, right):
    return lax.dot_general(
        left, right, (((1,), (1,)), ((), ())), preferred_element_type=jnp.float32
    )


def expert_math(rows_x, rows_q, wgate, wup, wdown):
    gate_pre = contract_cols(rows_x, wgate)
    up_pre = contract_cols(rows_x, wup)
    sig = jax.nn.sigmoid(gate_pre)
    act = gate_pre * sig
    hidden = (act * up_pre).astype(jnp.bfloat16)
    expert_out = jnp.dot(hidden, wdown, preferred_element_type=jnp.float32).astype(
        jnp.bfloat16
    )
    back = contract_cols(rows_q, wdown)
    d_gate = (back * up_pre * sig * (1.0 + gate_pre * (1.0 - sig))).astype(jnp.bfloat16)
    d_up = (back * act).astype(jnp.bfloat16)
    grad_gate = contract_rows(d_gate, rows_x)
    grad_up = contract_rows(d_up, rows_x)
    grad_down = contract_rows(hidden, rows_q)
    return expert_out, jnp.stack([grad_gate, grad_up, grad_down], axis=1)


def reduce_grads(grads, width):
    share = grads.shape[0] // lax.axis_size("dp")
    summed = lax.psum_scatter(grads, "dp", scatter_dimension=0, tiled=True)
    return summed.reshape(1, share, 3, width)


def source_slots(routes, experts):
    flat = routes.reshape(-1)
    onehot = (flat[:, None] == jnp.arange(experts, dtype=jnp.int32)[None, :]).astype(jnp.int32)
    before = jnp.cumsum(onehot, axis=0) - onehot
    return flat, jnp.sum(before * onehot, axis=1)


def local_a2a(tokens, masked, importance, routes, gates, cotangent, w_gate, w_up, w_down):
    tok_rows = tokens.shape[0]
    width = tokens.shape[1]
    topk = routes.shape[1]
    experts = lax.axis_size("expert")
    capacity = min(tok_rows, 3 * tok_rows * topk // (2 * experts))
    flat, slots = source_slots(routes, experts)
    target = flat * capacity + slots
    owner = jnp.arange(tok_rows * topk, dtype=jnp.int32) // topk
    coef = importance * masked.astype(jnp.float32)
    factor = (coef[:, None] * gates).reshape(-1)
    sent_x = jnp.zeros((experts * capacity, width), jnp.bfloat16).at[target].set(tokens[owner])
    scaled = (factor[:, None] * cotangent[owner].astype(jnp.float32)).astype(jnp.bfloat16)
    sent_q = jnp.zeros((experts * capacity, width), jnp.bfloat16).at[target].set(scaled)
    layout = (experts, capacity, width)
    recv_x = lax.all_to_all(sent_x.reshape(layout), "expert", 0, 0, tiled=True)
    recv_q = lax.all_to_all(sent_q.reshape(layout), "expert", 0, 0, tiled=True)
    expert_out, grads = expert_math(
        recv_x.reshape(-1, width), recv_q.reshape(-1, width), w_gate[0], w_up[0], w_down[0]
    )
    returned = lax.all_to_all(expert_out.reshape(layout), "expert", 0, 0, tiled=True)
    picked = returned.reshape(-1, width)[target].astype(jnp.float32)
    summed = jnp.sum(picked.reshape(tok_rows, topk, width) * gates[:, :, None], axis=1)
    return summed.astype(jnp.bfloat16), reduce_grads(grads, width)


def local_gather(tokens, masked, importance, routes, gates, cotangent, w_gate, w_up, w_down):
    tok_rows = tokens.shape[0]
    width = tokens.shape[1]
    topk = routes.shape[1]
    experts = lax.axis_size("expert")
    capacity = min(tok_rows, 3 * tok_rows * topk // (2 * experts))
    me = lax.axis_index("expert")
    coef = importance * masked.astype(jnp.float32)
    factor = coef[:, None] * gates
    meta = jnp.concatenate([routes.astype(jnp.float32), factor, gates], axis=1)

    all_x = lax.all_gather(tokens, "expert", axis=0, tiled=True)
    all_meta = lax.all_gather(meta, "expert", axis=0, tiled=True)
    all_c = lax.all_gather(cotangent, "expert", axis=0, tiled=True)

    all_routes = all_meta[:, :topk].astype(jnp.int32)
    hit = all_routes == me
    zero = jnp.zeros((), jnp.float32)
    fac = jnp.sum(jnp.where(hit, all_meta[:, topk:2 * topk], zero), axis=1)
    gte = jnp.sum(jnp.where(hit, all_meta[:, 2 * topk:], zero), axis=1)
    routed = jnp.any(hit, axis=1).reshape(experts, tok_rows)
    ahead = (
        lax.broadcasted_iota(jnp.int32, (tok_rows, tok_rows), 0)
        < lax.broadcasted_iota(jnp.int32, (tok_rows, tok_rows), 1)
    ).astype(jnp.bfloat16)
    rank = jnp.dot(
        routed.astype(jnp.bfloat16), ahead, preferred_element_type=jnp.float32
    ).astype(jnp.int32)
    slot_ids = lax.broadcasted_iota(jnp.int32, (experts, capacity, tok_rows), 1)
    pick = (routed[:, None, :] & (rank[:, None, :] == slot_ids)).astype(jnp.bfloat16)

    def select(values):
        rows = jnp.einsum(
            "sjt,std->sjd",
            pick,
            values.reshape(experts, tok_rows, width),
            preferred_element_type=jnp.float32,
        )
        return rows.astype(jnp.bfloat16).reshape(experts * capacity, width)

    rows_x = select(all_x)
    all_q = (fac[:, None] * all_c.astype(jnp.float32)).astype(jnp.bfloat16)
    rows_q = select(all_q)
    expert_out, grads = expert_math(rows_x, rows_q, w_gate[0], w_up[0], w_down[0])

    if RETURN == "scatter":
        dense = jnp.einsum(
            "sjt,sjd->std",
            pick,
            expert_out.reshape(experts, capacity, width),
            preferred_element_type=jnp.float32,
        ).reshape(experts * tok_rows, width)
        contrib = gte[:, None] * dense
        summed = lax.psum_scatter(contrib, "expert", scatter_dimension=0, tiled=True)
    else:
        returned = lax.all_to_all(
            expert_out.reshape(experts, capacity, width), "expert", 0, 0, tiled=True
        )
        flat, slots = source_slots(routes, experts)
        target = flat * capacity + slots
        choose = (
            target[:, None]
            == lax.broadcasted_iota(jnp.int32, (tok_rows * topk, experts * capacity), 1)
        ).astype(jnp.bfloat16)
        picked = jnp.dot(
            choose, returned.reshape(-1, width), preferred_element_type=jnp.float32
        )
        summed = jnp.sum(picked.reshape(tok_rows, topk, width) * gates[:, :, None], axis=1)
    return summed.astype(jnp.bfloat16), reduce_grads(grads, width)


def local(*args):
    tokens = args[0]
    if lax.axis_size("expert") * tokens.shape[0] <= GATHER_ROWS:
        return local_gather(*args)
    return local_a2a(*args)


def solution(mesh):
    in_specs = (
        P(("dp", "expert"), None),
        P(("dp", "expert")),
        P(("dp", "expert")),
        P(("dp", "expert"), None),
        P(("dp", "expert"), None),
        P(("dp", "expert"), None),
        P("expert", None, None),
        P("expert", None, None),
        P("expert", None, None),
    )
    out_specs = (P(("dp", "expert"), None), P("expert", "dp", None, None))
    return jax.shard_map(local, mesh=mesh, in_specs=in_specs, out_specs=out_specs, check_vma=False)
```

time: 297 us -> 222 us (0.75)
  the two profiles are of different devices: /device:TPU:15 before, /device:TPU:0 now
where the time goes in v1:
time: 222 us
  blocking collectives  96.4 us (43%)
  waiting for transfers between devices  70.2 us (32%)
  matrix products  24.7 us (11%)
  between operations  13.9 us (6%)
  other arithmetic  13.7 us (6%)
  local copies, waits for them, and re-layouts  2.59 us (1%)
    all_to_all x1, blocking collectives, local_gather(): lax.all_to_all(expert_out.reshape(experts, capacity, width), 'expert', 0,...  72.8 us
    all_gather x1, waiting for transfers between devices, local_gather(): all_c = lax.all_gather(cotangent, 'expert', axis=0, tiled=True)  46.4 us
    all_gather x1, blocking collectives, local_gather(): all_meta = lax.all_gather(meta, 'expert', axis=0, tiled=True)  23.6 us
    all_gather x1, waiting for transfers between devices, local_gather(): all_x = lax.all_gather(tokens, 'expert', axis=0, tiled=True)  22.4 us
    dot_general x3, matrix products, contract_rows(): lax.dot_general(left, right, (((0,), (0,)), ((), ())), preferred_element_...  6.45 us
    dot_general x3, matrix products, contract_cols(): lax.dot_general(left, right, (((1,), (1,)), ((), ())), preferred_element_...  5.98 us
    dot_general x2, matrix products, select(): jnp.einsum('sjt,std->sjd', pick, values.reshape(experts, tok_rows, width)...  5.8 us
    another operation x3, other arithmetic  4.63 us
  transfers between devices with their start and end apart: 3, of which 2 were waited for; matrix products, arithmetic and copies ran while one was open for 9% of the time, Pallas kernels for 0%

profile of v1, /device:TPU:0, one launch (start us, length us, event | category | flops | bytes accessed | tf_op | source)
XLA Modules:
  0.0 221.6 jit_solution(2674392483787027454)
XLA Ops:
  8.0 0.7 all-gather.5.cloned.1.call-update
  8.7 0.8 copy.20
  9.7 4.5 %reduce-window.6 = s32[16,8,128]{2,1,0:T(8,128)S(1)} reduce-window(s32[16,8,128]{2,1,0:T(8,128)S(1)} %fusion.27, s32[]{:T(128)} %constant.7.clone.1), window={size=1x1x128 pad=0_0x0_0x127_0}, to_apply=%region_0.1 | reduce-window | flops 2080768 | bytes 131076 | tf_op jit(solution)/shard_map/reduce-window
  14.8 0.7 convert_multiply_fusion
  15.5 0.7 broadcast_multiply_fusion
  16.2 0.8 multiply_add_fusion
  17.0 0.7 pad_maximum_fusion.1
  17.6 23.6 %all_gather.9 = f32[2048,24]{0,1:T(8,128)S(1)} all-gather(f32[128,24]{0,1:T(8,128)S(1)} %pad_maximum_fusion.1), channel_id=1, replica_groups=mesh['dp'=2,'expert'=16] {'expert'}, dimensions={0}, use_global_device_ids=true | all-gather | bytes 208896 | tf_op jit(solution)/shard_map/all_gather | solution.py:91
  41.4 22.4 %all-gather.3.cloned.1.call-done = bf16[2048,1024]{1,0:T(8,128)(2,1)} async-done(((bf16[128,1024]{1,0:T(8,128)(2,1)}), bf16[2048,1024]{1,0:T(8,128)(2,1)}) %all-gather.3.cloned.1.call-update) | async-done | bytes 4194320 | tf_op jit(solution)/shard_map/all_gather | solution.py:90
  63.8 4.8 %convolution_convert_fusion.2 = bf16[16,96,1024]{2,1,0:T(8,128)(2,1)} fusion(bf16[16,128,1024]{2,1,0:T(8,128)(2,1)} %bitcast.66, s32[16,128]{1,0:T(8,128)S(1)} %convolution_convert_fusion.3, pred[16,128]{1,0:T(8,128)(4,1)S(1)} %bitcast.76), kind=kOutput, calls=%fused_computation.14 | convolution fusion | flops 404619264 | bytes 7350272 | tf_op jit(solution)/shard_map/sjt,std->sjd/dot_general | solution.py:111
  68.7 46.4 %all-gather.5.cloned.1.call-done = bf16[2048,1024]{1,0:T(8,128)(2,1)} async-done(((bf16[128,1024]{1,0:T(8,128)(2,1)}), bf16[2048,1024]{1,0:T(8,128)(2,1)}) %all-gather.5.cloned.1.call-update) | async-done | bytes 4194320 | tf_op jit(solution)/shard_map/all_gather | solution.py:92
  115.1 2.9 %multiply_convert_fusion = bf16[2048,1024]{1,0:T(8,128)(2,1)S(1)} fusion(bf16[2048,1024]{1,0:T(8,128)(2,1)} %all-gather.5.cloned.1.call-done, f32[2048]{0:T(1024)S(1)} %get-tuple-element.2), kind=kLoop, calls=%fused_computation | loop fusion | flops 6291456 | bytes 8396800 | tf_op jit(solution)/shard_map/convert_element_type | solution.py:120
  118.0 1.0 convolution_convert_fusion.1
  119.0 0.9 copy-done.1
  120.2 1.8 fusion.12
  122.1 2.3 %multiply_convert_fusion.3 = (bf16[1536,512]{1,0:T(8,128)(2,1)S(1)}, f32[1536,512]{1,0:T(8,128)S(1)}) fusion(f32[1536,512]{1,0:T(8,128)S(1)} %fusion.12, bf16[1536,1024]{1,0:T(8,128)(2,1)S(1)} %bitcast.68, bf16[1,512,1024]{2,1,0:T(8,128)(2,1)S(1)} %copy-done.4), kind=kOutput, calls=%fused_computation.9 | convolution fusion | flops 1615331328 | bytes 12058624 | tf_op jit(solution)/shard_map/dot_general | solution.py:17
  124.4 1.8 fusion.7
  126.2 1.9 convolution_bitcast_fusion.1
  128.1 2.7 %convolution_bitcast_fusion.2 = f32[512,1,1024]{2,0,1:T(8,128)S(1)} fusion(bf16[1536,1024]{1,0:T(8,128)(2,1)S(1)} %bitcast.70, f32[1536,512]{1,0:T(8,128)S(1)} %fusion.12, f32[1536,512]{1,0:T(8,128)S(1)} %fusion.7, f32[1536,512]{1,0:T(8,128)S(1)} %get-tuple-element.7), kind=kOutput, calls=%fused_computation.17 | convolution fusion | flops 1618477056 | bytes 14680064 | tf_op jit(solution)/shard_map/dot_general | solution.py:11
  130.9 1.8 convolution_bitcast_fusion
  132.7 3.2 %pad_maximum_fusion = f32[512,3,1024]{2,0,1:T(8,128)} fusion(f32[512,1,1024]{2,0,1:T(8,128)S(1)} %convolution_bitcast_fusion, f32[512,1,1024]{2,0,1:T(8,128)S(1)} %convolution_bitcast_fusion.1, f32[512,1,1024]{2,0,1:T(8,128)S(1)} %convolution_bitcast_fusion.2), kind=kLoop, calls=%fused_computation.1 | loop fusion | flops 3145728 | bytes 12582912 | tf_op jit(solution)/shard_map/stack | solution.py:37
  135.9 1.8 convolution_convert_fusion
  137.8 72.8 %all_to_all.5 = bf16[16,96,1024]{2,1,0:T(8,128)(2,1)S(1)} all-to-all(bf16[16,96,1024]{2,1,0:T(8,128)(2,1)S(1)} %bitcast.74), channel_id=1, replica_groups=mesh['dp'=2,'expert'=16] {'expert'}, dimensions={0} | all-to-all | bytes 6291456 | tf_op jit(solution)/shard_map/all_to_all | solution.py:134
  210.6 4.6 %multiply_reduce_fusion = bf16[128,1024]{1,0:T(8,128)(2,1)} fusion(f32[128,8]{0,1:T(8,128)S(1)} %copy-done.2, bf16[1536,1024,1]{1,0,2:T(8,128)(2,1)S(1)} %bitcast.73, s32[128,8]{0,1:T(8,128)S(1)} %get-tuple-element.4), kind=kOutput, calls=%fused_computation.5 | convolution fusion | flops 3224764416 | bytes 3416064 | tf_op jit(solution)/shard_map/dot_general | solution.py:143
  (30 shorter events, 2.1 us)
Async XLA Ops:
  7.2 117.2 %copy-start = (bf16[1,512,1024]{2,1,0:T(8,128)(2,1)S(1)}, bf16[1,512,1024]{2,1,0:T(8,128)(2,1)}, u32[]{:S(2)}) copy-start(bf16[1,512,1024]{2,1,0:T(8,128)(2,1)} %param.17) | copy-start | bytes 3145732
  7.2 56.7 %all-gather.3.cloned.1.call-start = ((), (), s32[]{:S(2)}) async-start(), calls=%async_computation.2 | async-start | bytes 4456448 | tf_op jit(solution)/shard_map/all_gather | solution.py:90
  7.9 107.2 %all-gather.5.cloned.1.call-start = ((), (), s32[]{:S(2)}) async-start(), calls=%async_computation.3 | async-start | bytes 4456448 | tf_op jit(solution)/shard_map/all_gather | solution.py:92
  8.7 206.4 %reduce-scatter.2.cloned.1.call-start = ((), (), s32[]{:S(2)}) async-start(), calls=%async_computation.4 | async-start | bytes 9437184 | tf_op jit(solution)/shard_map/reduce_scatter | solution.py:42
  118.0 1.9 copy-start.1
  118.0 2.2 copy-start.3
  120.2 1.9 copy-start.4
  137.7 72.8 %copy-start.2 = (f32[128,8]{0,1:T(8,128)S(1)}, f32[128,8]{0,1:T(8,128)}, u32[]{:S(2)}) copy-start(f32[128,8]{0,1:T(8,128)} %param.13) | copy-start | bytes 12292
Sparse Core Ops, SparseCore 0:
  10.2 53.6 all-gather.2
  66.0 49.0 all-gather.4
  136.1 75.5 reduce-scatter.1

commit v2 on v1

--- a/solution.py
+++ b/solution.py
@@ -4,7 +4,7 @@
 from jax.sharding import PartitionSpec as P
 
 GATHER_ROWS = 2048
-RETURN = "a2a"
+RETURN = "scatter"
 
 
 def contract_rows(left, right):

time: 222 us -> 309 us (1.39)
  waiting for transfers between devices: 70.2 us -> 232 us
  blocking collectives: 96.4 us -> 23.8 us
  matrix products: 24.7 us -> 21.4 us
    reduce_scatter x0 -> x1, waiting for transfers between devices: none -> 90.1 us  [local_gather(): lax.psum_scatter(contrib, 'expert', scatter_dimension=0, tiled=True)]
    reduce_scatter x1, waiting for transfers between devices: 0.01 us -> 77.8 us  [reduce_grads(): summed = lax.psum_scatter(grads, 'dp', scatter_dimension=0, tiled=True)]
    all_to_all x1 -> x0, blocking collectives: 72.8 us -> none  [local_gather(): lax.all_to_all(expert_out.reshape(experts, capacity, width), 'expert', 0,...]
    all_gather x1, waiting for transfers between devices: 46.4 us -> 34.7 us  [local_gather(): all_c = lax.all_gather(cotangent, 'expert', axis=0, tiled=True)]
    all_gather x1, waiting for transfers between devices: 22.4 us -> 28.4 us  [local_gather(): all_x = lax.all_gather(tokens, 'expert', axis=0, tiled=True)]
    another operation x3 -> x0, other arithmetic: 4.63 us -> none
    mul x0 -> x1, other arithmetic: none -> 3.85 us  [local_gather(): contrib = gte[:, None] * dense]
    dot_general x1, matrix products: 4.55 us -> 1.3 us  [local_gather(): jnp.einsum('sjt,sjd->std', pick, expert_out.reshape(experts, capacity, wi...]
  transfers between devices with their start and end apart: 3 -> 4, of which waited for: 2 -> 4; matrix products, arithmetic and copies ran while one was open for 9% -> 12% of each run, Pallas kernels for 0% -> 0%
where the time goes in v2:
time: 309 us; the launch traced here: 308 us
  waiting for transfers between devices  232 us (75%)
  blocking collectives  23.8 us (8%)
  matrix products  21.4 us (7%)
  other arithmetic  14.7 us (5%)
  between operations  13.9 us (4%)
    reduce_scatter x1, waiting for transfers between devices, local_gather(): lax.psum_scatter(contrib, 'expert', scatter_dimension=0, tiled=True)  90.1 us
    reduce_scatter x1, waiting for transfers between devices, reduce_grads(): summed = lax.psum_scatter(grads, 'dp', scatter_dimension=0, tiled=True)  77.8 us
    all_gather x1, waiting for transfers between devices, local_gather(): all_c = lax.all_gather(cotangent, 'expert', axis=0, tiled=True)  34.7 us
    all_gather x1, waiting for transfers between devices, local_gather(): all_x = lax.all_gather(tokens, 'expert', axis=0, tiled=True)  28.4 us
    all_gather x1, blocking collectives, local_gather(): all_meta = lax.all_gather(meta, 'expert', axis=0, tiled=True)  23.8 us
    dot_general x3, matrix products, contract_cols(): lax.dot_general(left, right, (((1,), (1,)), ((), ())), preferred_element_...  7.63 us
    dot_general x3, matrix products, contract_rows(): lax.dot_general(left, right, (((0,), (0,)), ((), ())), preferred_element_...  6.24 us
  transfers between devices with their start and end apart: 4, of which 4 were waited for; matrix products, arithmetic and copies ran while one was open for 12% of the time, Pallas kernels for 0%

profile of v2, /device:TPU:0, one launch (start us, length us, event | category | flops | bytes accessed | tf_op | source)
XLA Modules:
  0.0 308.5 jit_solution(12384886933002429471)
XLA Ops:
  8.0 0.7 all-gather.5.cloned.1.call-update
  8.7 0.7 convert_element_type.42
  10.1 0.7 broadcast_multiply_fusion
  10.8 0.7 pad_maximum_fusion.1
  11.5 23.8 %all_gather.9 = f32[2048,24]{0,1:T(8,128)S(1)} all-gather(f32[128,24]{0,1:T(8,128)S(1)} %pad_maximum_fusion.1), channel_id=1, replica_groups=mesh['dp'=2,'expert'=16] {'expert'}, dimensions={0}, use_global_device_ids=true | all-gather | bytes 208896 | tf_op jit(solution)/shard_map/all_gather | solution.py:91
  35.5 28.4 %all-gather.3.cloned.1.call-done = bf16[2048,1024]{1,0:T(8,128)(2,1)} async-done(((bf16[128,1024]{1,0:T(8,128)(2,1)}), bf16[2048,1024]{1,0:T(8,128)(2,1)}) %all-gather.3.cloned.1.call-update) | async-done | bytes 4194320 | tf_op jit(solution)/shard_map/all_gather | solution.py:90
  63.9 3.2 %convolution_convert_fusion.2 = bf16[16,96,1024]{2,1,0:T(8,128)(2,1)S(1)} fusion(bf16[16,128,1024]{2,1,0:T(8,128)(2,1)} %bitcast.42, s32[16,128]{1,0:T(8,128)S(1)} %convolution_convert_fusion.3, pred[16,128]{1,0:T(8,128)(4,1)S(1)} %bitcast.50), kind=kOutput, calls=%fused_computation.10 | convolution fusion | flops 404619264 | bytes 7350272 | tf_op jit(solution)/shard_map/sjt,std->sjd/dot_general | solution.py:111
  67.2 1.8 fusion.6
  69.2 3.9 %multiply_convert_fusion.3 = (bf16[1536,512]{1,0:T(8,128)(2,1)S(1)}, f32[1536,512]{1,0:T(8,128)}) fusion(f32[1536,512]{1,0:T(8,128)S(1)} %fusion.6, bf16[1536,1024]{1,0:T(8,128)(2,1)S(1)} %bitcast.44, bf16[1,512,1024]{2,1,0:T(8,128)(2,1)S(1)} %copy-done.4), kind=kOutput, calls=%fused_computation.6 | convolution fusion | flops 1615331328 | bytes 12058624 | tf_op jit(solution)/shard_map/dot_general | solution.py:17
  73.2 1.8 convolution_convert_fusion
  75.0 1.3 fusion.10
  76.3 3.9 %bitcast_multiply_fusion = f32[2048,1024]{1,0:T(8,128)} fusion(f32[16,128,1024]{2,1,0:T(8,128)S(1)} %fusion.10, f32[2048]{0:T(1024)S(1)} %get-tuple-element.3), kind=kLoop, calls=%fused_computation | loop fusion | flops 2097152 | bytes 16785408 | tf_op jit(solution)/shard_map/mul | solution.py:131
  80.4 34.7 %all-gather.5.cloned.1.call-done = bf16[2048,1024]{1,0:T(8,128)(2,1)} async-done(((bf16[128,1024]{1,0:T(8,128)(2,1)}), bf16[2048,1024]{1,0:T(8,128)(2,1)}) %all-gather.5.cloned.1.call-update) | async-done | bytes 4194320 | tf_op jit(solution)/shard_map/all_gather | solution.py:92
  115.1 2.9 multiply_convert_fusion
  118.1 1.0 convolution_convert_fusion.1
  119.1 1.8 fusion.1
  120.9 1.8 convolution_bitcast_fusion
  122.8 1.3 copy-done.6
  124.1 1.9 convolution_bitcast_fusion.1
  126.4 2.5 convolution_bitcast_fusion.2
  128.9 3.4 %pad_maximum_fusion = f32[512,3,1024]{2,0,1:T(8,128)} fusion(f32[512,1,1024]{2,0,1:T(8,128)S(1)} %convolution_bitcast_fusion, f32[512,1,1024]{2,0,1:T(8,128)S(1)} %convolution_bitcast_fusion.1, f32[512,1,1024]{2,0,1:T(8,128)S(1)} %convolution_bitcast_fusion.2), kind=kLoop, calls=%fused_computation.2 | loop fusion | flops 3145728 | bytes 12582912 | tf_op jit(solution)/shard_map/stack | solution.py:37
  132.2 90.1 %reduce-scatter.3.cloned.1.call-done = f32[128,1024]{1,0:T(8,128)} async-done(((f32[2048,1024]{1,0:T(8,128)}), f32[128,1024]{1,0:T(8,128)}) %reduce-scatter.3.cloned.1.call-update) | async-done | bytes 524304 | tf_op jit(solution)/shard_map/reduce_scatter | solution.py:132
  222.4 1.8 convert_element_type.49
  224.2 77.8 %reduce-scatter.5.cloned.1.call-done = f32[256,3,1024]{2,0,1:T(8,128)} async-done(((f32[512,3,1024]{2,0,1:T(8,128)}), f32[256,3,1024]{2,0,1:T(8,128)}) %reduce-scatter.5.cloned.1.call-update) | async-done | bytes 3145744 | tf_op jit(solution)/shard_map/reduce_scatter | solution.py:42
  (26 shorter events, 2.5 us)
Async XLA Ops:
  7.2 66.0 %copy-start = (bf16[1,512,1024]{2,1,0:T(8,128)(2,1)S(1)}, bf16[1,512,1024]{2,1,0:T(8,128)(2,1)}, u32[]{:S(2)}) copy-start(bf16[1,512,1024]{2,1,0:T(8,128)(2,1)} %param.17) | copy-start | bytes 3145732
  7.2 56.7 %all-gather.3.cloned.1.call-start = ((), (), s32[]{:S(2)}) async-start(), calls=%async_computation.2 | async-start | bytes 4456448 | tf_op jit(solution)/shard_map/all_gather | solution.py:90
  7.9 107.2 %all-gather.5.cloned.1.call-start = ((), (), s32[]{:S(2)}) async-start(), calls=%async_computation.4 | async-start | bytes 4456448 | tf_op jit(solution)/shard_map/all_gather | solution.py:92
  8.7 213.7 %reduce-scatter.3.cloned.1.call-start = ((), (), s32[]{:S(2)}) async-start(), calls=%async_computation.3 | async-start | bytes 8912896 | tf_op jit(solution)/shard_map/reduce_scatter | solution.py:132
  63.9 3.3 %copy-start.3 = (bf16[1,512,1024]{2,1,0:T(8,128)(2,1)S(1)}, bf16[1,512,1024]{2,1,0:T(8,128)(2,1)}, u32[]{:S(2)}) copy-start(bf16[1,512,1024]{2,1,0:T(8,128)(2,1)} %param.15) | copy-start | bytes 3145732
  67.2 1.9 copy-start.1
  67.2 2.0 copy-start.4
  69.2 3.9 %copy-start.5 = (f32[1536,512]{1,0:T(8,128)}, f32[1536,512]{1,0:T(8,128)S(1)}, u32[]{:S(2)}) copy-start(f32[1536,512]{1,0:T(8,128)S(1)} %fusion.6) | copy-start | bytes 9437188
  80.2 221.8 %reduce-scatter.5.cloned.1.call-start = ((), (), s32[]{:S(2)}) async-start(), calls=%async_computation.5 | async-start | bytes 9437184 | tf_op jit(solution)/shard_map/reduce_scatter | solution.py:42
  120.9 1.9 copy-start.2
  120.9 3.2 %copy-start.6 = (f32[1536,512]{1,0:T(8,128)S(1)}, f32[1536,512]{1,0:T(8,128)}, u32[]{:S(2)}) copy-start(f32[1536,512]{1,0:T(8,128)} %copy-done.5) | copy-start | bytes 9437188
  124.1 2.3 copy-start.7
Sparse Core Ops, SparseCore 0:
  10.2 53.6 all-gather.2
  66.1 49.0 all-gather.4
  119.2 103.1 reduce-scatter.2
  225.1 76.7 reduce-scatter.4

commit v3 on v2

--- a/solution.py
+++ b/solution.py
@@ -4,7 +4,6 @@
 from jax.sharding import PartitionSpec as P
 
 GATHER_ROWS = 2048
-RETURN = "scatter"
 
 
 def contract_rows(left, right):
@@ -76,26 +75,60 @@
     return summed.astype(jnp.bfloat16), reduce_grads(grads, width)
 
 
+def exact_pieces(values):
+    high = lax.reduce_precision(values, exponent_bits=8, mantissa_bits=7)
+    rest = values - high
+    middle = lax.reduce_precision(rest, exponent_bits=8, mantissa_bits=7)
+    low = rest - middle
+    return [part.astype(jnp.bfloat16) for part in (high, middle, low)]
+
+
+def joined(pieces):
+    total = pieces[0].astype(jnp.float32) + pieces[1].astype(jnp.float32)
+    return total + pieces[2].astype(jnp.float32)
+
+
+def gather_replica(values):
+    mine = lax.all_gather(values, "ez", axis=0, tiled=True)
+    other = lax.ppermute(mine, "core", [(0, 1), (1, 0)])
+    return jnp.concatenate([mine, other], axis=0)
+
+
+def reduce_grads_dp(grad_half, width):
+    ndp = lax.axis_size("dp")
+    if ndp != 2:
+        grads = jnp.concatenate([grad_half(h) for h in range(ndp)], axis=0)
+        return reduce_grads(grads, width)
+    d = lax.axis_index("dp")
+    sent = lax.ppermute(grad_half(1 - d), "dp", [(0, 1), (1, 0)])
+    summed = grad_half(d) + sent
+    return summed.reshape(1, summed.shape[0], 3, width)
+
+
 def local_gather(tokens, masked, importance, routes, gates, cotangent, w_gate, w_up, w_down):
     tok_rows = tokens.shape[0]
     width = tokens.shape[1]
     topk = routes.shape[1]
-    experts = lax.axis_size("expert")
+    ncore = lax.axis_size("core")
+    nchip = lax.axis_size("ez")
+    experts = nchip * ncore
     capacity = min(tok_rows, 3 * tok_rows * topk // (2 * experts))
-    me = lax.axis_index("expert")
+    core = lax.axis_index("core")
+    me = lax.axis_index("ez") * ncore + core
     coef = importance * masked.astype(jnp.float32)
     factor = coef[:, None] * gates
-    meta = jnp.concatenate([routes.astype(jnp.float32), factor, gates], axis=1)
-
-    all_x = lax.all_gather(tokens, "expert", axis=0, tiled=True)
-    all_meta = lax.all_gather(meta, "expert", axis=0, tiled=True)
-    all_c = lax.all_gather(cotangent, "expert", axis=0, tiled=True)
-
-    all_routes = all_meta[:, :topk].astype(jnp.int32)
-    hit = all_routes == me
+    meta = [routes.astype(jnp.bfloat16)] + exact_pieces(factor) + exact_pieces(gates)
+    pad = (-topk * len(meta)) % 128
+    meta.append(jnp.zeros((tok_rows, pad), jnp.bfloat16))
+    packed = jnp.concatenate([tokens] + meta, axis=1)
+
+    all_p = gather_replica(packed)
+    all_c = gather_replica(cotangent)
+    all_x = all_p[:, :width]
+    cols = [all_p[:, width + topk * i: width + topk * (i + 1)] for i in range(7)]
+    hit = cols[0].astype(jnp.int32) == me
     zero = jnp.zeros((), jnp.float32)
-    fac = jnp.sum(jnp.where(hit, all_meta[:, topk:2 * topk], zero), axis=1)
-    gte = jnp.sum(jnp.where(hit, all_meta[:, 2 * topk:], zero), axis=1)
+    fac = jnp.sum(jnp.where(hit, joined(cols[1:4]), zero), axis=1)
     routed = jnp.any(hit, axis=1).reshape(experts, tok_rows)
     ahead = (
         lax.broadcasted_iota(jnp.int32, (tok_rows, tok_rows), 0)
@@ -119,52 +152,73 @@
     rows_x = select(all_x)
     all_q = (fac[:, None] * all_c.astype(jnp.float32)).astype(jnp.bfloat16)
     rows_q = select(all_q)
-    expert_out, grads = expert_math(rows_x, rows_q, w_gate[0], w_up[0], w_down[0])
-
-    if RETURN == "scatter":
-        dense = jnp.einsum(
-            "sjt,sjd->std",
-            pick,
-            expert_out.reshape(experts, capacity, width),
-            preferred_element_type=jnp.float32,
-        ).reshape(experts * tok_rows, width)
-        contrib = gte[:, None] * dense
-        summed = lax.psum_scatter(contrib, "expert", scatter_dimension=0, tiled=True)
-    else:
-        returned = lax.all_to_all(
-            expert_out.reshape(experts, capacity, width), "expert", 0, 0, tiled=True
+    wgate, wup, wdown = w_gate[0], w_up[0], w_down[0]
+    gate_pre = contract_cols(rows_x, wgate)
+    up_pre = contract_cols(rows_x, wup)
+    sig = jax.nn.sigmoid(gate_pre)
+    act = gate_pre * sig
+    hidden = (act * up_pre).astype(jnp.bfloat16)
+    expert_out = jnp.dot(hidden, wdown, preferred_element_type=jnp.float32).astype(
+        jnp.bfloat16
+    )
+
+    by_group = expert_out.reshape(ncore, nchip, capacity, width)
+    ordered = jnp.stack(
+        [lax.dynamic_index_in_dim(by_group, k ^ core, 0, keepdims=False) for k in range(ncore)],
+        axis=1,
+    ).reshape(experts, capacity, width)
+    returned = lax.all_to_all(ordered, ("ez", "core"), 0, 0, tiled=True)
+
+    back = contract_cols(rows_q, wdown)
+    d_gate = (back * up_pre * sig * (1.0 + gate_pre * (1.0 - sig))).astype(jnp.bfloat16)
+    d_up = (back * act).astype(jnp.bfloat16)
+    share = d_gate.shape[1] // lax.axis_size("dp")
+
+    def grad_half(h):
+        def part(v):
+            return lax.dynamic_slice_in_dim(v, h * share, share, axis=1)
+
+        return jnp.stack(
+            [
+                contract_rows(part(d_gate), rows_x),
+                contract_rows(part(d_up), rows_x),
+                contract_rows(part(hidden), rows_q),
+            ],
+            axis=1,
         )
-        flat, slots = source_slots(routes, experts)
-        target = flat * capacity + slots
-        choose = (
-            target[:, None]
-            == lax.broadcasted_iota(jnp.int32, (tok_rows * topk, experts * capacity), 1)
-        ).astype(jnp.bfloat16)
-        picked = jnp.dot(
-            choose, returned.reshape(-1, width), preferred_element_type=jnp.float32
-        )
-        summed = jnp.sum(picked.reshape(tok_rows, topk, width) * gates[:, :, None], axis=1)
-    return summed.astype(jnp.bfloat16), reduce_grads(grads, width)
-
-
-def local(*args):
-    tokens = args[0]
-    if lax.axis_size("expert") * tokens.shape[0] <= GATHER_ROWS:
-        return local_gather(*args)
-    return local_a2a(*args)
+
+    weight_grads = reduce_grads_dp(grad_half, width)
+
+    flat, slots = source_slots(routes, experts)
+    target = flat * capacity + slots
+    choose = (
+        target[:, None]
+        == lax.broadcasted_iota(jnp.int32, (tok_rows * topk, experts * capacity), 1)
+    ).astype(jnp.bfloat16)
+    picked = jnp.dot(choose, returned.reshape(-1, width), preferred_element_type=jnp.float32)
+    summed = jnp.sum(picked.reshape(tok_rows, topk, width) * gates[:, :, None], axis=1)
+    return summed.astype(jnp.bfloat16), weight_grads
+
+
+def specs(rows, experts):
+    return (
+        (P(rows, None), P(rows), P(rows), P(rows, None), P(rows, None), P(rows, None))
+        + (P(experts, None, None),) * 3,
+        (P(rows, None), P(experts, "dp", None, None)),
+    )
 
 
 def solution(mesh):
-    in_specs = (
-        P(("dp", "expert"), None),
-        P(("dp", "expert")),
-        P(("dp", "expert")),
-        P(("dp", "expert"), None),
-        P(("dp", "expert"), None),
-        P(("dp", "expert"), None),
-        P("expert", None, None),
-        P("expert", None, None),
-        P("expert", None, None),
-    )
-    out_specs = (P(("dp", "expert"), None), P("expert", "dp", None, None))
-    return jax.shard_map(local, mesh=mesh, in_specs=in_specs, out_specs=out_specs, check_vma=False)
+    ndp, nexp = mesh.shape["dp"], mesh.shape["expert"]
+    split = jax.sharding.Mesh(mesh.devices.reshape(ndp, nexp // 2, 2), ("dp", "ez", "core"))
+    ins, outs = specs(("dp", "ez", "core"), ("ez", "core"))
+    gathered = jax.shard_map(local_gather, mesh=split, in_specs=ins, out_specs=outs, check_vma=False)
+    ins, outs = specs(("dp", "expert"), "expert")
+    routed = jax.shard_map(local_a2a, mesh=mesh, in_specs=ins, out_specs=outs, check_vma=False)
+
+    def run(*args):
+        if args[0].shape[0] // ndp <= GATHER_ROWS:
+            return gathered(*args)
+        return routed(*args)
+
+    return run

time: 309 us -> 239 us (0.77)
  waiting for transfers between devices: 232 us -> 161 us
  blocking collectives: 23.8 us -> 0 us
  local copies, waits for them, and re-layouts: 1.87 us -> 9.72 us
  matrix products: 21.4 us -> 28.4 us
  starting transfers between devices: 0.34 us -> 6.06 us
  other arithmetic: 14.7 us -> 18.5 us
    reduce_scatter x2 -> x0, waiting for transfers between devices: 168 us -> none  [the longest x1 90.1 us: local_gather(): lax.psum_scatter(contrib, 'expert', scatter_dimension=0, tiled=True)]
    ppermute x0 -> x3, waiting for transfers between devices: none -> 63.8 us  [the longest x1 63.4 us: reduce_grads_dp(): sent = lax.ppermute(grad_half(1 - d), 'dp', [(0, 1), (1, 0)])]
    all_gather x2, waiting for transfers between devices: 63.1 us -> 96.6 us  [gather_replica(): mine = lax.all_gather(values, 'ez', axis=0, tiled=True)]
    all_gather x1 -> x0, blocking collectives: 23.8 us -> none  [local_gather(): all_meta = lax.all_gather(meta, 'expert', axis=0, tiled=True)]
    another operation x1 -> x5, other arithmetic: 3.36 us -> 8.53 us  [the longest x3 4.64 us: run(): return gathered(*args)]
    dot_general x2, matrix products: 3.14 us -> 8.25 us  [the longest x1 6.43 us: local_gather(): jnp.dot(choose, returned.reshape(-1, width), preferred_element_type=jnp.f...]
    convert_element_type x3 -> x2, other arithmetic: 5.39 us -> 0.7 us  [the longest x1 0.69 us: exact_pieces(): return [part.astype(jnp.bfloat16) for part in (high, middle, low)]]
    mul x2 -> x0, other arithmetic: 4.54 us -> none  [the longest x1 3.85 us: local_gather(): contrib = gte[:, None] * dense]
  transfers between devices with their start and end apart: 4 -> 6, of which waited for: 4 -> 4; matrix products, arithmetic and copies ran while one was open for 12% -> 13% of each run, Pallas kernels for 0% -> 0%
where the time goes in v3:
time: 239 us; the launch traced here: 238 us
  waiting for transfers between devices  161 us (67%)
  matrix products  28.4 us (12%)
  other arithmetic  18.5 us (8%)
  between operations  14.3 us (6%)
  local copies, waits for them, and re-layouts  9.72 us (4%)
  starting transfers between devices  6.06 us (3%)
    all_gather x2, waiting for transfers between devices, gather_replica(): mine = lax.all_gather(values, 'ez', axis=0, tiled=True)  96.6 us
    ppermute x1, waiting for transfers between devices, reduce_grads_dp(): sent = lax.ppermute(grad_half(1 - d), 'dp', [(0, 1), (1, 0)])  63.4 us
    dot_general x6, matrix products, contract_rows(): lax.dot_general(left, right, (((0,), (0,)), ((), ())), preferred_element_...  9.59 us
    dot_general x3, matrix products, contract_cols(): lax.dot_general(left, right, (((1,), (1,)), ((), ())), preferred_element_...  8.29 us
    dot_general x1, matrix products, local_gather(): jnp.dot(choose, returned.reshape(-1, width), preferred_element_type=jnp.f...  6.43 us
    unnamed x32, local copies, waits for them, and re-layouts  5.12 us
  transfers between devices with their start and end apart: 6, of which 4 were waited for; matrix products, arithmetic and copies ran while one was open for 13% of the time, Pallas kernels for 0%

profile of v3, /device:TPU:0, one launch (start us, length us, event | category | flops | bytes accessed | tf_op | source)
XLA Modules:
  0.0 238.1 jit_solution(3759558274556590759)
XLA Ops:
  8.9 4.5 %reduce-window.6 = s32[16,8,128]{2,1,0:T(8,128)S(1)} reduce-window(s32[16,8,128]{2,1,0:T(8,128)S(1)} %fusion.38, s32[]{:T(128)} %constant.14.clone.1), window={size=1x1x128 pad=0_0x0_0x127_0}, to_apply=%region_0.1 | reduce-window | flops 2080768 | bytes 131076 | tf_op jit(solution)/shard_map/reduce-window | solution.py:221
  17.1 1.8 concatenate.9
  18.9 43.2 %all-gather.5.cloned.1.call-done = bf16[1024,1024]{1,0:T(8,128)(2,1)} async-done(((bf16[128,1024]{1,0:T(8,128)(2,1)}), bf16[1024,1024]{1,0:T(8,128)(2,1)}) %all-gather.5.cloned.1.call-update) | async-done | bytes 2097168 | tf_op jit(solution)/shard_map/all_gather | solution.py:92
  62.2 53.3 %all-gather.3.cloned.1.call-done = bf16[1024,1152]{1,0:T(8,128)(2,1)} async-done(((bf16[128,1152]{1,0:T(8,128)(2,1)}), bf16[1024,1152]{1,0:T(8,128)(2,1)}) %all-gather.3.cloned.1.call-update) | async-done | bytes 2359312 | tf_op jit(solution)/shard_map/all_gather | solution.py:92
  115.5 2.0 constant_dynamic-update-slice_fusion.1
  117.8 2.0 pad_maximum_fusion
  123.8 1.8 fusion.18
  125.7 1.2 fusion.10
  126.9 1.8 fusion.15
  128.8 4.6 %multiply_convert_fusion.1 = (bf16[1536,512]{1,0:T(8,128)(2,1)}, bf16[1536,512]{1,0:T(8,128)(2,1)}, bf16[1536,512]{1,0:T(8,128)(2,1)S(1)}) fusion(f32[1536,512]{1,0:T(8,128)S(1)} %fusion.15, f32[1536,512]{1,0:T(8,128)S(1)} %fusion.18, bf16[1536,1024]{1,0:T(8,128)(2,1)S(1)} %bitcast.83, bf16[1,512,1024]{2,1,0:T(8,128)(2,1)S(1)} %copy-done), kind=kOutput, calls=%fused_computation.15 | convolution fusion | flops 1622409216 | bytes 15204352 | tf_op jit(solution)/shard_map/dot_general | solution.py:16
  133.4 1.8 convolution_convert_fusion
  135.6 2.0 pad_maximum_fusion.1
  137.5 4.5 %all-to-all-start = ((bf16[16,96,1024]{2,1,0:T(8,128)(2,1)}), bf16[16,96,1024]{2,1,0:T(8,128)(2,1)}, u32[]{:S(2)}, u32[]{:S(2)}) async-start(bf16[16,96,1024]{2,1,0:T(8,128)(2,1)} %bitcast.12), calls=%async_computation | async-start | bytes 6291456 | tf_op jit(solution)/shard_map/all_to_all | solution.py:170
  142.1 3.3 %convolution_bitcast_fusion = f32[256,1,1024]{2,0,1:T(8,128)S(1)} fusion(bf16[1536,1024]{1,0:T(8,128)(2,1)} %bitcast.89, bf16[1536,512]{1,0:T(8,128)(2,1)} %copy-done.10, s32[]{:T(128)S(6)} %select_n.25), kind=kOutput, calls=%fused_computation.24 | convolution fusion | flops 805306368 | bytes 4980740 | tf_op jit(solution)/shard_map/dot_general | solution.py:10
  145.6 1.0 convolution_bitcast_fusion.2
  146.8 1.0 convolution_bitcast_fusion.1
  147.8 1.9 pad_maximum_fusion.2
  149.8 1.5 collective-permute-start.2
  151.3 2.3 convolution_bitcast_fusion.5
  153.6 1.0 convolution_bitcast_fusion.4
  155.9 1.0 convolution_bitcast_fusion.3
  156.9 63.4 %collective-permute-done.2 = f32[256,3,1024]{2,0,1:T(8,128)} collective-permute-done((f32[256,3,1024]{2,0,1:T(8,128)}, f32[256,3,1024]{2,0,1:T(8,128)}, u32[]{:S(2)}, u32[]{:S(2)}) %collective-permute-start.2) | collective-permute-done | bytes 3145760 | tf_op jit(solution)/shard_map/ppermute | solution.py:103
  220.3 4.5 %fusion.7 = f32[1,256,3,1024]{3,1,2,0:T(8,128)} fusion(f32[256,3,1024]{2,0,1:T(8,128)} %collective-permute-done.2, f32[256,1,1024]{2,0,1:T(8,128)S(1)} %convolution_bitcast_fusion.3, f32[256,1,1024]{2,0,1:T(8,128)S(1)} %convolution_bitcast_fusion.4, f32[256,1,1024]{2,0,1:T(8,128)S(1)} %convolution_bitcast_fusion.5), kind=kLoop, calls=%fused_computation.12 | loop fusion | flops 2359296 | bytes 9437184 | tf_op jit(solution)/shard_map/reshape | solution.py:105
  224.8 6.4 %multiply_reduce_fusion = bf16[128,1024]{1,0:T(8,128)(2,1)} fusion(f32[128,8]{0,1:T(8,128)S(1)} %copy-done.7, bf16[1536,1024,1]{1,0,2:T(8,128)(2,1)} %bitcast.14, s32[128,8]{0,1:T(8,128)S(1)} %get-tuple-element.10), kind=kOutput, calls=%fused_computation.8 | convolution fusion | flops 3224764416 | bytes 3416064 | tf_op jit(solution)/shard_map/dot_general | solution.py:198
  (70 shorter events, 11.7 us)
Async XLA Ops:
  7.2 121.6 %copy-start = (bf16[1,512,1024]{2,1,0:T(8,128)(2,1)S(1)}, bf16[1,512,1024]{2,1,0:T(8,128)(2,1)}, u32[]{:S(2)}) copy-start(bf16[1,512,1024]{2,1,0:T(8,128)(2,1)} %param.15) | copy-start | bytes 3145732
  7.2 55.0 %all-gather.5.cloned.1.call-start = ((), (), s32[]{:S(2)}) async-start(), calls=%async_computation.2 | async-start | bytes 2359296 | tf_op jit(solution)/shard_map/all_gather | solution.py:92
  7.9 107.6 %all-gather.3.cloned.1.call-start = ((), (), s32[]{:S(2)}) async-start(), calls=%async_computation.1 | async-start | bytes 2654208 | tf_op jit(solution)/shard_map/all_gather | solution.py:92
  62.2 55.4 %collective-permute-start.1 = (bf16[1024,1024]{1,0:T(8,128)(2,1)}, bf16[1024,1024]{1,0:T(8,128)(2,1)}, u32[]{:S(2)}, u32[]{:S(2)}) collective-permute-start(bf16[1024,1024]{1,0:T(8,128)(2,1)} %all-gather.5.cloned.1.call-done), channel_id=1, source_target_pairs={{0,1},{1,0},{2,3},{3,2},{4,5},{5,4},{6,7},{7,6},{8,9},{9,8},{10,11... | collective-permute-start | bytes 6291464 | tf_op jit(solution)/shard_map/ppermute | solution.py:93
  115.5 4.7 %collective-permute-start = (bf16[1024,1152]{1,0:T(8,128)(2,1)}, bf16[1024,1152]{1,0:T(8,128)(2,1)S(1)}, u32[]{:S(2)}, u32[]{:S(2)}) collective-permute-start(bf16[1024,1152]{1,0:T(8,128)(2,1)} %all-gather.3.cloned.1.call-done), channel_id=1, source_target_pairs={{0,1},{1,0},{2,3},{3,2},{4,5},{5,4},{6,7},{7,6},{8,9},{9,8},{10,11... | collective-permute-start | bytes 7077896 | tf_op jit(solution)/shard_map/ppermute | solution.py:93
  115.5 2.3 copy-start.6
  122.6 1.2 copy-start.8
  123.6 5.2 %copy-start.2 = (bf16[16,96,1024]{2,1,0:T(8,128)(2,1)}, bf16[16,96,1024]{2,1,0:T(8,128)(2,1)S(1)}, u32[]{:S(2)}) copy-start(bf16[16,96,1024]{2,1,0:T(8,128)(2,1)S(1)} %convolution_convert_fusion.1) | copy-start | bytes 9437188
  125.7 1.2 copy-start.9
  126.9 6.5 %copy-start.4 = (bf16[16,96,1024]{2,1,0:T(8,128)(2,1)}, bf16[16,96,1024]{2,1,0:T(8,128)(2,1)S(1)}, u32[]{:S(2)}) copy-start(bf16[16,96,1024]{2,1,0:T(8,128)(2,1)S(1)} %fusion.10) | copy-start | bytes 9437188
  133.4 2.2 copy-start.10
  137.5 87.3 %all-to-all-start = ((bf16[16,96,1024]{2,1,0:T(8,128)(2,1)}), bf16[16,96,1024]{2,1,0:T(8,128)(2,1)}, u32[]{:S(2)}, u32[]{:S(2)}) async-start(bf16[16,96,1024]{2,1,0:T(8,128)(2,1)} %bitcast.12), calls=%async_computation | async-start | bytes 6291456 | tf_op jit(solution)/shard_map/all_to_all | solution.py:170
  142.0 3.3 %copy-start.3 = (bf16[16,96,1024]{2,1,0:T(8,128)(2,1)S(1)}, bf16[16,96,1024]{2,1,0:T(8,128)(2,1)}, u32[]{:S(2)}) copy-start(bf16[16,96,1024]{2,1,0:T(8,128)(2,1)} %copy-done.2) | copy-start | bytes 9437188
  142.1 3.5 %copy-start.14 = (bf16[1536,512]{1,0:T(8,128)(2,1)S(1)}, bf16[1536,512]{1,0:T(8,128)(2,1)}, u32[]{:S(2)}) copy-start(bf16[1536,512]{1,0:T(8,128)(2,1)} %get-tuple-element.2) | copy-start | bytes 4718596
  145.4 1.5 copy-start.12
  149.8 70.5 %collective-permute-start.2 = (f32[256,3,1024]{2,0,1:T(8,128)}, f32[256,3,1024]{2,0,1:T(8,128)}, u32[]{:S(2)}, u32[]{:S(2)}) collective-permute-start(f32[256,3,1024]{2,0,1:T(8,128)} %pad_maximum_fusion.2), channel_id=1, source_target_pairs={{0,16},{16,0},{1,17},{17,1},{2,18},{18,2},{3,19},{19,3},{4,20},{20... | collective-permute-start | bytes 9437192 | tf_op jit(solution)/shard_map/ppermute | solution.py:103
  151.3 2.3 copy-start.13
  153.5 1.9 copy-start.5
  153.5 2.3 copy-start.11
  156.9 67.9 %copy-start.7 = (f32[128,8]{0,1:T(8,128)S(1)}, f32[128,8]{0,1:T(8,128)}, u32[]{:S(2)}) copy-start(f32[128,8]{0,1:T(8,128)} %param.13) | copy-start | bytes 12292
  224.8 6.4 %copy-start.1 = (bf16[1,512,1024]{2,1,0:T(8,128)(2,1)S(1)}, bf16[1,512,1024]{2,1,0:T(8,128)(2,1)}, u32[]{:S(2)}) copy-start(bf16[1,512,1024]{2,1,0:T(8,128)(2,1)} %param.15) | copy-start | bytes 3145732
Sparse Core Ops, SparseCore 0:
  10.1 51.9 all-gather.4
  64.9 50.5 all-gather.2

commit v4 on v3

--- a/solution.py
+++ b/solution.py
@@ -120,12 +120,12 @@
     meta = [routes.astype(jnp.bfloat16)] + exact_pieces(factor) + exact_pieces(gates)
     pad = (-topk * len(meta)) % 128
     meta.append(jnp.zeros((tok_rows, pad), jnp.bfloat16))
-    packed = jnp.concatenate([tokens] + meta, axis=1)
+    packed = jnp.concatenate([tokens, cotangent] + meta, axis=1)
 
     all_p = gather_replica(packed)
-    all_c = gather_replica(cotangent)
     all_x = all_p[:, :width]
-    cols = [all_p[:, width + topk * i: width + topk * (i + 1)] for i in range(7)]
+    all_c = all_p[:, width:2 * width]
+    cols = [all_p[:, 2 * width + topk * i: 2 * width + topk * (i + 1)] for i in range(7)]
     hit = cols[0].astype(jnp.int32) == me
     zero = jnp.zeros((), jnp.float32)
     fac = jnp.sum(jnp.where(hit, joined(cols[1:4]), zero), axis=1)

time: 239 us -> 230 us (0.962)
  waiting for transfers between devices: 161 us -> 146 us
  matrix products: 28.4 us -> 33.2 us
    all_gather x2 -> x1, waiting for transfers between devices: 96.6 us -> 79.5 us  [gather_replica(): mine = lax.all_gather(values, 'ez', axis=0, tiled=True)]
    dot_general x6, matrix products: 9.59 us -> 14.7 us  [contract_rows(): lax.dot_general(left, right, (((0,), (0,)), ((), ())), preferred_element_...]
    ppermute x2 -> x1, waiting for transfers between devices: 0.41 us -> 5.29 us  [gather_replica(): other = lax.ppermute(mine, 'core', [(0, 1), (1, 0)])]
    concatenate x1, local copies, waits for them, and re-layouts: 0.36 us -> 2.89 us  [gather_replica(): return jnp.concatenate([mine, other], axis=0)]
    unnamed x32 -> x22, local copies, waits for them, and re-layouts: 5.12 us -> 4.71 us
  transfers between devices with their start and end apart: 6 -> 4, of which waited for: 4 -> 3; matrix products, arithmetic and copies ran while one was open for 13% -> 10% of each run, Pallas kernels for 0% -> 0%
where the time goes in v4:
time: 230 us; the launch traced here: 229 us
  waiting for transfers between devices  146 us (63%)
  matrix products  33.2 us (14%)
  other arithmetic  17.2 us (7%)
  between operations  14.3 us (6%)
  local copies, waits for them, and re-layouts  11.9 us (5%)
  starting transfers between devices  5.97 us (3%)
    all_gather x1, waiting for transfers between devices, gather_replica(): mine = lax.all_gather(values, 'ez', axis=0, tiled=True)  79.5 us
    ppermute x1, waiting for transfers between devices, reduce_grads_dp(): sent = lax.ppermute(grad_half(1 - d), 'dp', [(0, 1), (1, 0)])  61.6 us
    dot_general x6, matrix products, contract_rows(): lax.dot_general(left, right, (((0,), (0,)), ((), ())), preferred_element_...  14.7 us
    dot_general x3, matrix products, contract_cols(): lax.dot_general(left, right, (((1,), (1,)), ((), ())), preferred_element_...  8.12 us
    dot_general x1, matrix products, local_gather(): jnp.dot(choose, returned.reshape(-1, width), preferred_element_type=jnp.f...  6.44 us
    ppermute x1, waiting for transfers between devices, gather_replica(): other = lax.ppermute(mine, 'core', [(0, 1), (1, 0)])  5.29 us
    unnamed x22, local copies, waits for them, and re-layouts  4.71 us
    another operation x3, other arithmetic, run(): return gathered(*args)  4.64 us
  transfers between devices with their start and end apart: 4, of which 3 were waited for; matrix products, arithmetic and copies ran while one was open for 10% of the time, Pallas kernels for 0%

profile of v4, /device:TPU:0, one launch (start us, length us, event | category | flops | bytes accessed | tf_op | source)
XLA Modules:
  0.0 229.0 jit_solution(8494265381474410725)
XLA Ops:
  8.3 4.5 %reduce-window.6 = s32[16,8,128]{2,1,0:T(8,128)S(1)} reduce-window(s32[16,8,128]{2,1,0:T(8,128)S(1)} %fusion.31, s32[]{:T(128)} %constant.14.clone.1), window={size=1x1x128 pad=0_0x0_0x127_0}, to_apply=%region_0.1 | reduce-window | flops 2080768 | bytes 131076 | tf_op jit(solution)/shard_map/reduce-window | solution.py:221
  16.4 1.9 concatenate.6
  18.4 79.5 %all-gather.2.cloned.1.call-done = bf16[1024,2176]{1,0:T(8,128)(2,1)} async-done(((bf16[128,2176]{1,0:T(8,128)(2,1)}), bf16[1024,2176]{1,0:T(8,128)(2,1)}) %all-gather.2.cloned.1.call-update) | async-done | bytes 4456464 | tf_op jit(solution)/shard_map/all_gather | solution.py:92
  97.9 2.6 %constant_dynamic-update-slice_fusion.1 = bf16[2048,2176]{1,0:T(8,128)(2,1)S(1)} fusion(bf16[1024,2176]{1,0:T(8,128)(2,1)} %all-gather.2.cloned.1.call-done), kind=kLoop, calls=%fused_computation.59 | loop fusion | bytes 8912896
  100.5 5.3 %collective-permute-done = bf16[1024,2176]{1,0:T(8,128)(2,1)} collective-permute-done((bf16[1024,2176]{1,0:T(8,128)(2,1)}, bf16[1024,2176]{1,0:T(8,128)(2,1)}, u32[]{:S(2)}, u32[]{:S(2)}) %collective-permute-start) | collective-permute-done | bytes 4456480 | tf_op jit(solution)/shard_map/ppermute | solution.py:93
  105.8 2.9 %constant_dynamic-update-slice_fusion = bf16[2048,2176]{1,0:T(8,128)(2,1)S(1)} fusion(bf16[2048,2176]{1,0:T(8,128)(2,1)S(1)} %constant_dynamic-update-slice_fusion.1, bf16[1024,2176]{1,0:T(8,128)(2,1)} %collective-permute-done), kind=kLoop, calls=%fused_computation.58 | loop fusion | bytes 8912896 | tf_op jit(solution)/shard_map/concatenate | solution.py:94
  113.5 1.0 copy-done.7
  114.5 1.9 fusion.11
  116.4 1.8 fusion.8
  118.2 4.4 %multiply_convert_fusion.2 = (bf16[1536,512]{1,0:T(8,128)(2,1)}, bf16[1536,512]{1,0:T(8,128)(2,1)}, bf16[1536,512]{1,0:T(8,128)(2,1)S(1)}) fusion(f32[1536,512]{1,0:T(8,128)S(1)} %fusion.8, f32[1536,512]{1,0:T(8,128)S(1)} %fusion.11, bf16[1536,1024]{1,0:T(8,128)(2,1)S(1)} %bitcast.85, bf16[1,512,1024]{2,1,0:T(8,128)(2,1)S(1)} %copy-done), kind=kOutput, calls=%fused_computation.11 | convolution fusion | flops 1622409216 | bytes 15204352 | tf_op jit(solution)/shard_map/dot_general | solution.py:16
  122.7 1.8 convolution_convert_fusion
  124.8 2.0 pad_maximum_fusion
  126.8 4.5 %all-to-all-start = ((bf16[16,96,1024]{2,1,0:T(8,128)(2,1)}), bf16[16,96,1024]{2,1,0:T(8,128)(2,1)}, u32[]{:S(2)}, u32[]{:S(2)}) async-start(bf16[16,96,1024]{2,1,0:T(8,128)(2,1)} %bitcast.12), calls=%async_computation | async-start | bytes 6291456 | tf_op jit(solution)/shard_map/all_to_all | solution.py:170
  131.3 2.9 %convolution_bitcast_fusion = f32[256,1,1024]{2,0,1:T(8,128)S(1)} fusion(bf16[1536,1024]{1,0:T(8,128)(2,1)} %bitcast.82, bf16[1536,512]{1,0:T(8,128)(2,1)S(1)} %get-tuple-element.4, s32[]{:T(128)S(6)} %select_n.25), kind=kOutput, calls=%fused_computation.20 | convolution fusion | flops 805306368 | bytes 4980740 | tf_op jit(solution)/shard_map/dot_general | solution.py:10
  134.2 3.3 %convolution_bitcast_fusion.2 = f32[256,1,1024]{2,0,1:T(8,128)S(1)} fusion(bf16[1536,1024]{1,0:T(8,128)(2,1)} %bitcast.86, bf16[1536,512]{1,0:T(8,128)(2,1)} %get-tuple-element.2, s32[]{:T(128)S(6)} %select_n.25), kind=kOutput, calls=%fused_computation.22 | convolution fusion | flops 805306368 | bytes 4980740 | tf_op jit(solution)/shard_map/dot_general | solution.py:10
  137.7 1.0 convolution_bitcast_fusion.1
  138.8 1.9 pad_maximum_fusion.1
  140.7 1.4 collective-permute-start.1
  142.1 3.1 %convolution_bitcast_fusion.5 = f32[256,1,1024]{2,0,1:T(8,128)S(1)} fusion(bf16[1536,1024]{1,0:T(8,128)(2,1)} %bitcast.87, bf16[1536,512]{1,0:T(8,128)(2,1)} %get-tuple-element.2, s32[]{:T(128)S(6)} %select_n.24), kind=kOutput, calls=%fused_computation.25 | convolution fusion | flops 805306368 | bytes 4980740 | tf_op jit(solution)/shard_map/dot_general | solution.py:10
  145.3 3.3 %convolution_bitcast_fusion.4 = f32[256,1,1024]{2,0,1:T(8,128)S(1)} fusion(bf16[1536,1024]{1,0:T(8,128)(2,1)} %bitcast.88, bf16[1536,512]{1,0:T(8,128)(2,1)} %get-tuple-element.3, s32[]{:T(128)S(6)} %select_n.24), kind=kOutput, calls=%fused_computation.24 | convolution fusion | flops 805306368 | bytes 4980740 | tf_op jit(solution)/shard_map/dot_general | solution.py:10
  148.6 1.0 convolution_bitcast_fusion.3
  149.6 61.6 %collective-permute-done.1 = f32[256,3,1024]{2,0,1:T(8,128)} collective-permute-done((f32[256,3,1024]{2,0,1:T(8,128)}, f32[256,3,1024]{2,0,1:T(8,128)}, u32[]{:S(2)}, u32[]{:S(2)}) %collective-permute-start.1) | collective-permute-done | bytes 3145760 | tf_op jit(solution)/shard_map/ppermute | solution.py:103
  211.2 4.5 %fusion.3 = f32[1,256,3,1024]{3,1,2,0:T(8,128)} fusion(f32[256,3,1024]{2,0,1:T(8,128)} %collective-permute-done.1, f32[256,1,1024]{2,0,1:T(8,128)S(1)} %convolution_bitcast_fusion.3, f32[256,1,1024]{2,0,1:T(8,128)S(1)} %convolution_bitcast_fusion.4, f32[256,1,1024]{2,0,1:T(8,128)S(1)} %convolution_bitcast_fusion.5), kind=kLoop, calls=%fused_computation.8 | loop fusion | flops 2359296 | bytes 9437184 | tf_op jit(solution)/shard_map/reshape | solution.py:105
  215.7 6.4 %multiply_reduce_fusion = bf16[128,1024]{1,0:T(8,128)(2,1)} fusion(f32[128,8]{0,1:T(8,128)S(1)} %copy-done.6, bf16[1536,1024,1]{1,0,2:T(8,128)(2,1)} %bitcast.14, s32[128,8]{0,1:T(8,128)S(1)} %get-tuple-element.10), kind=kOutput, calls=%fused_computation.4 | convolution fusion | flops 3224764416 | bytes 3416064 | tf_op jit(solution)/shard_map/dot_general | solution.py:198
  (55 shorter events, 10.0 us)
Async XLA Ops:
  7.2 111.1 %copy-start = (bf16[1,512,1024]{2,1,0:T(8,128)(2,1)S(1)}, bf16[1,512,1024]{2,1,0:T(8,128)(2,1)}, u32[]{:S(2)}) copy-start(bf16[1,512,1024]{2,1,0:T(8,128)(2,1)} %param.15) | copy-start | bytes 3145732
  7.2 90.7 %all-gather.2.cloned.1.call-start = ((), (), s32[]{:S(2)}) async-start(), calls=%async_computation.1 | async-start | bytes 5013504 | tf_op jit(solution)/shard_map/all_gather | solution.py:92
  97.9 7.9 %collective-permute-start = (bf16[1024,2176]{1,0:T(8,128)(2,1)}, bf16[1024,2176]{1,0:T(8,128)(2,1)}, u32[]{:S(2)}, u32[]{:S(2)}) collective-permute-start(bf16[1024,2176]{1,0:T(8,128)(2,1)} %all-gather.2.cloned.1.call-done), channel_id=1, source_target_pairs={{0,1},{1,0},{2,3},{3,2},{4,5},{5,4},{6,7},{7,6},{8,9},{9,8},{10,11... | collective-permute-start | bytes 13369352 | tf_op jit(solution)/shard_map/ppermute | solution.py:93
  112.5 5.8 %copy-start.4 = (bf16[16,96,1024]{2,1,0:T(8,128)(2,1)}, bf16[16,96,1024]{2,1,0:T(8,128)(2,1)S(1)}, u32[]{:S(2)}) copy-start(bf16[16,96,1024]{2,1,0:T(8,128)(2,1)S(1)} %convolution_convert_fusion.2) | copy-start | bytes 9437188
  112.5 2.0 copy-start.7
  113.5 2.9 %copy-start.2 = (bf16[16,96,1024]{2,1,0:T(8,128)(2,1)}, bf16[16,96,1024]{2,1,0:T(8,128)(2,1)S(1)}, u32[]{:S(2)}) copy-start(bf16[16,96,1024]{2,1,0:T(8,128)(2,1)S(1)} %convolution_convert_fusion.1) | copy-start | bytes 9437188
  114.5 1.9 copy-start.8
  126.8 88.9 %all-to-all-start = ((bf16[16,96,1024]{2,1,0:T(8,128)(2,1)}), bf16[16,96,1024]{2,1,0:T(8,128)(2,1)}, u32[]{:S(2)}, u32[]{:S(2)}) async-start(bf16[16,96,1024]{2,1,0:T(8,128)(2,1)} %bitcast.12), calls=%async_computation | async-start | bytes 6291456 | tf_op jit(solution)/shard_map/all_to_all | solution.py:170
  134.2 3.3 %copy-start.5 = (bf16[16,96,1024]{2,1,0:T(8,128)(2,1)S(1)}, bf16[16,96,1024]{2,1,0:T(8,128)(2,1)}, u32[]{:S(2)}) copy-start(bf16[16,96,1024]{2,1,0:T(8,128)(2,1)} %copy-done.4) | copy-start | bytes 9437188
  134.2 3.5 %copy-start.9 = (bf16[1536,512]{1,0:T(8,128)(2,1)S(1)}, bf16[1536,512]{1,0:T(8,128)(2,1)}, u32[]{:S(2)}) copy-start(bf16[1536,512]{1,0:T(8,128)(2,1)} %get-tuple-element.3) | copy-start | bytes 4718596
  140.7 70.5 %collective-permute-start.1 = (f32[256,3,1024]{2,0,1:T(8,128)}, f32[256,3,1024]{2,0,1:T(8,128)}, u32[]{:S(2)}, u32[]{:S(2)}) collective-permute-start(f32[256,3,1024]{2,0,1:T(8,128)} %pad_maximum_fusion.1), channel_id=1, source_target_pairs={{0,16},{16,0},{1,17},{17,1},{2,18},{18,2},{3,19},{19,3},{4,20},{20... | collective-permute-start | bytes 9437192 | tf_op jit(solution)/shard_map/ppermute | solution.py:103
  145.3 3.3 %copy-start.3 = (bf16[16,96,1024]{2,1,0:T(8,128)(2,1)S(1)}, bf16[16,96,1024]{2,1,0:T(8,128)(2,1)}, u32[]{:S(2)}) copy-start(bf16[16,96,1024]{2,1,0:T(8,128)(2,1)} %copy-done.2) | copy-start | bytes 9437188
  149.6 66.1 %copy-start.6 = (f32[128,8]{0,1:T(8,128)S(1)}, f32[128,8]{0,1:T(8,128)}, u32[]{:S(2)}) copy-start(f32[128,8]{0,1:T(8,128)} %param.13) | copy-start | bytes 12292
  215.7 6.4 %copy-start.1 = (bf16[1,512,1024]{2,1,0:T(8,128)(2,1)S(1)}, bf16[1,512,1024]{2,1,0:T(8,128)(2,1)}, u32[]{:S(2)}) copy-start(bf16[1,512,1024]{2,1,0:T(8,128)(2,1)} %param.15) | copy-start | bytes 3145732
Sparse Core Ops, SparseCore 0:
  18.5 79.3 all-gather.1

commit v5 on v4

--- a/solution.py
+++ b/solution.py
@@ -90,8 +90,19 @@
 
 def gather_replica(values):
     mine = lax.all_gather(values, "ez", axis=0, tiled=True)
-    other = lax.ppermute(mine, "core", [(0, 1), (1, 0)])
-    return jnp.concatenate([mine, other], axis=0)
+    return [mine, lax.ppermute(mine, "core", [(0, 1), (1, 0)])]
+
+
+def slots_by_rank(routes, experts):
+    tok_rows = routes.shape[0]
+    onehot = routes[:, :, None] == lax.broadcasted_iota(jnp.int32, (1, 1, experts), 2)
+    hits = jnp.any(onehot, axis=1).astype(jnp.bfloat16)
+    before = (
+        lax.broadcasted_iota(jnp.int32, (tok_rows, tok_rows), 0)
+        > lax.broadcasted_iota(jnp.int32, (tok_rows, tok_rows), 1)
+    ).astype(jnp.bfloat16)
+    rank = jnp.dot(before, hits, preferred_element_type=jnp.float32).astype(jnp.int32)
+    return jnp.sum(jnp.where(onehot, rank[:, None, :], 0), axis=2)
 
 
 def reduce_grads_dp(grad_half, width):
@@ -122,10 +133,9 @@
     meta.append(jnp.zeros((tok_rows, pad), jnp.bfloat16))
     packed = jnp.concatenate([tokens, cotangent] + meta, axis=1)
 
-    all_p = gather_replica(packed)
-    all_x = all_p[:, :width]
-    all_c = all_p[:, width:2 * width]
-    cols = [all_p[:, 2 * width + topk * i: 2 * width + topk * (i + 1)] for i in range(7)]
+    halves = gather_replica(packed)
+    all_p = jnp.concatenate([h[:, 2 * width:] for h in halves], axis=0)
+    cols = [all_p[:, topk * i: topk * (i + 1)] for i in range(7)]
     hit = cols[0].astype(jnp.int32) == me
     zero = jnp.zeros((), jnp.float32)
     fac = jnp.sum(jnp.where(hit, joined(cols[1:4]), zero), axis=1)
@@ -140,18 +150,25 @@
     slot_ids = lax.broadcasted_iota(jnp.int32, (experts, capacity, tok_rows), 1)
     pick = (routed[:, None, :] & (rank[:, None, :] == slot_ids)).astype(jnp.bfloat16)
 
-    def select(values):
-        rows = jnp.einsum(
-            "sjt,std->sjd",
-            pick,
-            values.reshape(experts, tok_rows, width),
-            preferred_element_type=jnp.float32,
-        )
-        return rows.astype(jnp.bfloat16).reshape(experts * capacity, width)
-
-    rows_x = select(all_x)
-    all_q = (fac[:, None] * all_c.astype(jnp.float32)).astype(jnp.bfloat16)
-    rows_q = select(all_q)
+    def select(part, scale=None):
+        picked = []
+        for h, half in enumerate(halves):
+            values = half[:, part * width:(part + 1) * width]
+            if scale is not None:
+                rows = slice(h * nchip * tok_rows, (h + 1) * nchip * tok_rows)
+                values = (scale[rows, None] * values.astype(jnp.float32)).astype(jnp.bfloat16)
+            picked.append(
+                jnp.einsum(
+                    "sjt,std->sjd",
+                    pick[h * nchip:(h + 1) * nchip],
+                    values.reshape(nchip, tok_rows, width),
+                    preferred_element_type=jnp.float32,
+                ).astype(jnp.bfloat16)
+            )
+        return jnp.concatenate(picked, axis=0).reshape(experts * capacity, width)
+
+    rows_x = select(0)
+    rows_q = select(1, fac)
     wgate, wup, wdown = w_gate[0], w_up[0], w_down[0]
     gate_pre = contract_cols(rows_x, wgate)
     up_pre = contract_cols(rows_x, wup)
@@ -189,8 +206,7 @@
 
     weight_grads = reduce_grads_dp(grad_half, width)
 
-    flat, slots = source_slots(routes, experts)
-    target = flat * capacity + slots
+    target = (routes * capacity + slots_by_rank(routes, experts)).reshape(-1)
     choose = (
         target[:, None]
         == lax.broadcasted_iota(jnp.int32, (tok_rows * topk, experts * capacity), 1)

time: 230 us -> 228 us (level)
    slice x3 -> x5, local copies, waits for them, and re-layouts: 0.79 us -> 5.47 us  [the longest x2 3.53 us: select(): values = half[:, part * width:(part + 1) * width]]
    another operation x3 -> x0, other arithmetic: 4.64 us -> none  [run(): return gathered(*args)]
    concatenate x1 -> x0, local copies, waits for them, and re-layouts: 2.89 us -> none  [gather_replica(): return jnp.concatenate([mine, other], axis=0)]
    unnamed x22 -> x20, local copies, waits for them, and re-layouts: 4.71 us -> 1.97 us
where the time goes in v5:
time: 228 us; the launch traced here: 227 us
  waiting for transfers between devices  146 us (64%)
  matrix products  33.6 us (15%)
  other arithmetic  16.5 us (7%)
  between operations  14.3 us (6%)
  local copies, waits for them, and re-layouts  10.6 us (5%)
  starting transfers between devices  5.96 us (3%)
    all_gather x1, waiting for transfers between devices, gather_replica(): mine = lax.all_gather(values, 'ez', axis=0, tiled=True)  79.5 us
    ppermute x1, waiting for transfers between devices, reduce_grads_dp(): sent = lax.ppermute(grad_half(1 - d), 'dp', [(0, 1), (1, 0)])  61.6 us
    dot_general x6, matrix products, contract_rows(): lax.dot_general(left, right, (((0,), (0,)), ((), ())), preferred_element_...  14.7 us
    dot_general x3, matrix products, contract_cols(): lax.dot_general(left, right, (((1,), (1,)), ((), ())), preferred_element_...  8.1 us
    dot_general x1, matrix products, local_gather(): jnp.dot(choose, returned.reshape(-1, width), preferred_element_type=jnp.f...  6.44 us
    ppermute x1, waiting for transfers between devices, gather_replica(): return [mine, lax.ppermute(mine, 'core', [(0, 1), (1, 0)])]  5.14 us
  transfers between devices with their start and end apart: 4, of which 3 were waited for; matrix products, arithmetic and copies ran while one was open for 10% of the time, Pallas kernels for 0%

profile of v5, /device:TPU:0, one launch (start us, length us, event | category | flops | bytes accessed | tf_op | source)
XLA Modules:
  0.0 227.2 jit_solution(11878411657250176341)
XLA Ops:
  11.9 1.9 concatenate.12
  13.9 79.5 %all-gather.2.cloned.1.call-done = bf16[1024,2176]{1,0:T(8,128)(2,1)} async-done(((bf16[128,2176]{1,0:T(8,128)(2,1)}), bf16[1024,2176]{1,0:T(8,128)(2,1)}) %all-gather.2.cloned.1.call-update) | async-done | bytes 4456464 | tf_op jit(solution)/shard_map/all_gather | solution.py:92
  94.3 1.8 slice.62
  96.1 5.1 %collective-permute-done = bf16[1024,2176]{1,0:T(8,128)(2,1)} collective-permute-done((bf16[1024,2176]{1,0:T(8,128)(2,1)}, bf16[1024,2176]{1,0:T(8,128)(2,1)}, u32[]{:S(2)}, u32[]{:S(2)}) %collective-permute-start) | collective-permute-done | bytes 4456480 | tf_op jit(solution)/shard_map/ppermute | solution.py:93
  103.6 1.8 slice.63
  106.6 2.6 %multiply_convert_fusion = (bf16[1024,1024]{1,0:T(8,128)(2,1)S(1)}, bf16[1024,1024]{1,0:T(8,128)(2,1)S(1)}) fusion(bf16[1024,2176]{1,0:T(8,128)(2,1)} %collective-permute-done, f32[1024]{0:T(1024)S(1)} %get-tuple-element.10, bf16[1024,2176]{1,0:T(8,128)(2,1)} %all-gather.2.cloned.1.call-done, f32[1024]{0:T(1024)S(1)} %get-tuple-element.9), kind=kLoop, calls=%fused_computation.3 | loop fusion | flops 6291456 | bytes 8396800 | tf_op jit(solution)/shard_map/convert_element_type | solution.py:159
  111.0 1.7 copy-done.7
  112.7 1.8 fusion.11
  114.5 1.8 fusion.8
  116.4 4.4 %multiply_convert_fusion.3 = (bf16[1536,512]{1,0:T(8,128)(2,1)}, bf16[1536,512]{1,0:T(8,128)(2,1)}, bf16[1536,512]{1,0:T(8,128)(2,1)S(1)}) fusion(f32[1536,512]{1,0:T(8,128)S(1)} %fusion.8, f32[1536,512]{1,0:T(8,128)S(1)} %fusion.11, bf16[1536,1024]{1,0:T(8,128)(2,1)S(1)} %bitcast.70, bf16[1,512,1024]{2,1,0:T(8,128)(2,1)S(1)} %copy-done), kind=kOutput, calls=%fused_computation.14 | convolution fusion | flops 1622409216 | bytes 15204352 | tf_op jit(solution)/shard_map/dot_general | solution.py:16
  120.8 1.8 convolution_convert_fusion
  123.0 2.0 pad_maximum_fusion.1
  125.0 4.5 %all-to-all-start = ((bf16[16,96,1024]{2,1,0:T(8,128)(2,1)}), bf16[16,96,1024]{2,1,0:T(8,128)(2,1)}, u32[]{:S(2)}, u32[]{:S(2)}) async-start(bf16[16,96,1024]{2,1,0:T(8,128)(2,1)} %bitcast.11), calls=%async_computation | async-start | bytes 6291456 | tf_op jit(solution)/shard_map/all_to_all | solution.py:187
  129.5 2.9 %convolution_bitcast_fusion = f32[256,1,1024]{2,0,1:T(8,128)S(1)} fusion(bf16[1536,1024]{1,0:T(8,128)(2,1)} %bitcast.67, bf16[1536,512]{1,0:T(8,128)(2,1)S(1)} %get-tuple-element.6, s32[]{:T(128)S(6)} %select_n.30), kind=kOutput, calls=%fused_computation.25 | convolution fusion | flops 805306368 | bytes 4980740 | tf_op jit(solution)/shard_map/dot_general | solution.py:10
  132.4 3.3 %convolution_bitcast_fusion.2 = f32[256,1,1024]{2,0,1:T(8,128)S(1)} fusion(bf16[1536,1024]{1,0:T(8,128)(2,1)} %bitcast.71, bf16[1536,512]{1,0:T(8,128)(2,1)} %get-tuple-element.4, s32[]{:T(128)S(6)} %select_n.30), kind=kOutput, calls=%fused_computation.27 | convolution fusion | flops 805306368 | bytes 4980740 | tf_op jit(solution)/shard_map/dot_general | solution.py:10
  135.9 1.0 convolution_bitcast_fusion.1
  137.0 1.9 pad_maximum_fusion.3
  138.9 1.4 collective-permute-start.1
  140.3 3.1 %convolution_bitcast_fusion.5 = f32[256,1,1024]{2,0,1:T(8,128)S(1)} fusion(bf16[1536,1024]{1,0:T(8,128)(2,1)} %bitcast.72, bf16[1536,512]{1,0:T(8,128)(2,1)} %get-tuple-element.4, s32[]{:T(128)S(6)} %select_n.29), kind=kOutput, calls=%fused_computation.30 | convolution fusion | flops 805306368 | bytes 4980740 | tf_op jit(solution)/shard_map/dot_general | solution.py:10
  143.5 3.3 %convolution_bitcast_fusion.4 = f32[256,1,1024]{2,0,1:T(8,128)S(1)} fusion(bf16[1536,1024]{1,0:T(8,128)(2,1)} %bitcast.73, bf16[1536,512]{1,0:T(8,128)(2,1)} %get-tuple-element.5, s32[]{:T(128)S(6)} %select_n.29), kind=kOutput, calls=%fused_computation.29 | convolution fusion | flops 805306368 | bytes 4980740 | tf_op jit(solution)/shard_map/dot_general | solution.py:10
  146.8 1.0 convolution_bitcast_fusion.3
  147.8 61.6 %collective-permute-done.1 = f32[256,3,1024]{2,0,1:T(8,128)} collective-permute-done((f32[256,3,1024]{2,0,1:T(8,128)}, f32[256,3,1024]{2,0,1:T(8,128)}, u32[]{:S(2)}, u32[]{:S(2)}) %collective-permute-start.1) | collective-permute-done | bytes 3145760 | tf_op jit(solution)/shard_map/ppermute | solution.py:114
  209.4 4.5 %fusion.3 = f32[1,256,3,1024]{3,1,2,0:T(8,128)} fusion(f32[256,3,1024]{2,0,1:T(8,128)} %collective-permute-done.1, f32[256,1,1024]{2,0,1:T(8,128)S(1)} %convolution_bitcast_fusion.3, f32[256,1,1024]{2,0,1:T(8,128)S(1)} %convolution_bitcast_fusion.4, f32[256,1,1024]{2,0,1:T(8,128)S(1)} %convolution_bitcast_fusion.5), kind=kLoop, calls=%fused_computation.11 | loop fusion | flops 2359296 | bytes 9437184 | tf_op jit(solution)/shard_map/reshape | solution.py:116
  213.9 6.4 %multiply_reduce_fusion = bf16[128,1024]{1,0:T(8,128)(2,1)} fusion(f32[128,8]{0,1:T(8,128)S(1)} %copy-done.6, bf16[1536,1024,1]{1,0,2:T(8,128)(2,1)} %bitcast.13, s32[128,8]{0,1:T(8,128)S(1)} %get-tuple-element.14), kind=kOutput, calls=%fused_computation.5 | convolution fusion | flops 3224764416 | bytes 3416064 | tf_op jit(solution)/shard_map/dot_general | solution.py:214
  (50 shorter events, 11.5 us)
Async XLA Ops:
  7.2 109.2 %copy-start = (bf16[1,512,1024]{2,1,0:T(8,128)(2,1)S(1)}, bf16[1,512,1024]{2,1,0:T(8,128)(2,1)}, u32[]{:S(2)}) copy-start(bf16[1,512,1024]{2,1,0:T(8,128)(2,1)} %param.15) | copy-start | bytes 3145732
  7.2 86.2 %all-gather.2.cloned.1.call-start = ((), (), s32[]{:S(2)}) async-start(), calls=%async_computation.1 | async-start | bytes 5013504 | tf_op jit(solution)/shard_map/all_gather | solution.py:92
  93.4 7.9 %collective-permute-start = (bf16[1024,2176]{1,0:T(8,128)(2,1)}, bf16[1024,2176]{1,0:T(8,128)(2,1)}, u32[]{:S(2)}, u32[]{:S(2)}) collective-permute-start(bf16[1024,2176]{1,0:T(8,128)(2,1)} %all-gather.2.cloned.1.call-done), channel_id=1, source_target_pairs={{0,1},{1,0},{2,3},{3,2},{4,5},{5,4},{6,7},{7,6},{8,9},{9,8},{10,11... | collective-permute-start | bytes 13369352 | tf_op jit(solution)/shard_map/ppermute | solution.py:93
  110.6 3.9 %copy-start.2 = (bf16[16,96,1024]{2,1,0:T(8,128)(2,1)}, bf16[16,96,1024]{2,1,0:T(8,128)(2,1)S(1)}, u32[]{:S(2)}) copy-start(bf16[16,96,1024]{2,1,0:T(8,128)(2,1)S(1)} %pad_maximum_fusion.2) | copy-start | bytes 9437188
  110.7 2.0 copy-start.7
  111.0 5.4 %copy-start.4 = (bf16[16,96,1024]{2,1,0:T(8,128)(2,1)}, bf16[16,96,1024]{2,1,0:T(8,128)(2,1)S(1)}, u32[]{:S(2)}) copy-start(bf16[16,96,1024]{2,1,0:T(8,128)(2,1)S(1)} %pad_maximum_fusion) | copy-start | bytes 9437188
  112.7 1.9 copy-start.8
  125.0 88.9 %all-to-all-start = ((bf16[16,96,1024]{2,1,0:T(8,128)(2,1)}), bf16[16,96,1024]{2,1,0:T(8,128)(2,1)}, u32[]{:S(2)}, u32[]{:S(2)}) async-start(bf16[16,96,1024]{2,1,0:T(8,128)(2,1)} %bitcast.11), calls=%async_computation | async-start | bytes 6291456 | tf_op jit(solution)/shard_map/all_to_all | solution.py:187
  132.4 3.3 %copy-start.5 = (bf16[16,96,1024]{2,1,0:T(8,128)(2,1)S(1)}, bf16[16,96,1024]{2,1,0:T(8,128)(2,1)}, u32[]{:S(2)}) copy-start(bf16[16,96,1024]{2,1,0:T(8,128)(2,1)} %copy-done.4) | copy-start | bytes 9437188
  132.4 3.5 %copy-start.9 = (bf16[1536,512]{1,0:T(8,128)(2,1)S(1)}, bf16[1536,512]{1,0:T(8,128)(2,1)}, u32[]{:S(2)}) copy-start(bf16[1536,512]{1,0:T(8,128)(2,1)} %get-tuple-element.5) | copy-start | bytes 4718596
  138.9 70.5 %collective-permute-start.1 = (f32[256,3,1024]{2,0,1:T(8,128)}, f32[256,3,1024]{2,0,1:T(8,128)}, u32[]{:S(2)}, u32[]{:S(2)}) collective-permute-start(f32[256,3,1024]{2,0,1:T(8,128)} %pad_maximum_fusion.3), channel_id=1, source_target_pairs={{0,16},{16,0},{1,17},{17,1},{2,18},{18,2},{3,19},{19,3},{4,20},{20... | collective-permute-start | bytes 9437192 | tf_op jit(solution)/shard_map/ppermute | solution.py:114
  143.5 3.3 %copy-start.3 = (bf16[16,96,1024]{2,1,0:T(8,128)(2,1)S(1)}, bf16[16,96,1024]{2,1,0:T(8,128)(2,1)}, u32[]{:S(2)}) copy-start(bf16[16,96,1024]{2,1,0:T(8,128)(2,1)} %copy-done.2) | copy-start | bytes 9437188
  147.8 66.1 %copy-start.6 = (f32[128,8]{0,1:T(8,128)S(1)}, f32[128,8]{0,1:T(8,128)}, u32[]{:S(2)}) copy-start(f32[128,8]{0,1:T(8,128)} %param.13) | copy-start | bytes 12292
  213.9 6.4 %copy-start.1 = (bf16[1,512,1024]{2,1,0:T(8,128)(2,1)S(1)}, bf16[1,512,1024]{2,1,0:T(8,128)(2,1)}, u32[]{:S(2)}) copy-start(bf16[1,512,1024]{2,1,0:T(8,128)(2,1)} %param.15) | copy-start | bytes 3145732
Sparse Core Ops, SparseCore 0:
  14.0 79.3 all-gather.1

commit v6 on v5

--- a/solution.py
+++ b/solution.py
@@ -179,12 +179,25 @@
         jnp.bfloat16
     )
 
-    by_group = expert_out.reshape(ncore, nchip, capacity, width)
-    ordered = jnp.stack(
-        [lax.dynamic_index_in_dim(by_group, k ^ core, 0, keepdims=False) for k in range(ncore)],
-        axis=1,
-    ).reshape(experts, capacity, width)
-    returned = lax.all_to_all(ordered, ("ez", "core"), 0, 0, tiled=True)
+    dense = jnp.einsum(
+        "sjt,sjd->std",
+        pick,
+        expert_out.reshape(experts, capacity, width),
+        preferred_element_type=jnp.float32,
+    ).astype(jnp.bfloat16)
+    own_rows = nchip * tok_rows
+    from_partner = lax.ppermute(dense[nchip:], "core", [(0, 1), (1, 0)])
+    gate_cols = joined(cols[4:7])[:own_rows]
+    routes_own = cols[0][:own_rows].astype(jnp.int32)
+    gte = jnp.sum(jnp.where(hit[:own_rows], gate_cols, zero), axis=1)
+    gte_partner = jnp.sum(jnp.where(routes_own == (me ^ 1), gate_cols, zero), axis=1)
+    combined = (
+        gte[:, None] * dense[:nchip].reshape(own_rows, width).astype(jnp.float32)
+        + gte_partner[:, None] * from_partner.reshape(own_rows, width).astype(jnp.float32)
+    ).astype(jnp.bfloat16)
+    returned = lax.all_to_all(
+        combined.reshape(nchip, tok_rows, width), "ez", 0, 0, tiled=True
+    )
 
     back = contract_cols(rows_q, wdown)
     d_gate = (back * up_pre * sig * (1.0 + gate_pre * (1.0 - sig))).astype(jnp.bfloat16)
@@ -206,13 +219,7 @@
 
     weight_grads = reduce_grads_dp(grad_half, width)
 
-    target = (routes * capacity + slots_by_rank(routes, experts)).reshape(-1)
-    choose = (
-        target[:, None]
-        == lax.broadcasted_iota(jnp.int32, (tok_rows * topk, experts * capacity), 1)
-    ).astype(jnp.bfloat16)
-    picked = jnp.dot(choose, returned.reshape(-1, width), preferred_element_type=jnp.float32)
-    summed = jnp.sum(picked.reshape(tok_rows, topk, width) * gates[:, :, None], axis=1)
+    summed = jnp.sum(returned.astype(jnp.float32), axis=0)
     return summed.astype(jnp.bfloat16), weight_grads
 
 

time: 228 us -> 254 us (1.11)
  local copies, waits for them, and re-layouts: 10.6 us -> 29.7 us
  other arithmetic: 16.5 us -> 23.3 us
    reshape x0 -> x4, local copies, waits for them, and re-layouts: none -> 11.6 us  [select(): values.reshape(nchip, tok_rows, width)]
    unnamed x20 -> x52, local copies, waits for them, and re-layouts: 1.97 us -> 10.9 us
    dot_general x4, matrix products: 2.29 us -> 9.34 us  [select(): jnp.einsum('sjt,std->sjd', pick[h * nchip:(h + 1) * nchip], values.reshap...]
    dot_general x2 -> x1, matrix products: 6.58 us -> 1.3 us  [local_gather(): jnp.einsum('sjt,sjd->std', pick, expert_out.reshape(experts, capacity, wi...]
    unnamed x0 -> x7, other arithmetic: none -> 4.88 us
    ppermute x1, waiting for transfers between devices: 5.14 us -> 2.53 us  [gather_replica(): return [mine, lax.ppermute(mine, 'core', [(0, 1), (1, 0)])]]
  transfers between devices with their start and end apart: 4 -> 5, of which waited for: 3 -> 3; matrix products, arithmetic and copies ran while one was open for 10% -> 11% of each run, Pallas kernels for 0% -> 0%
where the time goes in v6:
time: 254 us
  waiting for transfers between devices  146 us (57%)
  matrix products  35.3 us (14%)
  local copies, waits for them, and re-layouts  29.7 us (12%)
  other arithmetic  23.3 us (9%)
  between operations  14.3 us (6%)
  starting transfers between devices  5.24 us (2%)
    all_gather x1, waiting for transfers between devices, gather_replica(): mine = lax.all_gather(values, 'ez', axis=0, tiled=True)  80.9 us
    ppermute x1, waiting for transfers between devices, reduce_grads_dp(): sent = lax.ppermute(grad_half(1 - d), 'dp', [(0, 1), (1, 0)])  62.3 us
    dot_general x6, matrix products, contract_rows(): lax.dot_general(left, right, (((0,), (0,)), ((), ())), preferred_element_...  14.5 us
    reshape x4, local copies, waits for them, and re-layouts, select(): values.reshape(nchip, tok_rows, width)  11.6 us
    unnamed x52, local copies, waits for them, and re-layouts  10.9 us
    dot_general x4, matrix products, select(): jnp.einsum('sjt,std->sjd', pick[h * nchip:(h + 1) * nchip], values.reshap...  9.34 us
    dot_general x3, matrix products, contract_cols(): lax.dot_general(left, right, (((1,), (1,)), ((), ())), preferred_element_...  8.25 us
  transfers between devices with their start and end apart: 5, of which 3 were waited for; matrix products, arithmetic and copies ran while one was open for 11% of the time, Pallas kernels for 0%

profile of v6, /device:TPU:0, one launch (start us, length us, event | category | flops | bytes accessed | tf_op | source)
XLA Modules:
  0.0 253.6 jit_solution(15894403947867619067)
XLA Ops:
  16.0 80.9 %all-gather.2.cloned.1.call-done = bf16[1024,2176]{0,1:T(8,128)(2,1)} async-done(((bf16[128,2176]{0,1:T(8,128)(2,1)}), bf16[1024,2176]{0,1:T(8,128)(2,1)}) %all-gather.2.cloned.1.call-update) | async-done | bytes 4456464 | tf_op jit(solution)/shard_map/all_gather | solution.py:92
  98.7 2.6 %copy.23 = bf16[1024,1024]{1,0:T(8,128)(2,1)} copy(bf16[1024,1024]{0,1:T(8,128)(2,1)S(1)} %slice.96) | data formatting | bytes 4194304 | tf_op jit(solution)/shard_map/reshape | solution.py:164
  102.2 2.5 collective-permute-done
  108.2 2.6 %copy.24 = bf16[1024,1024]{1,0:T(8,128)(2,1)} copy(bf16[1024,1024]{0,1:T(8,128)(2,1)S(1)} %slice.97) | data formatting | bytes 4194304 | tf_op jit(solution)/shard_map/reshape | solution.py:164
  110.8 4.8 %multiply_convert_fusion = (bf16[1024,1024]{0,1:T(8,128)(2,1)}, bf16[1024,1024]{0,1:T(8,128)(2,1)S(1)}) fusion(bf16[1024,2176]{0,1:T(8,128)(2,1)} %collective-permute-done, f32[1024]{0:T(1024)S(1)} %get-tuple-element.13, bf16[1024,2176]{0,1:T(8,128)(2,1)} %all-gather.2.cloned.1.call-done, f32[1024]{0:T(1024)S(1)} %get-tuple-element.12), kind=kLoop, calls=%fused_computation | loop fusion | flops 6291456 | bytes 8396800 | tf_op jit(solution)/shard_map/convert_element_type | solution.py:159
  115.6 3.9 %copy.26 = bf16[1024,1024]{1,0:T(8,128)(2,1)} copy(bf16[1024,1024]{0,1:T(8,128)(2,1)} %get-tuple-element.14) | data formatting | bytes 4194304 | tf_op jit(solution)/shard_map/reshape | solution.py:164
  119.7 3.5 %convolution_convert_fusion.4 = bf16[8,96,1024]{2,1,0:T(8,128)(2,1)} fusion(bf16[8,128,1024]{2,1,0:T(8,128)(2,1)} %bitcast.65, s32[16,128]{1,0:T(8,128)S(1)} %convolution_convert_fusion.6, pred[16,128]{1,0:T(8,128)(4,1)S(1)} %bitcast.70), kind=kOutput, calls=%fused_computation.17 | convolution fusion | flops 202506240 | bytes 3680256 | tf_op jit(solution)/shard_map/sjt,std->sjd/dot_general | solution.py:161
  124.9 1.8 convolution_convert_fusion.2
  126.7 2.5 %copy.25 = bf16[1024,1024]{1,0:T(8,128)(2,1)} copy(bf16[1024,1024]{0,1:T(8,128)(2,1)S(1)} %get-tuple-element.15) | data formatting | bytes 4194304 | tf_op jit(solution)/shard_map/reshape | solution.py:164
  129.3 2.3 convolution_convert_fusion.3
  135.2 1.8 fusion.2
  137.0 1.9 fusion.5
  138.9 4.5 %multiply_convert_fusion.3 = (bf16[1536,512]{1,0:T(8,128)(2,1)}, bf16[1536,512]{1,0:T(8,128)(2,1)}, bf16[1536,512]{1,0:T(8,128)(2,1)S(1)}) fusion(f32[1536,512]{1,0:T(8,128)S(1)} %fusion.2, f32[1536,512]{1,0:T(8,128)S(1)} %fusion.5, bf16[1536,1024]{1,0:T(8,128)(2,1)S(1)} %bitcast.56, bf16[1,512,1024]{2,1,0:T(8,128)(2,1)S(1)} %copy-done), kind=kOutput, calls=%fused_computation.10 | convolution fusion | flops 1622409216 | bytes 15204352 | tf_op jit(solution)/shard_map/dot_general | solution.py:16
  143.5 1.8 convolution_convert_fusion
  146.6 1.9 copy-done.2
  151.2 3.1 %convolution_bitcast_fusion = f32[256,1,1024]{2,0,1:T(8,128)S(1)} fusion(bf16[1536,1024]{1,0:T(8,128)(2,1)} %bitcast.62, bf16[1536,512]{1,0:T(8,128)(2,1)} %copy-done.19, s32[]{:T(128)S(6)} %select_n.25), kind=kOutput, calls=%fused_computation.19 | convolution fusion | flops 805306368 | bytes 4980740 | tf_op jit(solution)/shard_map/dot_general | solution.py:10
  154.4 4.0 %convolution_bitcast_fusion.2 = f32[256,1,1024]{2,0,1:T(8,128)} fusion(bf16[1536,1024]{1,0:T(8,128)(2,1)} %bitcast.57, bf16[1536,512]{1,0:T(8,128)(2,1)S(1)} %copy-done.23, s32[]{:T(128)S(6)} %select_n.25), kind=kOutput, calls=%fused_computation.21 | convolution fusion | flops 805306368 | bytes 4980740 | tf_op jit(solution)/shard_map/dot_general | solution.py:10
  158.4 2.0 convolution_bitcast_fusion.1
  161.0 2.1 add_convert_fusion
  163.1 3.6 %all-to-all-start = ((bf16[8,128,1024]{2,1,0:T(8,128)(2,1)}), bf16[8,128,1024]{2,1,0:T(8,128)(2,1)S(1)}, u32[]{:S(2)}, u32[]{:S(2)}) async-start(bf16[8,128,1024]{2,1,0:T(8,128)(2,1)} %add_convert_fusion), calls=%async_computation | async-start | bytes 4194304 | tf_op jit(solution)/shard_map/all_to_all | solution.py:198
  166.7 3.6 %pad_maximum_fusion.2 = f32[256,3,1024]{2,0,1:T(8,128)} fusion(f32[256,1,1024]{2,0,1:T(8,128)S(1)} %convolution_bitcast_fusion, f32[256,1,1024]{2,0,1:T(8,128)} %convolution_bitcast_fusion.1, f32[256,1,1024]{2,0,1:T(8,128)} %convolution_bitcast_fusion.2), kind=kLoop, calls=%fused_computation.8 | loop fusion | flops 1572864 | bytes 6291456 | tf_op jit(solution)/shard_map/stack | solution.py:211
  171.8 3.3 %convolution_bitcast_fusion.5 = f32[256,1,1024]{2,0,1:T(8,128)S(1)} fusion(bf16[1536,1024]{1,0:T(8,128)(2,1)} %bitcast.58, bf16[1536,512]{1,0:T(8,128)(2,1)} %get-tuple-element.6, s32[]{:T(128)S(6)} %select_n.24), kind=kOutput, calls=%fused_computation.24 | convolution fusion | flops 805306368 | bytes 4980740 | tf_op jit(solution)/shard_map/dot_general | solution.py:10
  178.7 62.3 %collective-permute-done.2 = f32[256,3,1024]{2,0,1:T(8,128)} collective-permute-done((f32[256,3,1024]{2,0,1:T(8,128)}, f32[256,3,1024]{2,0,1:T(8,128)}, u32[]{:S(2)}, u32[]{:S(2)}) %collective-permute-start.2) | collective-permute-done | bytes 3145760 | tf_op jit(solution)/shard_map/ppermute | solution.py:114
  241.0 4.6 %fusion = f32[1,256,3,1024]{3,1,2,0:T(8,128)} fusion(f32[256,3,1024]{2,0,1:T(8,128)} %collective-permute-done.2, f32[256,1,1024]{2,0,1:T(8,128)S(1)} %convolution_bitcast_fusion.3, f32[256,1,1024]{2,0,1:T(8,128)S(1)} %convolution_bitcast_fusion.4, f32[256,1,1024]{2,0,1:T(8,128)S(1)} %convolution_bitcast_fusion.5), kind=kLoop, calls=%fused_computation.7 | loop fusion | flops 2359296 | bytes 9437184 | tf_op jit(solution)/shard_map/reshape | solution.py:116
  (85 shorter events, 31.1 us)
Async XLA Ops:
  7.2 131.8 %copy-start = (bf16[1,512,1024]{2,1,0:T(8,128)(2,1)S(1)}, bf16[1,512,1024]{2,1,0:T(8,128)(2,1)}, u32[]{:S(2)}) copy-start(bf16[1,512,1024]{2,1,0:T(8,128)(2,1)} %param.15) | copy-start | bytes 3145732
  7.2 89.7 %all-gather.2.cloned.1.call-start = ((), (), s32[]{:S(2)}) async-start(), calls=%async_computation.1 | async-start | bytes 5013504 | tf_op jit(solution)/shard_map/all_gather | solution.py:92
  96.9 7.9 %collective-permute-start = (bf16[1024,2176]{0,1:T(8,128)(2,1)}, bf16[1024,2176]{0,1:T(8,128)(2,1)}, u32[]{:S(2)}, u32[]{:S(2)}) collective-permute-start(bf16[1024,2176]{0,1:T(8,128)(2,1)} %all-gather.2.cloned.1.call-done), channel_id=1, source_target_pairs={{0,1},{1,0},{2,3},{3,2},{4,5},{5,4},{6,7},{7,6},{8,9},{9,8},{10,11... | collective-permute-start | bytes 13369352 | tf_op jit(solution)/shard_map/ppermute | solution.py:93
  119.7 3.5 %copy-start.11 = (bf16[1024,1024]{1,0:T(8,128)(2,1)S(1)}, bf16[1024,1024]{1,0:T(8,128)(2,1)}, u32[]{:S(2)}) copy-start(bf16[1024,1024]{1,0:T(8,128)(2,1)} %copy.23) | copy-start | bytes 6291460
  129.3 2.3 copy-start.13
  129.3 2.5 copy-start.14
  133.2 5.7 %copy-start.4 = (bf16[16,96,1024]{2,1,0:T(8,128)(2,1)}, bf16[16,96,1024]{2,1,0:T(8,128)(2,1)S(1)}, u32[]{:S(2)}) copy-start(bf16[16,96,1024]{2,1,0:T(8,128)(2,1)S(1)} %pad_maximum_fusion) | copy-start | bytes 9437188
  133.2 2.0 copy-start.18
  133.5 3.6 %copy-start.7 = (bf16[16,96,1024]{2,1,0:T(8,128)(2,1)}, bf16[16,96,1024]{2,1,0:T(8,128)(2,1)S(1)}, u32[]{:S(2)}) copy-start(bf16[16,96,1024]{2,1,0:T(8,128)(2,1)S(1)} %pad_maximum_fusion.1) | copy-start | bytes 9437188
  135.2 1.9 copy-start.17
  143.5 1.8 copy-start.19
  146.6 1.9 copy-start.2
  150.2 10.3 %collective-permute-start.1 = (bf16[8,128,1024]{2,1,0:T(8,128)(2,1)}, bf16[8,128,1024]{2,1,0:T(8,128)(2,1)S(1)}, u32[]{:S(2)}, u32[]{:S(2)}) collective-permute-start(bf16[8,128,1024]{2,1,0:T(8,128)(2,1)} %slice.100), channel_id=1, source_target_pairs={{0,1},{1,0},{2,3},{3,2},{4,5},{5,4},{6,7},{7,6},{8,9},{9,8},{10,11... | collective-permute-start | bytes 6291464 | tf_op jit(solution)/shard_map/ppermute | solution.py:189
  150.3 4.1 %copy-start.23 = (bf16[1536,512]{1,0:T(8,128)(2,1)S(1)}, bf16[1536,512]{1,0:T(8,128)(2,1)}, u32[]{:S(2)}) copy-start(bf16[1536,512]{1,0:T(8,128)(2,1)} %get-tuple-element.6) | copy-start | bytes 4718596
  154.4 4.1 %copy-start.5 = (bf16[16,96,1024]{2,1,0:T(8,128)(2,1)S(1)}, bf16[16,96,1024]{2,1,0:T(8,128)(2,1)}, u32[]{:S(2)}) copy-start(bf16[16,96,1024]{2,1,0:T(8,128)(2,1)} %copy-done.4) | copy-start | bytes 9437188
  154.4 4.1 %copy-start.21 = (bf16[1536,512]{1,0:T(8,128)(2,1)S(1)}, bf16[1536,512]{1,0:T(8,128)(2,1)}, u32[]{:S(2)}) copy-start(bf16[1536,512]{1,0:T(8,128)(2,1)} %get-tuple-element.7) | copy-start | bytes 4718596
  158.4 2.6 %copy-start.3 = (bf16[16,128,1024]{2,1,0:T(8,128)(2,1)S(1)}, bf16[16,128,1024]{2,1,0:T(8,128)(2,1)}, u32[]{:S(2)}) copy-start(bf16[16,128,1024]{2,1,0:T(8,128)(2,1)} %copy-done.2) | copy-start | bytes 12582916
  163.1 82.5 %all-to-all-start = ((bf16[8,128,1024]{2,1,0:T(8,128)(2,1)}), bf16[8,128,1024]{2,1,0:T(8,128)(2,1)S(1)}, u32[]{:S(2)}, u32[]{:S(2)}) async-start(bf16[8,128,1024]{2,1,0:T(8,128)(2,1)} %add_convert_fusion), calls=%async_computation | async-start | bytes 4194304 | tf_op jit(solution)/shard_map/all_to_all | solution.py:198
  170.3 70.7 %collective-permute-start.2 = (f32[256,3,1024]{2,0,1:T(8,128)}, f32[256,3,1024]{2,0,1:T(8,128)}, u32[]{:S(2)}, u32[]{:S(2)}) collective-permute-start(f32[256,3,1024]{2,0,1:T(8,128)} %pad_maximum_fusion.2), channel_id=1, source_target_pairs={{0,16},{16,0},{1,17},{17,1},{2,18},{18,2},{3,19},{19,3},{4,20},{20... | collective-permute-start | bytes 9437192 | tf_op jit(solution)/shard_map/ppermute | solution.py:114
  171.8 3.3 %copy-start.6 = (bf16[16,96,1024]{2,1,0:T(8,128)(2,1)S(1)}, bf16[16,96,1024]{2,1,0:T(8,128)(2,1)}, u32[]{:S(2)}) copy-start(bf16[16,96,1024]{2,1,0:T(8,128)(2,1)} %copy-done.4) | copy-start | bytes 9437188
  171.8 3.5 %copy-start.22 = (bf16[1536,512]{1,0:T(8,128)(2,1)S(1)}, bf16[1536,512]{1,0:T(8,128)(2,1)}, u32[]{:S(2)}) copy-start(bf16[1536,512]{1,0:T(8,128)(2,1)} %get-tuple-element.7) | copy-start | bytes 4718596
  175.3 1.9 copy-start.8
  175.3 2.4 copy-start.20
  241.0 5.7 %copy-start.1 = (bf16[1,512,1024]{2,1,0:T(8,128)(2,1)S(1)}, bf16[1,512,1024]{2,1,0:T(8,128)(2,1)}, u32[]{:S(2)}) copy-start(bf16[1,512,1024]{2,1,0:T(8,128)(2,1)} %param.15) | copy-start | bytes 3145732
  (5 other events, 6.4 us)
Sparse Core Ops, SparseCore 0:
  16.1 80.6 all-gather.1

commit v7 on v5

--- a/solution.py
+++ b/solution.py
@@ -111,8 +111,8 @@
         grads = jnp.concatenate([grad_half(h) for h in range(ndp)], axis=0)
         return reduce_grads(grads, width)
     d = lax.axis_index("dp")
-    sent = lax.ppermute(grad_half(1 - d), "dp", [(0, 1), (1, 0)])
-    summed = grad_half(d) + sent
+    sent = lax.ppermute(grad_half(1 - d).astype(jnp.bfloat16), "dp", [(0, 1), (1, 0)])
+    summed = grad_half(d) + sent.astype(jnp.float32)
     return summed.reshape(1, summed.shape[0], 3, width)
 
 

time: 228 us -> 212 us (0.930)
  the two profiles are of different devices: /device:TPU:0 before, /device:TPU:11 now
where the time goes in v7:
time: 212 us
  waiting for transfers between devices  130 us (61%)
  matrix products  33.5 us (16%)
  between operations  14.3 us (7%)
  other arithmetic  13.8 us (7%)
  local copies, waits for them, and re-layouts  10.8 us (5%)
  starting transfers between devices  9.53 us (4%)
    all_gather x1, waiting for transfers between devices, gather_replica(): mine = lax.all_gather(values, 'ez', axis=0, tiled=True)  75.2 us
    ppermute x1, waiting for transfers between devices, reduce_grads_dp(): lax.ppermute(grad_half(1 - d).astype(jnp.bfloat16), 'dp', [(0, 1), (1, 0)])  26.8 us
    all_to_all x1, waiting for transfers between devices, local_gather(): returned = lax.all_to_all(ordered, ('ez', 'core'), 0, 0, tiled=True)  23 us
    dot_general x6, matrix products, contract_rows(): lax.dot_general(left, right, (((0,), (0,)), ((), ())), preferred_element_...  14.6 us
    dot_general x3, matrix products, contract_cols(): lax.dot_general(left, right, (((1,), (1,)), ((), ())), preferred_element_...  8.07 us
    all_to_all x1, starting transfers between devices, local_gather(): returned = lax.all_to_all(ordered, ('ez', 'core'), 0, 0, tiled=True)  6.53 us
    dot_general x1, matrix products, local_gather(): jnp.dot(choose, returned.reshape(-1, width), preferred_element_type=jnp.f...  6.43 us
    ppermute x1, waiting for transfers between devices, gather_replica(): return [mine, lax.ppermute(mine, 'core', [(0, 1), (1, 0)])]  4.77 us
  transfers between devices with their start and end apart: 4, of which 4 were waited for; matrix products, arithmetic and copies ran while one was open for 10% of the time, Pallas kernels for 0%

profile of v7, /device:TPU:11, one launch (start us, length us, event | category | flops | bytes accessed | tf_op | source)
XLA Modules:
  0.0 211.8 jit_solution(17091797138863409390)
XLA Ops:
  11.9 1.9 concatenate.12
  13.9 75.2 %all-gather.2.cloned.1.call-done = bf16[1024,2176]{1,0:T(8,128)(2,1)} async-done(((bf16[128,2176]{1,0:T(8,128)(2,1)}), bf16[1024,2176]{1,0:T(8,128)(2,1)}) %all-gather.2.cloned.1.call-update) | async-done | bytes 4456464 | tf_op jit(solution)/shard_map/all_gather | solution.py:92
  89.0 1.7 collective-permute-start
  91.7 1.8 slice.62
  93.5 4.8 %collective-permute-done = bf16[1024,2176]{1,0:T(8,128)(2,1)} collective-permute-done((bf16[1024,2176]{1,0:T(8,128)(2,1)}, bf16[1024,2176]{1,0:T(8,128)(2,1)}, u32[]{:S(2)}, u32[]{:S(2)}) %collective-permute-start) | collective-permute-done | bytes 4456480 | tf_op jit(solution)/shard_map/ppermute | solution.py:93
  100.6 1.8 slice.63
  103.6 2.6 %multiply_convert_fusion = (bf16[1024,1024]{1,0:T(8,128)(2,1)S(1)}, bf16[1024,1024]{1,0:T(8,128)(2,1)S(1)}) fusion(bf16[1024,2176]{1,0:T(8,128)(2,1)} %collective-permute-done, f32[1024]{0:T(1024)S(1)} %get-tuple-element.10, bf16[1024,2176]{1,0:T(8,128)(2,1)} %all-gather.2.cloned.1.call-done, f32[1024]{0:T(1024)S(1)} %get-tuple-element.9), kind=kLoop, calls=%fused_computation.3 | loop fusion | flops 6291456 | bytes 8396800 | tf_op jit(solution)/shard_map/convert_element_type | solution.py:159
  108.0 1.7 copy-done.7
  109.7 1.8 fusion.14
  111.6 1.8 fusion.11
  113.4 4.4 %multiply_convert_fusion.3 = (bf16[1536,512]{1,0:T(8,128)(2,1)}, bf16[1536,512]{1,0:T(8,128)(2,1)}, bf16[1536,512]{1,0:T(8,128)(2,1)S(1)}) fusion(f32[1536,512]{1,0:T(8,128)S(1)} %fusion.11, f32[1536,512]{1,0:T(8,128)S(1)} %fusion.14, bf16[1536,1024]{1,0:T(8,128)(2,1)S(1)} %bitcast.70, bf16[1,512,1024]{2,1,0:T(8,128)(2,1)S(1)} %copy-done), kind=kOutput, calls=%fused_computation.13 | convolution fusion | flops 1622409216 | bytes 15204352 | tf_op jit(solution)/shard_map/dot_general | solution.py:16
  117.8 1.8 convolution_convert_fusion
  120.0 2.0 pad_maximum_fusion.1
  122.0 6.5 %all-to-all-start = ((bf16[16,96,1024]{2,1,0:T(8,128)(2,1)}), bf16[16,96,1024]{2,1,0:T(8,128)(2,1)}, u32[]{:S(2)}, u32[]{:S(2)}) async-start(bf16[16,96,1024]{2,1,0:T(8,128)(2,1)} %bitcast.11), calls=%async_computation | async-start | bytes 6291456 | tf_op jit(solution)/shard_map/all_to_all | solution.py:187
  128.5 2.9 %fusion.10 = bf16[256,1,1024]{2,0,1:T(8,128)(2,1)S(1)} fusion(bf16[1536,1024]{1,0:T(8,128)(2,1)} %bitcast.67, bf16[1536,512]{1,0:T(8,128)(2,1)S(1)} %get-tuple-element.6, s32[]{:T(128)S(6)} %select_n.30), kind=kOutput, calls=%fused_computation.33 | convolution fusion | flops 805568512 | bytes 4456452 | tf_op jit(solution)/shard_map/dot_general | solution.py:10
  131.4 3.3 %fusion.8 = bf16[256,1,1024]{2,0,1:T(8,128)(2,1)S(1)} fusion(bf16[1536,1024]{1,0:T(8,128)(2,1)} %bitcast.71, bf16[1536,512]{1,0:T(8,128)(2,1)} %get-tuple-element.4, s32[]{:T(128)S(6)} %select_n.30), kind=kOutput, calls=%fused_computation.31 | convolution fusion | flops 805568512 | bytes 4456452 | tf_op jit(solution)/shard_map/dot_general | solution.py:10
  134.9 1.0 fusion.9
  136.2 1.3 collective-permute-start.1
  137.4 3.1 %convolution_bitcast_fusion.2 = f32[256,1,1024]{2,0,1:T(8,128)S(1)} fusion(bf16[1536,1024]{1,0:T(8,128)(2,1)} %bitcast.72, bf16[1536,512]{1,0:T(8,128)(2,1)} %get-tuple-element.4, s32[]{:T(128)S(6)} %select_n.29), kind=kOutput, calls=%fused_computation.27 | convolution fusion | flops 805306368 | bytes 4980740 | tf_op jit(solution)/shard_map/dot_general | solution.py:10
  140.6 3.3 %convolution_bitcast_fusion.1 = f32[256,1,1024]{2,0,1:T(8,128)S(1)} fusion(bf16[1536,1024]{1,0:T(8,128)(2,1)} %bitcast.73, bf16[1536,512]{1,0:T(8,128)(2,1)} %get-tuple-element.5, s32[]{:T(128)S(6)} %select_n.29), kind=kOutput, calls=%fused_computation.26 | convolution fusion | flops 805306368 | bytes 4980740 | tf_op jit(solution)/shard_map/dot_general | solution.py:10
  145.1 26.8 %collective-permute-done.1 = bf16[256,3,1024]{2,0,1:T(8,128)(2,1)} collective-permute-done((bf16[256,3,1024]{2,0,1:T(8,128)(2,1)S(1)}, bf16[256,3,1024]{2,0,1:T(8,128)(2,1)}, u32[]{:S(2)}, u32[]{:S(2)}) %collective-permute-start.1) | collective-permute-done | bytes 1572896 | tf_op jit(solution)/shard_map/ppermute | solution.py:114
  171.9 3.6 %fusion.3 = f32[1,256,3,1024]{3,1,2,0:T(8,128)} fusion(f32[256,1,1024]{2,0,1:T(8,128)S(1)} %convolution_bitcast_fusion, f32[256,1,1024]{2,0,1:T(8,128)S(1)} %convolution_bitcast_fusion.1, f32[256,1,1024]{2,0,1:T(8,128)S(1)} %convolution_bitcast_fusion.2, bf16[256,3,1024]{2,0,1:T(8,128)(2,1)} %collective-permute-done.1), kind=kLoop, calls=%fused_computation.11 | loop fusion | flops 3145728 | bytes 7864320 | tf_op jit(solution)/shard_map/reshape | solution.py:116
  175.5 23.0 %all-to-all-done = bf16[16,96,1024]{2,1,0:T(8,128)(2,1)} async-done(((bf16[16,96,1024]{2,1,0:T(8,128)(2,1)}), bf16[16,96,1024]{2,1,0:T(8,128)(2,1)}, u32[]{:S(2)}, u32[]{:S(2)}) %all-to-all-start) | async-done | bytes 3145760 | tf_op jit(solution)/shard_map/all_to_all | solution.py:187
  198.5 6.4 %multiply_reduce_fusion = bf16[128,1024]{1,0:T(8,128)(2,1)} fusion(f32[128,8]{0,1:T(8,128)S(1)} %copy-done.6, bf16[1536,1024,1]{1,0,2:T(8,128)(2,1)} %bitcast.13, s32[128,8]{0,1:T(8,128)S(1)} %get-tuple-element.14), kind=kOutput, calls=%fused_computation.5 | convolution fusion | flops 3224764416 | bytes 3416064 | tf_op jit(solution)/shard_map/dot_general | solution.py:214
  (54 shorter events, 12.9 us)
Async XLA Ops:
  7.2 106.2 %copy-start = (bf16[1,512,1024]{2,1,0:T(8,128)(2,1)S(1)}, bf16[1,512,1024]{2,1,0:T(8,128)(2,1)}, u32[]{:S(2)}) copy-start(bf16[1,512,1024]{2,1,0:T(8,128)(2,1)} %param.15) | copy-start | bytes 3145732
  7.2 81.9 %all-gather.2.cloned.1.call-start = ((), (), s32[]{:S(2)}) async-start(), calls=%async_computation.1 | async-start | bytes 5013504 | tf_op jit(solution)/shard_map/all_gather | solution.py:92
  89.0 9.2 %collective-permute-start = (bf16[1024,2176]{1,0:T(8,128)(2,1)}, bf16[1024,2176]{1,0:T(8,128)(2,1)}, u32[]{:S(2)}, u32[]{:S(2)}) collective-permute-start(bf16[1024,2176]{1,0:T(8,128)(2,1)} %all-gather.2.cloned.1.call-done), channel_id=1, source_target_pairs={{0,1},{1,0},{2,3},{3,2},{4,5},{5,4},{6,7},{7,6},{8,9},{9,8},{10,11... | collective-permute-start | bytes 13369352 | tf_op jit(solution)/shard_map/ppermute | solution.py:93
  107.7 3.9 %copy-start.2 = (bf16[16,96,1024]{2,1,0:T(8,128)(2,1)}, bf16[16,96,1024]{2,1,0:T(8,128)(2,1)S(1)}, u32[]{:S(2)}) copy-start(bf16[16,96,1024]{2,1,0:T(8,128)(2,1)S(1)} %pad_maximum_fusion.2) | copy-start | bytes 9437188
  107.7 2.0 copy-start.7
  108.0 5.4 %copy-start.4 = (bf16[16,96,1024]{2,1,0:T(8,128)(2,1)}, bf16[16,96,1024]{2,1,0:T(8,128)(2,1)S(1)}, u32[]{:S(2)}) copy-start(bf16[16,96,1024]{2,1,0:T(8,128)(2,1)S(1)} %pad_maximum_fusion) | copy-start | bytes 9437188
  109.7 1.9 copy-start.8
  117.8 10.7 %copy-start.9 = (bf16[1536,512]{1,0:T(8,128)(2,1)}, bf16[1536,512]{1,0:T(8,128)(2,1)S(1)}, u32[]{:S(2)}) copy-start(bf16[1536,512]{1,0:T(8,128)(2,1)S(1)} %get-tuple-element.6) | copy-start | bytes 4718596
  122.0 76.5 %all-to-all-start = ((bf16[16,96,1024]{2,1,0:T(8,128)(2,1)}), bf16[16,96,1024]{2,1,0:T(8,128)(2,1)}, u32[]{:S(2)}, u32[]{:S(2)}) async-start(bf16[16,96,1024]{2,1,0:T(8,128)(2,1)} %bitcast.11), calls=%async_computation | async-start | bytes 6291456 | tf_op jit(solution)/shard_map/all_to_all | solution.py:187
  131.4 3.3 %copy-start.5 = (bf16[16,96,1024]{2,1,0:T(8,128)(2,1)S(1)}, bf16[16,96,1024]{2,1,0:T(8,128)(2,1)}, u32[]{:S(2)}) copy-start(bf16[16,96,1024]{2,1,0:T(8,128)(2,1)} %copy-done.4) | copy-start | bytes 9437188
  131.4 3.5 %copy-start.11 = (bf16[1536,512]{1,0:T(8,128)(2,1)S(1)}, bf16[1536,512]{1,0:T(8,128)(2,1)}, u32[]{:S(2)}) copy-start(bf16[1536,512]{1,0:T(8,128)(2,1)} %get-tuple-element.5) | copy-start | bytes 4718596
  136.2 35.8 %collective-permute-start.1 = (bf16[256,3,1024]{2,0,1:T(8,128)(2,1)S(1)}, bf16[256,3,1024]{2,0,1:T(8,128)(2,1)}, u32[]{:S(2)}, u32[]{:S(2)}) collective-permute-start(bf16[256,3,1024]{2,0,1:T(8,128)(2,1)S(1)} %pad_maximum_fusion.3), channel_id=1, source_target_pairs={{0,16},{16,0},{1,17},{17,1},{2,18},{18,2},{3,19},{19,3},{4,20},{20... | collective-permute-start | bytes 4718600 | tf_op jit(solution)/shard_map/ppermute | solution.py:114
  140.6 3.3 %copy-start.3 = (bf16[16,96,1024]{2,1,0:T(8,128)(2,1)S(1)}, bf16[16,96,1024]{2,1,0:T(8,128)(2,1)}, u32[]{:S(2)}) copy-start(bf16[16,96,1024]{2,1,0:T(8,128)(2,1)} %copy-done.2) | copy-start | bytes 9437188
  140.6 3.5 %copy-start.10 = (bf16[1536,512]{1,0:T(8,128)(2,1)S(1)}, bf16[1536,512]{1,0:T(8,128)(2,1)}, u32[]{:S(2)}) copy-start(bf16[1536,512]{1,0:T(8,128)(2,1)} %copy-done.9) | copy-start | bytes 4718596
  145.1 53.4 %copy-start.6 = (f32[128,8]{0,1:T(8,128)S(1)}, f32[128,8]{0,1:T(8,128)}, u32[]{:S(2)}) copy-start(f32[128,8]{0,1:T(8,128)} %param.13) | copy-start | bytes 12292
  198.5 6.4 %copy-start.1 = (bf16[1,512,1024]{2,1,0:T(8,128)(2,1)S(1)}, bf16[1,512,1024]{2,1,0:T(8,128)(2,1)}, u32[]{:S(2)}) copy-start(bf16[1,512,1024]{2,1,0:T(8,128)(2,1)} %param.15) | copy-start | bytes 3145732
Sparse Core Ops, SparseCore 0:
  14.0 75.0 all-gather.1

commit v8 on v7

--- a/solution.py
+++ b/solution.py
@@ -93,6 +93,32 @@
     return [mine, lax.ppermute(mine, "core", [(0, 1), (1, 0)])]
 
 
+def ring_gather(block):
+    n = lax.axis_size("ez")
+    order = [2 * i for i in range(n // 2)] + [2 * i + 1 for i in reversed(range(n // 2))]
+    if n % 2:
+        order = list(range(n))
+    place = [0] * n
+    for p, c in enumerate(order):
+        place[c] = p
+    me = lax.axis_index("ez")
+    at = jnp.asarray(place, jnp.int32)[me]
+    ring = jnp.asarray(order, jnp.int32)
+    out = jnp.zeros((n,) + block.shape, block.dtype)
+    out = lax.dynamic_update_index_in_dim(out, block, me, 0)
+    ahead = [(order[i], order[(i + 1) % n]) for i in range(n)]
+    behind = [(order[i], order[(i - 1) % n]) for i in range(n)]
+    up, down = block, block
+    for step in range(1, n // 2 + 1):
+        up = lax.ppermute(up, "ez", ahead)
+        out = lax.dynamic_update_index_in_dim(out, up, ring[(at - step) % n], 0)
+        if step <= (n - 1) // 2:
+            down = lax.ppermute(down, "ez", behind)
+            out = lax.dynamic_update_index_in_dim(out, down, ring[(at + step) % n], 0)
+    mine = out.reshape((n * block.shape[0],) + block.shape[1:])
+    return [mine, lax.ppermute(mine, "core", [(0, 1), (1, 0)])]
+
+
 def slots_by_rank(routes, experts):
     tok_rows = routes.shape[0]
     onehot = routes[:, :, None] == lax.broadcasted_iota(jnp.int32, (1, 1, experts), 2)
@@ -131,10 +157,11 @@
     meta = [routes.astype(jnp.bfloat16)] + exact_pieces(factor) + exact_pieces(gates)
     pad = (-topk * len(meta)) % 128
     meta.append(jnp.zeros((tok_rows, pad), jnp.bfloat16))
-    packed = jnp.concatenate([tokens, cotangent] + meta, axis=1)
+    packed = jnp.concatenate([tokens] + meta, axis=1)
 
     halves = gather_replica(packed)
-    all_p = jnp.concatenate([h[:, 2 * width:] for h in halves], axis=0)
+    cot_halves = ring_gather(cotangent)
+    all_p = jnp.concatenate([h[:, width:] for h in halves], axis=0)
     cols = [all_p[:, topk * i: topk * (i + 1)] for i in range(7)]
     hit = cols[0].astype(jnp.int32) == me
     zero = jnp.zeros((), jnp.float32)
@@ -152,8 +179,8 @@
 
     def select(part, scale=None):
         picked = []
-        for h, half in enumerate(halves):
-            values = half[:, part * width:(part + 1) * width]
+        for h, half in enumerate(halves if part == 0 else cot_halves):
+            values = half[:, :width]
             if scale is not None:
                 rows = slice(h * nchip * tok_rows, (h + 1) * nchip * tok_rows)
                 values = (scale[rows, None] * values.astype(jnp.float32)).astype(jnp.bfloat16)

time: 212 us -> 207 us (0.976)
  waiting for transfers between devices: 130 us -> 88.7 us
  between operations: 14.3 us -> 32.4 us
  local copies, waits for them, and re-layouts: 10.8 us -> 25.7 us
  starting transfers between devices: 9.53 us -> 14.3 us
  matrix products: 33.5 us -> 30.6 us
    all_gather x1, waiting for transfers between devices: 75.2 us -> 27.3 us  [gather_replica(): mine = lax.all_gather(values, 'ez', axis=0, tiled=True)]
    dynamic_update_slice x0 -> x8, local copies, waits for them, and re-layouts: none -> 9.55 us  [the longest x4 4.78 us: ring_gather(): out = lax.dynamic_update_index_in_dim(out, up, ring[(at - step) % n], 0)]
    ppermute x0 -> x8, waiting for transfers between devices: none -> 8.31 us  [the longest x4 8.3 us: ring_gather(): up = lax.ppermute(up, 'ez', ahead)]
    ppermute x0 -> x8, starting transfers between devices: none -> 6.58 us  [the longest x3 4.05 us: ring_gather(): down = lax.ppermute(down, 'ez', behind)]
    dot_general x6, matrix products: 14.6 us -> 9.63 us  [contract_rows(): lax.dot_general(left, right, (((0,), (0,)), ((), ())), preferred_element_...]
    ppermute x1, waiting for transfers between devices: 4.77 us -> 0.01 us  [gather_replica(): return [mine, lax.ppermute(mine, 'core', [(0, 1), (1, 0)])]]
    dynamic_slice x0 -> x2, local copies, waits for them, and re-layouts: none -> 2.85 us  [the longest x1 1.61 us: ring_gather(): out = lax.dynamic_update_index_in_dim(out, up, ring[(at - step) % n], 0)]
    unnamed x24 -> x36, local copies, waits for them, and re-layouts: 2.19 us -> 4.25 us
  transfers between devices with their start and end apart: 4 -> 12, of which waited for: 4 -> 5; matrix products, arithmetic and copies ran while one was open for 10% -> 17% of each run, Pallas kernels for 0% -> 0%
where the time goes in v8:
time: 207 us; the launch traced here: 206 us
  waiting for transfers between devices  88.7 us (43%)
  between operations  32.4 us (16%)
  matrix products  30.6 us (15%)
  local copies, waits for them, and re-layouts  25.7 us (12%)
  other arithmetic  14.4 us (7%)
  starting transfers between devices  14.3 us (7%)
    ppermute x1, waiting for transfers between devices, reduce_grads_dp(): lax.ppermute(grad_half(1 - d).astype(jnp.bfloat16), 'dp', [(0, 1), (1, 0)])  28.7 us
    all_gather x1, waiting for transfers between devices, gather_replica(): mine = lax.all_gather(values, 'ez', axis=0, tiled=True)  27.3 us
    all_to_all x1, waiting for transfers between devices, local_gather(): returned = lax.all_to_all(ordered, ('ez', 'core'), 0, 0, tiled=True)  24.3 us
    dot_general x6, matrix products, contract_rows(): lax.dot_general(left, right, (((0,), (0,)), ((), ())), preferred_element_...  9.63 us
    dot_general x3, matrix products, contract_cols(): lax.dot_general(left, right, (((1,), (1,)), ((), ())), preferred_element_...  8.4 us
    ppermute x4, waiting for transfers between devices, ring_gather(): up = lax.ppermute(up, 'ez', ahead)  8.3 us
    dot_general x1, matrix products, local_gather(): jnp.dot(choose, returned.reshape(-1, width), preferred_element_type=jnp.f...  6.43 us
    all_to_all x1, starting transfers between devices, local_gather(): returned = lax.all_to_all(ordered, ('ez', 'core'), 0, 0, tiled=True)  4.99 us
  transfers between devices with their start and end apart: 12, of which 5 were waited for; matrix products, arithmetic and copies ran while one was open for 17% of the time, Pallas kernels for 0%

profile of v8, /device:TPU:11, one launch (start us, length us, event | category | flops | bytes accessed | tf_op | source)
XLA Modules:
  0.0 206.1 jit_solution(2523683125369578149)
XLA Ops:
  11.9 1.8 concatenate.12
  40.0 1.7 bitcast_dynamic-update-slice_fusion.6
  41.7 27.3 %all-gather.2.cloned.1.call-done = bf16[1024,1152]{1,0:T(8,128)(2,1)} async-done(((bf16[128,1152]{1,0:T(8,128)(2,1)}), bf16[1024,1152]{1,0:T(8,128)(2,1)}) %all-gather.2.cloned.1.call-update) | async-done | bytes 2359312 | tf_op jit(solution)/shard_map/all_gather | solution.py:92
  70.5 1.7 bitcast_dynamic-update-slice_fusion.5
  73.6 1.7 bitcast_dynamic-update-slice_fusion.4
  75.3 1.7 bitcast_dynamic-update-slice_fusion.3
  76.9 3.2 %collective-permute-done.5 = bf16[128,1024]{1,0:T(8,128)(2,1)S(1)} collective-permute-done((bf16[128,1024]{1,0:T(8,128)(2,1)}, bf16[128,1024]{1,0:T(8,128)(2,1)S(1)}, u32[]{:S(2)}, u32[]{:S(2)}) %collective-permute-start.5) | collective-permute-done | bytes 262176 | tf_op jit(solution)/shard_map/ppermute | solution.py:113
  81.8 5.1 %collective-permute-done.7 = bf16[128,1024]{1,0:T(8,128)(2,1)S(1)} collective-permute-done((bf16[128,1024]{1,0:T(8,128)(2,1)S(1)}, bf16[128,1024]{1,0:T(8,128)(2,1)S(1)}, u32[]{:S(2)}, u32[]{:S(2)}) %collective-permute-start.7) | collective-permute-done | bytes 262176 | tf_op jit(solution)/shard_map/ppermute | solution.py:113
  87.7 1.9 collective-permute-start.8
  93.6 2.3 %fusion.8 = bf16[8,96,1024]{2,1,0:T(8,128)(2,1)S(1)} fusion(bf16[8,128,1024]{2,1,0:T(8,128)(2,1)} %bitcast_dynamic-update-slice_fusion, f32[8,128]{1,0:T(8,128)S(1)} %get-tuple-element.9, s32[16,128]{1,0:T(8,128)S(1)} %convolution_convert_fusion.7, pred[16,128]{1,0:T(8,128)(4,1)S(1)} %bitcast.110), kind=kOutput, calls=%fused_computation.20 | convolution fusion | flops 205651968 | bytes 3684352 | tf_op jit(solution)/shard_map/sjt,std->sjd/dot_general | solution.py:188
  95.9 2.0 multiply_convert_fusion
  98.5 1.8 slice.64
  103.7 1.8 fusion.14
  106.8 1.8 fusion.17
  108.7 4.7 %multiply_convert_fusion.3 = (bf16[1536,512]{1,0:T(8,128)(2,1)}, bf16[1536,512]{1,0:T(8,128)(2,1)}, bf16[1536,512]{1,0:T(8,128)(2,1)S(1)}) fusion(f32[1536,512]{1,0:T(8,128)S(1)} %fusion.14, f32[1536,512]{1,0:T(8,128)S(1)} %fusion.17, bf16[1536,1024]{1,0:T(8,128)(2,1)S(1)} %bitcast.101, bf16[1,512,1024]{2,1,0:T(8,128)(2,1)S(1)} %copy-done), kind=kOutput, calls=%fused_computation.13 | convolution fusion | flops 1622409216 | bytes 15204352 | tf_op jit(solution)/shard_map/dot_general | solution.py:16
  113.4 1.8 convolution_convert_fusion
  115.6 2.0 pad_maximum_fusion.1
  117.6 5.0 %all-to-all-start = ((bf16[16,96,1024]{2,1,0:T(8,128)(2,1)}), bf16[16,96,1024]{2,1,0:T(8,128)(2,1)}, u32[]{:S(2)}, u32[]{:S(2)}) async-start(bf16[16,96,1024]{2,1,0:T(8,128)(2,1)} %bitcast.11), calls=%async_computation | async-start | bytes 6291456 | tf_op jit(solution)/shard_map/all_to_all | solution.py:214
  122.6 2.3 %fusion.13 = bf16[256,1,1024]{2,0,1:T(8,128)(2,1)S(1)} fusion(bf16[1536,1024]{1,0:T(8,128)(2,1)S(1)} %bitcast.98, bf16[1536,512]{1,0:T(8,128)(2,1)} %copy-done.13, s32[]{:T(128)S(6)} %select_n.130), kind=kOutput, calls=%fused_computation.35 | convolution fusion | flops 805568512 | bytes 4456452 | tf_op jit(solution)/shard_map/dot_general | solution.py:10
  130.2 3.3 %convolution_bitcast_fusion.2 = f32[256,1,1024]{2,0,1:T(8,128)S(1)} fusion(bf16[1536,1024]{1,0:T(8,128)(2,1)} %bitcast.102, bf16[1536,512]{1,0:T(8,128)(2,1)} %get-tuple-element.4, s32[]{:T(128)S(6)} %select_n.129), kind=kOutput, calls=%fused_computation.29 | convolution fusion | flops 805306368 | bytes 4980740 | tf_op jit(solution)/shard_map/dot_general | solution.py:10
  136.1 28.7 %collective-permute-done.9 = bf16[256,3,1024]{2,0,1:T(8,128)(2,1)} collective-permute-done((bf16[256,3,1024]{2,0,1:T(8,128)(2,1)}, bf16[256,3,1024]{2,0,1:T(8,128)(2,1)}, u32[]{:S(2)}, u32[]{:S(2)}) %collective-permute-start.9) | collective-permute-done | bytes 1572896 | tf_op jit(solution)/shard_map/ppermute | solution.py:140
  164.9 3.6 %fusion.3 = f32[1,256,3,1024]{3,1,2,0:T(8,128)} fusion(f32[256,1,1024]{2,0,1:T(8,128)S(1)} %convolution_bitcast_fusion, f32[256,1,1024]{2,0,1:T(8,128)S(1)} %convolution_bitcast_fusion.1, f32[256,1,1024]{2,0,1:T(8,128)S(1)} %convolution_bitcast_fusion.2, bf16[256,3,1024]{2,0,1:T(8,128)(2,1)} %collective-permute-done.9), kind=kLoop, calls=%fused_computation.11 | loop fusion | flops 3145728 | bytes 7864320 | tf_op jit(solution)/shard_map/reshape | solution.py:142
  168.5 24.3 %all-to-all-done = bf16[16,96,1024]{2,1,0:T(8,128)(2,1)} async-done(((bf16[16,96,1024]{2,1,0:T(8,128)(2,1)}), bf16[16,96,1024]{2,1,0:T(8,128)(2,1)}, u32[]{:S(2)}, u32[]{:S(2)}) %all-to-all-start) | async-done | bytes 3145760 | tf_op jit(solution)/shard_map/all_to_all | solution.py:214
  192.8 6.4 %multiply_reduce_fusion = bf16[128,1024]{1,0:T(8,128)(2,1)} fusion(f32[128,8]{0,1:T(8,128)S(1)} %copy-done.10, bf16[1536,1024,1]{1,0,2:T(8,128)(2,1)} %bitcast.13, s32[128,8]{0,1:T(8,128)S(1)} %get-tuple-element.14), kind=kOutput, calls=%fused_computation.5 | convolution fusion | flops 3224764416 | bytes 3416064 | tf_op jit(solution)/shard_map/dot_general | solution.py:241
  (93 shorter events, 35.8 us)
Async XLA Ops:
  7.2 101.5 %copy-start = (bf16[1,512,1024]{2,1,0:T(8,128)(2,1)S(1)}, bf16[1,512,1024]{2,1,0:T(8,128)(2,1)}, u32[]{:S(2)}) copy-start(bf16[1,512,1024]{2,1,0:T(8,128)(2,1)} %param.17) | copy-start | bytes 3145732
  7.2 30.6 %copy-start.9 = (bf16[128,1024]{1,0:T(8,128)(2,1)S(1)}, bf16[128,1024]{1,0:T(8,128)(2,1)}, u32[]{:S(2)}) copy-start(bf16[128,1024]{1,0:T(8,128)(2,1)} %param.16) | copy-start | bytes 786436
  7.2 61.8 %all-gather.2.cloned.1.call-start = ((), (), s32[]{:S(2)}) async-start(), calls=%async_computation.1 | async-start | bytes 2654208 | tf_op jit(solution)/shard_map/all_gather | solution.py:92
  13.8 24.7 %collective-permute-start.1 = (bf16[128,1024]{1,0:T(8,128)(2,1)}, bf16[128,1024]{1,0:T(8,128)(2,1)}, u32[]{:S(2)}, u32[]{:S(2)}) collective-permute-start(bf16[128,1024]{1,0:T(8,128)(2,1)} %param.16), channel_id=1, source_target_pairs={{0,4},{4,8},{8,12},{12,14},{14,10},{10,6},{6,2},{2,0},{1,5},{5,9},... | collective-permute-start | bytes 786440 | tf_op jit(solution)/shard_map/ppermute | solution.py:113
  14.0 24.7 %collective-permute-start.2 = (bf16[128,1024]{1,0:T(8,128)(2,1)}, bf16[128,1024]{1,0:T(8,128)(2,1)}, u32[]{:S(2)}, u32[]{:S(2)}) collective-permute-start(bf16[128,1024]{1,0:T(8,128)(2,1)} %param.16), channel_id=1, source_target_pairs={{0,2},{4,0},{8,4},{12,8},{14,12},{10,14},{6,10},{2,6},{1,3},{5,1},... | collective-permute-start | bytes 786440 | tf_op jit(solution)/shard_map/ppermute | solution.py:116
  38.5 33.6 %collective-permute-start.3 = (bf16[128,1024]{1,0:T(8,128)(2,1)}, bf16[128,1024]{1,0:T(8,128)(2,1)}, u32[]{:S(2)}, u32[]{:S(2)}) collective-permute-start(bf16[128,1024]{1,0:T(8,128)(2,1)} %collective-permute-done.1), channel_id=1, source_target_pairs={{0,4},{4,8},{8,12},{12,14},{14,10},{10,6},{6,2},{2,0},{1,5},{5,9},... | collective-permute-start | bytes 786440 | tf_op jit(solution)/shard_map/ppermute | solution.py:113
  38.7 33.4 %collective-permute-start.4 = (bf16[128,1024]{1,0:T(8,128)(2,1)}, bf16[128,1024]{1,0:T(8,128)(2,1)}, u32[]{:S(2)}, u32[]{:S(2)}) collective-permute-start(bf16[128,1024]{1,0:T(8,128)(2,1)} %collective-permute-done.2), channel_id=1, source_target_pairs={{0,2},{4,0},{8,4},{12,8},{14,12},{10,14},{6,10},{2,6},{1,3},{5,1},... | collective-permute-start | bytes 786440 | tf_op jit(solution)/shard_map/ppermute | solution.py:116
  69.0 20.6 %copy-start.7 = (bf16[1024,1152]{1,0:T(8,128)(2,1)S(1)}, bf16[1024,1152]{1,0:T(8,128)(2,1)}, u32[]{:S(2)}) copy-start(bf16[1024,1152]{1,0:T(8,128)(2,1)} %all-gather.2.cloned.1.call-done) | copy-start | bytes 7077892
  69.0 22.3 %collective-permute-start = (bf16[1024,1152]{1,0:T(8,128)(2,1)}, bf16[1024,1152]{1,0:T(8,128)(2,1)}, u32[]{:S(2)}, u32[]{:S(2)}) collective-permute-start(bf16[1024,1152]{1,0:T(8,128)(2,1)} %all-gather.2.cloned.1.call-done), channel_id=1, source_target_pairs={{0,1},{1,0},{2,3},{3,2},{4,5},{5,4},{6,7},{7,6},{8,9},{9,8},{10,11... | collective-permute-start | bytes 7077896 | tf_op jit(solution)/shard_map/ppermute | solution.py:93
  72.1 8.0 %collective-permute-start.5 = (bf16[128,1024]{1,0:T(8,128)(2,1)}, bf16[128,1024]{1,0:T(8,128)(2,1)S(1)}, u32[]{:S(2)}, u32[]{:S(2)}) collective-permute-start(bf16[128,1024]{1,0:T(8,128)(2,1)} %collective-permute-done.3), channel_id=1, source_target_pairs={{0,4},{4,8},{8,12},{12,14},{14,10},{10,6},{6,2},{2,0},{1,5},{5,9},... | collective-permute-start | bytes 786440 | tf_op jit(solution)/shard_map/ppermute | solution.py:113
  72.1 8.9 %collective-permute-start.6 = (bf16[128,1024]{1,0:T(8,128)(2,1)}, bf16[128,1024]{1,0:T(8,128)(2,1)S(1)}, u32[]{:S(2)}, u32[]{:S(2)}) collective-permute-start(bf16[128,1024]{1,0:T(8,128)(2,1)} %collective-permute-done.4), channel_id=1, source_target_pairs={{0,2},{4,0},{8,4},{12,8},{14,12},{10,14},{6,10},{2,6},{1,3},{5,1},... | collective-permute-start | bytes 786440 | tf_op jit(solution)/shard_map/ppermute | solution.py:116
  80.1 6.8 %collective-permute-start.7 = (bf16[128,1024]{1,0:T(8,128)(2,1)S(1)}, bf16[128,1024]{1,0:T(8,128)(2,1)S(1)}, u32[]{:S(2)}, u32[]{:S(2)}) collective-permute-start(bf16[128,1024]{1,0:T(8,128)(2,1)S(1)} %collective-permute-done.5), channel_id=1, source_target_pairs={{0,4},{4,8},{8,12},{12,14},{14,10},{10,6},{6,2},{2,0},{1,5},{5,9},... | collective-permute-start | bytes 786440 | tf_op jit(solution)/shard_map/ppermute | solution.py:113
  87.7 8.3 %collective-permute-start.8 = (bf16[1024,1024]{1,0:T(8,128)(2,1)}, bf16[1024,1024]{1,0:T(8,128)(2,1)}, u32[]{:S(2)}, u32[]{:S(2)}) collective-permute-start(bf16[1024,1024]{1,0:T(8,128)(2,1)} %bitcast.37), channel_id=1, source_target_pairs={{0,1},{1,0},{2,3},{3,2},{4,5},{5,4},{6,7},{7,6},{8,9},{9,8},{10,11... | collective-permute-start | bytes 6291464 | tf_op jit(solution)/shard_map/ppermute | solution.py:119
  102.8 2.8 %copy-start.2 = (bf16[16,96,1024]{2,1,0:T(8,128)(2,1)}, bf16[16,96,1024]{2,1,0:T(8,128)(2,1)S(1)}, u32[]{:S(2)}) copy-start(bf16[16,96,1024]{2,1,0:T(8,128)(2,1)S(1)} %pad_maximum_fusion.2) | copy-start | bytes 9437188
  105.9 7.5 %copy-start.4 = (bf16[16,96,1024]{2,1,0:T(8,128)(2,1)}, bf16[16,96,1024]{2,1,0:T(8,128)(2,1)S(1)}, u32[]{:S(2)}) copy-start(bf16[16,96,1024]{2,1,0:T(8,128)(2,1)S(1)} %pad_maximum_fusion) | copy-start | bytes 9437188
  117.6 5.0 %copy-start.3 = (bf16[16,96,1024]{2,1,0:T(8,128)(2,1)S(1)}, bf16[16,96,1024]{2,1,0:T(8,128)(2,1)}, u32[]{:S(2)}) copy-start(bf16[16,96,1024]{2,1,0:T(8,128)(2,1)} %copy-done.2) | copy-start | bytes 9437188
  117.6 75.2 %all-to-all-start = ((bf16[16,96,1024]{2,1,0:T(8,128)(2,1)}), bf16[16,96,1024]{2,1,0:T(8,128)(2,1)}, u32[]{:S(2)}, u32[]{:S(2)}) async-start(bf16[16,96,1024]{2,1,0:T(8,128)(2,1)} %bitcast.11), calls=%async_computation | async-start | bytes 6291456 | tf_op jit(solution)/shard_map/all_to_all | solution.py:214
  122.6 2.3 %copy-start.5 = (bf16[16,96,1024]{2,1,0:T(8,128)(2,1)S(1)}, bf16[16,96,1024]{2,1,0:T(8,128)(2,1)}, u32[]{:S(2)}) copy-start(bf16[16,96,1024]{2,1,0:T(8,128)(2,1)} %copy-done.4) | copy-start | bytes 9437188
  122.6 2.6 %copy-start.17 = (bf16[1536,512]{1,0:T(8,128)(2,1)S(1)}, bf16[1536,512]{1,0:T(8,128)(2,1)}, u32[]{:S(2)}) copy-start(bf16[1536,512]{1,0:T(8,128)(2,1)} %get-tuple-element.4) | copy-start | bytes 4718596
  128.9 35.9 %collective-permute-start.9 = (bf16[256,3,1024]{2,0,1:T(8,128)(2,1)}, bf16[256,3,1024]{2,0,1:T(8,128)(2,1)}, u32[]{:S(2)}, u32[]{:S(2)}) collective-permute-start(bf16[256,3,1024]{2,0,1:T(8,128)(2,1)} %pad_maximum_fusion.3), channel_id=1, source_target_pairs={{0,16},{16,0},{1,17},{17,1},{2,18},{18,2},{3,19},{19,3},{4,20},{20... | collective-permute-start | bytes 4718600 | tf_op jit(solution)/shard_map/ppermute | solution.py:140
  130.1 3.3 %copy-start.6 = (bf16[16,96,1024]{2,1,0:T(8,128)(2,1)S(1)}, bf16[16,96,1024]{2,1,0:T(8,128)(2,1)}, u32[]{:S(2)}) copy-start(bf16[16,96,1024]{2,1,0:T(8,128)(2,1)} %copy-done.4) | copy-start | bytes 9437188
  130.1 3.5 %copy-start.16 = (bf16[1536,512]{1,0:T(8,128)(2,1)S(1)}, bf16[1536,512]{1,0:T(8,128)(2,1)}, u32[]{:S(2)}) copy-start(bf16[1536,512]{1,0:T(8,128)(2,1)} %get-tuple-element.5) | copy-start | bytes 4718596
  136.1 56.7 %copy-start.10 = (f32[128,8]{0,1:T(8,128)S(1)}, f32[128,8]{0,1:T(8,128)}, u32[]{:S(2)}) copy-start(f32[128,8]{0,1:T(8,128)} %param.15) | copy-start | bytes 12292
  192.8 6.4 %copy-start.1 = (bf16[1,512,1024]{2,1,0:T(8,128)(2,1)S(1)}, bf16[1,512,1024]{2,1,0:T(8,128)(2,1)}, u32[]{:S(2)}) copy-start(bf16[1,512,1024]{2,1,0:T(8,128)(2,1)} %param.17) | copy-start | bytes 3145732
  (6 other events, 9.1 us)
Sparse Core Ops, SparseCore 0:
  13.9 55.0 all-gather.1

commit v9 on v8

--- a/solution.py
+++ b/solution.py
@@ -233,13 +233,18 @@
 
     weight_grads = reduce_grads_dp(grad_half, width)
 
-    target = (routes * capacity + slots_by_rank(routes, experts)).reshape(-1)
-    choose = (
-        target[:, None]
-        == lax.broadcasted_iota(jnp.int32, (tok_rows * topk, experts * capacity), 1)
-    ).astype(jnp.bfloat16)
-    picked = jnp.dot(choose, returned.reshape(-1, width), preferred_element_type=jnp.float32)
-    summed = jnp.sum(picked.reshape(tok_rows, topk, width) * gates[:, :, None], axis=1)
+    target = routes * capacity + slots_by_rank(routes, experts)
+    match = target[:, :, None] == lax.broadcasted_iota(
+        jnp.int32, (1, 1, experts * capacity), 2
+    )
+    flat_back = returned.reshape(-1, width)
+    parts = []
+    for piece in exact_pieces(gates):
+        weights = jnp.sum(
+            jnp.where(match, piece.astype(jnp.float32)[:, :, None], zero), axis=1
+        ).astype(jnp.bfloat16)
+        parts.append(jnp.dot(weights, flat_back, preferred_element_type=jnp.float32))
+    summed = (parts[0] + parts[1]) + parts[2]
     return summed.astype(jnp.bfloat16), weight_grads
 
 

time: 207 us -> 208 us (level)
  the two profiles are of different devices: /device:TPU:11 before, /device:TPU:15 now
where the time goes in v9:
time: 208 us; the launch traced here: 207 us
  waiting for transfers between devices  81.2 us (39%)
  matrix products  35.1 us (17%)
  between operations  32.1 us (15%)
  local copies, waits for them, and re-layouts  26.3 us (13%)
  other arithmetic  19.3 us (9%)
  starting transfers between devices  13.2 us (6%)
    all_gather x1, waiting for transfers between devices, gather_replica(): mine = lax.all_gather(values, 'ez', axis=0, tiled=True)  27.3 us
    all_to_all x1, waiting for transfers between devices, local_gather(): returned = lax.all_to_all(ordered, ('ez', 'core'), 0, 0, tiled=True)  23.2 us
    ppermute x1, waiting for transfers between devices, reduce_grads_dp(): lax.ppermute(grad_half(1 - d).astype(jnp.bfloat16), 'dp', [(0, 1), (1, 0)])  22.4 us
    dot_general x6, matrix products, contract_rows(): lax.dot_general(left, right, (((0,), (0,)), ((), ())), preferred_element_...  12.4 us
    dot_general x3, matrix products, contract_cols(): lax.dot_general(left, right, (((1,), (1,)), ((), ())), preferred_element_...  8.4 us
    ppermute x4, waiting for transfers between devices, ring_gather(): up = lax.ppermute(up, 'ez', ahead)  8.3 us
    dot_general x3, matrix products, local_gather(): jnp.dot(weights, flat_back, preferred_element_type=jnp.float32)  8.2 us
    reduce_sum x1, other arithmetic, local_gather(): jnp.sum(jnp.where(match, piece.astype(jnp.float32)[:, :, None], zero), ax...  6.12 us
  transfers between devices with their start and end apart: 12, of which 5 were waited for; matrix products, arithmetic and copies ran while one was open for 21% of the time, Pallas kernels for 0%

profile of v9, /device:TPU:15, one launch (start us, length us, event | category | flops | bytes accessed | tf_op | source)
XLA Modules:
  0.0 207.2 jit_solution(15487340130193472415)
XLA Ops:
  11.9 1.8 concatenate.12
  41.2 27.3 %all-gather.2.cloned.1.call-done = bf16[1024,1152]{1,0:T(8,128)(2,1)} async-done(((bf16[128,1152]{1,0:T(8,128)(2,1)}), bf16[1024,1152]{1,0:T(8,128)(2,1)}) %all-gather.2.cloned.1.call-update) | async-done | bytes 2359312 | tf_op jit(solution)/shard_map/all_gather | solution.py:92
  76.5 3.2 %collective-permute-done.5 = bf16[128,1024]{1,0:T(8,128)(2,1)S(1)} collective-permute-done((bf16[128,1024]{1,0:T(8,128)(2,1)}, bf16[128,1024]{1,0:T(8,128)(2,1)S(1)}, u32[]{:S(2)}, u32[]{:S(2)}) %collective-permute-start.5) | collective-permute-done | bytes 262176 | tf_op jit(solution)/shard_map/ppermute | solution.py:113
  81.4 5.1 %collective-permute-done.7 = bf16[128,1024]{1,0:T(8,128)(2,1)S(1)} collective-permute-done((bf16[128,1024]{1,0:T(8,128)(2,1)S(1)}, bf16[128,1024]{1,0:T(8,128)(2,1)S(1)}, u32[]{:S(2)}, u32[]{:S(2)}) %collective-permute-start.7) | collective-permute-done | bytes 262176 | tf_op jit(solution)/shard_map/ppermute | solution.py:113
  87.2 1.9 collective-permute-start.8
  93.2 2.3 %fusion.4 = bf16[8,96,1024]{2,1,0:T(8,128)(2,1)S(1)} fusion(bf16[8,128,1024]{2,1,0:T(8,128)(2,1)} %bitcast_dynamic-update-slice_fusion, f32[8,128]{1,0:T(8,128)S(1)} %get-tuple-element.12, s32[16,128]{1,0:T(8,128)S(1)} %convolution_convert_fusion.7, pred[16,128]{1,0:T(8,128)(4,1)S(1)} %bitcast.109), kind=kOutput, calls=%fused_computation.19 | convolution fusion | flops 205651968 | bytes 3684352 | tf_op jit(solution)/shard_map/sjt,std->sjd/dot_general | solution.py:188
  95.5 2.0 multiply_convert_fusion
  98.1 1.8 slice.64
  103.3 1.8 fusion.9
  106.4 1.8 fusion.12
  108.3 4.7 %multiply_convert_fusion.3 = (bf16[1536,512]{1,0:T(8,128)(2,1)}, bf16[1536,512]{1,0:T(8,128)(2,1)}, bf16[1536,512]{1,0:T(8,128)(2,1)S(1)}) fusion(f32[1536,512]{1,0:T(8,128)S(1)} %fusion.9, f32[1536,512]{1,0:T(8,128)S(1)} %fusion.12, bf16[1536,1024]{1,0:T(8,128)(2,1)S(1)} %bitcast.100, bf16[1,512,1024]{2,1,0:T(8,128)(2,1)S(1)} %copy-done), kind=kOutput, calls=%fused_computation.13 | convolution fusion | flops 1622409216 | bytes 15204352 | tf_op jit(solution)/shard_map/dot_general | solution.py:16
  113.0 1.8 convolution_convert_fusion
  115.2 2.0 pad_maximum_fusion.1
  117.1 4.7 %all-to-all-start = ((bf16[16,96,1024]{2,1,0:T(8,128)(2,1)}), bf16[16,96,1024]{2,1,0:T(8,128)(2,1)}, u32[]{:S(2)}, u32[]{:S(2)}) async-start(bf16[16,96,1024]{2,1,0:T(8,128)(2,1)} %bitcast.95), calls=%async_computation | async-start | bytes 6291456 | tf_op jit(solution)/shard_map/all_to_all | solution.py:214
  121.9 2.9 %fusion.7 = bf16[256,1,1024]{2,0,1:T(8,128)(2,1)S(1)} fusion(bf16[1536,1024]{1,0:T(8,128)(2,1)} %bitcast.97, bf16[1536,512]{1,0:T(8,128)(2,1)S(1)} %get-tuple-element.9, s32[]{:T(128)S(6)} %select_n.143), kind=kOutput, calls=%fused_computation.36 | convolution fusion | flops 805568512 | bytes 4456452 | tf_op jit(solution)/shard_map/dot_general | solution.py:10
  124.8 3.3 %fusion.5 = bf16[256,1,1024]{2,0,1:T(8,128)(2,1)S(1)} fusion(bf16[1536,1024]{1,0:T(8,128)(2,1)} %bitcast.101, bf16[1536,512]{1,0:T(8,128)(2,1)} %get-tuple-element.7, s32[]{:T(128)S(6)} %select_n.143), kind=kOutput, calls=%fused_computation.34 | convolution fusion | flops 805568512 | bytes 4456452 | tf_op jit(solution)/shard_map/dot_general | solution.py:10
  130.3 6.1 %select_reduce_fusion = (bf16[128,1536]{1,0:T(8,128)(2,1)S(1)}, bf16[128,1536]{1,0:T(8,128)(2,1)S(1)}, bf16[128,1536]{1,0:T(8,128)(2,1)S(1)}) fusion(f32[128,8]{1,0:T(8,128)S(1)} %copy.49, s32[128,8]{1,0:T(8,128)S(1)} %copy.39, f32[128,8]{1,0:T(8,128)S(1)} %copy.48, f32[128,8]{1,0:T(8,128)S(1)} %copy.40), kind=kLoop, calls=%fused_computation | loop fusion | flops 10420224 | bytes 1196032 | tf_op jit(solution)/shard_map/reduce_sum | solution.py:243
  136.4 3.2 %convolution_bitcast_fusion.2 = f32[256,1,1024]{2,0,1:T(8,128)S(1)} fusion(bf16[1536,1024]{1,0:T(8,128)(2,1)} %bitcast.102, bf16[1536,512]{1,0:T(8,128)(2,1)} %get-tuple-element.7, s32[]{:T(128)S(6)} %select_n.142), kind=kOutput, calls=%fused_computation.28 | convolution fusion | flops 805306368 | bytes 4980740 | tf_op jit(solution)/shard_map/dot_general | solution.py:10
  143.0 22.4 %collective-permute-done.9 = bf16[256,3,1024]{2,0,1:T(8,128)(2,1)} collective-permute-done((bf16[256,3,1024]{2,0,1:T(8,128)(2,1)S(1)}, bf16[256,3,1024]{2,0,1:T(8,128)(2,1)}, u32[]{:S(2)}, u32[]{:S(2)}) %collective-permute-start.9) | collective-permute-done | bytes 1572896 | tf_op jit(solution)/shard_map/ppermute | solution.py:140
  165.3 3.6 %fusion = f32[1,256,3,1024]{3,1,2,0:T(8,128)} fusion(f32[256,1,1024]{2,0,1:T(8,128)S(1)} %convolution_bitcast_fusion, f32[256,1,1024]{2,0,1:T(8,128)S(1)} %convolution_bitcast_fusion.1, f32[256,1,1024]{2,0,1:T(8,128)S(1)} %convolution_bitcast_fusion.2, bf16[256,3,1024]{2,0,1:T(8,128)(2,1)} %collective-permute-done.9), kind=kLoop, calls=%fused_computation.11 | loop fusion | flops 3145728 | bytes 7864320 | tf_op jit(solution)/shard_map/reshape | solution.py:142
  168.9 23.2 %all-to-all-done = bf16[16,96,1024]{2,1,0:T(8,128)(2,1)} async-done(((bf16[16,96,1024]{2,1,0:T(8,128)(2,1)}), bf16[16,96,1024]{2,1,0:T(8,128)(2,1)}, u32[]{:S(2)}, u32[]{:S(2)}) %all-to-all-start) | async-done | bytes 3145760 | tf_op jit(solution)/shard_map/all_to_all | solution.py:214
  192.1 2.5 %fusion.54 = f32[128,1024]{1,0:T(8,128)S(1)} fusion(bf16[128,1536]{1,0:T(8,128)(2,1)S(1)} %get-tuple-element.4, bf16[1536,1024]{1,0:T(8,128)(2,1)} %bitcast.11), kind=kOutput, calls=%fused_computation.114 | convolution fusion | flops 402653184 | bytes 4063232 | tf_op jit(solution)/shard_map/dot_general | solution.py:246
  194.6 2.6 %convolution_add_fusion.1 = f32[128,1024]{1,0:T(8,128)S(1)} fusion(f32[128,1024]{1,0:T(8,128)S(1)} %fusion.54, bf16[1536,1024]{1,0:T(8,128)(2,1)} %bitcast.11, bf16[128,1536]{1,0:T(8,128)(2,1)S(1)} %get-tuple-element.3), kind=kOutput, calls=%fused_computation.33 | convolution fusion | flops 402784256 | bytes 4587520 | tf_op jit(solution)/shard_map/dot_general | solution.py:246
  197.1 3.2 %fusion.8 = bf16[128,1024]{1,0:T(8,128)(2,1)} fusion(f32[128,1024]{1,0:T(8,128)S(1)} %convolution_add_fusion.1, bf16[1536,1024]{1,0:T(8,128)(2,1)} %bitcast.11, bf16[128,1536]{1,0:T(8,128)(2,1)S(1)} %get-tuple-element.2), kind=kOutput, calls=%fused_computation.37 | convolution fusion | flops 402915328 | bytes 4325376 | tf_op jit(solution)/shard_map/dot_general | solution.py:246
  (96 shorter events, 40.0 us)
Async XLA Ops:
  7.2 101.1 %copy-start = (bf16[1,512,1024]{2,1,0:T(8,128)(2,1)S(1)}, bf16[1,512,1024]{2,1,0:T(8,128)(2,1)}, u32[]{:S(2)}) copy-start(bf16[1,512,1024]{2,1,0:T(8,128)(2,1)} %param.17) | copy-start | bytes 3145732
  7.2 30.2 %copy-start.9 = (bf16[128,1024]{1,0:T(8,128)(2,1)S(1)}, bf16[128,1024]{1,0:T(8,128)(2,1)}, u32[]{:S(2)}) copy-start(bf16[128,1024]{1,0:T(8,128)(2,1)} %param.16) | copy-start | bytes 786436
  7.2 61.3 %all-gather.2.cloned.1.call-start = ((), (), s32[]{:S(2)}) async-start(), calls=%async_computation.1 | async-start | bytes 2654208 | tf_op jit(solution)/shard_map/all_gather | solution.py:92
  13.8 24.3 %collective-permute-start.1 = (bf16[128,1024]{1,0:T(8,128)(2,1)}, bf16[128,1024]{1,0:T(8,128)(2,1)}, u32[]{:S(2)}, u32[]{:S(2)}) collective-permute-start(bf16[128,1024]{1,0:T(8,128)(2,1)} %param.16), channel_id=1, source_target_pairs={{0,4},{4,8},{8,12},{12,14},{14,10},{10,6},{6,2},{2,0},{1,5},{5,9},... | collective-permute-start | bytes 786440 | tf_op jit(solution)/shard_map/ppermute | solution.py:113
  14.0 24.3 %collective-permute-start.2 = (bf16[128,1024]{1,0:T(8,128)(2,1)}, bf16[128,1024]{1,0:T(8,128)(2,1)}, u32[]{:S(2)}, u32[]{:S(2)}) collective-permute-start(bf16[128,1024]{1,0:T(8,128)(2,1)} %param.16), channel_id=1, source_target_pairs={{0,2},{4,0},{8,4},{12,8},{14,12},{10,14},{6,10},{2,6},{1,3},{5,1},... | collective-permute-start | bytes 786440 | tf_op jit(solution)/shard_map/ppermute | solution.py:116
  38.1 33.6 %collective-permute-start.3 = (bf16[128,1024]{1,0:T(8,128)(2,1)}, bf16[128,1024]{1,0:T(8,128)(2,1)}, u32[]{:S(2)}, u32[]{:S(2)}) collective-permute-start(bf16[128,1024]{1,0:T(8,128)(2,1)} %collective-permute-done.1), channel_id=1, source_target_pairs={{0,4},{4,8},{8,12},{12,14},{14,10},{10,6},{6,2},{2,0},{1,5},{5,9},... | collective-permute-start | bytes 786440 | tf_op jit(solution)/shard_map/ppermute | solution.py:113
  38.3 33.4 %collective-permute-start.4 = (bf16[128,1024]{1,0:T(8,128)(2,1)}, bf16[128,1024]{1,0:T(8,128)(2,1)}, u32[]{:S(2)}, u32[]{:S(2)}) collective-permute-start(bf16[128,1024]{1,0:T(8,128)(2,1)} %collective-permute-done.2), channel_id=1, source_target_pairs={{0,2},{4,0},{8,4},{12,8},{14,12},{10,14},{6,10},{2,6},{1,3},{5,1},... | collective-permute-start | bytes 786440 | tf_op jit(solution)/shard_map/ppermute | solution.py:116
  68.5 20.6 %copy-start.7 = (bf16[1024,1152]{1,0:T(8,128)(2,1)S(1)}, bf16[1024,1152]{1,0:T(8,128)(2,1)}, u32[]{:S(2)}) copy-start(bf16[1024,1152]{1,0:T(8,128)(2,1)} %all-gather.2.cloned.1.call-done) | copy-start | bytes 7077892
  68.5 22.3 %collective-permute-start = (bf16[1024,1152]{1,0:T(8,128)(2,1)}, bf16[1024,1152]{1,0:T(8,128)(2,1)}, u32[]{:S(2)}, u32[]{:S(2)}) collective-permute-start(bf16[1024,1152]{1,0:T(8,128)(2,1)} %all-gather.2.cloned.1.call-done), channel_id=1, source_target_pairs={{0,1},{1,0},{2,3},{3,2},{4,5},{5,4},{6,7},{7,6},{8,9},{9,8},{10,11... | collective-permute-start | bytes 7077896 | tf_op jit(solution)/shard_map/ppermute | solution.py:93
  71.7 8.0 %collective-permute-start.5 = (bf16[128,1024]{1,0:T(8,128)(2,1)}, bf16[128,1024]{1,0:T(8,128)(2,1)S(1)}, u32[]{:S(2)}, u32[]{:S(2)}) collective-permute-start(bf16[128,1024]{1,0:T(8,128)(2,1)} %collective-permute-done.3), channel_id=1, source_target_pairs={{0,4},{4,8},{8,12},{12,14},{14,10},{10,6},{6,2},{2,0},{1,5},{5,9},... | collective-permute-start | bytes 786440 | tf_op jit(solution)/shard_map/ppermute | solution.py:113
  71.7 8.9 %collective-permute-start.6 = (bf16[128,1024]{1,0:T(8,128)(2,1)}, bf16[128,1024]{1,0:T(8,128)(2,1)S(1)}, u32[]{:S(2)}, u32[]{:S(2)}) collective-permute-start(bf16[128,1024]{1,0:T(8,128)(2,1)} %collective-permute-done.4), channel_id=1, source_target_pairs={{0,2},{4,0},{8,4},{12,8},{14,12},{10,14},{6,10},{2,6},{1,3},{5,1},... | collective-permute-start | bytes 786440 | tf_op jit(solution)/shard_map/ppermute | solution.py:116
  79.7 6.8 %collective-permute-start.7 = (bf16[128,1024]{1,0:T(8,128)(2,1)S(1)}, bf16[128,1024]{1,0:T(8,128)(2,1)S(1)}, u32[]{:S(2)}, u32[]{:S(2)}) collective-permute-start(bf16[128,1024]{1,0:T(8,128)(2,1)S(1)} %collective-permute-done.5), channel_id=1, source_target_pairs={{0,4},{4,8},{8,12},{12,14},{14,10},{10,6},{6,2},{2,0},{1,5},{5,9},... | collective-permute-start | bytes 786440 | tf_op jit(solution)/shard_map/ppermute | solution.py:113
  87.2 8.3 %collective-permute-start.8 = (bf16[1024,1024]{1,0:T(8,128)(2,1)}, bf16[1024,1024]{1,0:T(8,128)(2,1)}, u32[]{:S(2)}, u32[]{:S(2)}) collective-permute-start(bf16[1024,1024]{1,0:T(8,128)(2,1)} %bitcast.35), channel_id=1, source_target_pairs={{0,1},{1,0},{2,3},{3,2},{4,5},{5,4},{6,7},{7,6},{8,9},{9,8},{10,11... | collective-permute-start | bytes 6291464 | tf_op jit(solution)/shard_map/ppermute | solution.py:119
  102.3 2.8 %copy-start.2 = (bf16[16,96,1024]{2,1,0:T(8,128)(2,1)}, bf16[16,96,1024]{2,1,0:T(8,128)(2,1)S(1)}, u32[]{:S(2)}) copy-start(bf16[16,96,1024]{2,1,0:T(8,128)(2,1)S(1)} %pad_maximum_fusion.2) | copy-start | bytes 9437188
  105.4 2.8 %copy-start.4 = (bf16[16,96,1024]{2,1,0:T(8,128)(2,1)}, bf16[16,96,1024]{2,1,0:T(8,128)(2,1)S(1)}, u32[]{:S(2)}) copy-start(bf16[16,96,1024]{2,1,0:T(8,128)(2,1)S(1)} %pad_maximum_fusion) | copy-start | bytes 9437188
  113.0 8.9 %copy-start.12 = (bf16[1536,512]{1,0:T(8,128)(2,1)}, bf16[1536,512]{1,0:T(8,128)(2,1)S(1)}, u32[]{:S(2)}) copy-start(bf16[1536,512]{1,0:T(8,128)(2,1)S(1)} %get-tuple-element.9) | copy-start | bytes 4718596
  117.1 75.0 %all-to-all-start = ((bf16[16,96,1024]{2,1,0:T(8,128)(2,1)}), bf16[16,96,1024]{2,1,0:T(8,128)(2,1)}, u32[]{:S(2)}, u32[]{:S(2)}) async-start(bf16[16,96,1024]{2,1,0:T(8,128)(2,1)} %bitcast.95), calls=%async_computation | async-start | bytes 6291456 | tf_op jit(solution)/shard_map/all_to_all | solution.py:214
  124.8 3.3 %copy-start.5 = (bf16[16,96,1024]{2,1,0:T(8,128)(2,1)S(1)}, bf16[16,96,1024]{2,1,0:T(8,128)(2,1)}, u32[]{:S(2)}) copy-start(bf16[16,96,1024]{2,1,0:T(8,128)(2,1)} %copy-done.4) | copy-start | bytes 9437188
  124.8 3.5 %copy-start.14 = (bf16[1536,512]{1,0:T(8,128)(2,1)S(1)}, bf16[1536,512]{1,0:T(8,128)(2,1)}, u32[]{:S(2)}) copy-start(bf16[1536,512]{1,0:T(8,128)(2,1)} %get-tuple-element.8) | copy-start | bytes 4718596
  129.5 35.8 %collective-permute-start.9 = (bf16[256,3,1024]{2,0,1:T(8,128)(2,1)S(1)}, bf16[256,3,1024]{2,0,1:T(8,128)(2,1)}, u32[]{:S(2)}, u32[]{:S(2)}) collective-permute-start(bf16[256,3,1024]{2,0,1:T(8,128)(2,1)S(1)} %pad_maximum_fusion.3), channel_id=1, source_target_pairs={{0,16},{16,0},{1,17},{17,1},{2,18},{18,2},{3,19},{19,3},{4,20},{20... | collective-permute-start | bytes 4718600 | tf_op jit(solution)/shard_map/ppermute | solution.py:140
  130.3 9.3 %copy-start.6 = (bf16[16,96,1024]{2,1,0:T(8,128)(2,1)S(1)}, bf16[16,96,1024]{2,1,0:T(8,128)(2,1)}, u32[]{:S(2)}) copy-start(bf16[16,96,1024]{2,1,0:T(8,128)(2,1)} %copy-done.4) | copy-start | bytes 9437188
  130.3 9.3 %copy-start.15 = (bf16[1536,512]{1,0:T(8,128)(2,1)S(1)}, bf16[1536,512]{1,0:T(8,128)(2,1)}, u32[]{:S(2)}) copy-start(bf16[1536,512]{1,0:T(8,128)(2,1)} %get-tuple-element.8) | copy-start | bytes 4718596
  139.6 2.3 %copy-start.13 = (bf16[1536,512]{1,0:T(8,128)(2,1)S(1)}, bf16[1536,512]{1,0:T(8,128)(2,1)}, u32[]{:S(2)}) copy-start(bf16[1536,512]{1,0:T(8,128)(2,1)} %copy-done.12) | copy-start | bytes 4718596
  194.6 5.8 %copy-start.1 = (bf16[1,512,1024]{2,1,0:T(8,128)(2,1)S(1)}, bf16[1,512,1024]{2,1,0:T(8,128)(2,1)}, u32[]{:S(2)}) copy-start(bf16[1,512,1024]{2,1,0:T(8,128)(2,1)} %param.17) | copy-start | bytes 3145732
  (4 other events, 6.0 us)
Sparse Core Ops, SparseCore 0:
  13.9 54.5 all-gather.1

commit v10 on v8

--- a/solution.py
+++ b/solution.py
@@ -159,9 +159,14 @@
     meta.append(jnp.zeros((tok_rows, pad), jnp.bfloat16))
     packed = jnp.concatenate([tokens] + meta, axis=1)
 
-    halves = gather_replica(packed)
+    gathered = lax.all_gather(packed, ("ez", "core"), axis=0, tiled=True)
     cot_halves = ring_gather(cotangent)
-    all_p = jnp.concatenate([h[:, width:] for h in halves], axis=0)
+    on_core0 = core == 0
+    cot_by_core = [
+        jnp.where(on_core0, cot_halves[0], cot_halves[1]),
+        jnp.where(on_core0, cot_halves[1], cot_halves[0]),
+    ]
+    all_p = gathered[:, width:]
     cols = [all_p[:, topk * i: topk * (i + 1)] for i in range(7)]
     hit = cols[0].astype(jnp.int32) == me
     zero = jnp.zeros((), jnp.float32)
@@ -177,25 +182,28 @@
     slot_ids = lax.broadcasted_iota(jnp.int32, (experts, capacity, tok_rows), 1)
     pick = (routed[:, None, :] & (rank[:, None, :] == slot_ids)).astype(jnp.bfloat16)
 
-    def select(part, scale=None):
-        picked = []
-        for h, half in enumerate(halves if part == 0 else cot_halves):
-            values = half[:, :width]
-            if scale is not None:
-                rows = slice(h * nchip * tok_rows, (h + 1) * nchip * tok_rows)
-                values = (scale[rows, None] * values.astype(jnp.float32)).astype(jnp.bfloat16)
-            picked.append(
-                jnp.einsum(
-                    "sjt,std->sjd",
-                    pick[h * nchip:(h + 1) * nchip],
-                    values.reshape(nchip, tok_rows, width),
-                    preferred_element_type=jnp.float32,
-                ).astype(jnp.bfloat16)
-            )
-        return jnp.concatenate(picked, axis=0).reshape(experts * capacity, width)
-
-    rows_x = select(0)
-    rows_q = select(1, fac)
+    rows_x = jnp.einsum(
+        "sjt,std->sjd",
+        pick,
+        gathered[:, :width].reshape(experts, tok_rows, width),
+        preferred_element_type=jnp.float32,
+    ).astype(jnp.bfloat16).reshape(experts * capacity, width)
+    pick_by_core = pick.reshape(nchip, ncore, capacity, tok_rows)
+    fac_by_core = fac.reshape(nchip, ncore, tok_rows)
+    rows_q = []
+    for k in range(ncore):
+        scaled = fac_by_core[:, k, :, None] * cot_by_core[k].reshape(
+            nchip, tok_rows, width
+        ).astype(jnp.float32)
+        rows_q.append(
+            jnp.einsum(
+                "sjt,std->sjd",
+                pick_by_core[:, k],
+                scaled.astype(jnp.bfloat16),
+                preferred_element_type=jnp.float32,
+            ).astype(jnp.bfloat16)
+        )
+    rows_q = jnp.stack(rows_q, axis=1).reshape(experts * capacity, width)
     wgate, wup, wdown = w_gate[0], w_up[0], w_down[0]
     gate_pre = contract_cols(rows_x, wgate)
     up_pre = contract_cols(rows_x, wup)
@@ -206,11 +214,7 @@
         jnp.bfloat16
     )
 
-    by_group = expert_out.reshape(ncore, nchip, capacity, width)
-    ordered = jnp.stack(
-        [lax.dynamic_index_in_dim(by_group, k ^ core, 0, keepdims=False) for k in range(ncore)],
-        axis=1,
-    ).reshape(experts, capacity, width)
+    ordered = expert_out.reshape(experts, capacity, width)
     returned = lax.all_to_all(ordered, ("ez", "core"), 0, 0, tiled=True)
 
     back = contract_cols(rows_q, wdown)

time: 207 us -> 198 us (0.957)
  the two profiles are of different devices: /device:TPU:11 before, /device:TPU:15 now
where the time goes in v10:
time: 198 us; the launch traced here: 197 us
  waiting for transfers between devices  86.7 us (44%)
  between operations  32.3 us (16%)
  matrix products  31.1 us (16%)
  starting transfers between devices  16.9 us (9%)
  other arithmetic  15.8 us (8%)
  local copies, waits for them, and re-layouts  14.4 us (7%)
    ppermute x4, waiting for transfers between devices, ring_gather(): up = lax.ppermute(up, 'ez', ahead)  29.2 us
    ppermute x1, waiting for transfers between devices, reduce_grads_dp(): lax.ppermute(grad_half(1 - d).astype(jnp.bfloat16), 'dp', [(0, 1), (1, 0)])  28.6 us
    all_to_all x1, waiting for transfers between devices, local_gather(): returned = lax.all_to_all(ordered, ('ez', 'core'), 0, 0, tiled=True)  24.9 us
    dot_general x6, matrix products, contract_rows(): lax.dot_general(left, right, (((0,), (0,)), ((), ())), preferred_element_...  10.4 us
    dot_general x3, matrix products, contract_cols(): lax.dot_general(left, right, (((1,), (1,)), ((), ())), preferred_element_...  8.24 us
    all_to_all x1, starting transfers between devices, local_gather(): returned = lax.all_to_all(ordered, ('ez', 'core'), 0, 0, tiled=True)  7.96 us
    dot_general x1, matrix products, local_gather(): jnp.dot(choose, returned.reshape(-1, width), preferred_element_type=jnp.f...  6.35 us
  transfers between devices with their start and end apart: 11, of which 6 were waited for; matrix products, arithmetic and copies ran while one was open for 12% of the time, Pallas kernels for 0%

profile of v10, /device:TPU:15, one launch (start us, length us, event | category | flops | bytes accessed | tf_op | source)
XLA Modules:
  0.0 197.2 jit_solution(3172714353301527872)
XLA Ops:
  11.9 1.8 concatenate.3
  21.2 1.6 fusion.61
  39.9 3.4 %collective-permute-done.2 = bf16[128,1024]{1,0:T(8,128)(2,1)S(1)} collective-permute-done((bf16[128,1024]{1,0:T(8,128)(2,1)}, bf16[128,1024]{1,0:T(8,128)(2,1)S(1)}, u32[]{:S(2)}, u32[]{:S(2)}) %collective-permute-start.2) | collective-permute-done | bytes 262176 | tf_op jit(solution)/shard_map/ppermute | solution.py:113
  44.7 16.2 %collective-permute-done.4 = bf16[128,1024]{1,0:T(8,128)(2,1)S(1)} collective-permute-done((bf16[128,1024]{1,0:T(8,128)(2,1)S(1)}, bf16[128,1024]{1,0:T(8,128)(2,1)S(1)}, u32[]{:S(2)}, u32[]{:S(2)}) %collective-permute-start.4) | collective-permute-done | bytes 262176 | tf_op jit(solution)/shard_map/ppermute | solution.py:113
  61.0 1.8 collective-permute-start.6
  62.9 9.6 %collective-permute-done.6 = bf16[128,1024]{1,0:T(8,128)(2,1)S(1)} collective-permute-done((bf16[128,1024]{1,0:T(8,128)(2,1)S(1)}, bf16[128,1024]{1,0:T(8,128)(2,1)S(1)}, u32[]{:S(2)}, u32[]{:S(2)}) %collective-permute-start.6) | collective-permute-done | bytes 262176 | tf_op jit(solution)/shard_map/ppermute | solution.py:113
  72.6 2.4 %collective-permute-start.7 = (bf16[1024,1024]{1,0:T(8,128)(2,1)S(1)}, bf16[1024,1024]{1,0:T(8,128)(2,1)}, u32[]{:S(2)}, u32[]{:S(2)}) collective-permute-start(bf16[1024,1024]{1,0:T(8,128)(2,1)S(1)} %bitcast.109), channel_id=1, source_target_pairs={{0,1},{1,0},{2,3},{3,2},{4,5},{5,4},{6,7},{7,6},{8,9},{9,8},{10,11... | collective-permute-start | bytes 6291464 | tf_op jit(solution)/shard_map/ppermute | solution.py:119
  74.9 3.9 %collective-permute-done.7 = bf16[1024,1024]{1,0:T(8,128)(2,1)} collective-permute-done((bf16[1024,1024]{1,0:T(8,128)(2,1)S(1)}, bf16[1024,1024]{1,0:T(8,128)(2,1)}, u32[]{:S(2)}, u32[]{:S(2)}) %collective-permute-start.7) | collective-permute-done | bytes 2097184 | tf_op jit(solution)/shard_map/ppermute | solution.py:119
  78.8 3.9 %broadcast_select_fusion.1 = (bf16[1024,1024]{1,0:T(8,128)(2,1)}, bf16[1024,1024]{1,0:T(8,128)(2,1)S(1)}) fusion(bf16[1024,1024]{1,0:T(8,128)(2,1)} %collective-permute-done.7, pred[]{:T(512)S(6)} %eq.82, bf16[8,128,1024]{2,1,0:T(8,128)(2,1)} %copy-done.2), kind=kLoop, calls=%fused_computation.24 | loop fusion | flops 2097152 | bytes 8388609 | tf_op jit(solution)/shard_map/jit(_where)/select_n | solution.py:166
  82.7 1.4 fusion.50
  84.3 2.6 %select_reduce_fusion = f32[2048]{0:T(1024)S(1)} fusion(bf16[2048,1152]{1,0:T(8,128)(2,1)} %all-gather.2.cloned.1.call-done, s32[]{:T(128)S(6)} %add.127), kind=kLoop, calls=%fused_computation.48 | loop fusion | flops 145408 | bytes 139268 | tf_op jit(solution)/shard_map/reduce_sum | solution.py:173
  89.2 1.7 copy-done.6
  90.9 1.8 fusion.31
  92.8 2.2 %slice-done = bf16[2048,1024]{1,0:T(8,128)(2,1)S(1)} async-done(((bf16[2048,1152]{1,0:T(8,128)(2,1)}), bf16[2048,1024]{1,0:T(8,128)(2,1)S(1)}, s32[]{:S(2)}) %slice-start) | async-done | bytes 4194328 | tf_op jit(solution)/shard_map/slice | solution.py:188
  96.2 1.8 fusion.34
  98.0 4.6 %multiply_convert_fusion.1 = (bf16[1536,512]{1,0:T(8,128)(2,1)}, bf16[1536,512]{1,0:T(8,128)(2,1)}, bf16[1536,512]{1,0:T(8,128)(2,1)S(1)}) fusion(f32[1536,512]{1,0:T(8,128)S(1)} %fusion.31, f32[1536,512]{1,0:T(8,128)S(1)} %fusion.34, bf16[1536,1024]{1,0:T(8,128)(2,1)S(1)} %bitcast.111, bf16[1,512,1024]{2,1,0:T(8,128)(2,1)S(1)} %copy-done), kind=kOutput, calls=%fused_computation.13 | convolution fusion | flops 1622409216 | bytes 15204352 | tf_op jit(solution)/shard_map/dot_general | solution.py:16
  102.6 3.5 %convolution_convert_fusion = bf16[1536,1024]{1,0:T(8,128)(2,1)} fusion(bf16[1536,512]{1,0:T(8,128)(2,1)S(1)} %get-tuple-element.4, bf16[1,512,1024]{2,1,0:T(8,128)(2,1)S(1)} %copy-done.11), kind=kOutput, calls=%fused_computation.8 | convolution fusion | flops 1612185600 | bytes 5767168 | tf_op jit(solution)/shard_map/dot_general | solution.py:213
  106.1 8.0 %all-to-all-start = ((bf16[16,96,1024]{2,1,0:T(8,128)(2,1)}), bf16[16,96,1024]{2,1,0:T(8,128)(2,1)}, u32[]{:S(2)}, u32[]{:S(2)}) async-start(bf16[16,96,1024]{2,1,0:T(8,128)(2,1)} %bitcast.119), calls=%async_computation | async-start | bytes 6291456 | tf_op jit(solution)/shard_map/all_to_all | solution.py:218
  114.1 3.1 %fusion.30 = bf16[256,1,1024]{2,0,1:T(8,128)(2,1)S(1)} fusion(bf16[1536,1024]{1,0:T(8,128)(2,1)} %bitcast.117, bf16[1536,512]{1,0:T(8,128)(2,1)S(1)} %get-tuple-element.4, s32[]{:T(128)S(6)} %select_n.136), kind=kOutput, calls=%fused_computation.38 | convolution fusion | flops 805568512 | bytes 4456452 | tf_op jit(solution)/shard_map/dot_general | solution.py:10
  120.0 3.3 %convolution_bitcast_fusion.2 = f32[256,1,1024]{2,0,1:T(8,128)S(1)} fusion(bf16[1536,1024]{1,0:T(8,128)(2,1)} %bitcast.112, bf16[1536,512]{1,0:T(8,128)(2,1)} %get-tuple-element.2, s32[]{:T(128)S(6)} %select_n.135), kind=kOutput, calls=%fused_computation.32 | convolution fusion | flops 805306368 | bytes 4980740 | tf_op jit(solution)/shard_map/dot_general | solution.py:10
  126.9 28.6 %collective-permute-done.8 = bf16[256,3,1024]{2,0,1:T(8,128)(2,1)} collective-permute-done((bf16[256,3,1024]{2,0,1:T(8,128)(2,1)S(1)}, bf16[256,3,1024]{2,0,1:T(8,128)(2,1)}, u32[]{:S(2)}, u32[]{:S(2)}) %collective-permute-start.8) | collective-permute-done | bytes 1572896 | tf_op jit(solution)/shard_map/ppermute | solution.py:140
  155.6 3.6 %fusion.5 = f32[1,256,3,1024]{3,1,2,0:T(8,128)} fusion(f32[256,1,1024]{2,0,1:T(8,128)S(1)} %convolution_bitcast_fusion, f32[256,1,1024]{2,0,1:T(8,128)S(1)} %convolution_bitcast_fusion.1, f32[256,1,1024]{2,0,1:T(8,128)S(1)} %convolution_bitcast_fusion.2, bf16[256,3,1024]{2,0,1:T(8,128)(2,1)} %collective-permute-done.8), kind=kLoop, calls=%fused_computation.11 | loop fusion | flops 3145728 | bytes 7864320 | tf_op jit(solution)/shard_map/reshape | solution.py:142
  159.2 24.9 %all-to-all-done = bf16[16,96,1024]{2,1,0:T(8,128)(2,1)} async-done(((bf16[16,96,1024]{2,1,0:T(8,128)(2,1)}), bf16[16,96,1024]{2,1,0:T(8,128)(2,1)}, u32[]{:S(2)}, u32[]{:S(2)}) %all-to-all-start) | async-done | bytes 3145760 | tf_op jit(solution)/shard_map/all_to_all | solution.py:218
  184.0 6.4 %multiply_reduce_fusion = bf16[128,1024]{1,0:T(8,128)(2,1)} fusion(f32[128,8]{0,1:T(8,128)S(1)} %copy-done.9, bf16[1536,1024,1]{1,0,2:T(8,128)(2,1)} %bitcast.9, s32[128,8]{0,1:T(8,128)S(1)} %get-tuple-element.12), kind=kOutput, calls=%fused_computation.7 | convolution fusion | flops 3224764416 | bytes 3416064 | tf_op jit(solution)/shard_map/dot_general | solution.py:245
  (88 shorter events, 23.0 us)
Async XLA Ops:
  7.2 90.9 %copy-start = (bf16[1,512,1024]{2,1,0:T(8,128)(2,1)S(1)}, bf16[1,512,1024]{2,1,0:T(8,128)(2,1)}, u32[]{:S(2)}) copy-start(bf16[1,512,1024]{2,1,0:T(8,128)(2,1)} %param.17) | copy-start | bytes 3145732
  7.2 29.2 %copy-start.8 = (bf16[128,1024]{1,0:T(8,128)(2,1)S(1)}, bf16[128,1024]{1,0:T(8,128)(2,1)}, u32[]{:S(2)}) copy-start(bf16[128,1024]{1,0:T(8,128)(2,1)} %param.16) | copy-start | bytes 786436
  7.2 75.5 %all-gather.2.cloned.1.call-start = ((), (), s32[]{:S(2)}) async-start(), calls=%async_computation.1 | async-start | bytes 5013504 | tf_op jit(solution)/shard_map/all_gather | solution.py:162
  13.8 22.6 %collective-permute-start = (bf16[128,1024]{1,0:T(8,128)(2,1)}, bf16[128,1024]{1,0:T(8,128)(2,1)}, u32[]{:S(2)}, u32[]{:S(2)}) collective-permute-start(bf16[128,1024]{1,0:T(8,128)(2,1)} %param.16), channel_id=1, source_target_pairs={{0,4},{4,8},{8,12},{12,14},{14,10},{10,6},{6,2},{2,0},{1,5},{5,9},... | collective-permute-start | bytes 786440 | tf_op jit(solution)/shard_map/ppermute | solution.py:113
  14.0 22.6 %collective-permute-start.1 = (bf16[128,1024]{1,0:T(8,128)(2,1)}, bf16[128,1024]{1,0:T(8,128)(2,1)}, u32[]{:S(2)}, u32[]{:S(2)}) collective-permute-start(bf16[128,1024]{1,0:T(8,128)(2,1)} %param.16), channel_id=1, source_target_pairs={{0,2},{4,0},{8,4},{12,8},{14,12},{10,14},{6,10},{2,6},{1,3},{5,1},... | collective-permute-start | bytes 786440 | tf_op jit(solution)/shard_map/ppermute | solution.py:116
  36.4 6.8 %collective-permute-start.2 = (bf16[128,1024]{1,0:T(8,128)(2,1)}, bf16[128,1024]{1,0:T(8,128)(2,1)S(1)}, u32[]{:S(2)}, u32[]{:S(2)}) collective-permute-start(bf16[128,1024]{1,0:T(8,128)(2,1)} %collective-permute-done), channel_id=1, source_target_pairs={{0,4},{4,8},{8,12},{12,14},{14,10},{10,6},{6,2},{2,0},{1,5},{5,9},... | collective-permute-start | bytes 786440 | tf_op jit(solution)/shard_map/ppermute | solution.py:113
  36.6 6.8 %collective-permute-start.3 = (bf16[128,1024]{1,0:T(8,128)(2,1)}, bf16[128,1024]{1,0:T(8,128)(2,1)S(1)}, u32[]{:S(2)}, u32[]{:S(2)}) collective-permute-start(bf16[128,1024]{1,0:T(8,128)(2,1)} %collective-permute-done.1), channel_id=1, source_target_pairs={{0,2},{4,0},{8,4},{12,8},{14,12},{10,14},{6,10},{2,6},{1,3},{5,1},... | collective-permute-start | bytes 786440 | tf_op jit(solution)/shard_map/ppermute | solution.py:116
  43.2 17.7 %collective-permute-start.4 = (bf16[128,1024]{1,0:T(8,128)(2,1)S(1)}, bf16[128,1024]{1,0:T(8,128)(2,1)S(1)}, u32[]{:S(2)}, u32[]{:S(2)}) collective-permute-start(bf16[128,1024]{1,0:T(8,128)(2,1)S(1)} %collective-permute-done.2), channel_id=1, source_target_pairs={{0,4},{4,8},{8,12},{12,14},{14,10},{10,6},{6,2},{2,0},{1,5},{5,9},... | collective-permute-start | bytes 786440 | tf_op jit(solution)/shard_map/ppermute | solution.py:113
  43.4 19.4 %collective-permute-start.5 = (bf16[128,1024]{1,0:T(8,128)(2,1)S(1)}, bf16[128,1024]{1,0:T(8,128)(2,1)S(1)}, u32[]{:S(2)}, u32[]{:S(2)}) collective-permute-start(bf16[128,1024]{1,0:T(8,128)(2,1)S(1)} %collective-permute-done.3), channel_id=1, source_target_pairs={{0,2},{4,0},{8,4},{12,8},{14,12},{10,14},{6,10},{2,6},{1,3},{5,1},... | collective-permute-start | bytes 786440 | tf_op jit(solution)/shard_map/ppermute | solution.py:116
  61.0 11.6 %collective-permute-start.6 = (bf16[128,1024]{1,0:T(8,128)(2,1)S(1)}, bf16[128,1024]{1,0:T(8,128)(2,1)S(1)}, u32[]{:S(2)}, u32[]{:S(2)}) collective-permute-start(bf16[128,1024]{1,0:T(8,128)(2,1)S(1)} %collective-permute-done.4), channel_id=1, source_target_pairs={{0,4},{4,8},{8,12},{12,14},{14,10},{10,6},{6,2},{2,0},{1,5},{5,9},... | collective-permute-start | bytes 786440 | tf_op jit(solution)/shard_map/ppermute | solution.py:113
  72.5 2.4 %copy-start.2 = (bf16[8,128,1024]{2,1,0:T(8,128)(2,1)}, bf16[8,128,1024]{2,1,0:T(8,128)(2,1)S(1)}, u32[]{:S(2)}) copy-start(bf16[8,128,1024]{2,1,0:T(8,128)(2,1)S(1)} %bitcast_dynamic-update-slice_fusion) | copy-start | bytes 6291460
  72.6 6.3 %collective-permute-start.7 = (bf16[1024,1024]{1,0:T(8,128)(2,1)S(1)}, bf16[1024,1024]{1,0:T(8,128)(2,1)}, u32[]{:S(2)}, u32[]{:S(2)}) collective-permute-start(bf16[1024,1024]{1,0:T(8,128)(2,1)S(1)} %bitcast.109), channel_id=1, source_target_pairs={{0,1},{1,0},{2,3},{3,2},{4,5},{5,4},{6,7},{7,6},{8,9},{9,8},{10,11... | collective-permute-start | bytes 6291464 | tf_op jit(solution)/shard_map/ppermute | solution.py:119
  84.2 2.8 %copy-start.1 = (bf16[1024,1024]{1,0:T(8,128)(2,1)S(1)}, bf16[1024,1024]{1,0:T(8,128)(2,1)}, u32[]{:S(2)}) copy-start(bf16[1024,1024]{1,0:T(8,128)(2,1)} %get-tuple-element.5) | copy-start | bytes 6291460
  88.8 2.1 %copy-start.11 = (bf16[1,512,1024]{2,1,0:T(8,128)(2,1)S(1)}, bf16[1,512,1024]{2,1,0:T(8,128)(2,1)}, u32[]{:S(2)}) copy-start(bf16[1,512,1024]{2,1,0:T(8,128)(2,1)} %param.19) | copy-start | bytes 3145732
  92.8 2.2 %slice-start = ((bf16[2048,1152]{1,0:T(8,128)(2,1)}), bf16[2048,1024]{1,0:T(8,128)(2,1)S(1)}, s32[]{:S(2)}) async-start(bf16[2048,1152]{1,0:T(8,128)(2,1)} %all-gather.2.cloned.1.call-done), calls=%async_computation.2 | async-start | bytes 8388608 | tf_op jit(solution)/shard_map/slice | solution.py:188
  102.6 11.5 %copy-start.12 = (bf16[1536,512]{1,0:T(8,128)(2,1)}, bf16[1536,512]{1,0:T(8,128)(2,1)S(1)}, u32[]{:S(2)}) copy-start(bf16[1536,512]{1,0:T(8,128)(2,1)S(1)} %get-tuple-element.4) | copy-start | bytes 4718596
  106.1 78.0 %all-to-all-start = ((bf16[16,96,1024]{2,1,0:T(8,128)(2,1)}), bf16[16,96,1024]{2,1,0:T(8,128)(2,1)}, u32[]{:S(2)}, u32[]{:S(2)}) async-start(bf16[16,96,1024]{2,1,0:T(8,128)(2,1)} %bitcast.119), calls=%async_computation | async-start | bytes 6291456 | tf_op jit(solution)/shard_map/all_to_all | solution.py:218
  114.1 3.1 %copy-start.4 = (bf16[16,96,1024]{2,1,0:T(8,128)(2,1)S(1)}, bf16[16,96,1024]{2,1,0:T(8,128)(2,1)}, u32[]{:S(2)}) copy-start(bf16[16,96,1024]{2,1,0:T(8,128)(2,1)} %copy-done.3) | copy-start | bytes 9437188
  114.1 3.3 %copy-start.16 = (bf16[1536,512]{1,0:T(8,128)(2,1)S(1)}, bf16[1536,512]{1,0:T(8,128)(2,1)}, u32[]{:S(2)}) copy-start(bf16[1536,512]{1,0:T(8,128)(2,1)} %get-tuple-element.2) | copy-start | bytes 4718596
  119.8 35.8 %collective-permute-start.8 = (bf16[256,3,1024]{2,0,1:T(8,128)(2,1)S(1)}, bf16[256,3,1024]{2,0,1:T(8,128)(2,1)}, u32[]{:S(2)}, u32[]{:S(2)}) collective-permute-start(bf16[256,3,1024]{2,0,1:T(8,128)(2,1)S(1)} %pad_maximum_fusion.1), channel_id=1, source_target_pairs={{0,16},{16,0},{1,17},{17,1},{2,18},{18,2},{3,19},{19,3},{4,20},{20... | collective-permute-start | bytes 4718600 | tf_op jit(solution)/shard_map/ppermute | solution.py:140
  120.0 3.3 %copy-start.5 = (bf16[16,96,1024]{2,1,0:T(8,128)(2,1)S(1)}, bf16[16,96,1024]{2,1,0:T(8,128)(2,1)}, u32[]{:S(2)}) copy-start(bf16[16,96,1024]{2,1,0:T(8,128)(2,1)} %copy-done.3) | copy-start | bytes 9437188
  120.0 3.5 %copy-start.15 = (bf16[1536,512]{1,0:T(8,128)(2,1)S(1)}, bf16[1536,512]{1,0:T(8,128)(2,1)}, u32[]{:S(2)}) copy-start(bf16[1536,512]{1,0:T(8,128)(2,1)} %get-tuple-element.3) | copy-start | bytes 4718596
  123.6 2.4 %copy-start.13 = (bf16[1536,512]{1,0:T(8,128)(2,1)S(1)}, bf16[1536,512]{1,0:T(8,128)(2,1)}, u32[]{:S(2)}) copy-start(bf16[1536,512]{1,0:T(8,128)(2,1)} %copy-done.12) | copy-start | bytes 4718596
  126.9 57.1 %copy-start.9 = (f32[128,8]{0,1:T(8,128)S(1)}, f32[128,8]{0,1:T(8,128)}, u32[]{:S(2)}) copy-start(f32[128,8]{0,1:T(8,128)} %param.15) | copy-start | bytes 12292
  (5 other events, 8.3 us)
Sparse Core Ops, SparseCore 0:
  13.9 65.3 all-gather.1

commit v11 on v10

--- a/solution.py
+++ b/solution.py
@@ -214,8 +214,29 @@
         jnp.bfloat16
     )
 
-    ordered = expert_out.reshape(experts, capacity, width)
-    returned = lax.all_to_all(ordered, ("ez", "core"), 0, 0, tiled=True)
+    pick_k = pick.reshape(nchip, ncore, capacity, tok_rows)
+    out_k = expert_out.reshape(nchip, ncore, capacity, width)
+    dense = [
+        jnp.einsum(
+            "sjt,sjd->std", pick_k[:, k], out_k[:, k], preferred_element_type=jnp.float32
+        ).astype(jnp.bfloat16)
+        for k in range(ncore)
+    ]
+    mine = jnp.where(on_core0, dense[0], dense[1])
+    from_partner = lax.ppermute(
+        jnp.where(on_core0, dense[1], dense[0]), "core", [(0, 1), (1, 0)]
+    )
+    gate_all = joined(cols[4:7]).reshape(nchip, ncore, tok_rows, topk)
+    routes_all = cols[0].astype(jnp.int32).reshape(nchip, ncore, tok_rows, topk)
+    gate_own = jnp.where(on_core0, gate_all[:, 0], gate_all[:, 1])
+    routes_own = jnp.where(on_core0, routes_all[:, 0], routes_all[:, 1])
+    gte = jnp.sum(jnp.where(routes_own == me, gate_own, zero), axis=2)
+    gte_partner = jnp.sum(jnp.where(routes_own == (me ^ 1), gate_own, zero), axis=2)
+    combined = (
+        gte[:, :, None] * mine.astype(jnp.float32)
+        + gte_partner[:, :, None] * from_partner.astype(jnp.float32)
+    ).astype(jnp.bfloat16)
+    returned = lax.all_to_all(combined, "ez", 0, 0, tiled=True)
 
     back = contract_cols(rows_q, wdown)
     d_gate = (back * up_pre * sig * (1.0 + gate_pre * (1.0 - sig))).astype(jnp.bfloat16)
@@ -237,13 +258,7 @@
 
     weight_grads = reduce_grads_dp(grad_half, width)
 
-    target = (routes * capacity + slots_by_rank(routes, experts)).reshape(-1)
-    choose = (
-        target[:, None]
-        == lax.broadcasted_iota(jnp.int32, (tok_rows * topk, experts * capacity), 1)
-    ).astype(jnp.bfloat16)
-    picked = jnp.dot(choose, returned.reshape(-1, width), preferred_element_type=jnp.float32)
-    summed = jnp.sum(picked.reshape(tok_rows, topk, width) * gates[:, :, None], axis=1)
+    summed = jnp.sum(returned.astype(jnp.float32), axis=0)
     return summed.astype(jnp.bfloat16), weight_grads
 
 

time: 198 us -> 183 us (0.924)
  the two profiles are of different devices: /device:TPU:15 before, /device:TPU:0 now
where the time goes in v11:
time: 183 us; the launch traced here: 182 us
  waiting for transfers between devices  61.7 us (34%)
  between operations  32.2 us (18%)
  matrix products  27 us (15%)
  other arithmetic  24.7 us (13%)
  starting transfers between devices  21.5 us (12%)
  local copies, waits for them, and re-layouts  15.2 us (8%)
    ppermute x1, waiting for transfers between devices, reduce_grads_dp(): lax.ppermute(grad_half(1 - d).astype(jnp.bfloat16), 'dp', [(0, 1), (1, 0)])  28 us
    ppermute x4, waiting for transfers between devices, ring_gather(): up = lax.ppermute(up, 'ez', ahead)  20.6 us
    dot_general x6, matrix products, contract_rows(): lax.dot_general(left, right, (((0,), (0,)), ((), ())), preferred_element_...  10.6 us
    dot_general x3, matrix products, contract_cols(): lax.dot_general(left, right, (((1,), (1,)), ((), ())), preferred_element_...  8.4 us
    ppermute x4, starting transfers between devices, ring_gather(): up = lax.ppermute(up, 'ez', ahead)  7.97 us
    ppermute x3, starting transfers between devices, ring_gather(): down = lax.ppermute(down, 'ez', behind)  7.29 us
    ppermute x3, waiting for transfers between devices, ring_gather(): down = lax.ppermute(down, 'ez', behind)  6.06 us
    reduce_sum x1, other arithmetic, local_gather(): fac = jnp.sum(jnp.where(hit, joined(cols[1:4]), zero), axis=1)  5.1 us
  transfers between devices with their start and end apart: 12, of which 7 were waited for; matrix products, arithmetic and copies ran while one was open for 14% of the time, Pallas kernels for 0%

profile of v11, /device:TPU:0, one launch (start us, length us, event | category | flops | bytes accessed | tf_op | source)
XLA Modules:
  0.0 182.4 jit_solution(9902872153161785576)
XLA Ops:
  12.1 3.0 %collective-permute-start.2 = (bf16[128,1024]{1,0:T(8,128)(2,1)}, bf16[128,1024]{1,0:T(8,128)(2,1)}, u32[]{:S(2)}, u32[]{:S(2)}) collective-permute-start(bf16[128,1024]{1,0:T(8,128)(2,1)} %param.16), channel_id=1, source_target_pairs={{0,2},{4,0},{8,4},{12,8},{14,12},{10,14},{6,10},{2,6},{1,3},{5,1},... | collective-permute-start | bytes 786440 | tf_op jit(solution)/shard_map/ppermute | solution.py:116
  36.3 1.9 %collective-permute-start.4 = (bf16[128,1024]{1,0:T(8,128)(2,1)}, bf16[128,1024]{1,0:T(8,128)(2,1)S(1)}, u32[]{:S(2)}, u32[]{:S(2)}) collective-permute-start(bf16[128,1024]{1,0:T(8,128)(2,1)} %collective-permute-done.2), channel_id=1, source_target_pairs={{0,2},{4,0},{8,4},{12,8},{14,12},{10,14},{6,10},{2,6},{1,3},{5,1},... | collective-permute-start | bytes 786440 | tf_op jit(solution)/shard_map/ppermute | solution.py:116
  40.3 6.1 %collective-permute-done.4 = bf16[128,1024]{1,0:T(8,128)(2,1)S(1)} collective-permute-done((bf16[128,1024]{1,0:T(8,128)(2,1)}, bf16[128,1024]{1,0:T(8,128)(2,1)S(1)}, u32[]{:S(2)}, u32[]{:S(2)}) %collective-permute-start.4) | collective-permute-done | bytes 262176 | tf_op jit(solution)/shard_map/ppermute | solution.py:116
  46.4 2.4 %collective-permute-start.6 = (bf16[128,1024]{1,0:T(8,128)(2,1)S(1)}, bf16[128,1024]{1,0:T(8,128)(2,1)S(1)}, u32[]{:S(2)}, u32[]{:S(2)}) collective-permute-start(bf16[128,1024]{1,0:T(8,128)(2,1)S(1)} %collective-permute-done.4), channel_id=1, source_target_pairs={{0,2},{4,0},{8,4},{12,8},{14,12},{10,14},{6,10},{2,6},{1,3},{5,1},... | collective-permute-start | bytes 786440 | tf_op jit(solution)/shard_map/ppermute | solution.py:116
  48.8 2.8 %collective-permute-start.5 = (bf16[128,1024]{1,0:T(8,128)(2,1)S(1)}, bf16[128,1024]{1,0:T(8,128)(2,1)S(1)}, u32[]{:S(2)}, u32[]{:S(2)}) collective-permute-start(bf16[128,1024]{1,0:T(8,128)(2,1)S(1)} %collective-permute-done.3), channel_id=1, source_target_pairs={{0,4},{4,8},{8,12},{12,14},{14,10},{10,6},{6,2},{2,0},{1,5},{5,9},... | collective-permute-start | bytes 786440 | tf_op jit(solution)/shard_map/ppermute | solution.py:113
  51.7 11.9 %collective-permute-done.5 = bf16[128,1024]{1,0:T(8,128)(2,1)S(1)} collective-permute-done((bf16[128,1024]{1,0:T(8,128)(2,1)S(1)}, bf16[128,1024]{1,0:T(8,128)(2,1)S(1)}, u32[]{:S(2)}, u32[]{:S(2)}) %collective-permute-start.5) | collective-permute-done | bytes 262176 | tf_op jit(solution)/shard_map/ppermute | solution.py:113
  63.5 4.8 %collective-permute-start.7 = (bf16[128,1024]{1,0:T(8,128)(2,1)S(1)}, bf16[128,1024]{1,0:T(8,128)(2,1)S(1)}, u32[]{:S(2)}, u32[]{:S(2)}) collective-permute-start(bf16[128,1024]{1,0:T(8,128)(2,1)S(1)} %collective-permute-done.5), channel_id=1, source_target_pairs={{0,4},{4,8},{8,12},{12,14},{14,10},{10,6},{6,2},{2,0},{1,5},{5,9},... | collective-permute-start | bytes 786440 | tf_op jit(solution)/shard_map/ppermute | solution.py:113
  68.4 8.7 %collective-permute-done.7 = bf16[128,1024]{1,0:T(8,128)(2,1)S(1)} collective-permute-done((bf16[128,1024]{1,0:T(8,128)(2,1)S(1)}, bf16[128,1024]{1,0:T(8,128)(2,1)S(1)}, u32[]{:S(2)}, u32[]{:S(2)}) %collective-permute-start.7) | collective-permute-done | bytes 262176 | tf_op jit(solution)/shard_map/ppermute | solution.py:113
  78.5 3.0 %collective-permute-done.8 = bf16[1024,1024]{1,0:T(8,128)(2,1)} collective-permute-done((bf16[1024,1024]{1,0:T(8,128)(2,1)S(1)}, bf16[1024,1024]{1,0:T(8,128)(2,1)}, u32[]{:S(2)}, u32[]{:S(2)}) %collective-permute-start.8) | collective-permute-done | bytes 2097184 | tf_op jit(solution)/shard_map/ppermute | solution.py:119
  81.5 3.9 %broadcast_select_fusion.1 = (bf16[1024,1024]{1,0:T(8,128)(2,1)}, bf16[1024,1024]{1,0:T(8,128)(2,1)S(1)}) fusion(bf16[1024,1024]{1,0:T(8,128)(2,1)} %collective-permute-done.8, pred[]{:T(512)S(6)} %eq.46, bf16[8,128,1024]{2,1,0:T(8,128)(2,1)} %copy-done.4), kind=kLoop, calls=%fused_computation.20 | loop fusion | flops 2097152 | bytes 8388609 | tf_op jit(solution)/shard_map/jit(_where)/select_n | solution.py:166
  87.0 5.1 %select_reduce_fusion = (f32[2048]{0:T(1024)S(1)}, f32[2048,8]{1,0:T(8,128)}) fusion(bf16[2048,1152]{1,0:T(8,128)(2,1)} %all-gather.2.cloned.1.call-done, s32[]{:T(128)S(6)} %add.132), kind=kLoop, calls=%fused_computation.48 | loop fusion | flops 227328 | bytes 303108 | tf_op jit(solution)/shard_map/reduce_sum | solution.py:173
  94.3 3.3 %slice-done = bf16[2048,1024]{1,0:T(8,128)(2,1)S(1)} async-done(((bf16[2048,1152]{1,0:T(8,128)(2,1)}), bf16[2048,1024]{1,0:T(8,128)(2,1)S(1)}, s32[]{:S(2)}) %slice-start) | async-done | bytes 4194328 | tf_op jit(solution)/shard_map/slice | solution.py:188
  98.8 1.8 %fusion.25 = f32[1536,512]{1,0:T(8,128)S(1)} fusion(bf16[1536,1024]{1,0:T(8,128)(2,1)S(1)} %bitcast.126, bf16[1,512,1024]{2,1,0:T(8,128)(2,1)S(1)} %copy-done.13), kind=kOutput, calls=%fused_computation.41 | convolution fusion | flops 1610612736 | bytes 7340032 | tf_op jit(solution)/shard_map/dot_general | solution.py:16
  100.8 1.8 %fusion.28 = f32[1536,512]{1,0:T(8,128)S(1)} fusion(bf16[1536,1024]{1,0:T(8,128)(2,1)S(1)} %bitcast.120, bf16[1,512,1024]{2,1,0:T(8,128)(2,1)S(1)} %copy-done.12), kind=kOutput, calls=%fused_computation.44 | convolution fusion | flops 1610612736 | bytes 7340032 | tf_op jit(solution)/shard_map/dot_general | solution.py:16
  102.7 4.7 %multiply_convert_fusion.1 = (bf16[1536,512]{1,0:T(8,128)(2,1)}, bf16[1536,512]{1,0:T(8,128)(2,1)}, bf16[1536,512]{1,0:T(8,128)(2,1)S(1)}) fusion(f32[1536,512]{1,0:T(8,128)S(1)} %fusion.25, f32[1536,512]{1,0:T(8,128)S(1)} %fusion.28, bf16[1536,1024]{1,0:T(8,128)(2,1)S(1)} %bitcast.121, bf16[1,512,1024]{2,1,0:T(8,128)(2,1)S(1)} %copy-done), kind=kOutput, calls=%fused_computation.10 | convolution fusion | flops 1622409216 | bytes 15204352 | tf_op jit(solution)/shard_map/dot_general | solution.py:16
  107.4 1.8 %convolution_convert_fusion = bf16[1536,1024]{1,0:T(8,128)(2,1)S(1)} fusion(bf16[1536,512]{1,0:T(8,128)(2,1)S(1)} %get-tuple-element.6, bf16[1,512,1024]{2,1,0:T(8,128)(2,1)S(1)} %copy-done.13), kind=kOutput, calls=%fused_computation.5 | convolution fusion | flops 1612185600 | bytes 5767168 | tf_op jit(solution)/shard_map/dot_general | solution.py:213
  110.1 2.8 %broadcast_select_fusion.2 = (bf16[8,128,1024]{2,1,0:T(8,128)(2,1)}, bf16[8,128,1024]{2,1,0:T(8,128)(2,1)}) fusion(bf16[8,128,1024]{2,1,0:T(8,128)(2,1)S(1)} %convolution_convert_fusion.3, pred[]{:T(512)S(6)} %eq.46, bf16[8,2,96,1024]{3,2,1,0:T(8,128)(2,1)S(1)} %bitcast.130, pred[8,2,96,128]{3,2,0,1:T(32,128)(4,1)S(1)} %fusion.38), kind=kOutput, calls=%fused_computation.21 | convolution fusion | flops 203423744 | bytes 7962625 | tf_op jit(solution)/shard_map/sjt,sjd->std/dot_general | solution.py:220
  114.7 2.7 %collective-permute-done = bf16[8,128,1024]{2,1,0:T(8,128)(2,1)} collective-permute-done((bf16[8,128,1024]{2,1,0:T(8,128)(2,1)}, bf16[8,128,1024]{2,1,0:T(8,128)(2,1)}, u32[]{:S(2)}, u32[]{:S(2)}) %collective-permute-start) | collective-permute-done | bytes 2097184 | tf_op jit(solution)/shard_map/ppermute | solution.py:226
  117.4 4.0 %add_convert_fusion = bf16[8,128,1024]{2,1,0:T(8,128)(2,1)} fusion(bf16[8,128,1024]{2,1,0:T(8,128)(2,1)} %collective-permute-done, f32[8,128]{1,0:T(8,128)S(1)} %get-tuple-element.3, bf16[8,128,1024]{2,1,0:T(8,128)(2,1)S(1)} %convolution_convert_fusion.3, bf16[8,128,1024]{2,1,0:T(8,128)(2,1)S(1)} %copy-done.2, f32[8,128]{1,0:T(8,128)S(1)} %get-tuple-element.2, ...), kind=kLoop, calls=%fused_computation.4 | loop fusion | flops 7340032 | bytes 8396801 | tf_op jit(solution)/shard_map/convert_element_type | solution.py:238
  121.4 4.5 %all-to-all-start = ((bf16[8,128,1024]{2,1,0:T(8,128)(2,1)}), bf16[8,128,1024]{2,1,0:T(8,128)(2,1)S(1)}, u32[]{:S(2)}, u32[]{:S(2)}) async-start(bf16[8,128,1024]{2,1,0:T(8,128)(2,1)} %add_convert_fusion), calls=%async_computation | async-start | bytes 4194304 | tf_op jit(solution)/shard_map/all_to_all | solution.py:239
  125.9 3.3 %fusion.24 = bf16[256,1,1024]{2,0,1:T(8,128)(2,1)S(1)} fusion(bf16[1536,1024]{1,0:T(8,128)(2,1)} %bitcast.127, bf16[1536,512]{1,0:T(8,128)(2,1)} %copy-done.14, s32[]{:T(128)S(6)} %select_n.176), kind=kOutput, calls=%fused_computation.39 | convolution fusion | flops 805568512 | bytes 4456452 | tf_op jit(solution)/shard_map/dot_general | solution.py:10
  134.5 3.3 %convolution_bitcast_fusion.2 = f32[256,1,1024]{2,0,1:T(8,128)S(1)} fusion(bf16[1536,1024]{1,0:T(8,128)(2,1)} %bitcast.122, bf16[1536,512]{1,0:T(8,128)(2,1)} %get-tuple-element.4, s32[]{:T(128)S(6)} %select_n.175), kind=kOutput, calls=%fused_computation.33 | convolution fusion | flops 805306368 | bytes 4980740 | tf_op jit(solution)/shard_map/dot_general | solution.py:10
  141.4 28.0 %collective-permute-done.9 = bf16[256,3,1024]{2,0,1:T(8,128)(2,1)} collective-permute-done((bf16[256,3,1024]{2,0,1:T(8,128)(2,1)}, bf16[256,3,1024]{2,0,1:T(8,128)(2,1)}, u32[]{:S(2)}, u32[]{:S(2)}) %collective-permute-start.9) | collective-permute-done | bytes 1572896 | tf_op jit(solution)/shard_map/ppermute | solution.py:140
  169.5 3.7 %fusion.2 = f32[1,256,3,1024]{3,1,2,0:T(8,128)} fusion(f32[256,1,1024]{2,0,1:T(8,128)S(1)} %convolution_bitcast_fusion, f32[256,1,1024]{2,0,1:T(8,128)S(1)} %convolution_bitcast_fusion.1, f32[256,1,1024]{2,0,1:T(8,128)S(1)} %convolution_bitcast_fusion.2, bf16[256,3,1024]{2,0,1:T(8,128)(2,1)} %collective-permute-done.9), kind=kLoop, calls=%fused_computation.8 | loop fusion | flops 3145728 | bytes 7864320 | tf_op jit(solution)/shard_map/reshape | solution.py:142
  (96 shorter events, 30.7 us)
Async XLA Ops:
  7.2 95.5 %copy-start = (bf16[1,512,1024]{2,1,0:T(8,128)(2,1)S(1)}, bf16[1,512,1024]{2,1,0:T(8,128)(2,1)}, u32[]{:S(2)}) copy-start(bf16[1,512,1024]{2,1,0:T(8,128)(2,1)} %param.17) | copy-start | bytes 3145732
  7.2 29.0 %copy-start.11 = (bf16[128,1024]{1,0:T(8,128)(2,1)S(1)}, bf16[128,1024]{1,0:T(8,128)(2,1)}, u32[]{:S(2)}) copy-start(bf16[128,1024]{1,0:T(8,128)(2,1)} %param.16) | copy-start | bytes 786436
  7.2 78.2 %all-gather.2.cloned.1.call-start = ((), (), s32[]{:S(2)}) async-start(), calls=%async_computation.1 | async-start | bytes 5013504 | tf_op jit(solution)/shard_map/all_gather | solution.py:162
  12.1 24.1 %collective-permute-start.2 = (bf16[128,1024]{1,0:T(8,128)(2,1)}, bf16[128,1024]{1,0:T(8,128)(2,1)}, u32[]{:S(2)}, u32[]{:S(2)}) collective-permute-start(bf16[128,1024]{1,0:T(8,128)(2,1)} %param.16), channel_id=1, source_target_pairs={{0,2},{4,0},{8,4},{12,8},{14,12},{10,14},{6,10},{2,6},{1,3},{5,1},... | collective-permute-start | bytes 786440 | tf_op jit(solution)/shard_map/ppermute | solution.py:116
  15.1 23.1 %collective-permute-start.1 = (bf16[128,1024]{1,0:T(8,128)(2,1)}, bf16[128,1024]{1,0:T(8,128)(2,1)}, u32[]{:S(2)}, u32[]{:S(2)}) collective-permute-start(bf16[128,1024]{1,0:T(8,128)(2,1)} %param.16), channel_id=1, source_target_pairs={{0,4},{4,8},{8,12},{12,14},{14,10},{10,6},{6,2},{2,0},{1,5},{5,9},... | collective-permute-start | bytes 786440 | tf_op jit(solution)/shard_map/ppermute | solution.py:113
  36.3 10.1 %collective-permute-start.4 = (bf16[128,1024]{1,0:T(8,128)(2,1)}, bf16[128,1024]{1,0:T(8,128)(2,1)S(1)}, u32[]{:S(2)}, u32[]{:S(2)}) collective-permute-start(bf16[128,1024]{1,0:T(8,128)(2,1)} %collective-permute-done.2), channel_id=1, source_target_pairs={{0,2},{4,0},{8,4},{12,8},{14,12},{10,14},{6,10},{2,6},{1,3},{5,1},... | collective-permute-start | bytes 786440 | tf_op jit(solution)/shard_map/ppermute | solution.py:116
  38.2 10.6 %collective-permute-start.3 = (bf16[128,1024]{1,0:T(8,128)(2,1)}, bf16[128,1024]{1,0:T(8,128)(2,1)S(1)}, u32[]{:S(2)}, u32[]{:S(2)}) collective-permute-start(bf16[128,1024]{1,0:T(8,128)(2,1)} %collective-permute-done.1), channel_id=1, source_target_pairs={{0,4},{4,8},{8,12},{12,14},{14,10},{10,6},{6,2},{2,0},{1,5},{5,9},... | collective-permute-start | bytes 786440 | tf_op jit(solution)/shard_map/ppermute | solution.py:113
  46.4 22.0 %collective-permute-start.6 = (bf16[128,1024]{1,0:T(8,128)(2,1)S(1)}, bf16[128,1024]{1,0:T(8,128)(2,1)S(1)}, u32[]{:S(2)}, u32[]{:S(2)}) collective-permute-start(bf16[128,1024]{1,0:T(8,128)(2,1)S(1)} %collective-permute-done.4), channel_id=1, source_target_pairs={{0,2},{4,0},{8,4},{12,8},{14,12},{10,14},{6,10},{2,6},{1,3},{5,1},... | collective-permute-start | bytes 786440 | tf_op jit(solution)/shard_map/ppermute | solution.py:116
  48.8 14.8 %collective-permute-start.5 = (bf16[128,1024]{1,0:T(8,128)(2,1)S(1)}, bf16[128,1024]{1,0:T(8,128)(2,1)S(1)}, u32[]{:S(2)}, u32[]{:S(2)}) collective-permute-start(bf16[128,1024]{1,0:T(8,128)(2,1)S(1)} %collective-permute-done.3), channel_id=1, source_target_pairs={{0,4},{4,8},{8,12},{12,14},{14,10},{10,6},{6,2},{2,0},{1,5},{5,9},... | collective-permute-start | bytes 786440 | tf_op jit(solution)/shard_map/ppermute | solution.py:113
  63.5 13.6 %collective-permute-start.7 = (bf16[128,1024]{1,0:T(8,128)(2,1)S(1)}, bf16[128,1024]{1,0:T(8,128)(2,1)S(1)}, u32[]{:S(2)}, u32[]{:S(2)}) collective-permute-start(bf16[128,1024]{1,0:T(8,128)(2,1)S(1)} %collective-permute-done.5), channel_id=1, source_target_pairs={{0,4},{4,8},{8,12},{12,14},{14,10},{10,6},{6,2},{2,0},{1,5},{5,9},... | collective-permute-start | bytes 786440 | tf_op jit(solution)/shard_map/ppermute | solution.py:113
  77.2 4.4 %collective-permute-start.8 = (bf16[1024,1024]{1,0:T(8,128)(2,1)S(1)}, bf16[1024,1024]{1,0:T(8,128)(2,1)}, u32[]{:S(2)}, u32[]{:S(2)}) collective-permute-start(bf16[1024,1024]{1,0:T(8,128)(2,1)S(1)} %bitcast.117), channel_id=1, source_target_pairs={{0,1},{1,0},{2,3},{3,2},{4,5},{5,4},{6,7},{7,6},{8,9},{9,8},{10,11... | collective-permute-start | bytes 6291464 | tf_op jit(solution)/shard_map/ppermute | solution.py:119
  86.8 5.4 %copy-start.3 = (bf16[1024,1024]{1,0:T(8,128)(2,1)S(1)}, bf16[1024,1024]{1,0:T(8,128)(2,1)}, u32[]{:S(2)}) copy-start(bf16[1024,1024]{1,0:T(8,128)(2,1)} %get-tuple-element.9) | copy-start | bytes 6291460
  94.3 4.3 %copy-start.9 = (bf16[8,2,96,1024]{3,2,1,0:T(8,128)(2,1)}, bf16[8,2,96,1024]{3,2,1,0:T(8,128)(2,1)S(1)}, u32[]{:S(2)}) copy-start(bf16[8,2,96,1024]{3,2,1,0:T(8,128)(2,1)S(1)} %copy.34) | copy-start | bytes 9437188
  94.3 3.3 %slice-start = ((bf16[2048,1152]{1,0:T(8,128)(2,1)}), bf16[2048,1024]{1,0:T(8,128)(2,1)S(1)}, s32[]{:S(2)}) async-start(bf16[2048,1152]{1,0:T(8,128)(2,1)} %all-gather.2.cloned.1.call-done), calls=%async_computation.2 | async-start | bytes 8388608 | tf_op jit(solution)/shard_map/slice | solution.py:188
  98.6 4.1 %copy-start.6 = (bf16[16,96,1024]{2,1,0:T(8,128)(2,1)}, bf16[16,96,1024]{2,1,0:T(8,128)(2,1)S(1)}, u32[]{:S(2)}) copy-start(bf16[16,96,1024]{2,1,0:T(8,128)(2,1)S(1)} %convolution_convert_fusion.1) | copy-start | bytes 9437188
  110.1 4.2 %copy-start.5 = (f32[2048,8]{1,0:T(8,128)S(1)}, f32[2048,8]{1,0:T(8,128)}, u32[]{:S(2)}) copy-start(f32[2048,8]{1,0:T(8,128)} %get-tuple-element.8) | copy-start | bytes 196612
  112.9 4.5 %collective-permute-start = (bf16[8,128,1024]{2,1,0:T(8,128)(2,1)}, bf16[8,128,1024]{2,1,0:T(8,128)(2,1)}, u32[]{:S(2)}, u32[]{:S(2)}) collective-permute-start(bf16[8,128,1024]{2,1,0:T(8,128)(2,1)} %get-tuple-element.26), channel_id=1, source_target_pairs={{0,1},{1,0},{2,3},{3,2},{4,5},{5,4},{6,7},{7,6},{8,9},{9,8},{10,11... | collective-permute-start | bytes 6291464 | tf_op jit(solution)/shard_map/ppermute | solution.py:226
  113.0 4.4 %copy-start.2 = (bf16[8,128,1024]{2,1,0:T(8,128)(2,1)S(1)}, bf16[8,128,1024]{2,1,0:T(8,128)(2,1)}, u32[]{:S(2)}) copy-start(bf16[8,128,1024]{2,1,0:T(8,128)(2,1)} %get-tuple-element.27) | copy-start | bytes 6291460
  121.4 53.0 %all-to-all-start = ((bf16[8,128,1024]{2,1,0:T(8,128)(2,1)}), bf16[8,128,1024]{2,1,0:T(8,128)(2,1)S(1)}, u32[]{:S(2)}, u32[]{:S(2)}) async-start(bf16[8,128,1024]{2,1,0:T(8,128)(2,1)} %add_convert_fusion), calls=%async_computation | async-start | bytes 4194304 | tf_op jit(solution)/shard_map/all_to_all | solution.py:239
  125.9 3.3 %copy-start.7 = (bf16[16,96,1024]{2,1,0:T(8,128)(2,1)S(1)}, bf16[16,96,1024]{2,1,0:T(8,128)(2,1)}, u32[]{:S(2)}) copy-start(bf16[16,96,1024]{2,1,0:T(8,128)(2,1)} %copy-done.6) | copy-start | bytes 9437188
  125.9 3.5 %copy-start.18 = (bf16[1536,512]{1,0:T(8,128)(2,1)S(1)}, bf16[1536,512]{1,0:T(8,128)(2,1)}, u32[]{:S(2)}) copy-start(bf16[1536,512]{1,0:T(8,128)(2,1)} %get-tuple-element.4) | copy-start | bytes 4718596
  133.0 36.5 %collective-permute-start.9 = (bf16[256,3,1024]{2,0,1:T(8,128)(2,1)}, bf16[256,3,1024]{2,0,1:T(8,128)(2,1)}, u32[]{:S(2)}, u32[]{:S(2)}) collective-permute-start(bf16[256,3,1024]{2,0,1:T(8,128)(2,1)} %pad_maximum_fusion.1), channel_id=1, source_target_pairs={{0,16},{16,0},{1,17},{17,1},{2,18},{18,2},{3,19},{19,3},{4,20},{20... | collective-permute-start | bytes 4718600 | tf_op jit(solution)/shard_map/ppermute | solution.py:140
  134.5 3.5 %copy-start.17 = (bf16[1536,512]{1,0:T(8,128)(2,1)S(1)}, bf16[1536,512]{1,0:T(8,128)(2,1)}, u32[]{:S(2)}) copy-start(bf16[1536,512]{1,0:T(8,128)(2,1)} %get-tuple-element.5) | copy-start | bytes 4718596
  169.5 6.1 %copy-start.1 = (bf16[1,512,1024]{2,1,0:T(8,128)(2,1)S(1)}, bf16[1,512,1024]{2,1,0:T(8,128)(2,1)}, u32[]{:S(2)}) copy-start(bf16[1,512,1024]{2,1,0:T(8,128)(2,1)} %param.17) | copy-start | bytes 3145732
  (8 other events, 15.4 us)
Sparse Core Ops, SparseCore 0:
  12.3 59.9 all-gather.1

commit v12 on v11

--- a/solution.py
+++ b/solution.py
@@ -155,23 +155,28 @@
     coef = importance * masked.astype(jnp.float32)
     factor = coef[:, None] * gates
     meta = [routes.astype(jnp.bfloat16)] + exact_pieces(factor) + exact_pieces(gates)
-    pad = (-topk * len(meta)) % 128
-    meta.append(jnp.zeros((tok_rows, pad), jnp.bfloat16))
-    packed = jnp.concatenate([tokens] + meta, axis=1)
+    meta_rows = jnp.concatenate([m.T for m in meta], axis=0)
+    lines = -(-meta_rows.size // width)
+    lines += (-(tok_rows + lines)) % 8
+    flat_meta = jnp.pad(meta_rows.reshape(-1), (0, lines * width - meta_rows.size))
+    packed = jnp.concatenate([tokens, flat_meta.reshape(lines, width)], axis=0)
 
     gathered = lax.all_gather(packed, ("ez", "core"), axis=0, tiled=True)
+    gathered = gathered.reshape(experts, tok_rows + lines, width)
     cot_halves = ring_gather(cotangent)
     on_core0 = core == 0
     cot_by_core = [
         jnp.where(on_core0, cot_halves[0], cot_halves[1]),
         jnp.where(on_core0, cot_halves[1], cot_halves[0]),
     ]
-    all_p = gathered[:, width:]
-    cols = [all_p[:, topk * i: topk * (i + 1)] for i in range(7)]
-    hit = cols[0].astype(jnp.int32) == me
+    meta_all = gathered[:, tok_rows:].reshape(experts, lines * width)
+    meta_all = meta_all[:, :meta_rows.size].reshape(experts, len(meta), topk, tok_rows)
+    routes_t = meta_all[:, 0].astype(jnp.int32)
+    hit = routes_t == me
     zero = jnp.zeros((), jnp.float32)
-    fac = jnp.sum(jnp.where(hit, joined(cols[1:4]), zero), axis=1)
-    routed = jnp.any(hit, axis=1).reshape(experts, tok_rows)
+    fac = jnp.sum(jnp.where(hit, joined([meta_all[:, i] for i in (1, 2, 3)]), zero), axis=1)
+    gate_t = joined([meta_all[:, i] for i in (4, 5, 6)])
+    routed = jnp.any(hit, axis=1)
     ahead = (
         lax.broadcasted_iota(jnp.int32, (tok_rows, tok_rows), 0)
         < lax.broadcasted_iota(jnp.int32, (tok_rows, tok_rows), 1)
@@ -185,7 +190,7 @@
     rows_x = jnp.einsum(
         "sjt,std->sjd",
         pick,
-        gathered[:, :width].reshape(experts, tok_rows, width),
+        gathered[:, :tok_rows],
         preferred_element_type=jnp.float32,
     ).astype(jnp.bfloat16).reshape(experts * capacity, width)
     pick_by_core = pick.reshape(nchip, ncore, capacity, tok_rows)
@@ -226,12 +231,12 @@
     from_partner = lax.ppermute(
         jnp.where(on_core0, dense[1], dense[0]), "core", [(0, 1), (1, 0)]
     )
-    gate_all = joined(cols[4:7]).reshape(nchip, ncore, tok_rows, topk)
-    routes_all = cols[0].astype(jnp.int32).reshape(nchip, ncore, tok_rows, topk)
+    gate_all = gate_t.reshape(nchip, ncore, topk, tok_rows)
+    routes_all = routes_t.reshape(nchip, ncore, topk, tok_rows)
     gate_own = jnp.where(on_core0, gate_all[:, 0], gate_all[:, 1])
     routes_own = jnp.where(on_core0, routes_all[:, 0], routes_all[:, 1])
-    gte = jnp.sum(jnp.where(routes_own == me, gate_own, zero), axis=2)
-    gte_partner = jnp.sum(jnp.where(routes_own == (me ^ 1), gate_own, zero), axis=2)
+    gte = jnp.sum(jnp.where(routes_own == me, gate_own, zero), axis=1)
+    gte_partner = jnp.sum(jnp.where(routes_own == (me ^ 1), gate_own, zero), axis=1)
     combined = (
         gte[:, :, None] * mine.astype(jnp.float32)
         + gte_partner[:, :, None] * from_partner.astype(jnp.float32)

time: 183 us -> 180 us (0.984)
  local copies, waits for them, and re-layouts: 15.2 us -> 11.1 us
  other arithmetic: 24.7 us -> 22 us
  matrix products: 27 us -> 29.1 us
    reduce_sum x2, other arithmetic: 5.45 us -> 0.08 us  [the longest x1 0.05 us: local_gather(): jnp.sum(jnp.where(hit, joined([meta_all[:, i] for i in (1, 2, 3)]), zero)...]
    unnamed x0 -> x6, other arithmetic: none -> 4.28 us
    convert_element_type x3 -> x1, other arithmetic: 2.79 us -> 0.01 us  [local_gather(): routes_t = meta_all[:, 0].astype(jnp.int32)]
    concatenate x0 -> x2, other arithmetic: none -> 2.41 us  [the longest x1 1.71 us: local_gather(): packed = jnp.concatenate([tokens, flat_meta.reshape(lines, width)], axis=0)]
    ppermute x4, waiting for transfers between devices: 20.6 us -> 18.2 us  [ring_gather(): up = lax.ppermute(up, 'ez', ahead)]
    slice x2 -> x1, local copies, waits for them, and re-layouts: 3.32 us -> 0.97 us  [local_gather(): meta_all = gathered[:, tok_rows:].reshape(experts, lines * width)]
    dot_general x1, matrix products: 0.97 us -> 3.31 us  [local_gather(): jnp.einsum('sjt,std->sjd', pick, gathered[:, :tok_rows], preferred_elemen...]
    unnamed x38 -> x37, local copies, waits for them, and re-layouts: 3.68 us -> 4.46 us
where the time goes in v12:
time: 180 us; the launch traced here: 179 us
  waiting for transfers between devices  62.8 us (35%)
  between operations  32.6 us (18%)
  matrix products  29.1 us (16%)
  other arithmetic  22 us (12%)
  starting transfers between devices  21.7 us (12%)
  local copies, waits for them, and re-layouts  11.1 us (6%)
    ppermute x1, waiting for transfers between devices, reduce_grads_dp(): lax.ppermute(grad_half(1 - d).astype(jnp.bfloat16), 'dp', [(0, 1), (1, 0)])  28.7 us
    ppermute x4, waiting for transfers between devices, ring_gather(): up = lax.ppermute(up, 'ez', ahead)  18.2 us
    dot_general x6, matrix products, contract_rows(): lax.dot_general(left, right, (((0,), (0,)), ((), ())), preferred_element_...  10.6 us
    dot_general x3, matrix products, contract_cols(): lax.dot_general(left, right, (((1,), (1,)), ((), ())), preferred_element_...  8.27 us
    ppermute x4, starting transfers between devices, ring_gather(): up = lax.ppermute(up, 'ez', ahead)  8.27 us
    ppermute x3, waiting for transfers between devices, ring_gather(): down = lax.ppermute(down, 'ez', behind)  7.53 us
    ppermute x3, starting transfers between devices, ring_gather(): down = lax.ppermute(down, 'ez', behind)  7.3 us
    unnamed x37, local copies, waits for them, and re-layouts  4.46 us
  transfers between devices with their start and end apart: 12, of which 7 were waited for; matrix products, arithmetic and copies ran while one was open for 14% of the time, Pallas kernels for 0%

profile of v12, /device:TPU:0, one launch (start us, length us, event | category | flops | bytes accessed | tf_op | source)
XLA Modules:
  0.0 179.4 jit_solution(16275617445583158167)
XLA Ops:
  12.9 1.7 pad_maximum_fusion.2
  14.7 3.0 %collective-permute-start.2 = (bf16[128,1024]{1,0:T(8,128)(2,1)}, bf16[128,1024]{1,0:T(8,128)(2,1)}, u32[]{:S(2)}, u32[]{:S(2)}) collective-permute-start(bf16[128,1024]{1,0:T(8,128)(2,1)} %param.16), channel_id=1, source_target_pairs={{0,2},{4,0},{8,4},{12,8},{14,12},{10,14},{6,10},{2,6},{1,3},{5,1},... | collective-permute-start | bytes 786440 | tf_op jit(solution)/shard_map/ppermute | solution.py:116
  39.1 1.9 %collective-permute-start.4 = (bf16[128,1024]{1,0:T(8,128)(2,1)}, bf16[128,1024]{1,0:T(8,128)(2,1)S(1)}, u32[]{:S(2)}, u32[]{:S(2)}) collective-permute-start(bf16[128,1024]{1,0:T(8,128)(2,1)} %collective-permute-done.2), channel_id=1, source_target_pairs={{0,2},{4,0},{8,4},{12,8},{14,12},{10,14},{6,10},{2,6},{1,3},{5,1},... | collective-permute-start | bytes 786440 | tf_op jit(solution)/shard_map/ppermute | solution.py:116
  43.2 7.5 %collective-permute-done.4 = bf16[128,1024]{1,0:T(8,128)(2,1)S(1)} collective-permute-done((bf16[128,1024]{1,0:T(8,128)(2,1)}, bf16[128,1024]{1,0:T(8,128)(2,1)S(1)}, u32[]{:S(2)}, u32[]{:S(2)}) %collective-permute-start.4) | collective-permute-done | bytes 262176 | tf_op jit(solution)/shard_map/ppermute | solution.py:116
  50.7 2.4 %collective-permute-start.6 = (bf16[128,1024]{1,0:T(8,128)(2,1)S(1)}, bf16[128,1024]{1,0:T(8,128)(2,1)S(1)}, u32[]{:S(2)}, u32[]{:S(2)}) collective-permute-start(bf16[128,1024]{1,0:T(8,128)(2,1)S(1)} %collective-permute-done.4), channel_id=1, source_target_pairs={{0,2},{4,0},{8,4},{12,8},{14,12},{10,14},{6,10},{2,6},{1,3},{5,1},... | collective-permute-start | bytes 786440 | tf_op jit(solution)/shard_map/ppermute | solution.py:116
  53.1 3.1 %collective-permute-start.5 = (bf16[128,1024]{1,0:T(8,128)(2,1)S(1)}, bf16[128,1024]{1,0:T(8,128)(2,1)S(1)}, u32[]{:S(2)}, u32[]{:S(2)}) collective-permute-start(bf16[128,1024]{1,0:T(8,128)(2,1)S(1)} %collective-permute-done.3), channel_id=1, source_target_pairs={{0,4},{4,8},{8,12},{12,14},{14,10},{10,6},{6,2},{2,0},{1,5},{5,9},... | collective-permute-start | bytes 786440 | tf_op jit(solution)/shard_map/ppermute | solution.py:113
  56.2 9.8 %collective-permute-done.5 = bf16[128,1024]{1,0:T(8,128)(2,1)S(1)} collective-permute-done((bf16[128,1024]{1,0:T(8,128)(2,1)S(1)}, bf16[128,1024]{1,0:T(8,128)(2,1)S(1)}, u32[]{:S(2)}, u32[]{:S(2)}) %collective-permute-start.5) | collective-permute-done | bytes 262176 | tf_op jit(solution)/shard_map/ppermute | solution.py:113
  66.0 4.9 %collective-permute-start.7 = (bf16[128,1024]{1,0:T(8,128)(2,1)S(1)}, bf16[128,1024]{1,0:T(8,128)(2,1)S(1)}, u32[]{:S(2)}, u32[]{:S(2)}) collective-permute-start(bf16[128,1024]{1,0:T(8,128)(2,1)S(1)} %collective-permute-done.5), channel_id=1, source_target_pairs={{0,4},{4,8},{8,12},{12,14},{14,10},{10,6},{6,2},{2,0},{1,5},{5,9},... | collective-permute-start | bytes 786440 | tf_op jit(solution)/shard_map/ppermute | solution.py:113
  71.0 8.4 %collective-permute-done.7 = bf16[128,1024]{1,0:T(8,128)(2,1)S(1)} collective-permute-done((bf16[128,1024]{1,0:T(8,128)(2,1)S(1)}, bf16[128,1024]{1,0:T(8,128)(2,1)S(1)}, u32[]{:S(2)}, u32[]{:S(2)}) %collective-permute-start.7) | collective-permute-done | bytes 262176 | tf_op jit(solution)/shard_map/ppermute | solution.py:113
  80.7 3.0 %collective-permute-done.8 = bf16[1024,1024]{1,0:T(8,128)(2,1)} collective-permute-done((bf16[1024,1024]{1,0:T(8,128)(2,1)S(1)}, bf16[1024,1024]{1,0:T(8,128)(2,1)}, u32[]{:S(2)}, u32[]{:S(2)}) %collective-permute-start.8) | collective-permute-done | bytes 2097184 | tf_op jit(solution)/shard_map/ppermute | solution.py:119
  83.8 3.9 %broadcast_select_fusion.1 = (bf16[1024,1024]{1,0:T(8,128)(2,1)}, bf16[1024,1024]{1,0:T(8,128)(2,1)S(1)}) fusion(bf16[1024,1024]{1,0:T(8,128)(2,1)} %collective-permute-done.8, pred[]{:T(512)S(6)} %eq.47, bf16[8,128,1024]{2,1,0:T(8,128)(2,1)} %copy-done.3), kind=kLoop, calls=%fused_computation.22 | loop fusion | flops 2097152 | bytes 8388609 | tf_op jit(solution)/shard_map/jit(_where)/select_n | solution.py:169
  89.1 3.3 %fusion.6 = bf16[16,96,1024]{2,1,0:T(8,128)(2,1)S(1)} fusion(bf16[16,136,1024]{2,1,0:T(8,128)(2,1)} %bitcast.148, s32[16,128]{1,0:T(8,128)S(1)} %convolution_convert_fusion.6, pred[16,128]{1,0:T(8,128)(4,1)S(1)} %fusion.62), kind=kOutput, calls=%fused_computation.16 | convolution fusion | flops 404619264 | bytes 7350272 | tf_op jit(solution)/shard_map/sjt,std->sjd/dot_general | solution.py:190
  95.5 1.8 %fusion.30 = f32[1536,512]{1,0:T(8,128)S(1)} fusion(bf16[1536,1024]{1,0:T(8,128)(2,1)S(1)} %bitcast.155, bf16[1,512,1024]{2,1,0:T(8,128)(2,1)S(1)} %copy-done.11), kind=kOutput, calls=%fused_computation.43 | convolution fusion | flops 1610612736 | bytes 7340032 | tf_op jit(solution)/shard_map/dot_general | solution.py:16
  97.4 1.8 %fusion.33 = f32[1536,512]{1,0:T(8,128)S(1)} fusion(bf16[1536,1024]{1,0:T(8,128)(2,1)S(1)} %bitcast.149, bf16[1,512,1024]{2,1,0:T(8,128)(2,1)S(1)} %copy-done.10), kind=kOutput, calls=%fused_computation.46 | convolution fusion | flops 1610612736 | bytes 7340032 | tf_op jit(solution)/shard_map/dot_general | solution.py:16
  99.3 4.6 %multiply_convert_fusion.1 = (bf16[1536,512]{1,0:T(8,128)(2,1)}, bf16[1536,512]{1,0:T(8,128)(2,1)}, bf16[1536,512]{1,0:T(8,128)(2,1)S(1)}) fusion(f32[1536,512]{1,0:T(8,128)S(1)} %fusion.30, f32[1536,512]{1,0:T(8,128)S(1)} %fusion.33, bf16[1536,1024]{1,0:T(8,128)(2,1)S(1)} %bitcast.150, bf16[1,512,1024]{2,1,0:T(8,128)(2,1)S(1)} %copy-done), kind=kOutput, calls=%fused_computation.12 | convolution fusion | flops 1622409216 | bytes 15204352 | tf_op jit(solution)/shard_map/dot_general | solution.py:16
  103.9 1.8 %convolution_convert_fusion = bf16[1536,1024]{1,0:T(8,128)(2,1)S(1)} fusion(bf16[1536,512]{1,0:T(8,128)(2,1)S(1)} %get-tuple-element.6, bf16[1,512,1024]{2,1,0:T(8,128)(2,1)S(1)} %copy-done.11), kind=kOutput, calls=%fused_computation.7 | convolution fusion | flops 1612185600 | bytes 5767168 | tf_op jit(solution)/shard_map/dot_general | solution.py:218
  106.5 2.8 %broadcast_select_fusion.2 = (bf16[8,128,1024]{2,1,0:T(8,128)(2,1)}, bf16[8,128,1024]{2,1,0:T(8,128)(2,1)}) fusion(bf16[8,128,1024]{2,1,0:T(8,128)(2,1)S(1)} %convolution_convert_fusion.2, pred[]{:T(512)S(6)} %eq.47, bf16[8,2,96,1024]{3,2,1,0:T(8,128)(2,1)S(1)} %bitcast.159, pred[8,2,96,128]{3,2,0,1:T(32,128)(4,1)S(1)} %fusion.43), kind=kOutput, calls=%fused_computation.23 | convolution fusion | flops 203423744 | bytes 7962625 | tf_op jit(solution)/shard_map/sjt,sjd->std/dot_general | solution.py:225
  109.5 4.3 %collective-permute-done = bf16[8,128,1024]{2,1,0:T(8,128)(2,1)} collective-permute-done((bf16[8,128,1024]{2,1,0:T(8,128)(2,1)}, bf16[8,128,1024]{2,1,0:T(8,128)(2,1)}, u32[]{:S(2)}, u32[]{:S(2)}) %collective-permute-start) | collective-permute-done | bytes 2097184 | tf_op jit(solution)/shard_map/ppermute | solution.py:231
  113.8 4.1 %add_convert_fusion = bf16[8,128,1024]{2,1,0:T(8,128)(2,1)} fusion(bf16[8,128,1024]{2,1,0:T(8,128)(2,1)} %collective-permute-done, f32[8,128]{1,0:T(8,128)S(1)} %get-tuple-element.3, bf16[8,128,1024]{2,1,0:T(8,128)(2,1)S(1)} %convolution_convert_fusion.2, bf16[8,128,1024]{2,1,0:T(8,128)(2,1)} %get-tuple-element.21, f32[8,128]{1,0:T(8,128)S(1)} %get-tuple-element.2, ...), kind=kLoop, calls=%fused_computation.6 | loop fusion | flops 7340032 | bytes 8396801 | tf_op jit(solution)/shard_map/convert_element_type | solution.py:243
  117.9 4.4 %all-to-all-start = ((bf16[8,128,1024]{2,1,0:T(8,128)(2,1)}), bf16[8,128,1024]{2,1,0:T(8,128)(2,1)S(1)}, u32[]{:S(2)}, u32[]{:S(2)}) async-start(bf16[8,128,1024]{2,1,0:T(8,128)(2,1)} %add_convert_fusion), calls=%async_computation | async-start | bytes 4194304 | tf_op jit(solution)/shard_map/all_to_all | solution.py:244
  122.3 3.3 %fusion.29 = bf16[256,1,1024]{2,0,1:T(8,128)(2,1)S(1)} fusion(bf16[1536,1024]{1,0:T(8,128)(2,1)} %bitcast.156, bf16[1536,512]{1,0:T(8,128)(2,1)} %copy-done.12, s32[]{:T(128)S(6)} %select_n.177), kind=kOutput, calls=%fused_computation.41 | convolution fusion | flops 805568512 | bytes 4456452 | tf_op jit(solution)/shard_map/dot_general | solution.py:10
  131.1 3.3 %convolution_bitcast_fusion.2 = f32[256,1,1024]{2,0,1:T(8,128)S(1)} fusion(bf16[1536,1024]{1,0:T(8,128)(2,1)} %bitcast.151, bf16[1536,512]{1,0:T(8,128)(2,1)} %get-tuple-element.4, s32[]{:T(128)S(6)} %select_n.176), kind=kOutput, calls=%fused_computation.35 | convolution fusion | flops 805306368 | bytes 4980740 | tf_op jit(solution)/shard_map/dot_general | solution.py:10
  138.0 28.7 %collective-permute-done.9 = bf16[256,3,1024]{2,0,1:T(8,128)(2,1)} collective-permute-done((bf16[256,3,1024]{2,0,1:T(8,128)(2,1)}, bf16[256,3,1024]{2,0,1:T(8,128)(2,1)}, u32[]{:S(2)}, u32[]{:S(2)}) %collective-permute-start.9) | collective-permute-done | bytes 1572896 | tf_op jit(solution)/shard_map/ppermute | solution.py:140
  166.7 3.7 %fusion.4 = f32[1,256,3,1024]{3,1,2,0:T(8,128)} fusion(f32[256,1,1024]{2,0,1:T(8,128)S(1)} %convolution_bitcast_fusion, f32[256,1,1024]{2,0,1:T(8,128)S(1)} %convolution_bitcast_fusion.1, f32[256,1,1024]{2,0,1:T(8,128)S(1)} %convolution_bitcast_fusion.2, bf16[256,3,1024]{2,0,1:T(8,128)(2,1)} %collective-permute-done.9), kind=kLoop, calls=%fused_computation.10 | loop fusion | flops 3145728 | bytes 7864320 | tf_op jit(solution)/shard_map/reshape | solution.py:142
  (93 shorter events, 29.2 us)
Async XLA Ops:
  7.2 92.1 %copy-start = (bf16[1,512,1024]{2,1,0:T(8,128)(2,1)S(1)}, bf16[1,512,1024]{2,1,0:T(8,128)(2,1)}, u32[]{:S(2)}) copy-start(bf16[1,512,1024]{2,1,0:T(8,128)(2,1)} %param.17) | copy-start | bytes 3145732
  7.2 31.9 %copy-start.9 = (bf16[128,1024]{1,0:T(8,128)(2,1)S(1)}, bf16[128,1024]{1,0:T(8,128)(2,1)}, u32[]{:S(2)}) copy-start(bf16[128,1024]{1,0:T(8,128)(2,1)} %param.16) | copy-start | bytes 786436
  7.2 80.5 %all-gather.2.cloned.1.call-start = ((), (), s32[]{:S(2)}) async-start(), calls=%async_computation.1 | async-start | bytes 4734976 | tf_op jit(solution)/shard_map/all_gather | solution.py:164
  14.7 24.5 %collective-permute-start.2 = (bf16[128,1024]{1,0:T(8,128)(2,1)}, bf16[128,1024]{1,0:T(8,128)(2,1)}, u32[]{:S(2)}, u32[]{:S(2)}) collective-permute-start(bf16[128,1024]{1,0:T(8,128)(2,1)} %param.16), channel_id=1, source_target_pairs={{0,2},{4,0},{8,4},{12,8},{14,12},{10,14},{6,10},{2,6},{1,3},{5,1},... | collective-permute-start | bytes 786440 | tf_op jit(solution)/shard_map/ppermute | solution.py:116
  17.6 23.4 %collective-permute-start.1 = (bf16[128,1024]{1,0:T(8,128)(2,1)}, bf16[128,1024]{1,0:T(8,128)(2,1)}, u32[]{:S(2)}, u32[]{:S(2)}) collective-permute-start(bf16[128,1024]{1,0:T(8,128)(2,1)} %param.16), channel_id=1, source_target_pairs={{0,4},{4,8},{8,12},{12,14},{14,10},{10,6},{6,2},{2,0},{1,5},{5,9},... | collective-permute-start | bytes 786440 | tf_op jit(solution)/shard_map/ppermute | solution.py:113
  39.1 11.6 %collective-permute-start.4 = (bf16[128,1024]{1,0:T(8,128)(2,1)}, bf16[128,1024]{1,0:T(8,128)(2,1)S(1)}, u32[]{:S(2)}, u32[]{:S(2)}) collective-permute-start(bf16[128,1024]{1,0:T(8,128)(2,1)} %collective-permute-done.2), channel_id=1, source_target_pairs={{0,2},{4,0},{8,4},{12,8},{14,12},{10,14},{6,10},{2,6},{1,3},{5,1},... | collective-permute-start | bytes 786440 | tf_op jit(solution)/shard_map/ppermute | solution.py:116
  41.1 12.0 %collective-permute-start.3 = (bf16[128,1024]{1,0:T(8,128)(2,1)}, bf16[128,1024]{1,0:T(8,128)(2,1)S(1)}, u32[]{:S(2)}, u32[]{:S(2)}) collective-permute-start(bf16[128,1024]{1,0:T(8,128)(2,1)} %collective-permute-done.1), channel_id=1, source_target_pairs={{0,4},{4,8},{8,12},{12,14},{14,10},{10,6},{6,2},{2,0},{1,5},{5,9},... | collective-permute-start | bytes 786440 | tf_op jit(solution)/shard_map/ppermute | solution.py:113
  50.7 20.2 %collective-permute-start.6 = (bf16[128,1024]{1,0:T(8,128)(2,1)S(1)}, bf16[128,1024]{1,0:T(8,128)(2,1)S(1)}, u32[]{:S(2)}, u32[]{:S(2)}) collective-permute-start(bf16[128,1024]{1,0:T(8,128)(2,1)S(1)} %collective-permute-done.4), channel_id=1, source_target_pairs={{0,2},{4,0},{8,4},{12,8},{14,12},{10,14},{6,10},{2,6},{1,3},{5,1},... | collective-permute-start | bytes 786440 | tf_op jit(solution)/shard_map/ppermute | solution.py:116
  53.1 12.9 %collective-permute-start.5 = (bf16[128,1024]{1,0:T(8,128)(2,1)S(1)}, bf16[128,1024]{1,0:T(8,128)(2,1)S(1)}, u32[]{:S(2)}, u32[]{:S(2)}) collective-permute-start(bf16[128,1024]{1,0:T(8,128)(2,1)S(1)} %collective-permute-done.3), channel_id=1, source_target_pairs={{0,4},{4,8},{8,12},{12,14},{14,10},{10,6},{6,2},{2,0},{1,5},{5,9},... | collective-permute-start | bytes 786440 | tf_op jit(solution)/shard_map/ppermute | solution.py:113
  66.0 13.3 %collective-permute-start.7 = (bf16[128,1024]{1,0:T(8,128)(2,1)S(1)}, bf16[128,1024]{1,0:T(8,128)(2,1)S(1)}, u32[]{:S(2)}, u32[]{:S(2)}) collective-permute-start(bf16[128,1024]{1,0:T(8,128)(2,1)S(1)} %collective-permute-done.5), channel_id=1, source_target_pairs={{0,4},{4,8},{8,12},{12,14},{14,10},{10,6},{6,2},{2,0},{1,5},{5,9},... | collective-permute-start | bytes 786440 | tf_op jit(solution)/shard_map/ppermute | solution.py:113
  79.4 4.4 %collective-permute-start.8 = (bf16[1024,1024]{1,0:T(8,128)(2,1)S(1)}, bf16[1024,1024]{1,0:T(8,128)(2,1)}, u32[]{:S(2)}, u32[]{:S(2)}) collective-permute-start(bf16[1024,1024]{1,0:T(8,128)(2,1)S(1)} %bitcast.146), channel_id=1, source_target_pairs={{0,1},{1,0},{2,3},{3,2},{4,5},{5,4},{6,7},{7,6},{8,9},{9,8},{10,11... | collective-permute-start | bytes 6291464 | tf_op jit(solution)/shard_map/ppermute | solution.py:119
  89.1 3.5 %copy-start.2 = (bf16[1024,1024]{1,0:T(8,128)(2,1)S(1)}, bf16[1024,1024]{1,0:T(8,128)(2,1)}, u32[]{:S(2)}) copy-start(bf16[1024,1024]{1,0:T(8,128)(2,1)} %get-tuple-element.7) | copy-start | bytes 6291460
  92.5 6.8 %copy-start.4 = (bf16[16,96,1024]{2,1,0:T(8,128)(2,1)}, bf16[16,96,1024]{2,1,0:T(8,128)(2,1)S(1)}, u32[]{:S(2)}) copy-start(bf16[16,96,1024]{2,1,0:T(8,128)(2,1)S(1)} %fusion.6) | copy-start | bytes 9437188
  94.7 2.6 %copy-start.7 = (bf16[8,2,96,1024]{3,2,1,0:T(8,128)(2,1)}, bf16[8,2,96,1024]{3,2,1,0:T(8,128)(2,1)S(1)}, u32[]{:S(2)}) copy-start(bf16[8,2,96,1024]{3,2,1,0:T(8,128)(2,1)S(1)} %copy.20) | copy-start | bytes 9437188
  109.3 4.5 %collective-permute-start = (bf16[8,128,1024]{2,1,0:T(8,128)(2,1)}, bf16[8,128,1024]{2,1,0:T(8,128)(2,1)}, u32[]{:S(2)}, u32[]{:S(2)}) collective-permute-start(bf16[8,128,1024]{2,1,0:T(8,128)(2,1)} %get-tuple-element.20), channel_id=1, source_target_pairs={{0,1},{1,0},{2,3},{3,2},{4,5},{5,4},{6,7},{7,6},{8,9},{9,8},{10,11... | collective-permute-start | bytes 6291464 | tf_op jit(solution)/shard_map/ppermute | solution.py:231
  117.9 53.6 %all-to-all-start = ((bf16[8,128,1024]{2,1,0:T(8,128)(2,1)}), bf16[8,128,1024]{2,1,0:T(8,128)(2,1)S(1)}, u32[]{:S(2)}, u32[]{:S(2)}) async-start(bf16[8,128,1024]{2,1,0:T(8,128)(2,1)} %add_convert_fusion), calls=%async_computation | async-start | bytes 4194304 | tf_op jit(solution)/shard_map/all_to_all | solution.py:244
  122.2 3.3 %copy-start.5 = (bf16[16,96,1024]{2,1,0:T(8,128)(2,1)S(1)}, bf16[16,96,1024]{2,1,0:T(8,128)(2,1)}, u32[]{:S(2)}) copy-start(bf16[16,96,1024]{2,1,0:T(8,128)(2,1)} %copy-done.4) | copy-start | bytes 9437188
  122.3 3.5 %copy-start.16 = (bf16[1536,512]{1,0:T(8,128)(2,1)S(1)}, bf16[1536,512]{1,0:T(8,128)(2,1)}, u32[]{:S(2)}) copy-start(bf16[1536,512]{1,0:T(8,128)(2,1)} %get-tuple-element.4) | copy-start | bytes 4718596
  129.5 37.1 %collective-permute-start.9 = (bf16[256,3,1024]{2,0,1:T(8,128)(2,1)}, bf16[256,3,1024]{2,0,1:T(8,128)(2,1)}, u32[]{:S(2)}, u32[]{:S(2)}) collective-permute-start(bf16[256,3,1024]{2,0,1:T(8,128)(2,1)} %pad_maximum_fusion.1), channel_id=1, source_target_pairs={{0,16},{16,0},{1,17},{17,1},{2,18},{18,2},{3,19},{19,3},{4,20},{20... | collective-permute-start | bytes 4718600 | tf_op jit(solution)/shard_map/ppermute | solution.py:140
  131.1 3.3 %copy-start.6 = (bf16[16,96,1024]{2,1,0:T(8,128)(2,1)S(1)}, bf16[16,96,1024]{2,1,0:T(8,128)(2,1)}, u32[]{:S(2)}) copy-start(bf16[16,96,1024]{2,1,0:T(8,128)(2,1)} %copy-done.4) | copy-start | bytes 9437188
  131.1 3.5 %copy-start.15 = (bf16[1536,512]{1,0:T(8,128)(2,1)S(1)}, bf16[1536,512]{1,0:T(8,128)(2,1)}, u32[]{:S(2)}) copy-start(bf16[1536,512]{1,0:T(8,128)(2,1)} %get-tuple-element.5) | copy-start | bytes 4718596
  134.6 1.9 %copy-start.8 = (bf16[8,2,96,1024]{3,2,1,0:T(8,128)(2,1)S(1)}, bf16[8,2,96,1024]{3,2,1,0:T(8,128)(2,1)}, u32[]{:S(2)}) copy-start(bf16[8,2,96,1024]{3,2,1,0:T(8,128)(2,1)} %copy-done.7) | copy-start | bytes 9437188
  134.6 2.4 %copy-start.13 = (bf16[1536,512]{1,0:T(8,128)(2,1)S(1)}, bf16[1536,512]{1,0:T(8,128)(2,1)}, u32[]{:S(2)}) copy-start(bf16[1536,512]{1,0:T(8,128)(2,1)} %copy-done.12) | copy-start | bytes 4718596
  166.7 5.9 %copy-start.1 = (bf16[1,512,1024]{2,1,0:T(8,128)(2,1)S(1)}, bf16[1,512,1024]{2,1,0:T(8,128)(2,1)}, u32[]{:S(2)}) copy-start(bf16[1,512,1024]{2,1,0:T(8,128)(2,1)} %param.17) | copy-start | bytes 3145732
  (5 other events, 7.7 us)
Sparse Core Ops, SparseCore 0:
  14.8 58.5 all-gather.1

commit v13 on v12

--- a/solution.py
+++ b/solution.py
@@ -221,16 +221,16 @@
 
     pick_k = pick.reshape(nchip, ncore, capacity, tok_rows)
     out_k = expert_out.reshape(nchip, ncore, capacity, width)
-    dense = [
-        jnp.einsum(
-            "sjt,sjd->std", pick_k[:, k], out_k[:, k], preferred_element_type=jnp.float32
+    def dense_for(k):
+        return jnp.einsum(
+            "sjt,sjd->std",
+            lax.dynamic_index_in_dim(pick_k, k, 1, keepdims=False),
+            lax.dynamic_index_in_dim(out_k, k, 1, keepdims=False),
+            preferred_element_type=jnp.float32,
         ).astype(jnp.bfloat16)
-        for k in range(ncore)
-    ]
-    mine = jnp.where(on_core0, dense[0], dense[1])
-    from_partner = lax.ppermute(
-        jnp.where(on_core0, dense[1], dense[0]), "core", [(0, 1), (1, 0)]
-    )
+
+    from_partner = lax.ppermute(dense_for(1 - core), "core", [(0, 1), (1, 0)])
+    mine = dense_for(core)
     gate_all = gate_t.reshape(nchip, ncore, topk, tok_rows)
     routes_all = routes_t.reshape(nchip, ncore, topk, tok_rows)
     gate_own = jnp.where(on_core0, gate_all[:, 0], gate_all[:, 1])

time: 180 us -> 179 us (level)
  other arithmetic: 22 us -> 18.5 us
  matrix products: 29.1 us -> 31.5 us
    convert_element_type x1 -> x0, other arithmetic: 4.06 us -> none  [local_gather(): combined = (gte[:, :, None] * mine.astype(jnp.float32) + gte_partner[:, :...]
    dot_general x2, matrix products: 3.6 us -> 5.89 us  [dense_for(): jnp.einsum('sjt,sjd->std', lax.dynamic_index_in_dim(pick_k, k, 1, keepdim...]
    unnamed x37 -> x39, local copies, waits for them, and re-layouts: 4.46 us -> 5.92 us
where the time goes in v13:
time: 179 us; the launch traced here: 178 us
  waiting for transfers between devices  61.2 us (34%)
  between operations  32.6 us (18%)
  matrix products  31.5 us (18%)
  starting transfers between devices  21.9 us (12%)
  other arithmetic  18.5 us (10%)
  local copies, waits for them, and re-layouts  12.6 us (7%)
    ppermute x1, waiting for transfers between devices, reduce_grads_dp(): lax.ppermute(grad_half(1 - d).astype(jnp.bfloat16), 'dp', [(0, 1), (1, 0)])  28 us
    ppermute x4, waiting for transfers between devices, ring_gather(): up = lax.ppermute(up, 'ez', ahead)  18.2 us
    dot_general x6, matrix products, contract_rows(): lax.dot_general(left, right, (((0,), (0,)), ((), ())), preferred_element_...  10.6 us
    ppermute x4, starting transfers between devices, ring_gather(): up = lax.ppermute(up, 'ez', ahead)  8.47 us
    dot_general x3, matrix products, contract_cols(): lax.dot_general(left, right, (((1,), (1,)), ((), ())), preferred_element_...  8.32 us
    ppermute x3, starting transfers between devices, ring_gather(): down = lax.ppermute(down, 'ez', behind)  7.29 us
    ppermute x3, waiting for transfers between devices, ring_gather(): down = lax.ppermute(down, 'ez', behind)  7.25 us
    unnamed x39, local copies, waits for them, and re-layouts  5.92 us
  transfers between devices with their start and end apart: 12, of which 7 were waited for; matrix products, arithmetic and copies ran while one was open for 14% of the time, Pallas kernels for 0%

profile of v13, /device:TPU:0, one launch (start us, length us, event | category | flops | bytes accessed | tf_op | source)
XLA Modules:
  0.0 178.3 jit_solution(1197800302986954213)
XLA Ops:
  12.9 1.7 pad_maximum_fusion.2
  14.6 3.0 %collective-permute-start.2 = (bf16[128,1024]{1,0:T(8,128)(2,1)}, bf16[128,1024]{1,0:T(8,128)(2,1)}, u32[]{:S(2)}, u32[]{:S(2)}) collective-permute-start(bf16[128,1024]{1,0:T(8,128)(2,1)} %param.16), channel_id=1, source_target_pairs={{0,2},{4,0},{8,4},{12,8},{14,12},{10,14},{6,10},{2,6},{1,3},{5,1},... | collective-permute-start | bytes 786440 | tf_op jit(solution)/shard_map/ppermute | solution.py:116
  39.0 1.9 %collective-permute-start.4 = (bf16[128,1024]{1,0:T(8,128)(2,1)}, bf16[128,1024]{1,0:T(8,128)(2,1)S(1)}, u32[]{:S(2)}, u32[]{:S(2)}) collective-permute-start(bf16[128,1024]{1,0:T(8,128)(2,1)} %collective-permute-done.2), channel_id=1, source_target_pairs={{0,2},{4,0},{8,4},{12,8},{14,12},{10,14},{6,10},{2,6},{1,3},{5,1},... | collective-permute-start | bytes 786440 | tf_op jit(solution)/shard_map/ppermute | solution.py:116
  43.1 7.2 %collective-permute-done.4 = bf16[128,1024]{1,0:T(8,128)(2,1)S(1)} collective-permute-done((bf16[128,1024]{1,0:T(8,128)(2,1)}, bf16[128,1024]{1,0:T(8,128)(2,1)S(1)}, u32[]{:S(2)}, u32[]{:S(2)}) %collective-permute-start.4) | collective-permute-done | bytes 262176 | tf_op jit(solution)/shard_map/ppermute | solution.py:116
  50.4 2.4 %collective-permute-start.6 = (bf16[128,1024]{1,0:T(8,128)(2,1)S(1)}, bf16[128,1024]{1,0:T(8,128)(2,1)S(1)}, u32[]{:S(2)}, u32[]{:S(2)}) collective-permute-start(bf16[128,1024]{1,0:T(8,128)(2,1)S(1)} %collective-permute-done.4), channel_id=1, source_target_pairs={{0,2},{4,0},{8,4},{12,8},{14,12},{10,14},{6,10},{2,6},{1,3},{5,1},... | collective-permute-start | bytes 786440 | tf_op jit(solution)/shard_map/ppermute | solution.py:116
  52.7 3.3 %collective-permute-start.5 = (bf16[128,1024]{1,0:T(8,128)(2,1)S(1)}, bf16[128,1024]{1,0:T(8,128)(2,1)S(1)}, u32[]{:S(2)}, u32[]{:S(2)}) collective-permute-start(bf16[128,1024]{1,0:T(8,128)(2,1)S(1)} %collective-permute-done.3), channel_id=1, source_target_pairs={{0,4},{4,8},{8,12},{12,14},{14,10},{10,6},{6,2},{2,0},{1,5},{5,9},... | collective-permute-start | bytes 786440 | tf_op jit(solution)/shard_map/ppermute | solution.py:113
  56.1 9.8 %collective-permute-done.5 = bf16[128,1024]{1,0:T(8,128)(2,1)S(1)} collective-permute-done((bf16[128,1024]{1,0:T(8,128)(2,1)S(1)}, bf16[128,1024]{1,0:T(8,128)(2,1)S(1)}, u32[]{:S(2)}, u32[]{:S(2)}) %collective-permute-start.5) | collective-permute-done | bytes 262176 | tf_op jit(solution)/shard_map/ppermute | solution.py:113
  65.9 4.8 %collective-permute-start.7 = (bf16[128,1024]{1,0:T(8,128)(2,1)S(1)}, bf16[128,1024]{1,0:T(8,128)(2,1)S(1)}, u32[]{:S(2)}, u32[]{:S(2)}) collective-permute-start(bf16[128,1024]{1,0:T(8,128)(2,1)S(1)} %collective-permute-done.5), channel_id=1, source_target_pairs={{0,4},{4,8},{8,12},{12,14},{14,10},{10,6},{6,2},{2,0},{1,5},{5,9},... | collective-permute-start | bytes 786440 | tf_op jit(solution)/shard_map/ppermute | solution.py:113
  70.8 8.4 %collective-permute-done.7 = bf16[128,1024]{1,0:T(8,128)(2,1)S(1)} collective-permute-done((bf16[128,1024]{1,0:T(8,128)(2,1)S(1)}, bf16[128,1024]{1,0:T(8,128)(2,1)S(1)}, u32[]{:S(2)}, u32[]{:S(2)}) %collective-permute-start.7) | collective-permute-done | bytes 262176 | tf_op jit(solution)/shard_map/ppermute | solution.py:113
  80.5 3.0 %collective-permute-done.8 = bf16[1024,1024]{1,0:T(8,128)(2,1)} collective-permute-done((bf16[1024,1024]{1,0:T(8,128)(2,1)S(1)}, bf16[1024,1024]{1,0:T(8,128)(2,1)}, u32[]{:S(2)}, u32[]{:S(2)}) %collective-permute-start.8) | collective-permute-done | bytes 2097184 | tf_op jit(solution)/shard_map/ppermute | solution.py:119
  83.6 3.9 %broadcast_select_fusion.1 = (bf16[1024,1024]{1,0:T(8,128)(2,1)}, bf16[1024,1024]{1,0:T(8,128)(2,1)S(1)}) fusion(bf16[1024,1024]{1,0:T(8,128)(2,1)} %collective-permute-done.8, pred[]{:T(512)S(6)} %eq.47, bf16[8,128,1024]{2,1,0:T(8,128)(2,1)} %copy-done.2), kind=kLoop, calls=%fused_computation.22 | loop fusion | flops 2097152 | bytes 8388609 | tf_op jit(solution)/shard_map/jit(_where)/select_n | solution.py:169
  88.9 3.3 %fusion.6 = bf16[16,96,1024]{2,1,0:T(8,128)(2,1)S(1)} fusion(bf16[16,136,1024]{2,1,0:T(8,128)(2,1)} %bitcast.144, s32[16,128]{1,0:T(8,128)S(1)} %convolution_convert_fusion.5, pred[16,128]{1,0:T(8,128)(4,1)S(1)} %fusion.72), kind=kOutput, calls=%fused_computation.16 | convolution fusion | flops 404619264 | bytes 7350272 | tf_op jit(solution)/shard_map/sjt,std->sjd/dot_general | solution.py:190
  95.3 1.8 %fusion.34 = f32[1536,512]{1,0:T(8,128)S(1)} fusion(bf16[1536,1024]{1,0:T(8,128)(2,1)S(1)} %bitcast.151, bf16[1,512,1024]{2,1,0:T(8,128)(2,1)S(1)} %copy-done.12), kind=kOutput, calls=%fused_computation.43 | convolution fusion | flops 1610612736 | bytes 7340032 | tf_op jit(solution)/shard_map/dot_general | solution.py:16
  97.2 1.8 %fusion.37 = f32[1536,512]{1,0:T(8,128)S(1)} fusion(bf16[1536,1024]{1,0:T(8,128)(2,1)S(1)} %bitcast.145, bf16[1,512,1024]{2,1,0:T(8,128)(2,1)S(1)} %copy-done.11), kind=kOutput, calls=%fused_computation.46 | convolution fusion | flops 1610612736 | bytes 7340032 | tf_op jit(solution)/shard_map/dot_general | solution.py:16
  99.1 4.6 %multiply_convert_fusion.1 = (bf16[1536,512]{1,0:T(8,128)(2,1)}, bf16[1536,512]{1,0:T(8,128)(2,1)}, bf16[1536,512]{1,0:T(8,128)(2,1)S(1)}) fusion(f32[1536,512]{1,0:T(8,128)S(1)} %fusion.34, f32[1536,512]{1,0:T(8,128)S(1)} %fusion.37, bf16[1536,1024]{1,0:T(8,128)(2,1)S(1)} %bitcast.146, bf16[1,512,1024]{2,1,0:T(8,128)(2,1)S(1)} %copy-done), kind=kOutput, calls=%fused_computation.12 | convolution fusion | flops 1622409216 | bytes 15204352 | tf_op jit(solution)/shard_map/dot_general | solution.py:16
  103.7 1.8 %convolution_convert_fusion = bf16[1536,1024]{1,0:T(8,128)(2,1)S(1)} fusion(bf16[1536,512]{1,0:T(8,128)(2,1)S(1)} %get-tuple-element.6, bf16[1,512,1024]{2,1,0:T(8,128)(2,1)S(1)} %copy-done.12), kind=kOutput, calls=%fused_computation.7 | convolution fusion | flops 1612185600 | bytes 5767168 | tf_op jit(solution)/shard_map/dot_general | solution.py:218
  107.2 2.1 %convolution_convert_fusion.1 = bf16[8,128,1024]{2,1,0:T(8,128)(2,1)} fusion(bf16[8,2,96,1024]{3,2,1,0:T(8,128)(2,1)S(1)} %bitcast.154, s32[]{:T(128)S(6)} %select_n.146, pred[8,2,96,128]{3,2,0,1:T(32,128)(4,1)S(1)} %fusion.47), kind=kOutput, calls=%fused_computation.23 | convolution fusion | flops 202375168 | bytes 3769344 | tf_op jit(solution)/shard_map/sjt,sjd->std/dot_general | solution.py:225
  110.3 3.4 %collective-permute-done = bf16[8,128,1024]{2,1,0:T(8,128)(2,1)S(1)} collective-permute-done((bf16[8,128,1024]{2,1,0:T(8,128)(2,1)}, bf16[8,128,1024]{2,1,0:T(8,128)(2,1)S(1)}, u32[]{:S(2)}, u32[]{:S(2)}) %collective-permute-start) | collective-permute-done | bytes 2097184 | tf_op jit(solution)/shard_map/ppermute | solution.py:232
  113.7 3.8 %add_convert_fusion = bf16[8,128,1024]{2,1,0:T(8,128)(2,1)} fusion(bf16[8,128,1024]{2,1,0:T(8,128)(2,1)S(1)} %collective-permute-done, f32[8,128]{1,0:T(8,128)S(1)} %get-tuple-element.3, f32[8,128]{1,0:T(8,128)S(1)} %get-tuple-element.2, bf16[8,2,96,1024]{3,2,1,0:T(8,128)(2,1)} %bitcast.155, s32[]{:T(128)S(6)} %select_n.144, ...), kind=kOutput, calls=%fused_computation.6 | convolution fusion | flops 208666624 | bytes 5874688 | tf_op jit(solution)/shard_map/sjt,sjd->std/dot_general | solution.py:225
  117.5 4.3 %all-to-all-start = ((bf16[8,128,1024]{2,1,0:T(8,128)(2,1)}), bf16[8,128,1024]{2,1,0:T(8,128)(2,1)S(1)}, u32[]{:S(2)}, u32[]{:S(2)}) async-start(bf16[8,128,1024]{2,1,0:T(8,128)(2,1)} %add_convert_fusion), calls=%async_computation | async-start | bytes 4194304 | tf_op jit(solution)/shard_map/all_to_all | solution.py:244
  121.8 3.3 %fusion.33 = bf16[256,1,1024]{2,0,1:T(8,128)(2,1)S(1)} fusion(bf16[1536,1024]{1,0:T(8,128)(2,1)} %bitcast.152, bf16[1536,512]{1,0:T(8,128)(2,1)} %copy-done.13, s32[]{:T(128)S(6)} %select_n.174), kind=kOutput, calls=%fused_computation.41 | convolution fusion | flops 805568512 | bytes 4456452 | tf_op jit(solution)/shard_map/dot_general | solution.py:10
  130.6 3.3 %convolution_bitcast_fusion.2 = f32[256,1,1024]{2,0,1:T(8,128)S(1)} fusion(bf16[1536,1024]{1,0:T(8,128)(2,1)} %bitcast.147, bf16[1536,512]{1,0:T(8,128)(2,1)} %get-tuple-element.4, s32[]{:T(128)S(6)} %select_n.173), kind=kOutput, calls=%fused_computation.35 | convolution fusion | flops 805306368 | bytes 4980740 | tf_op jit(solution)/shard_map/dot_general | solution.py:10
  137.4 28.0 %collective-permute-done.9 = bf16[256,3,1024]{2,0,1:T(8,128)(2,1)} collective-permute-done((bf16[256,3,1024]{2,0,1:T(8,128)(2,1)}, bf16[256,3,1024]{2,0,1:T(8,128)(2,1)}, u32[]{:S(2)}, u32[]{:S(2)}) %collective-permute-start.9) | collective-permute-done | bytes 1572896 | tf_op jit(solution)/shard_map/ppermute | solution.py:140
  165.4 3.6 %fusion.4 = f32[1,256,3,1024]{3,1,2,0:T(8,128)} fusion(f32[256,1,1024]{2,0,1:T(8,128)S(1)} %convolution_bitcast_fusion, f32[256,1,1024]{2,0,1:T(8,128)S(1)} %convolution_bitcast_fusion.1, f32[256,1,1024]{2,0,1:T(8,128)S(1)} %convolution_bitcast_fusion.2, bf16[256,3,1024]{2,0,1:T(8,128)(2,1)} %collective-permute-done.9), kind=kLoop, calls=%fused_computation.10 | loop fusion | flops 3145728 | bytes 7864320 | tf_op jit(solution)/shard_map/reshape | solution.py:142
  (94 shorter events, 31.0 us)
Async XLA Ops:
  7.2 91.9 %copy-start = (bf16[1,512,1024]{2,1,0:T(8,128)(2,1)S(1)}, bf16[1,512,1024]{2,1,0:T(8,128)(2,1)}, u32[]{:S(2)}) copy-start(bf16[1,512,1024]{2,1,0:T(8,128)(2,1)} %param.17) | copy-start | bytes 3145732
  7.2 31.8 %copy-start.10 = (bf16[128,1024]{1,0:T(8,128)(2,1)S(1)}, bf16[128,1024]{1,0:T(8,128)(2,1)}, u32[]{:S(2)}) copy-start(bf16[128,1024]{1,0:T(8,128)(2,1)} %param.16) | copy-start | bytes 786436
  7.2 80.3 %all-gather.2.cloned.1.call-start = ((), (), s32[]{:S(2)}) async-start(), calls=%async_computation.1 | async-start | bytes 4734976 | tf_op jit(solution)/shard_map/all_gather | solution.py:164
  14.6 24.4 %collective-permute-start.2 = (bf16[128,1024]{1,0:T(8,128)(2,1)}, bf16[128,1024]{1,0:T(8,128)(2,1)}, u32[]{:S(2)}, u32[]{:S(2)}) collective-permute-start(bf16[128,1024]{1,0:T(8,128)(2,1)} %param.16), channel_id=1, source_target_pairs={{0,2},{4,0},{8,4},{12,8},{14,12},{10,14},{6,10},{2,6},{1,3},{5,1},... | collective-permute-start | bytes 786440 | tf_op jit(solution)/shard_map/ppermute | solution.py:116
  17.6 23.3 %collective-permute-start.1 = (bf16[128,1024]{1,0:T(8,128)(2,1)}, bf16[128,1024]{1,0:T(8,128)(2,1)}, u32[]{:S(2)}, u32[]{:S(2)}) collective-permute-start(bf16[128,1024]{1,0:T(8,128)(2,1)} %param.16), channel_id=1, source_target_pairs={{0,4},{4,8},{8,12},{12,14},{14,10},{10,6},{6,2},{2,0},{1,5},{5,9},... | collective-permute-start | bytes 786440 | tf_op jit(solution)/shard_map/ppermute | solution.py:113
  39.0 11.3 %collective-permute-start.4 = (bf16[128,1024]{1,0:T(8,128)(2,1)}, bf16[128,1024]{1,0:T(8,128)(2,1)S(1)}, u32[]{:S(2)}, u32[]{:S(2)}) collective-permute-start(bf16[128,1024]{1,0:T(8,128)(2,1)} %collective-permute-done.2), channel_id=1, source_target_pairs={{0,2},{4,0},{8,4},{12,8},{14,12},{10,14},{6,10},{2,6},{1,3},{5,1},... | collective-permute-start | bytes 786440 | tf_op jit(solution)/shard_map/ppermute | solution.py:116
  41.0 11.8 %collective-permute-start.3 = (bf16[128,1024]{1,0:T(8,128)(2,1)}, bf16[128,1024]{1,0:T(8,128)(2,1)S(1)}, u32[]{:S(2)}, u32[]{:S(2)}) collective-permute-start(bf16[128,1024]{1,0:T(8,128)(2,1)} %collective-permute-done.1), channel_id=1, source_target_pairs={{0,4},{4,8},{8,12},{12,14},{14,10},{10,6},{6,2},{2,0},{1,5},{5,9},... | collective-permute-start | bytes 786440 | tf_op jit(solution)/shard_map/ppermute | solution.py:113
  50.4 20.4 %collective-permute-start.6 = (bf16[128,1024]{1,0:T(8,128)(2,1)S(1)}, bf16[128,1024]{1,0:T(8,128)(2,1)S(1)}, u32[]{:S(2)}, u32[]{:S(2)}) collective-permute-start(bf16[128,1024]{1,0:T(8,128)(2,1)S(1)} %collective-permute-done.4), channel_id=1, source_target_pairs={{0,2},{4,0},{8,4},{12,8},{14,12},{10,14},{6,10},{2,6},{1,3},{5,1},... | collective-permute-start | bytes 786440 | tf_op jit(solution)/shard_map/ppermute | solution.py:116
  52.7 13.2 %collective-permute-start.5 = (bf16[128,1024]{1,0:T(8,128)(2,1)S(1)}, bf16[128,1024]{1,0:T(8,128)(2,1)S(1)}, u32[]{:S(2)}, u32[]{:S(2)}) collective-permute-start(bf16[128,1024]{1,0:T(8,128)(2,1)S(1)} %collective-permute-done.3), channel_id=1, source_target_pairs={{0,4},{4,8},{8,12},{12,14},{14,10},{10,6},{6,2},{2,0},{1,5},{5,9},... | collective-permute-start | bytes 786440 | tf_op jit(solution)/shard_map/ppermute | solution.py:113
  65.9 13.3 %collective-permute-start.7 = (bf16[128,1024]{1,0:T(8,128)(2,1)S(1)}, bf16[128,1024]{1,0:T(8,128)(2,1)S(1)}, u32[]{:S(2)}, u32[]{:S(2)}) collective-permute-start(bf16[128,1024]{1,0:T(8,128)(2,1)S(1)} %collective-permute-done.5), channel_id=1, source_target_pairs={{0,4},{4,8},{8,12},{12,14},{14,10},{10,6},{6,2},{2,0},{1,5},{5,9},... | collective-permute-start | bytes 786440 | tf_op jit(solution)/shard_map/ppermute | solution.py:113
  79.2 4.4 %collective-permute-start.8 = (bf16[1024,1024]{1,0:T(8,128)(2,1)S(1)}, bf16[1024,1024]{1,0:T(8,128)(2,1)}, u32[]{:S(2)}, u32[]{:S(2)}) collective-permute-start(bf16[1024,1024]{1,0:T(8,128)(2,1)S(1)} %bitcast.142), channel_id=1, source_target_pairs={{0,1},{1,0},{2,3},{3,2},{4,5},{5,4},{6,7},{7,6},{8,9},{9,8},{10,11... | collective-permute-start | bytes 6291464 | tf_op jit(solution)/shard_map/ppermute | solution.py:119
  88.6 3.6 %copy-start.9 = (bf16[2,8,56,128]{3,2,1,0:T(8,128)(2,1)}, bf16[2,8,56,128]{3,2,1,0:T(8,128)(2,1)S(1)}, u32[]{:S(2)}) copy-start(bf16[2,8,56,128]{3,2,1,0:T(8,128)(2,1)S(1)} %copy.18) | copy-start | bytes 688132
  88.9 3.5 %copy-start.1 = (bf16[1024,1024]{1,0:T(8,128)(2,1)S(1)}, bf16[1024,1024]{1,0:T(8,128)(2,1)}, u32[]{:S(2)}) copy-start(bf16[1024,1024]{1,0:T(8,128)(2,1)} %get-tuple-element.7) | copy-start | bytes 6291460
  92.3 6.8 %copy-start.3 = (bf16[16,96,1024]{2,1,0:T(8,128)(2,1)}, bf16[16,96,1024]{2,1,0:T(8,128)(2,1)S(1)}, u32[]{:S(2)}) copy-start(bf16[16,96,1024]{2,1,0:T(8,128)(2,1)S(1)} %fusion.6) | copy-start | bytes 9437188
  94.5 2.6 %copy-start.6 = (bf16[8,2,96,1024]{3,2,1,0:T(8,128)(2,1)}, bf16[8,2,96,1024]{3,2,1,0:T(8,128)(2,1)S(1)}, u32[]{:S(2)}) copy-start(bf16[8,2,96,1024]{3,2,1,0:T(8,128)(2,1)S(1)} %copy.16) | copy-start | bytes 9437188
  109.4 4.4 %collective-permute-start = (bf16[8,128,1024]{2,1,0:T(8,128)(2,1)}, bf16[8,128,1024]{2,1,0:T(8,128)(2,1)S(1)}, u32[]{:S(2)}, u32[]{:S(2)}) collective-permute-start(bf16[8,128,1024]{2,1,0:T(8,128)(2,1)} %convolution_convert_fusion.1), channel_id=1, source_target_pairs={{0,1},{1,0},{2,3},{3,2},{4,5},{5,4},{6,7},{7,6},{8,9},{9,8},{10,11... | collective-permute-start | bytes 6291464 | tf_op jit(solution)/shard_map/ppermute | solution.py:232
  117.5 52.9 %all-to-all-start = ((bf16[8,128,1024]{2,1,0:T(8,128)(2,1)}), bf16[8,128,1024]{2,1,0:T(8,128)(2,1)S(1)}, u32[]{:S(2)}, u32[]{:S(2)}) async-start(bf16[8,128,1024]{2,1,0:T(8,128)(2,1)} %add_convert_fusion), calls=%async_computation | async-start | bytes 4194304 | tf_op jit(solution)/shard_map/all_to_all | solution.py:244
  121.8 3.3 %copy-start.4 = (bf16[16,96,1024]{2,1,0:T(8,128)(2,1)S(1)}, bf16[16,96,1024]{2,1,0:T(8,128)(2,1)}, u32[]{:S(2)}) copy-start(bf16[16,96,1024]{2,1,0:T(8,128)(2,1)} %copy-done.3) | copy-start | bytes 9437188
  121.8 3.5 %copy-start.17 = (bf16[1536,512]{1,0:T(8,128)(2,1)S(1)}, bf16[1536,512]{1,0:T(8,128)(2,1)}, u32[]{:S(2)}) copy-start(bf16[1536,512]{1,0:T(8,128)(2,1)} %get-tuple-element.4) | copy-start | bytes 4718596
  129.0 36.5 %collective-permute-start.9 = (bf16[256,3,1024]{2,0,1:T(8,128)(2,1)}, bf16[256,3,1024]{2,0,1:T(8,128)(2,1)}, u32[]{:S(2)}, u32[]{:S(2)}) collective-permute-start(bf16[256,3,1024]{2,0,1:T(8,128)(2,1)} %pad_maximum_fusion.1), channel_id=1, source_target_pairs={{0,16},{16,0},{1,17},{17,1},{2,18},{18,2},{3,19},{19,3},{4,20},{20... | collective-permute-start | bytes 4718600 | tf_op jit(solution)/shard_map/ppermute | solution.py:140
  130.5 3.3 %copy-start.5 = (bf16[16,96,1024]{2,1,0:T(8,128)(2,1)S(1)}, bf16[16,96,1024]{2,1,0:T(8,128)(2,1)}, u32[]{:S(2)}) copy-start(bf16[16,96,1024]{2,1,0:T(8,128)(2,1)} %copy-done.3) | copy-start | bytes 9437188
  130.6 3.5 %copy-start.16 = (bf16[1536,512]{1,0:T(8,128)(2,1)S(1)}, bf16[1536,512]{1,0:T(8,128)(2,1)}, u32[]{:S(2)}) copy-start(bf16[1536,512]{1,0:T(8,128)(2,1)} %get-tuple-element.5) | copy-start | bytes 4718596
  134.1 1.9 %copy-start.7 = (bf16[8,2,96,1024]{3,2,1,0:T(8,128)(2,1)S(1)}, bf16[8,2,96,1024]{3,2,1,0:T(8,128)(2,1)}, u32[]{:S(2)}) copy-start(bf16[8,2,96,1024]{3,2,1,0:T(8,128)(2,1)} %copy-done.6) | copy-start | bytes 9437188
  134.1 2.4 %copy-start.14 = (bf16[1536,512]{1,0:T(8,128)(2,1)S(1)}, bf16[1536,512]{1,0:T(8,128)(2,1)}, u32[]{:S(2)}) copy-start(bf16[1536,512]{1,0:T(8,128)(2,1)} %copy-done.13) | copy-start | bytes 4718596
  (6 other events, 9.4 us)
Sparse Core Ops, SparseCore 0:
  14.8 58.4 all-gather.1

commit v14 on v13

--- a/solution.py
+++ b/solution.py
@@ -163,12 +163,8 @@
 
     gathered = lax.all_gather(packed, ("ez", "core"), axis=0, tiled=True)
     gathered = gathered.reshape(experts, tok_rows + lines, width)
-    cot_halves = ring_gather(cotangent)
+    all_cot = lax.all_gather(cotangent, ("ez", "core"), axis=0, tiled=True)
     on_core0 = core == 0
-    cot_by_core = [
-        jnp.where(on_core0, cot_halves[0], cot_halves[1]),
-        jnp.where(on_core0, cot_halves[1], cot_halves[0]),
-    ]
     meta_all = gathered[:, tok_rows:].reshape(experts, lines * width)
     meta_all = meta_all[:, :meta_rows.size].reshape(experts, len(meta), topk, tok_rows)
     routes_t = meta_all[:, 0].astype(jnp.int32)
@@ -193,22 +189,10 @@
         gathered[:, :tok_rows],
         preferred_element_type=jnp.float32,
     ).astype(jnp.bfloat16).reshape(experts * capacity, width)
-    pick_by_core = pick.reshape(nchip, ncore, capacity, tok_rows)
-    fac_by_core = fac.reshape(nchip, ncore, tok_rows)
-    rows_q = []
-    for k in range(ncore):
-        scaled = fac_by_core[:, k, :, None] * cot_by_core[k].reshape(
-            nchip, tok_rows, width
-        ).astype(jnp.float32)
-        rows_q.append(
-            jnp.einsum(
-                "sjt,std->sjd",
-                pick_by_core[:, k],
-                scaled.astype(jnp.bfloat16),
-                preferred_element_type=jnp.float32,
-            ).astype(jnp.bfloat16)
-        )
-    rows_q = jnp.stack(rows_q, axis=1).reshape(experts * capacity, width)
+    scaled = fac[:, :, None] * all_cot.reshape(experts, tok_rows, width).astype(jnp.float32)
+    rows_q = jnp.einsum(
+        "sjt,std->sjd", pick, scaled.astype(jnp.bfloat16), preferred_element_type=jnp.float32
+    ).astype(jnp.bfloat16).reshape(experts * capacity, width)
     wgate, wup, wdown = w_gate[0], w_up[0], w_down[0]
     gate_pre = contract_cols(rows_x, wgate)
     up_pre = contract_cols(rows_x, wup)

time: 179 us -> 209 us (1.17)
  waiting for transfers between devices: 61.2 us -> 133 us
  between operations: 32.6 us -> 14.3 us
  starting transfers between devices: 21.9 us -> 5.59 us
  local copies, waits for them, and re-layouts: 12.6 us -> 6.19 us
  other arithmetic: 18.5 us -> 13.6 us
  matrix products: 31.5 us -> 35 us
    all_gather x1, waiting for transfers between devices: 0.01 us -> 54.1 us  [local_gather(): gathered = lax.all_gather(packed, ('ez', 'core'), axis=0, tiled=True)]
    all_gather x0 -> x1, waiting for transfers between devices: none -> 45 us  [local_gather(): all_cot = lax.all_gather(cotangent, ('ez', 'core'), axis=0, tiled=True)]
    ppermute x8 -> x0, waiting for transfers between devices: 28.5 us -> none  [the longest x4 18.2 us: ring_gather(): up = lax.ppermute(up, 'ez', ahead)]
    ppermute x8 -> x0, starting transfers between devices: 15.8 us -> none  [the longest x4 8.47 us: ring_gather(): up = lax.ppermute(up, 'ez', ahead)]
    select_n x1 -> x0, other arithmetic: 3.87 us -> none  [local_gather(): jnp.where(on_core0, cot_halves[0], cot_halves[1])]
    dynamic_slice x2 -> x0, local copies, waits for them, and re-layouts: 2.84 us -> none  [the longest x1 1.61 us: ring_gather(): out = lax.dynamic_update_index_in_dim(out, up, ring[(at - step) % n], 0)]
    dynamic_update_slice x8 -> x0, local copies, waits for them, and re-layouts: 2.11 us -> none  [the longest x4 1.06 us: ring_gather(): out = lax.dynamic_update_index_in_dim(out, up, ring[(at - step) % n], 0)]
    dot_general x2 -> x1, matrix products: 1.36 us -> 3.45 us  [local_gather(): jnp.einsum('sjt,std->sjd', pick, scaled.astype(jnp.bfloat16), preferred_e...]
  transfers between devices with their start and end apart: 12 -> 5, of which waited for: 7 -> 5; matrix products, arithmetic and copies ran while one was open for 14% -> 10% of each run, Pallas kernels for 0% -> 0%
where the time goes in v14:
time: 209 us; the launch traced here: 208 us
  waiting for transfers between devices  133 us (64%)
  matrix products  35 us (17%)
  between operations  14.3 us (7%)
  other arithmetic  13.6 us (7%)
  local copies, waits for them, and re-layouts  6.19 us (3%)
  starting transfers between devices  5.59 us (3%)
    all_gather x1, waiting for transfers between devices, local_gather(): gathered = lax.all_gather(packed, ('ez', 'core'), axis=0, tiled=True)  54.1 us
    all_gather x1, waiting for transfers between devices, local_gather(): all_cot = lax.all_gather(cotangent, ('ez', 'core'), axis=0, tiled=True)  45 us
    ppermute x1, waiting for transfers between devices, reduce_grads_dp(): lax.ppermute(grad_half(1 - d).astype(jnp.bfloat16), 'dp', [(0, 1), (1, 0)])  28.5 us
    dot_general x6, matrix products, contract_rows(): lax.dot_general(left, right, (((0,), (0,)), ((), ())), preferred_element_...  10.6 us
    dot_general x3, matrix products, contract_cols(): lax.dot_general(left, right, (((1,), (1,)), ((), ())), preferred_element_...  8.23 us
    dot_general x2, matrix products, dense_for(): jnp.einsum('sjt,sjd->std', lax.dynamic_index_in_dim(pick_k, k, 1, keepdim...  5.89 us
    unnamed x33, local copies, waits for them, and re-layouts  5.17 us
    dot_general x1, matrix products, local_gather(): jnp.einsum('sjt,std->sjd', pick, gathered[:, :tok_rows], preferred_elemen...  4.84 us
  transfers between devices with their start and end apart: 5, of which 5 were waited for; matrix products, arithmetic and copies ran while one was open for 10% of the time, Pallas kernels for 0%

profile of v14, /device:TPU:0, one launch (start us, length us, event | category | flops | bytes accessed | tf_op | source)
XLA Modules:
  0.0 208.1 jit_solution(11447380879749998733)
XLA Ops:
  12.9 1.7 pad_maximum_fusion.1
  15.3 54.1 %all-gather.3.cloned.1.call-done = bf16[2176,1024]{1,0:T(8,128)(2,1)} async-done(((bf16[136,1024]{1,0:T(8,128)(2,1)}), bf16[2176,1024]{1,0:T(8,128)(2,1)}) %all-gather.3.cloned.1.call-update) | async-done | bytes 4456464 | tf_op jit(solution)/shard_map/all_gather | solution.py:164
  70.9 4.8 %fusion.8 = bf16[16,96,1024]{2,1,0:T(8,128)(2,1)} fusion(bf16[16,136,1024]{2,1,0:T(8,128)(2,1)} %bitcast.93, s32[16,128]{1,0:T(8,128)S(1)} %convolution_convert_fusion.5, pred[16,128]{1,0:T(8,128)(4,1)S(1)} %fusion.62), kind=kOutput, calls=%fused_computation.15 | convolution fusion | flops 404619264 | bytes 7350272 | tf_op jit(solution)/shard_map/sjt,std->sjd/dot_general | solution.py:186
  75.7 45.0 %all-gather.5.cloned.1.call-done = bf16[2048,1024]{1,0:T(8,128)(2,1)} async-done(((bf16[128,1024]{1,0:T(8,128)(2,1)}), bf16[2048,1024]{1,0:T(8,128)(2,1)}) %all-gather.5.cloned.1.call-update) | async-done | bytes 4194320 | tf_op jit(solution)/shard_map/all_gather | solution.py:166
  120.7 3.5 %fusion.11 = bf16[16,96,1024]{2,1,0:T(8,128)(2,1)S(1)} fusion(bf16[16,128,1024]{2,1,0:T(8,128)(2,1)} %bitcast.94, f32[16,128]{1,0:T(8,128)S(1)} %get-tuple-element.7, s32[16,128]{1,0:T(8,128)S(1)} %convolution_convert_fusion.5, pred[16,128]{1,0:T(8,128)(4,1)S(1)} %fusion.62), kind=kOutput, calls=%fused_computation.16 | convolution fusion | flops 410910720 | bytes 7358464 | tf_op jit(solution)/shard_map/sjt,std->sjd/dot_general | solution.py:193
  124.2 1.8 fusion.21
  126.0 1.1 copy-done.1
  127.5 1.8 fusion.24
  129.3 4.6 %multiply_convert_fusion.1 = (bf16[1536,512]{1,0:T(8,128)(2,1)}, bf16[1536,512]{1,0:T(8,128)(2,1)}, bf16[1536,512]{1,0:T(8,128)(2,1)S(1)}) fusion(f32[1536,512]{1,0:T(8,128)S(1)} %fusion.21, f32[1536,512]{1,0:T(8,128)S(1)} %fusion.24, bf16[1536,1024]{1,0:T(8,128)(2,1)S(1)} %bitcast.97, bf16[1,512,1024]{2,1,0:T(8,128)(2,1)S(1)} %copy-done), kind=kOutput, calls=%fused_computation.11 | convolution fusion | flops 1622409216 | bytes 15204352 | tf_op jit(solution)/shard_map/dot_general | solution.py:16
  133.9 1.8 convolution_convert_fusion
  135.9 1.5 copy-done.6
  137.4 2.1 %convolution_convert_fusion.1 = bf16[8,128,1024]{2,1,0:T(8,128)(2,1)} fusion(bf16[8,2,96,1024]{3,2,1,0:T(8,128)(2,1)S(1)} %bitcast.104, s32[]{:T(128)S(6)} %select_n.56, pred[8,2,96,128]{3,2,0,1:T(32,128)(4,1)S(1)} %fusion.34), kind=kOutput, calls=%fused_computation.17 | convolution fusion | flops 202375168 | bytes 3769344 | tf_op jit(solution)/shard_map/sjt,sjd->std/dot_general | solution.py:209
  139.8 4.1 %collective-permute-done = bf16[8,128,1024]{2,1,0:T(8,128)(2,1)S(1)} collective-permute-done((bf16[8,128,1024]{2,1,0:T(8,128)(2,1)}, bf16[8,128,1024]{2,1,0:T(8,128)(2,1)S(1)}, u32[]{:S(2)}, u32[]{:S(2)}) %collective-permute-start) | collective-permute-done | bytes 2097184 | tf_op jit(solution)/shard_map/ppermute | solution.py:216
  143.8 3.8 %add_convert_fusion = bf16[8,128,1024]{2,1,0:T(8,128)(2,1)} fusion(bf16[8,128,1024]{2,1,0:T(8,128)(2,1)S(1)} %collective-permute-done, f32[8,128]{1,0:T(8,128)S(1)} %get-tuple-element.3, f32[8,128]{1,0:T(8,128)S(1)} %get-tuple-element.2, bf16[8,2,96,1024]{3,2,1,0:T(8,128)(2,1)} %bitcast.105, s32[]{:T(128)S(6)} %select_n.54, ...), kind=kOutput, calls=%fused_computation.6 | convolution fusion | flops 208666624 | bytes 5874688 | tf_op jit(solution)/shard_map/sjt,sjd->std/dot_general | solution.py:209
  147.6 3.8 %all-to-all-start = ((bf16[8,128,1024]{2,1,0:T(8,128)(2,1)}), bf16[8,128,1024]{2,1,0:T(8,128)(2,1)S(1)}, u32[]{:S(2)}, u32[]{:S(2)}) async-start(bf16[8,128,1024]{2,1,0:T(8,128)(2,1)} %add_convert_fusion), calls=%async_computation | async-start | bytes 4194304 | tf_op jit(solution)/shard_map/all_to_all | solution.py:228
  151.5 3.3 %fusion.20 = bf16[256,1,1024]{2,0,1:T(8,128)(2,1)S(1)} fusion(bf16[1536,1024]{1,0:T(8,128)(2,1)} %bitcast.102, bf16[1536,512]{1,0:T(8,128)(2,1)} %copy-done.10, s32[]{:T(128)S(6)} %select_n.59), kind=kOutput, calls=%fused_computation.31 | convolution fusion | flops 805568512 | bytes 4456452 | tf_op jit(solution)/shard_map/dot_general | solution.py:10
  155.0 1.0 fusion.18
  157.2 1.3 pad_maximum_fusion
  158.6 1.5 collective-permute-start.1
  160.1 3.3 %convolution_bitcast_fusion.2 = f32[256,1,1024]{2,0,1:T(8,128)S(1)} fusion(bf16[1536,1024]{1,0:T(8,128)(2,1)} %bitcast.95, bf16[1536,512]{1,0:T(8,128)(2,1)} %get-tuple-element.4, s32[]{:T(128)S(6)} %select_n.58), kind=kOutput, calls=%fused_computation.25 | convolution fusion | flops 805306368 | bytes 4980740 | tf_op jit(solution)/shard_map/dot_general | solution.py:10
  166.9 28.5 %collective-permute-done.1 = bf16[256,3,1024]{2,0,1:T(8,128)(2,1)} collective-permute-done((bf16[256,3,1024]{2,0,1:T(8,128)(2,1)}, bf16[256,3,1024]{2,0,1:T(8,128)(2,1)}, u32[]{:S(2)}, u32[]{:S(2)}) %collective-permute-start.1) | collective-permute-done | bytes 1572896 | tf_op jit(solution)/shard_map/ppermute | solution.py:140
  195.5 3.6 %fusion.6 = f32[1,256,3,1024]{3,1,2,0:T(8,128)} fusion(f32[256,1,1024]{2,0,1:T(8,128)S(1)} %convolution_bitcast_fusion, f32[256,1,1024]{2,0,1:T(8,128)S(1)} %convolution_bitcast_fusion.1, f32[256,1,1024]{2,0,1:T(8,128)S(1)} %convolution_bitcast_fusion.2, bf16[256,3,1024]{2,0,1:T(8,128)(2,1)} %collective-permute-done.1), kind=kLoop, calls=%fused_computation.9 | loop fusion | flops 3145728 | bytes 7864320 | tf_op jit(solution)/shard_map/reshape | solution.py:142
  199.1 1.1 all-to-all-done
  200.1 1.1 reduce_sum.41
  (59 shorter events, 13.6 us)
Async XLA Ops:
  7.2 122.1 %copy-start = (bf16[1,512,1024]{2,1,0:T(8,128)(2,1)S(1)}, bf16[1,512,1024]{2,1,0:T(8,128)(2,1)}, u32[]{:S(2)}) copy-start(bf16[1,512,1024]{2,1,0:T(8,128)(2,1)} %param.15) | copy-start | bytes 3145732
  7.2 62.2 %all-gather.3.cloned.1.call-start = ((), (), s32[]{:S(2)}) async-start(), calls=%async_computation.1 | async-start | bytes 4734976 | tf_op jit(solution)/shard_map/all_gather | solution.py:164
  14.6 106.1 %all-gather.5.cloned.1.call-start = ((), (), s32[]{:S(2)}) async-start(), calls=%async_computation.2 | async-start | bytes 4456448 | tf_op jit(solution)/shard_map/all_gather | solution.py:166
  120.7 3.5 %copy-start.9 = (bf16[1,512,1024]{2,1,0:T(8,128)(2,1)S(1)}, bf16[1,512,1024]{2,1,0:T(8,128)(2,1)}, u32[]{:S(2)}) copy-start(bf16[1,512,1024]{2,1,0:T(8,128)(2,1)} %param.17) | copy-start | bytes 3145732
  124.1 1.9 copy-start.4
  124.2 3.0 %copy-start.1 = (bf16[16,96,1024]{2,1,0:T(8,128)(2,1)S(1)}, bf16[16,96,1024]{2,1,0:T(8,128)(2,1)}, u32[]{:S(2)}) copy-start(bf16[16,96,1024]{2,1,0:T(8,128)(2,1)} %fusion.8) | copy-start | bytes 9437188
  124.2 3.3 %copy-start.8 = (bf16[1,512,1024]{2,1,0:T(8,128)(2,1)S(1)}, bf16[1,512,1024]{2,1,0:T(8,128)(2,1)}, u32[]{:S(2)}) copy-start(bf16[1,512,1024]{2,1,0:T(8,128)(2,1)} %param.16) | copy-start | bytes 3145732
  133.9 1.8 copy-start.10
  135.7 1.7 copy-start.6
  135.9 3.6 %copy-start.7 = (pred[8,2,96,128]{3,2,0,1:T(32,128)(4,1)}, pred[8,2,96,128]{3,2,0,1:T(32,128)(4,1)S(1)}, u32[]{:S(2)}) copy-start(pred[8,2,96,128]{3,2,0,1:T(32,128)(4,1)S(1)} %fusion.34) | copy-start | bytes 589828
  139.5 4.4 %collective-permute-start = (bf16[8,128,1024]{2,1,0:T(8,128)(2,1)}, bf16[8,128,1024]{2,1,0:T(8,128)(2,1)S(1)}, u32[]{:S(2)}, u32[]{:S(2)}) collective-permute-start(bf16[8,128,1024]{2,1,0:T(8,128)(2,1)} %convolution_convert_fusion.1), channel_id=1, source_target_pairs={{0,1},{1,0},{2,3},{3,2},{4,5},{5,4},{6,7},{7,6},{8,9},{9,8},{10,11... | collective-permute-start | bytes 6291464 | tf_op jit(solution)/shard_map/ppermute | solution.py:216
  147.6 52.5 %all-to-all-start = ((bf16[8,128,1024]{2,1,0:T(8,128)(2,1)}), bf16[8,128,1024]{2,1,0:T(8,128)(2,1)S(1)}, u32[]{:S(2)}, u32[]{:S(2)}) async-start(bf16[8,128,1024]{2,1,0:T(8,128)(2,1)} %add_convert_fusion), calls=%async_computation | async-start | bytes 4194304 | tf_op jit(solution)/shard_map/all_to_all | solution.py:228
  151.4 3.3 %copy-start.2 = (bf16[16,96,1024]{2,1,0:T(8,128)(2,1)S(1)}, bf16[16,96,1024]{2,1,0:T(8,128)(2,1)}, u32[]{:S(2)}) copy-start(bf16[16,96,1024]{2,1,0:T(8,128)(2,1)} %fusion.8) | copy-start | bytes 9437188
  151.5 3.5 %copy-start.14 = (bf16[1536,512]{1,0:T(8,128)(2,1)S(1)}, bf16[1536,512]{1,0:T(8,128)(2,1)}, u32[]{:S(2)}) copy-start(bf16[1536,512]{1,0:T(8,128)(2,1)} %get-tuple-element.4) | copy-start | bytes 4718596
  154.8 1.5 copy-start.12
  158.6 36.9 %collective-permute-start.1 = (bf16[256,3,1024]{2,0,1:T(8,128)(2,1)}, bf16[256,3,1024]{2,0,1:T(8,128)(2,1)}, u32[]{:S(2)}, u32[]{:S(2)}) collective-permute-start(bf16[256,3,1024]{2,0,1:T(8,128)(2,1)} %pad_maximum_fusion), channel_id=1, source_target_pairs={{0,16},{16,0},{1,17},{17,1},{2,18},{18,2},{3,19},{19,3},{4,20},{20... | collective-permute-start | bytes 4718600 | tf_op jit(solution)/shard_map/ppermute | solution.py:140
  160.1 3.3 %copy-start.3 = (bf16[16,96,1024]{2,1,0:T(8,128)(2,1)S(1)}, bf16[16,96,1024]{2,1,0:T(8,128)(2,1)}, u32[]{:S(2)}) copy-start(bf16[16,96,1024]{2,1,0:T(8,128)(2,1)} %fusion.8) | copy-start | bytes 9437188
  160.1 3.5 %copy-start.13 = (bf16[1536,512]{1,0:T(8,128)(2,1)S(1)}, bf16[1536,512]{1,0:T(8,128)(2,1)}, u32[]{:S(2)}) copy-start(bf16[1536,512]{1,0:T(8,128)(2,1)} %get-tuple-element.5) | copy-start | bytes 4718596
  163.6 1.9 copy-start.5
  163.6 2.4 %copy-start.11 = (bf16[1536,512]{1,0:T(8,128)(2,1)S(1)}, bf16[1536,512]{1,0:T(8,128)(2,1)}, u32[]{:S(2)}) copy-start(bf16[1536,512]{1,0:T(8,128)(2,1)} %copy-done.10) | copy-start | bytes 4718596
Sparse Core Ops, SparseCore 0:
  14.7 54.6 all-gather.2
  71.6 49.0 all-gather.4

commit v15 on v13

--- a/solution.py
+++ b/solution.py
@@ -109,14 +109,22 @@
     ahead = [(order[i], order[(i + 1) % n]) for i in range(n)]
     behind = [(order[i], order[(i - 1) % n]) for i in range(n)]
     up, down = block, block
-    for step in range(1, n // 2 + 1):
+    both = (n - 1) // 2
+    for step in range(1, both + 1):
         up = lax.ppermute(up, "ez", ahead)
         out = lax.dynamic_update_index_in_dim(out, up, ring[(at - step) % n], 0)
-        if step <= (n - 1) // 2:
-            down = lax.ppermute(down, "ez", behind)
-            out = lax.dynamic_update_index_in_dim(out, down, ring[(at + step) % n], 0)
-    mine = out.reshape((n * block.shape[0],) + block.shape[1:])
-    return [mine, lax.ppermute(mine, "core", [(0, 1), (1, 0)])]
+        down = lax.ppermute(down, "ez", behind)
+        out = lax.dynamic_update_index_in_dim(out, down, ring[(at + step) % n], 0)
+
+    def finish(after):
+        last, held, _ = lax.optimization_barrier((up, out, after))
+        for step in range(both + 1, n // 2 + 1):
+            last = lax.ppermute(last, "ez", ahead)
+            held = lax.dynamic_update_index_in_dim(held, last, ring[(at - step) % n], 0)
+        mine = held.reshape((n * block.shape[0],) + block.shape[1:])
+        return [mine, lax.ppermute(mine, "core", [(0, 1), (1, 0)])]
+
+    return finish
 
 
 def slots_by_rank(routes, experts):
@@ -163,12 +171,8 @@
 
     gathered = lax.all_gather(packed, ("ez", "core"), axis=0, tiled=True)
     gathered = gathered.reshape(experts, tok_rows + lines, width)
-    cot_halves = ring_gather(cotangent)
+    finish_cot = ring_gather(cotangent)
     on_core0 = core == 0
-    cot_by_core = [
-        jnp.where(on_core0, cot_halves[0], cot_halves[1]),
-        jnp.where(on_core0, cot_halves[1], cot_halves[0]),
-    ]
     meta_all = gathered[:, tok_rows:].reshape(experts, lines * width)
     meta_all = meta_all[:, :meta_rows.size].reshape(experts, len(meta), topk, tok_rows)
     routes_t = meta_all[:, 0].astype(jnp.int32)
@@ -193,6 +197,11 @@
         gathered[:, :tok_rows],
         preferred_element_type=jnp.float32,
     ).astype(jnp.bfloat16).reshape(experts * capacity, width)
+    cot_halves = finish_cot(rows_x)
+    cot_by_core = [
+        jnp.where(on_core0, cot_halves[0], cot_halves[1]),
+        jnp.where(on_core0, cot_halves[1], cot_halves[0]),
+    ]
     pick_by_core = pick.reshape(nchip, ncore, capacity, tok_rows)
     fac_by_core = fac.reshape(nchip, ncore, tok_rows)
     rows_q = []

time: 179 us -> 182 us (1.017)
  waiting for transfers between devices: 61.2 us -> 65.8 us
  starting transfers between devices: 21.9 us -> 17.8 us
  matrix products: 31.5 us -> 35.1 us
  other arithmetic: 18.5 us -> 16.5 us
    ppermute x3, starting transfers between devices: 7.29 us -> 0.29 us  [ring_gather(): down = lax.ppermute(down, 'ez', behind)]
    all_gather x1, waiting for transfers between devices: 0.01 us -> 4.98 us  [local_gather(): gathered = lax.all_gather(packed, ('ez', 'core'), axis=0, tiled=True)]
    ppermute x1 -> x2, starting transfers between devices: 0.07 us -> 4.51 us  [the longest x1 4.43 us: finish(): last = lax.ppermute(last, 'ez', ahead)]
    ppermute x4 -> x3, waiting for transfers between devices: 18.2 us -> 15.8 us  [ring_gather(): up = lax.ppermute(up, 'ez', ahead)]
    dot_general x3, matrix products: 8.32 us -> 10.4 us  [contract_cols(): lax.dot_general(left, right, (((1,), (1,)), ((), ())), preferred_element_...]
    select_n x1, other arithmetic: 3.87 us -> 1.87 us  [local_gather(): jnp.where(on_core0, cot_halves[0], cot_halves[1])]
    ppermute x4 -> x3, starting transfers between devices: 8.47 us -> 6.89 us  [ring_gather(): up = lax.ppermute(up, 'ez', ahead)]
    ppermute x1 -> x2, waiting for transfers between devices: 3.05 us -> 4.58 us  [the longest x1 4.58 us: finish(): last = lax.ppermute(last, 'ez', ahead)]
  transfers between devices with their start and end apart: 12 -> 12, of which waited for: 7 -> 8; matrix products, arithmetic and copies ran while one was open for 14% -> 15% of each run, Pallas kernels for 0% -> 0%
where the time goes in v15:
time: 182 us; the launch traced here: 181 us
  waiting for transfers between devices  65.8 us (36%)
  matrix products  35.1 us (19%)
  between operations  32.4 us (18%)
  starting transfers between devices  17.8 us (10%)
  other arithmetic  16.5 us (9%)
  local copies, waits for them, and re-layouts  13.5 us (7%)
    ppermute x1, waiting for transfers between devices, reduce_grads_dp(): lax.ppermute(grad_half(1 - d).astype(jnp.bfloat16), 'dp', [(0, 1), (1, 0)])  28.3 us
    ppermute x3, waiting for transfers between devices, ring_gather(): up = lax.ppermute(up, 'ez', ahead)  15.8 us
    dot_general x6, matrix products, contract_rows(): lax.dot_general(left, right, (((0,), (0,)), ((), ())), preferred_element_...  10.6 us
    dot_general x3, matrix products, contract_cols(): lax.dot_general(left, right, (((1,), (1,)), ((), ())), preferred_element_...  10.4 us
    ppermute x3, waiting for transfers between devices, ring_gather(): down = lax.ppermute(down, 'ez', behind)  7.49 us
    ppermute x3, starting transfers between devices, ring_gather(): up = lax.ppermute(up, 'ez', ahead)  6.89 us
    dot_general x2, matrix products, dense_for(): jnp.einsum('sjt,sjd->std', lax.dynamic_index_in_dim(pick_k, k, 1, keepdim...  5.89 us
    unnamed x33, local copies, waits for them, and re-layouts  5.02 us
  transfers between devices with their start and end apart: 12, of which 8 were waited for; matrix products, arithmetic and copies ran while one was open for 15% of the time, Pallas kernels for 0%

profile of v15, /device:TPU:0, one launch (start us, length us, event | category | flops | bytes accessed | tf_op | source)
XLA Modules:
  0.0 181.1 jit_solution(18116428993338190598)
XLA Ops:
  12.9 1.7 pad_maximum_fusion.2
  14.6 3.1 %collective-permute-start.1 = (bf16[128,1024]{1,0:T(8,128)(2,1)}, bf16[128,1024]{1,0:T(8,128)(2,1)}, u32[]{:S(2)}, u32[]{:S(2)}) collective-permute-start(bf16[128,1024]{1,0:T(8,128)(2,1)} %param.16), channel_id=1, source_target_pairs={{0,4},{4,8},{8,12},{12,14},{14,10},{10,6},{6,2},{2,0},{1,5},{5,9},... | collective-permute-start | bytes 786440 | tf_op jit(solution)/shard_map/ppermute | solution.py:114
  37.1 2.1 %collective-permute-start.2 = (bf16[128,1024]{1,0:T(8,128)(2,1)}, bf16[128,1024]{1,0:T(8,128)(2,1)S(1)}, u32[]{:S(2)}, u32[]{:S(2)}) collective-permute-start(bf16[128,1024]{1,0:T(8,128)(2,1)} %collective-permute-done.1), channel_id=1, source_target_pairs={{0,4},{4,8},{8,12},{12,14},{14,10},{10,6},{6,2},{2,0},{1,5},{5,9},... | collective-permute-start | bytes 786440 | tf_op jit(solution)/shard_map/ppermute | solution.py:114
  41.2 4.0 %collective-permute-done.2 = bf16[128,1024]{1,0:T(8,128)(2,1)S(1)} collective-permute-done((bf16[128,1024]{1,0:T(8,128)(2,1)}, bf16[128,1024]{1,0:T(8,128)(2,1)S(1)}, u32[]{:S(2)}, u32[]{:S(2)}) %collective-permute-start.2) | collective-permute-done | bytes 262176 | tf_op jit(solution)/shard_map/ppermute | solution.py:114
  45.1 1.7 collective-permute-start.3
  47.2 11.8 %collective-permute-done.3 = bf16[128,1024]{1,0:T(8,128)(2,1)} collective-permute-done((bf16[128,1024]{1,0:T(8,128)(2,1)S(1)}, bf16[128,1024]{1,0:T(8,128)(2,1)}, u32[]{:S(2)}, u32[]{:S(2)}) %collective-permute-start.3) | collective-permute-done | bytes 262176 | tf_op jit(solution)/shard_map/ppermute | solution.py:114
  60.0 7.5 %collective-permute-done.6 = bf16[128,1024]{1,0:T(8,128)(2,1)S(1)} collective-permute-done((bf16[128,1024]{1,0:T(8,128)(2,1)S(1)}, bf16[128,1024]{1,0:T(8,128)(2,1)S(1)}, u32[]{:S(2)}, u32[]{:S(2)}) %collective-permute-start.6) | collective-permute-done | bytes 262176 | tf_op jit(solution)/shard_map/ppermute | solution.py:116
  67.6 5.0 %all-gather.2.cloned.1.call-done = bf16[2176,1024]{1,0:T(8,128)(2,1)} async-done(((bf16[136,1024]{1,0:T(8,128)(2,1)}), bf16[2176,1024]{1,0:T(8,128)(2,1)}) %all-gather.2.cloned.1.call-update) | async-done | bytes 4456464 | tf_op jit(solution)/shard_map/all_gather | solution.py:172
  73.9 4.8 %fusion.6 = bf16[16,96,1024]{2,1,0:T(8,128)(2,1)} fusion(bf16[16,136,1024]{2,1,0:T(8,128)(2,1)} %bitcast.144, s32[16,128]{1,0:T(8,128)S(1)} %convolution_convert_fusion.5, pred[16,128]{1,0:T(8,128)(4,1)S(1)} %fusion.72), kind=kOutput, calls=%fused_computation.16 | convolution fusion | flops 404619264 | bytes 7350272 | tf_op jit(solution)/shard_map/sjt,std->sjd/dot_general | solution.py:194
  78.7 4.4 %collective-permute-start.7 = (bf16[128,1024]{1,0:T(8,128)(2,1)}, bf16[128,1024]{1,0:T(8,128)(2,1)}, u32[]{:S(2)}, u32[]{:S(2)}) collective-permute-start(bf16[128,1024]{1,0:T(8,128)(2,1)} %collective-permute-done.3), channel_id=1, source_target_pairs={{0,4},{4,8},{8,12},{12,14},{14,10},{10,6},{6,2},{2,0},{1,5},{5,9},... | collective-permute-start | bytes 786440 | tf_op jit(solution)/shard_map/ppermute | solution.py:122
  84.9 4.6 %collective-permute-done.7 = bf16[128,1024]{1,0:T(8,128)(2,1)} collective-permute-done((bf16[128,1024]{1,0:T(8,128)(2,1)}, bf16[128,1024]{1,0:T(8,128)(2,1)}, u32[]{:S(2)}, u32[]{:S(2)}) %collective-permute-start.7) | collective-permute-done | bytes 262176 | tf_op jit(solution)/shard_map/ppermute | solution.py:122
  90.8 4.0 %fusion.37 = f32[1536,512]{1,0:T(8,128)S(1)} fusion(bf16[1536,1024]{1,0:T(8,128)(2,1)} %bitcast.145, bf16[1,512,1024]{2,1,0:T(8,128)(2,1)} %param.18), kind=kOutput, calls=%fused_computation.46 | convolution fusion | flops 1610612736 | bytes 7340032 | tf_op jit(solution)/shard_map/dot_general | solution.py:16
  94.8 1.9 %broadcast_select_fusion.1 = (bf16[1024,1024]{1,0:T(8,128)(2,1)S(1)}, bf16[1024,1024]{1,0:T(8,128)(2,1)S(1)}) fusion(bf16[1024,1024]{1,0:T(8,128)(2,1)} %collective-permute-done.8, pred[]{:T(512)S(6)} %eq.47, bf16[8,128,1024]{2,1,0:T(8,128)(2,1)S(1)} %bitcast_dynamic-update-slice_fusion), kind=kLoop, calls=%fused_computation.22 | loop fusion | flops 2097152 | bytes 8388609 | tf_op jit(solution)/shard_map/jit(_where)/select_n | solution.py:202
  99.7 1.8 %fusion.34 = f32[1536,512]{1,0:T(8,128)S(1)} fusion(bf16[1536,1024]{1,0:T(8,128)(2,1)S(1)} %bitcast.151, bf16[1,512,1024]{2,1,0:T(8,128)(2,1)S(1)} %copy-done.9), kind=kOutput, calls=%fused_computation.43 | convolution fusion | flops 1610612736 | bytes 7340032 | tf_op jit(solution)/shard_map/dot_general | solution.py:16
  101.8 4.5 %multiply_convert_fusion.1 = (bf16[1536,512]{1,0:T(8,128)(2,1)}, bf16[1536,512]{1,0:T(8,128)(2,1)}, bf16[1536,512]{1,0:T(8,128)(2,1)S(1)}) fusion(f32[1536,512]{1,0:T(8,128)S(1)} %fusion.34, f32[1536,512]{1,0:T(8,128)S(1)} %fusion.37, bf16[1536,1024]{1,0:T(8,128)(2,1)S(1)} %bitcast.147, bf16[1,512,1024]{2,1,0:T(8,128)(2,1)S(1)} %copy-done), kind=kOutput, calls=%fused_computation.12 | convolution fusion | flops 1622409216 | bytes 15204352 | tf_op jit(solution)/shard_map/dot_general | solution.py:16
  106.3 1.8 %convolution_convert_fusion = bf16[1536,1024]{1,0:T(8,128)(2,1)S(1)} fusion(bf16[1536,512]{1,0:T(8,128)(2,1)S(1)} %get-tuple-element.10, bf16[1,512,1024]{2,1,0:T(8,128)(2,1)S(1)} %copy-done.9), kind=kOutput, calls=%fused_computation.7 | convolution fusion | flops 1612185600 | bytes 5767168 | tf_op jit(solution)/shard_map/dot_general | solution.py:227
  109.8 2.1 %convolution_convert_fusion.1 = bf16[8,128,1024]{2,1,0:T(8,128)(2,1)} fusion(bf16[8,2,96,1024]{3,2,1,0:T(8,128)(2,1)S(1)} %bitcast.154, s32[]{:T(128)S(6)} %select_n.146, pred[8,2,96,128]{3,2,0,1:T(32,128)(4,1)S(1)} %fusion.47), kind=kOutput, calls=%fused_computation.23 | convolution fusion | flops 202375168 | bytes 3769344 | tf_op jit(solution)/shard_map/sjt,sjd->std/dot_general | solution.py:234
  113.2 3.2 %collective-permute-done = bf16[8,128,1024]{2,1,0:T(8,128)(2,1)S(1)} collective-permute-done((bf16[8,128,1024]{2,1,0:T(8,128)(2,1)}, bf16[8,128,1024]{2,1,0:T(8,128)(2,1)S(1)}, u32[]{:S(2)}, u32[]{:S(2)}) %collective-permute-start) | collective-permute-done | bytes 2097184 | tf_op jit(solution)/shard_map/ppermute | solution.py:241
  116.4 3.8 %add_convert_fusion = bf16[8,128,1024]{2,1,0:T(8,128)(2,1)} fusion(bf16[8,128,1024]{2,1,0:T(8,128)(2,1)S(1)} %collective-permute-done, f32[8,128]{1,0:T(8,128)S(1)} %get-tuple-element.7, f32[8,128]{1,0:T(8,128)S(1)} %get-tuple-element.6, bf16[8,2,96,1024]{3,2,1,0:T(8,128)(2,1)} %bitcast.155, s32[]{:T(128)S(6)} %select_n.144, ...), kind=kOutput, calls=%fused_computation.6 | convolution fusion | flops 208666624 | bytes 5874688 | tf_op jit(solution)/shard_map/sjt,sjd->std/dot_general | solution.py:234
  120.2 4.1 %all-to-all-start = ((bf16[8,128,1024]{2,1,0:T(8,128)(2,1)}), bf16[8,128,1024]{2,1,0:T(8,128)(2,1)S(1)}, u32[]{:S(2)}, u32[]{:S(2)}) async-start(bf16[8,128,1024]{2,1,0:T(8,128)(2,1)} %add_convert_fusion), calls=%async_computation | async-start | bytes 4194304 | tf_op jit(solution)/shard_map/all_to_all | solution.py:253
  124.3 3.3 %fusion.33 = bf16[256,1,1024]{2,0,1:T(8,128)(2,1)S(1)} fusion(bf16[1536,1024]{1,0:T(8,128)(2,1)} %bitcast.152, bf16[1536,512]{1,0:T(8,128)(2,1)} %copy-done.10, s32[]{:T(128)S(6)} %select_n.174), kind=kOutput, calls=%fused_computation.41 | convolution fusion | flops 805568512 | bytes 4456452 | tf_op jit(solution)/shard_map/dot_general | solution.py:10
  133.0 3.3 %convolution_bitcast_fusion.2 = f32[256,1,1024]{2,0,1:T(8,128)S(1)} fusion(bf16[1536,1024]{1,0:T(8,128)(2,1)} %bitcast.146, bf16[1536,512]{1,0:T(8,128)(2,1)} %get-tuple-element.8, s32[]{:T(128)S(6)} %select_n.173), kind=kOutput, calls=%fused_computation.35 | convolution fusion | flops 805306368 | bytes 4980740 | tf_op jit(solution)/shard_map/dot_general | solution.py:10
  139.9 28.3 %collective-permute-done.9 = bf16[256,3,1024]{2,0,1:T(8,128)(2,1)} collective-permute-done((bf16[256,3,1024]{2,0,1:T(8,128)(2,1)}, bf16[256,3,1024]{2,0,1:T(8,128)(2,1)}, u32[]{:S(2)}, u32[]{:S(2)}) %collective-permute-start.9) | collective-permute-done | bytes 1572896 | tf_op jit(solution)/shard_map/ppermute | solution.py:148
  168.2 3.6 %fusion.4 = f32[1,256,3,1024]{3,1,2,0:T(8,128)} fusion(f32[256,1,1024]{2,0,1:T(8,128)S(1)} %convolution_bitcast_fusion, f32[256,1,1024]{2,0,1:T(8,128)S(1)} %convolution_bitcast_fusion.1, f32[256,1,1024]{2,0,1:T(8,128)S(1)} %convolution_bitcast_fusion.2, bf16[256,3,1024]{2,0,1:T(8,128)(2,1)} %collective-permute-done.9), kind=kLoop, calls=%fused_computation.10 | loop fusion | flops 3145728 | bytes 7864320 | tf_op jit(solution)/shard_map/reshape | solution.py:150
  (88 shorter events, 32.3 us)
Async XLA Ops:
  7.2 94.4 %copy-start = (bf16[1,512,1024]{2,1,0:T(8,128)(2,1)S(1)}, bf16[1,512,1024]{2,1,0:T(8,128)(2,1)}, u32[]{:S(2)}) copy-start(bf16[1,512,1024]{2,1,0:T(8,128)(2,1)} %param.17) | copy-start | bytes 3145732
  7.2 29.9 %copy-start.8 = (bf16[128,1024]{1,0:T(8,128)(2,1)S(1)}, bf16[128,1024]{1,0:T(8,128)(2,1)}, u32[]{:S(2)}) copy-start(bf16[128,1024]{1,0:T(8,128)(2,1)} %param.16) | copy-start | bytes 786436
  7.2 65.3 %all-gather.2.cloned.1.call-start = ((), (), s32[]{:S(2)}) async-start(), calls=%async_computation.1 | async-start | bytes 4734976 | tf_op jit(solution)/shard_map/all_gather | solution.py:172
  14.6 22.5 %collective-permute-start.1 = (bf16[128,1024]{1,0:T(8,128)(2,1)}, bf16[128,1024]{1,0:T(8,128)(2,1)}, u32[]{:S(2)}, u32[]{:S(2)}) collective-permute-start(bf16[128,1024]{1,0:T(8,128)(2,1)} %param.16), channel_id=1, source_target_pairs={{0,4},{4,8},{8,12},{12,14},{14,10},{10,6},{6,2},{2,0},{1,5},{5,9},... | collective-permute-start | bytes 786440 | tf_op jit(solution)/shard_map/ppermute | solution.py:114
  17.7 21.5 %collective-permute-start.4 = (bf16[128,1024]{1,0:T(8,128)(2,1)}, bf16[128,1024]{1,0:T(8,128)(2,1)}, u32[]{:S(2)}, u32[]{:S(2)}) collective-permute-start(bf16[128,1024]{1,0:T(8,128)(2,1)} %param.16), channel_id=1, source_target_pairs={{0,2},{4,0},{8,4},{12,8},{14,12},{10,14},{6,10},{2,6},{1,3},{5,1},... | collective-permute-start | bytes 786440 | tf_op jit(solution)/shard_map/ppermute | solution.py:116
  37.1 8.0 %collective-permute-start.2 = (bf16[128,1024]{1,0:T(8,128)(2,1)}, bf16[128,1024]{1,0:T(8,128)(2,1)S(1)}, u32[]{:S(2)}, u32[]{:S(2)}) collective-permute-start(bf16[128,1024]{1,0:T(8,128)(2,1)} %collective-permute-done.1), channel_id=1, source_target_pairs={{0,4},{4,8},{8,12},{12,14},{14,10},{10,6},{6,2},{2,0},{1,5},{5,9},... | collective-permute-start | bytes 786440 | tf_op jit(solution)/shard_map/ppermute | solution.py:114
  39.2 7.7 %collective-permute-start.5 = (bf16[128,1024]{1,0:T(8,128)(2,1)}, bf16[128,1024]{1,0:T(8,128)(2,1)S(1)}, u32[]{:S(2)}, u32[]{:S(2)}) collective-permute-start(bf16[128,1024]{1,0:T(8,128)(2,1)} %collective-permute-done.4), channel_id=1, source_target_pairs={{0,2},{4,0},{8,4},{12,8},{14,12},{10,14},{6,10},{2,6},{1,3},{5,1},... | collective-permute-start | bytes 786440 | tf_op jit(solution)/shard_map/ppermute | solution.py:116
  45.1 13.9 %collective-permute-start.3 = (bf16[128,1024]{1,0:T(8,128)(2,1)S(1)}, bf16[128,1024]{1,0:T(8,128)(2,1)}, u32[]{:S(2)}, u32[]{:S(2)}) collective-permute-start(bf16[128,1024]{1,0:T(8,128)(2,1)S(1)} %collective-permute-done.2), channel_id=1, source_target_pairs={{0,4},{4,8},{8,12},{12,14},{14,10},{10,6},{6,2},{2,0},{1,5},{5,9},... | collective-permute-start | bytes 786440 | tf_op jit(solution)/shard_map/ppermute | solution.py:114
  46.9 20.6 %collective-permute-start.6 = (bf16[128,1024]{1,0:T(8,128)(2,1)S(1)}, bf16[128,1024]{1,0:T(8,128)(2,1)S(1)}, u32[]{:S(2)}, u32[]{:S(2)}) collective-permute-start(bf16[128,1024]{1,0:T(8,128)(2,1)S(1)} %collective-permute-done.5), channel_id=1, source_target_pairs={{0,2},{4,0},{8,4},{12,8},{14,12},{10,14},{6,10},{2,6},{1,3},{5,1},... | collective-permute-start | bytes 786440 | tf_op jit(solution)/shard_map/ppermute | solution.py:116
  73.7 16.9 %copy-start.7 = (bf16[2,8,56,128]{3,2,1,0:T(8,128)(2,1)}, bf16[2,8,56,128]{3,2,1,0:T(8,128)(2,1)S(1)}, u32[]{:S(2)}) copy-start(bf16[2,8,56,128]{3,2,1,0:T(8,128)(2,1)S(1)} %copy.18) | copy-start | bytes 688132
  78.7 10.7 %collective-permute-start.7 = (bf16[128,1024]{1,0:T(8,128)(2,1)}, bf16[128,1024]{1,0:T(8,128)(2,1)}, u32[]{:S(2)}, u32[]{:S(2)}) collective-permute-start(bf16[128,1024]{1,0:T(8,128)(2,1)} %collective-permute-done.3), channel_id=1, source_target_pairs={{0,4},{4,8},{8,12},{12,14},{14,10},{10,6},{6,2},{2,0},{1,5},{5,9},... | collective-permute-start | bytes 786440 | tf_op jit(solution)/shard_map/ppermute | solution.py:122
  90.4 4.4 %collective-permute-start.8 = (bf16[1024,1024]{1,0:T(8,128)(2,1)S(1)}, bf16[1024,1024]{1,0:T(8,128)(2,1)}, u32[]{:S(2)}, u32[]{:S(2)}) collective-permute-start(bf16[1024,1024]{1,0:T(8,128)(2,1)S(1)} %bitcast.142), channel_id=1, source_target_pairs={{0,1},{1,0},{2,3},{3,2},{4,5},{5,4},{6,7},{7,6},{8,9},{9,8},{10,11... | collective-permute-start | bytes 6291464 | tf_op jit(solution)/shard_map/ppermute | solution.py:125
  98.8 2.7 %copy-start.4 = (bf16[8,2,96,1024]{3,2,1,0:T(8,128)(2,1)}, bf16[8,2,96,1024]{3,2,1,0:T(8,128)(2,1)S(1)}, u32[]{:S(2)}) copy-start(bf16[8,2,96,1024]{3,2,1,0:T(8,128)(2,1)S(1)} %copy.16) | copy-start | bytes 9437188
  99.7 2.1 %copy-start.1 = (bf16[16,96,1024]{2,1,0:T(8,128)(2,1)S(1)}, bf16[16,96,1024]{2,1,0:T(8,128)(2,1)}, u32[]{:S(2)}) copy-start(bf16[16,96,1024]{2,1,0:T(8,128)(2,1)} %fusion.6) | copy-start | bytes 9437188
  106.3 1.8 %copy-start.10 = (bf16[1536,512]{1,0:T(8,128)(2,1)}, bf16[1536,512]{1,0:T(8,128)(2,1)S(1)}, u32[]{:S(2)}) copy-start(bf16[1536,512]{1,0:T(8,128)(2,1)S(1)} %get-tuple-element.10) | copy-start | bytes 4718596
  112.0 4.5 %collective-permute-start = (bf16[8,128,1024]{2,1,0:T(8,128)(2,1)}, bf16[8,128,1024]{2,1,0:T(8,128)(2,1)S(1)}, u32[]{:S(2)}, u32[]{:S(2)}) collective-permute-start(bf16[8,128,1024]{2,1,0:T(8,128)(2,1)} %convolution_convert_fusion.1), channel_id=1, source_target_pairs={{0,1},{1,0},{2,3},{3,2},{4,5},{5,4},{6,7},{7,6},{8,9},{9,8},{10,11... | collective-permute-start | bytes 6291464 | tf_op jit(solution)/shard_map/ppermute | solution.py:241
  120.2 53.0 %all-to-all-start = ((bf16[8,128,1024]{2,1,0:T(8,128)(2,1)}), bf16[8,128,1024]{2,1,0:T(8,128)(2,1)S(1)}, u32[]{:S(2)}, u32[]{:S(2)}) async-start(bf16[8,128,1024]{2,1,0:T(8,128)(2,1)} %add_convert_fusion), calls=%async_computation | async-start | bytes 4194304 | tf_op jit(solution)/shard_map/all_to_all | solution.py:253
  124.3 3.3 %copy-start.2 = (bf16[16,96,1024]{2,1,0:T(8,128)(2,1)S(1)}, bf16[16,96,1024]{2,1,0:T(8,128)(2,1)}, u32[]{:S(2)}) copy-start(bf16[16,96,1024]{2,1,0:T(8,128)(2,1)} %fusion.6) | copy-start | bytes 9437188
  124.3 3.5 %copy-start.14 = (bf16[1536,512]{1,0:T(8,128)(2,1)S(1)}, bf16[1536,512]{1,0:T(8,128)(2,1)}, u32[]{:S(2)}) copy-start(bf16[1536,512]{1,0:T(8,128)(2,1)} %get-tuple-element.8) | copy-start | bytes 4718596
  131.4 36.7 %collective-permute-start.9 = (bf16[256,3,1024]{2,0,1:T(8,128)(2,1)}, bf16[256,3,1024]{2,0,1:T(8,128)(2,1)}, u32[]{:S(2)}, u32[]{:S(2)}) collective-permute-start(bf16[256,3,1024]{2,0,1:T(8,128)(2,1)} %pad_maximum_fusion.1), channel_id=1, source_target_pairs={{0,16},{16,0},{1,17},{17,1},{2,18},{18,2},{3,19},{19,3},{4,20},{20... | collective-permute-start | bytes 4718600 | tf_op jit(solution)/shard_map/ppermute | solution.py:148
  133.0 3.3 %copy-start.3 = (bf16[16,96,1024]{2,1,0:T(8,128)(2,1)S(1)}, bf16[16,96,1024]{2,1,0:T(8,128)(2,1)}, u32[]{:S(2)}) copy-start(bf16[16,96,1024]{2,1,0:T(8,128)(2,1)} %fusion.6) | copy-start | bytes 9437188
  133.0 3.5 %copy-start.13 = (bf16[1536,512]{1,0:T(8,128)(2,1)S(1)}, bf16[1536,512]{1,0:T(8,128)(2,1)}, u32[]{:S(2)}) copy-start(bf16[1536,512]{1,0:T(8,128)(2,1)} %get-tuple-element.9) | copy-start | bytes 4718596
  136.5 1.9 %copy-start.5 = (bf16[8,2,96,1024]{3,2,1,0:T(8,128)(2,1)S(1)}, bf16[8,2,96,1024]{3,2,1,0:T(8,128)(2,1)}, u32[]{:S(2)}) copy-start(bf16[8,2,96,1024]{3,2,1,0:T(8,128)(2,1)} %copy-done.4) | copy-start | bytes 9437188
  136.5 2.4 %copy-start.11 = (bf16[1536,512]{1,0:T(8,128)(2,1)S(1)}, bf16[1536,512]{1,0:T(8,128)(2,1)}, u32[]{:S(2)}) copy-start(bf16[1536,512]{1,0:T(8,128)(2,1)} %copy-done.10) | copy-start | bytes 4718596
  (3 other events, 4.4 us)
Sparse Core Ops, SparseCore 0:
  14.7 57.7 all-gather.1

commit v16 on v14

--- a/solution.py
+++ b/solution.py
@@ -163,7 +163,7 @@
 
     gathered = lax.all_gather(packed, ("ez", "core"), axis=0, tiled=True)
     gathered = gathered.reshape(experts, tok_rows + lines, width)
-    all_cot = lax.all_gather(cotangent, ("ez", "core"), axis=0, tiled=True)
+    cot_halves = ring_gather(cotangent)
     on_core0 = core == 0
     meta_all = gathered[:, tok_rows:].reshape(experts, lines * width)
     meta_all = meta_all[:, :meta_rows.size].reshape(experts, len(meta), topk, tok_rows)
@@ -189,10 +189,23 @@
         gathered[:, :tok_rows],
         preferred_element_type=jnp.float32,
     ).astype(jnp.bfloat16).reshape(experts * capacity, width)
-    scaled = fac[:, :, None] * all_cot.reshape(experts, tok_rows, width).astype(jnp.float32)
-    rows_q = jnp.einsum(
-        "sjt,std->sjd", pick, scaled.astype(jnp.bfloat16), preferred_element_type=jnp.float32
-    ).astype(jnp.bfloat16).reshape(experts * capacity, width)
+    pick_by_core = pick.reshape(nchip, ncore, capacity, tok_rows)
+    fac_by_core = fac.reshape(nchip, ncore, tok_rows)
+    core_ids = lax.broadcasted_iota(jnp.int32, (1, ncore, 1, 1), 1)
+    rows_q = 0.0
+    for h, half in enumerate(cot_halves):
+        k = h ^ core
+        scaled = lax.dynamic_index_in_dim(fac_by_core, k, 1, keepdims=False)[:, :, None] * half.reshape(
+            nchip, tok_rows, width
+        ).astype(jnp.float32)
+        masked_pick = jnp.where(core_ids == k, pick_by_core, jnp.zeros((), pick_by_core.dtype))
+        rows_q = rows_q + jnp.einsum(
+            "ikjt,itd->ikjd",
+            masked_pick,
+            scaled.astype(jnp.bfloat16),
+            preferred_element_type=jnp.float32,
+        )
+    rows_q = rows_q.astype(jnp.bfloat16).reshape(experts * capacity, width)
     wgate, wup, wdown = w_gate[0], w_up[0], w_down[0]
     gate_pre = contract_cols(rows_x, wgate)
     up_pre = contract_cols(rows_x, wup)

time: 209 us -> 175 us (0.84)
  waiting for transfers between devices: 133 us -> 56.5 us
  starting transfers between devices: 5.59 us -> 27 us
  between operations: 14.3 us -> 32.2 us
  local copies, waits for them, and re-layouts: 6.19 us -> 9.35 us
    all_gather x1, waiting for transfers between devices: 54.1 us -> 0.02 us  [local_gather(): gathered = lax.all_gather(packed, ('ez', 'core'), axis=0, tiled=True)]
    all_gather x1 -> x0, waiting for transfers between devices: 45 us -> none  [local_gather(): all_cot = lax.all_gather(cotangent, ('ez', 'core'), axis=0, tiled=True)]
    ppermute x0 -> x8, waiting for transfers between devices: none -> 22 us  [the longest x4 18.3 us: ring_gather(): up = lax.ppermute(up, 'ez', ahead)]
    ppermute x0 -> x8, starting transfers between devices: none -> 15.5 us  [the longest x4 15.4 us: ring_gather(): up = lax.ppermute(up, 'ez', ahead)]
    all_to_all x1, starting transfers between devices: 3.78 us -> 9.53 us  [local_gather(): returned = lax.all_to_all(combined, 'ez', 0, 0, tiled=True)]
    dynamic_slice x0 -> x3, local copies, waits for them, and re-layouts: none -> 2.85 us  [the longest x1 1.6 us: ring_gather(): out = lax.dynamic_update_index_in_dim(out, up, ring[(at - step) % n], 0)]
    dynamic_update_slice x0 -> x8, local copies, waits for them, and re-layouts: none -> 2.1 us  [the longest x4 1.05 us: ring_gather(): out = lax.dynamic_update_index_in_dim(out, up, ring[(at - step) % n], 0)]
    dot_general x1 -> x2, matrix products: 3.45 us -> 4.91 us  [local_gather(): jnp.einsum('ikjt,itd->ikjd', masked_pick, scaled.astype(jnp.bfloat16), pr...]
  transfers between devices with their start and end apart: 5 -> 12, of which waited for: 5 -> 8; matrix products, arithmetic and copies ran while one was open for 10% -> 15% of each run, Pallas kernels for 0% -> 0%
where the time goes in v16:
time: 175 us; the launch traced here: 174 us
  waiting for transfers between devices  56.5 us (32%)
  matrix products  35 us (20%)
  between operations  32.2 us (18%)
  starting transfers between devices  27 us (15%)
  other arithmetic  13.6 us (8%)
  local copies, waits for them, and re-layouts  9.35 us (5%)
    ppermute x1, waiting for transfers between devices, reduce_grads_dp(): lax.ppermute(grad_half(1 - d).astype(jnp.bfloat16), 'dp', [(0, 1), (1, 0)])  29.2 us
    ppermute x4, waiting for transfers between devices, ring_gather(): up = lax.ppermute(up, 'ez', ahead)  18.3 us
    ppermute x4, starting transfers between devices, ring_gather(): up = lax.ppermute(up, 'ez', ahead)  15.4 us
    dot_general x6, matrix products, contract_rows(): lax.dot_general(left, right, (((0,), (0,)), ((), ())), preferred_element_...  10.6 us
    all_to_all x1, starting transfers between devices, local_gather(): returned = lax.all_to_all(combined, 'ez', 0, 0, tiled=True)  9.53 us
    dot_general x3, matrix products, contract_cols(): lax.dot_general(left, right, (((1,), (1,)), ((), ())), preferred_element_...  8.28 us
    dot_general x2, matrix products, dense_for(): jnp.einsum('sjt,sjd->std', lax.dynamic_index_in_dim(pick_k, k, 1, keepdim...  5.92 us
    dot_general x2, matrix products, local_gather(): jnp.einsum('ikjt,itd->ikjd', masked_pick, scaled.astype(jnp.bfloat16), pr...  4.91 us
  transfers between devices with their start and end apart: 12, of which 8 were waited for; matrix products, arithmetic and copies ran while one was open for 15% of the time, Pallas kernels for 0%

profile of v16, /device:TPU:0, one launch (start us, length us, event | category | flops | bytes accessed | tf_op | source)
XLA Modules:
  0.0 173.6 jit_solution(9999193234729484769)
XLA Ops:
  12.9 1.7 pad_maximum_fusion.1
  14.6 3.1 %collective-permute-start.1 = (bf16[128,1024]{1,0:T(8,128)(2,1)}, bf16[128,1024]{1,0:T(8,128)(2,1)}, u32[]{:S(2)}, u32[]{:S(2)}) collective-permute-start(bf16[128,1024]{1,0:T(8,128)(2,1)} %param.16), channel_id=1, source_target_pairs={{0,4},{4,8},{8,12},{12,14},{14,10},{10,6},{6,2},{2,0},{1,5},{5,9},... | collective-permute-start | bytes 786440 | tf_op jit(solution)/shard_map/ppermute | solution.py:113
  38.6 2.1 %collective-permute-start.3 = (bf16[128,1024]{1,0:T(8,128)(2,1)}, bf16[128,1024]{1,0:T(8,128)(2,1)S(1)}, u32[]{:S(2)}, u32[]{:S(2)}) collective-permute-start(bf16[128,1024]{1,0:T(8,128)(2,1)} %collective-permute-done.1), channel_id=1, source_target_pairs={{0,4},{4,8},{8,12},{12,14},{14,10},{10,6},{6,2},{2,0},{1,5},{5,9},... | collective-permute-start | bytes 786440 | tf_op jit(solution)/shard_map/ppermute | solution.py:113
  42.7 6.8 %collective-permute-done.3 = bf16[128,1024]{1,0:T(8,128)(2,1)S(1)} collective-permute-done((bf16[128,1024]{1,0:T(8,128)(2,1)}, bf16[128,1024]{1,0:T(8,128)(2,1)S(1)}, u32[]{:S(2)}, u32[]{:S(2)}) %collective-permute-start.3) | collective-permute-done | bytes 262176 | tf_op jit(solution)/shard_map/ppermute | solution.py:113
  49.5 4.1 %collective-permute-start.5 = (bf16[128,1024]{1,0:T(8,128)(2,1)S(1)}, bf16[128,1024]{1,0:T(8,128)(2,1)S(1)}, u32[]{:S(2)}, u32[]{:S(2)}) collective-permute-start(bf16[128,1024]{1,0:T(8,128)(2,1)S(1)} %collective-permute-done.3), channel_id=1, source_target_pairs={{0,4},{4,8},{8,12},{12,14},{14,10},{10,6},{6,2},{2,0},{1,5},{5,9},... | collective-permute-start | bytes 786440 | tf_op jit(solution)/shard_map/ppermute | solution.py:113
  54.8 8.1 %collective-permute-done.5 = bf16[128,1024]{1,0:T(8,128)(2,1)S(1)} collective-permute-done((bf16[128,1024]{1,0:T(8,128)(2,1)S(1)}, bf16[128,1024]{1,0:T(8,128)(2,1)S(1)}, u32[]{:S(2)}, u32[]{:S(2)}) %collective-permute-start.5) | collective-permute-done | bytes 262176 | tf_op jit(solution)/shard_map/ppermute | solution.py:113
  62.9 6.1 %collective-permute-start.7 = (bf16[128,1024]{1,0:T(8,128)(2,1)S(1)}, bf16[128,1024]{1,0:T(8,128)(2,1)S(1)}, u32[]{:S(2)}, u32[]{:S(2)}) collective-permute-start(bf16[128,1024]{1,0:T(8,128)(2,1)S(1)} %collective-permute-done.5), channel_id=1, source_target_pairs={{0,4},{4,8},{8,12},{12,14},{14,10},{10,6},{6,2},{2,0},{1,5},{5,9},... | collective-permute-start | bytes 786440 | tf_op jit(solution)/shard_map/ppermute | solution.py:113
  69.0 2.6 %collective-permute-done.6 = bf16[128,1024]{1,0:T(8,128)(2,1)S(1)} collective-permute-done((bf16[128,1024]{1,0:T(8,128)(2,1)S(1)}, bf16[128,1024]{1,0:T(8,128)(2,1)S(1)}, u32[]{:S(2)}, u32[]{:S(2)}) %collective-permute-start.6) | collective-permute-done | bytes 262176 | tf_op jit(solution)/shard_map/ppermute | solution.py:116
  71.7 3.4 %collective-permute-done.7 = bf16[128,1024]{1,0:T(8,128)(2,1)S(1)} collective-permute-done((bf16[128,1024]{1,0:T(8,128)(2,1)S(1)}, bf16[128,1024]{1,0:T(8,128)(2,1)S(1)}, u32[]{:S(2)}, u32[]{:S(2)}) %collective-permute-start.7) | collective-permute-done | bytes 262176 | tf_op jit(solution)/shard_map/ppermute | solution.py:113
  76.9 3.2 %fusion.5 = bf16[16,96,1024]{2,1,0:T(8,128)(2,1)S(1)} fusion(bf16[16,136,1024]{2,1,0:T(8,128)(2,1)} %bitcast.138, s32[16,128]{1,0:T(8,128)S(1)} %convolution_convert_fusion.5, pred[16,128]{1,0:T(8,128)(4,1)S(1)} %fusion.64), kind=kOutput, calls=%fused_computation.15 | convolution fusion | flops 404619264 | bytes 7350272 | tf_op jit(solution)/shard_map/sjt,std->sjd/dot_general | solution.py:186
  80.1 3.8 %fusion.11 = f32[8,2,96,1024]{3,2,1,0:T(8,128)S(1)} fusion(bf16[8,128,1024]{2,1,0:T(8,128)(2,1)} %bitcast.61, f32[8,128]{1,0:T(8,128)S(1)} %bitcast.163, pred[2]{0:T(512)(128)(4,1)S(1)} %iota_compare_fusion.4, s32[8,2,128]{2,1,0:T(2,128)S(1)} %bitcast.158, pred[8,2,128]{2,1,0:T(4,128)(4,1)S(1)} %and.48), kind=kOutput, calls=%fused_computation.18 | convolution fusion | flops 406585344 | bytes 8402946 | tf_op jit(solution)/shard_map/ikjt,itd->ikjd/dot_general | solution.py:202
  85.1 1.9 %fusion.22 = f32[1536,512]{1,0:T(8,128)S(1)} fusion(bf16[1536,1024]{1,0:T(8,128)(2,1)S(1)} %bitcast.147, bf16[1,512,1024]{2,1,0:T(8,128)(2,1)S(1)} %copy-done.9), kind=kOutput, calls=%fused_computation.37 | convolution fusion | flops 1610612736 | bytes 7340032 | tf_op jit(solution)/shard_map/dot_general | solution.py:16
  87.2 1.8 %fusion.25 = f32[1536,512]{1,0:T(8,128)S(1)} fusion(bf16[1536,1024]{1,0:T(8,128)(2,1)S(1)} %bitcast.139, bf16[1,512,1024]{2,1,0:T(8,128)(2,1)S(1)} %copy-done.8), kind=kOutput, calls=%fused_computation.40 | convolution fusion | flops 1610612736 | bytes 7340032 | tf_op jit(solution)/shard_map/dot_general | solution.py:16
  89.0 4.6 %multiply_convert_fusion.2 = (bf16[1536,512]{1,0:T(8,128)(2,1)}, bf16[1536,512]{1,0:T(8,128)(2,1)}, bf16[1536,512]{1,0:T(8,128)(2,1)S(1)}) fusion(f32[1536,512]{1,0:T(8,128)S(1)} %fusion.22, f32[1536,512]{1,0:T(8,128)S(1)} %fusion.25, bf16[1536,1024]{1,0:T(8,128)(2,1)S(1)} %bitcast.140, bf16[1,512,1024]{2,1,0:T(8,128)(2,1)S(1)} %copy-done), kind=kOutput, calls=%fused_computation.11 | convolution fusion | flops 1622409216 | bytes 15204352 | tf_op jit(solution)/shard_map/dot_general | solution.py:16
  93.6 1.8 %convolution_convert_fusion = bf16[1536,1024]{1,0:T(8,128)(2,1)S(1)} fusion(bf16[1536,512]{1,0:T(8,128)(2,1)S(1)} %get-tuple-element.6, bf16[1,512,1024]{2,1,0:T(8,128)(2,1)S(1)} %copy-done.9), kind=kOutput, calls=%fused_computation.7 | convolution fusion | flops 1612185600 | bytes 5767168 | tf_op jit(solution)/shard_map/dot_general | solution.py:215
  95.5 1.6 copy-done.4
  97.1 2.1 %convolution_convert_fusion.1 = bf16[8,128,1024]{2,1,0:T(8,128)(2,1)} fusion(bf16[8,2,96,1024]{3,2,1,0:T(8,128)(2,1)S(1)} %bitcast.145, s32[]{:T(128)S(6)} %select_n.146, pred[8,2,96,128]{3,2,1,0:T(32,128)(4,1)S(1)} %fusion.35), kind=kOutput, calls=%fused_computation.21 | convolution fusion | flops 202375168 | bytes 3769344 | tf_op jit(solution)/shard_map/sjt,sjd->std/dot_general | solution.py:222
  99.7 3.9 %collective-permute-done = bf16[8,128,1024]{2,1,0:T(8,128)(2,1)S(1)} collective-permute-done((bf16[8,128,1024]{2,1,0:T(8,128)(2,1)}, bf16[8,128,1024]{2,1,0:T(8,128)(2,1)S(1)}, u32[]{:S(2)}, u32[]{:S(2)}) %collective-permute-start) | collective-permute-done | bytes 2097184 | tf_op jit(solution)/shard_map/ppermute | solution.py:229
  103.7 3.8 %add_convert_fusion.1 = bf16[8,128,1024]{2,1,0:T(8,128)(2,1)} fusion(bf16[8,128,1024]{2,1,0:T(8,128)(2,1)S(1)} %collective-permute-done, f32[8,128]{1,0:T(8,128)S(1)} %get-tuple-element.3, f32[8,128]{1,0:T(8,128)S(1)} %get-tuple-element.2, bf16[8,2,96,1024]{3,2,1,0:T(8,128)(2,1)} %bitcast.146, s32[]{:T(128)S(6)} %select_n.144, ...), kind=kOutput, calls=%fused_computation.6 | convolution fusion | flops 208666624 | bytes 5874688 | tf_op jit(solution)/shard_map/sjt,sjd->std/dot_general | solution.py:222
  107.5 9.5 %all-to-all-start = ((bf16[8,128,1024]{2,1,0:T(8,128)(2,1)}), bf16[8,128,1024]{2,1,0:T(8,128)(2,1)S(1)}, u32[]{:S(2)}, u32[]{:S(2)}) async-start(bf16[8,128,1024]{2,1,0:T(8,128)(2,1)} %add_convert_fusion.1), calls=%async_computation | async-start | bytes 4194304 | tf_op jit(solution)/shard_map/all_to_all | solution.py:241
  117.0 3.3 %fusion.21 = bf16[256,1,1024]{2,0,1:T(8,128)(2,1)S(1)} fusion(bf16[1536,1024]{1,0:T(8,128)(2,1)} %bitcast.148, bf16[1536,512]{1,0:T(8,128)(2,1)} %copy-done.14, s32[]{:T(128)S(6)} %select_n.174), kind=kOutput, calls=%fused_computation.35 | convolution fusion | flops 805568512 | bytes 4456452 | tf_op jit(solution)/shard_map/dot_general | solution.py:10
  125.6 3.3 %convolution_bitcast_fusion = f32[256,1,1024]{2,0,1:T(8,128)S(1)} fusion(bf16[1536,1024]{1,0:T(8,128)(2,1)} %bitcast.149, bf16[1536,512]{1,0:T(8,128)(2,1)} %copy-done.14, s32[]{:T(128)S(6)} %select_n.173), kind=kOutput, calls=%fused_computation.27 | convolution fusion | flops 805306368 | bytes 4980740 | tf_op jit(solution)/shard_map/dot_general | solution.py:10
  131.6 29.2 %collective-permute-done.9 = bf16[256,3,1024]{2,0,1:T(8,128)(2,1)} collective-permute-done((bf16[256,3,1024]{2,0,1:T(8,128)(2,1)}, bf16[256,3,1024]{2,0,1:T(8,128)(2,1)}, u32[]{:S(2)}, u32[]{:S(2)}) %collective-permute-start.9) | collective-permute-done | bytes 1572896 | tf_op jit(solution)/shard_map/ppermute | solution.py:140
  160.7 3.6 %fusion.3 = f32[1,256,3,1024]{3,1,2,0:T(8,128)} fusion(f32[256,1,1024]{2,0,1:T(8,128)S(1)} %convolution_bitcast_fusion, f32[256,1,1024]{2,0,1:T(8,128)S(1)} %convolution_bitcast_fusion.1, f32[256,1,1024]{2,0,1:T(8,128)S(1)} %convolution_bitcast_fusion.2, bf16[256,3,1024]{2,0,1:T(8,128)(2,1)} %collective-permute-done.9), kind=kLoop, calls=%fused_computation.9 | loop fusion | flops 3145728 | bytes 7864320 | tf_op jit(solution)/shard_map/reshape | solution.py:142
  (85 shorter events, 25.9 us)
Async XLA Ops:
  7.2 81.8 %copy-start = (bf16[1,512,1024]{2,1,0:T(8,128)(2,1)S(1)}, bf16[1,512,1024]{2,1,0:T(8,128)(2,1)}, u32[]{:S(2)}) copy-start(bf16[1,512,1024]{2,1,0:T(8,128)(2,1)} %param.17) | copy-start | bytes 3145732
  7.2 31.4 %copy-start.7 = (bf16[128,1024]{1,0:T(8,128)(2,1)S(1)}, bf16[128,1024]{1,0:T(8,128)(2,1)}, u32[]{:S(2)}) copy-start(bf16[128,1024]{1,0:T(8,128)(2,1)} %param.16) | copy-start | bytes 786436
  7.2 68.0 %all-gather.2.cloned.1.call-start = ((), (), s32[]{:S(2)}) async-start(), calls=%async_computation.1 | async-start | bytes 4734976 | tf_op jit(solution)/shard_map/all_gather | solution.py:164
  14.6 24.0 %collective-permute-start.1 = (bf16[128,1024]{1,0:T(8,128)(2,1)}, bf16[128,1024]{1,0:T(8,128)(2,1)}, u32[]{:S(2)}, u32[]{:S(2)}) collective-permute-start(bf16[128,1024]{1,0:T(8,128)(2,1)} %param.16), channel_id=1, source_target_pairs={{0,4},{4,8},{8,12},{12,14},{14,10},{10,6},{6,2},{2,0},{1,5},{5,9},... | collective-permute-start | bytes 786440 | tf_op jit(solution)/shard_map/ppermute | solution.py:113
  17.7 23.0 %collective-permute-start.2 = (bf16[128,1024]{1,0:T(8,128)(2,1)}, bf16[128,1024]{1,0:T(8,128)(2,1)}, u32[]{:S(2)}, u32[]{:S(2)}) collective-permute-start(bf16[128,1024]{1,0:T(8,128)(2,1)} %param.16), channel_id=1, source_target_pairs={{0,2},{4,0},{8,4},{12,8},{14,12},{10,14},{6,10},{2,6},{1,3},{5,1},... | collective-permute-start | bytes 786440 | tf_op jit(solution)/shard_map/ppermute | solution.py:116
  38.6 10.9 %collective-permute-start.3 = (bf16[128,1024]{1,0:T(8,128)(2,1)}, bf16[128,1024]{1,0:T(8,128)(2,1)S(1)}, u32[]{:S(2)}, u32[]{:S(2)}) collective-permute-start(bf16[128,1024]{1,0:T(8,128)(2,1)} %collective-permute-done.1), channel_id=1, source_target_pairs={{0,4},{4,8},{8,12},{12,14},{14,10},{10,6},{6,2},{2,0},{1,5},{5,9},... | collective-permute-start | bytes 786440 | tf_op jit(solution)/shard_map/ppermute | solution.py:113
  40.7 14.0 %collective-permute-start.4 = (bf16[128,1024]{1,0:T(8,128)(2,1)}, bf16[128,1024]{1,0:T(8,128)(2,1)S(1)}, u32[]{:S(2)}, u32[]{:S(2)}) collective-permute-start(bf16[128,1024]{1,0:T(8,128)(2,1)} %collective-permute-done.2), channel_id=1, source_target_pairs={{0,2},{4,0},{8,4},{12,8},{14,12},{10,14},{6,10},{2,6},{1,3},{5,1},... | collective-permute-start | bytes 786440 | tf_op jit(solution)/shard_map/ppermute | solution.py:116
  49.5 13.4 %collective-permute-start.5 = (bf16[128,1024]{1,0:T(8,128)(2,1)S(1)}, bf16[128,1024]{1,0:T(8,128)(2,1)S(1)}, u32[]{:S(2)}, u32[]{:S(2)}) collective-permute-start(bf16[128,1024]{1,0:T(8,128)(2,1)S(1)} %collective-permute-done.3), channel_id=1, source_target_pairs={{0,4},{4,8},{8,12},{12,14},{14,10},{10,6},{6,2},{2,0},{1,5},{5,9},... | collective-permute-start | bytes 786440 | tf_op jit(solution)/shard_map/ppermute | solution.py:113
  54.7 16.9 %collective-permute-start.6 = (bf16[128,1024]{1,0:T(8,128)(2,1)S(1)}, bf16[128,1024]{1,0:T(8,128)(2,1)S(1)}, u32[]{:S(2)}, u32[]{:S(2)}) collective-permute-start(bf16[128,1024]{1,0:T(8,128)(2,1)S(1)} %collective-permute-done.4), channel_id=1, source_target_pairs={{0,2},{4,0},{8,4},{12,8},{14,12},{10,14},{6,10},{2,6},{1,3},{5,1},... | collective-permute-start | bytes 786440 | tf_op jit(solution)/shard_map/ppermute | solution.py:116
  62.9 12.2 %collective-permute-start.7 = (bf16[128,1024]{1,0:T(8,128)(2,1)S(1)}, bf16[128,1024]{1,0:T(8,128)(2,1)S(1)}, u32[]{:S(2)}, u32[]{:S(2)}) collective-permute-start(bf16[128,1024]{1,0:T(8,128)(2,1)S(1)} %collective-permute-done.5), channel_id=1, source_target_pairs={{0,4},{4,8},{8,12},{12,14},{14,10},{10,6},{6,2},{2,0},{1,5},{5,9},... | collective-permute-start | bytes 786440 | tf_op jit(solution)/shard_map/ppermute | solution.py:113
  75.1 5.0 %collective-permute-start.8 = (bf16[1024,1024]{1,0:T(8,128)(2,1)S(1)}, bf16[1024,1024]{1,0:T(8,128)(2,1)}, u32[]{:S(2)}, u32[]{:S(2)}) collective-permute-start(bf16[1024,1024]{1,0:T(8,128)(2,1)S(1)} %bitcast.136), channel_id=1, source_target_pairs={{0,1},{1,0},{2,3},{3,2},{4,5},{5,4},{6,7},{7,6},{8,9},{9,8},{10,11... | collective-permute-start | bytes 6291464 | tf_op jit(solution)/shard_map/ppermute | solution.py:119
  76.8 18.6 %copy-start.6 = (pred[8,2,96,128]{3,2,1,0:T(32,128)(4,1)}, pred[8,2,96,128]{3,2,1,0:T(32,128)(4,1)S(1)}, u32[]{:S(2)}) copy-start(pred[8,2,96,128]{3,2,1,0:T(32,128)(4,1)S(1)} %fusion.35) | copy-start | bytes 589828
  80.1 8.9 %copy-start.1 = (bf16[16,96,1024]{2,1,0:T(8,128)(2,1)}, bf16[16,96,1024]{2,1,0:T(8,128)(2,1)S(1)}, u32[]{:S(2)}) copy-start(bf16[16,96,1024]{2,1,0:T(8,128)(2,1)S(1)} %fusion.5) | copy-start | bytes 9437188
  85.1 2.0 %copy-start.5 = (bf16[8,2,96,1024]{3,2,1,0:T(8,128)(2,1)}, bf16[8,2,96,1024]{3,2,1,0:T(8,128)(2,1)S(1)}, u32[]{:S(2)}) copy-start(bf16[8,2,96,1024]{3,2,1,0:T(8,128)(2,1)S(1)} %add_convert_fusion) | copy-start | bytes 9437188
  85.1 2.0 %copy-start.8 = (bf16[1,512,1024]{2,1,0:T(8,128)(2,1)S(1)}, bf16[1,512,1024]{2,1,0:T(8,128)(2,1)}, u32[]{:S(2)}) copy-start(bf16[1,512,1024]{2,1,0:T(8,128)(2,1)} %param.18) | copy-start | bytes 3145732
  93.6 1.9 %copy-start.14 = (bf16[1536,512]{1,0:T(8,128)(2,1)}, bf16[1536,512]{1,0:T(8,128)(2,1)S(1)}, u32[]{:S(2)}) copy-start(bf16[1536,512]{1,0:T(8,128)(2,1)S(1)} %get-tuple-element.6) | copy-start | bytes 4718596
  95.4 1.7 copy-start.4
  99.2 4.5 %collective-permute-start = (bf16[8,128,1024]{2,1,0:T(8,128)(2,1)}, bf16[8,128,1024]{2,1,0:T(8,128)(2,1)S(1)}, u32[]{:S(2)}, u32[]{:S(2)}) collective-permute-start(bf16[8,128,1024]{2,1,0:T(8,128)(2,1)} %convolution_convert_fusion.1), channel_id=1, source_target_pairs={{0,1},{1,0},{2,3},{3,2},{4,5},{5,4},{6,7},{7,6},{8,9},{9,8},{10,11... | collective-permute-start | bytes 6291464 | tf_op jit(solution)/shard_map/ppermute | solution.py:229
  107.5 58.2 %all-to-all-start = ((bf16[8,128,1024]{2,1,0:T(8,128)(2,1)}), bf16[8,128,1024]{2,1,0:T(8,128)(2,1)S(1)}, u32[]{:S(2)}, u32[]{:S(2)}) async-start(bf16[8,128,1024]{2,1,0:T(8,128)(2,1)} %add_convert_fusion.1), calls=%async_computation | async-start | bytes 4194304 | tf_op jit(solution)/shard_map/all_to_all | solution.py:241
  117.0 3.3 %copy-start.2 = (bf16[16,96,1024]{2,1,0:T(8,128)(2,1)S(1)}, bf16[16,96,1024]{2,1,0:T(8,128)(2,1)}, u32[]{:S(2)}) copy-start(bf16[16,96,1024]{2,1,0:T(8,128)(2,1)} %copy-done.1) | copy-start | bytes 9437188
  117.0 3.5 %copy-start.10 = (bf16[1536,512]{1,0:T(8,128)(2,1)S(1)}, bf16[1536,512]{1,0:T(8,128)(2,1)}, u32[]{:S(2)}) copy-start(bf16[1536,512]{1,0:T(8,128)(2,1)} %get-tuple-element.4) | copy-start | bytes 4718596
  124.1 36.6 %collective-permute-start.9 = (bf16[256,3,1024]{2,0,1:T(8,128)(2,1)}, bf16[256,3,1024]{2,0,1:T(8,128)(2,1)}, u32[]{:S(2)}, u32[]{:S(2)}) collective-permute-start(bf16[256,3,1024]{2,0,1:T(8,128)(2,1)} %pad_maximum_fusion), channel_id=1, source_target_pairs={{0,16},{16,0},{1,17},{17,1},{2,18},{18,2},{3,19},{19,3},{4,20},{20... | collective-permute-start | bytes 4718600 | tf_op jit(solution)/shard_map/ppermute | solution.py:140
  125.6 3.3 %copy-start.3 = (bf16[16,96,1024]{2,1,0:T(8,128)(2,1)S(1)}, bf16[16,96,1024]{2,1,0:T(8,128)(2,1)}, u32[]{:S(2)}) copy-start(bf16[16,96,1024]{2,1,0:T(8,128)(2,1)} %copy-done.1) | copy-start | bytes 9437188
  125.6 3.5 %copy-start.13 = (bf16[1536,512]{1,0:T(8,128)(2,1)S(1)}, bf16[1536,512]{1,0:T(8,128)(2,1)}, u32[]{:S(2)}) copy-start(bf16[1536,512]{1,0:T(8,128)(2,1)} %get-tuple-element.5) | copy-start | bytes 4718596
  (3 other events, 4.1 us)
Sparse Core Ops, SparseCore 0:
  14.7 58.7 all-gather.1

commit v17 on v14

--- a/solution.py
+++ b/solution.py
@@ -163,7 +163,7 @@
 
     gathered = lax.all_gather(packed, ("ez", "core"), axis=0, tiled=True)
     gathered = gathered.reshape(experts, tok_rows + lines, width)
-    all_cot = lax.all_gather(cotangent, ("ez", "core"), axis=0, tiled=True)
+    cot_halves = ring_gather(cotangent)
     on_core0 = core == 0
     meta_all = gathered[:, tok_rows:].reshape(experts, lines * width)
     meta_all = meta_all[:, :meta_rows.size].reshape(experts, len(meta), topk, tok_rows)
@@ -189,10 +189,6 @@
         gathered[:, :tok_rows],
         preferred_element_type=jnp.float32,
     ).astype(jnp.bfloat16).reshape(experts * capacity, width)
-    scaled = fac[:, :, None] * all_cot.reshape(experts, tok_rows, width).astype(jnp.float32)
-    rows_q = jnp.einsum(
-        "sjt,std->sjd", pick, scaled.astype(jnp.bfloat16), preferred_element_type=jnp.float32
-    ).astype(jnp.bfloat16).reshape(experts * capacity, width)
     wgate, wup, wdown = w_gate[0], w_up[0], w_down[0]
     gate_pre = contract_cols(rows_x, wgate)
     up_pre = contract_cols(rows_x, wup)
@@ -227,6 +223,24 @@
     ).astype(jnp.bfloat16)
     returned = lax.all_to_all(combined, "ez", 0, 0, tiled=True)
 
+    cot_halves, _ = lax.optimization_barrier((cot_halves, expert_out))
+    pick_by_core = pick.reshape(nchip, ncore, capacity, tok_rows)
+    fac_by_core = fac.reshape(nchip, ncore, tok_rows)
+    core_ids = lax.broadcasted_iota(jnp.int32, (1, ncore, 1, 1), 1)
+    rows_q = 0.0
+    for h, half in enumerate(cot_halves):
+        k = h ^ core
+        scaled = lax.dynamic_index_in_dim(fac_by_core, k, 1, keepdims=False)[:, :, None] * half.reshape(
+            nchip, tok_rows, width
+        ).astype(jnp.float32)
+        masked_pick = jnp.where(core_ids == k, pick_by_core, jnp.zeros((), pick_by_core.dtype))
+        rows_q = rows_q + jnp.einsum(
+            "ikjt,itd->ikjd",
+            masked_pick,
+            scaled.astype(jnp.bfloat16),
+            preferred_element_type=jnp.float32,
+        )
+    rows_q = rows_q.astype(jnp.bfloat16).reshape(experts * capacity, width)
     back = contract_cols(rows_q, wdown)
     d_gate = (back * up_pre * sig * (1.0 + gate_pre * (1.0 - sig))).astype(jnp.bfloat16)
     d_up = (back * act).astype(jnp.bfloat16)

time: 209 us -> 172 us (0.82)
  waiting for transfers between devices: 133 us -> 51.7 us
  starting transfers between devices: 5.59 us -> 26.5 us
  between operations: 14.3 us -> 32.3 us
  local copies, waits for them, and re-layouts: 6.19 us -> 10.6 us
    all_gather x1, waiting for transfers between devices: 54.1 us -> 0.02 us  [local_gather(): gathered = lax.all_gather(packed, ('ez', 'core'), axis=0, tiled=True)]
    all_gather x1 -> x0, waiting for transfers between devices: 45 us -> none  [local_gather(): all_cot = lax.all_gather(cotangent, ('ez', 'core'), axis=0, tiled=True)]
    ppermute x0 -> x8, waiting for transfers between devices: none -> 22.6 us  [the longest x4 18 us: ring_gather(): up = lax.ppermute(up, 'ez', ahead)]
    ppermute x0 -> x8, starting transfers between devices: none -> 14.9 us  [the longest x4 14.9 us: ring_gather(): up = lax.ppermute(up, 'ez', ahead)]
    all_to_all x1, starting transfers between devices: 3.78 us -> 9.5 us  [local_gather(): returned = lax.all_to_all(combined, 'ez', 0, 0, tiled=True)]
    ppermute x1, waiting for transfers between devices: 4.07 us -> 0.01 us  [local_gather(): from_partner = lax.ppermute(dense_for(1 - core), 'core', [(0, 1), (1, 0)])]
    dot_general x3, matrix products: 8.23 us -> 11.5 us  [contract_cols(): lax.dot_general(left, right, (((1,), (1,)), ((), ())), preferred_element_...]
    dynamic_slice x0 -> x3, local copies, waits for them, and re-layouts: none -> 2.85 us  [the longest x1 1.6 us: ring_gather(): out = lax.dynamic_update_index_in_dim(out, up, ring[(at - step) % n], 0)]
  transfers between devices with their start and end apart: 5 -> 12, of which waited for: 5 -> 6; matrix products, arithmetic and copies ran while one was open for 10% -> 26% of each run, Pallas kernels for 0% -> 0%
where the time goes in v17:
time: 172 us; the launch traced here: 171 us
  waiting for transfers between devices  51.7 us (30%)
  matrix products  35.9 us (21%)
  between operations  32.3 us (19%)
  starting transfers between devices  26.5 us (15%)
  other arithmetic  13.8 us (8%)
  local copies, waits for them, and re-layouts  10.6 us (6%)
    ppermute x1, waiting for transfers between devices, reduce_grads_dp(): lax.ppermute(grad_half(1 - d).astype(jnp.bfloat16), 'dp', [(0, 1), (1, 0)])  29.1 us
    ppermute x4, waiting for transfers between devices, ring_gather(): up = lax.ppermute(up, 'ez', ahead)  18 us
    ppermute x4, starting transfers between devices, ring_gather(): up = lax.ppermute(up, 'ez', ahead)  14.9 us
    dot_general x3, matrix products, contract_cols(): lax.dot_general(left, right, (((1,), (1,)), ((), ())), preferred_element_...  11.5 us
    all_to_all x1, starting transfers between devices, local_gather(): returned = lax.all_to_all(combined, 'ez', 0, 0, tiled=True)  9.5 us
    dot_general x6, matrix products, contract_rows(): lax.dot_general(left, right, (((0,), (0,)), ((), ())), preferred_element_...  9.21 us
    dot_general x2, matrix products, dense_for(): jnp.einsum('sjt,sjd->std', lax.dynamic_index_in_dim(pick_k, k, 1, keepdim...  6.05 us
    ppermute x3, waiting for transfers between devices, ring_gather(): down = lax.ppermute(down, 'ez', behind)  4.52 us
  transfers between devices with their start and end apart: 12, of which 6 were waited for; matrix products, arithmetic and copies ran while one was open for 26% of the time, Pallas kernels for 0%

profile of v17, /device:TPU:0, one launch (start us, length us, event | category | flops | bytes accessed | tf_op | source)
XLA Modules:
  0.0 170.7 jit_solution(5804703808028721480)
XLA Ops:
  12.9 1.7 pad_maximum_fusion.1
  14.6 3.1 %collective-permute-start.1 = (bf16[128,1024]{1,0:T(8,128)(2,1)}, bf16[128,1024]{1,0:T(8,128)(2,1)}, u32[]{:S(2)}, u32[]{:S(2)}) collective-permute-start(bf16[128,1024]{1,0:T(8,128)(2,1)} %param.16), channel_id=1, source_target_pairs={{0,4},{4,8},{8,12},{12,14},{14,10},{10,6},{6,2},{2,0},{1,5},{5,9},... | collective-permute-start | bytes 786440 | tf_op jit(solution)/shard_map/ppermute | solution.py:113
  38.7 2.1 %collective-permute-start.3 = (bf16[128,1024]{1,0:T(8,128)(2,1)}, bf16[128,1024]{1,0:T(8,128)(2,1)S(1)}, u32[]{:S(2)}, u32[]{:S(2)}) collective-permute-start(bf16[128,1024]{1,0:T(8,128)(2,1)} %collective-permute-done.1), channel_id=1, source_target_pairs={{0,4},{4,8},{8,12},{12,14},{14,10},{10,6},{6,2},{2,0},{1,5},{5,9},... | collective-permute-start | bytes 786440 | tf_op jit(solution)/shard_map/ppermute | solution.py:113
  42.8 7.2 %collective-permute-done.3 = bf16[128,1024]{1,0:T(8,128)(2,1)S(1)} collective-permute-done((bf16[128,1024]{1,0:T(8,128)(2,1)}, bf16[128,1024]{1,0:T(8,128)(2,1)S(1)}, u32[]{:S(2)}, u32[]{:S(2)}) %collective-permute-start.3) | collective-permute-done | bytes 262176 | tf_op jit(solution)/shard_map/ppermute | solution.py:113
  49.9 3.8 %collective-permute-start.5 = (bf16[128,1024]{1,0:T(8,128)(2,1)S(1)}, bf16[128,1024]{1,0:T(8,128)(2,1)S(1)}, u32[]{:S(2)}, u32[]{:S(2)}) collective-permute-start(bf16[128,1024]{1,0:T(8,128)(2,1)S(1)} %collective-permute-done.3), channel_id=1, source_target_pairs={{0,4},{4,8},{8,12},{12,14},{14,10},{10,6},{6,2},{2,0},{1,5},{5,9},... | collective-permute-start | bytes 786440 | tf_op jit(solution)/shard_map/ppermute | solution.py:113
  53.7 1.8 %collective-permute-done.4 = bf16[128,1024]{1,0:T(8,128)(2,1)S(1)} collective-permute-done((bf16[128,1024]{1,0:T(8,128)(2,1)}, bf16[128,1024]{1,0:T(8,128)(2,1)S(1)}, u32[]{:S(2)}, u32[]{:S(2)}) %collective-permute-start.4) | collective-permute-done | bytes 262176 | tf_op jit(solution)/shard_map/ppermute | solution.py:116
  55.6 7.5 %collective-permute-done.5 = bf16[128,1024]{1,0:T(8,128)(2,1)S(1)} collective-permute-done((bf16[128,1024]{1,0:T(8,128)(2,1)S(1)}, bf16[128,1024]{1,0:T(8,128)(2,1)S(1)}, u32[]{:S(2)}, u32[]{:S(2)}) %collective-permute-start.5) | collective-permute-done | bytes 262176 | tf_op jit(solution)/shard_map/ppermute | solution.py:113
  63.1 6.0 %collective-permute-start.7 = (bf16[128,1024]{1,0:T(8,128)(2,1)S(1)}, bf16[128,1024]{1,0:T(8,128)(2,1)S(1)}, u32[]{:S(2)}, u32[]{:S(2)}) collective-permute-start(bf16[128,1024]{1,0:T(8,128)(2,1)S(1)} %collective-permute-done.5), channel_id=1, source_target_pairs={{0,4},{4,8},{8,12},{12,14},{14,10},{10,6},{6,2},{2,0},{1,5},{5,9},... | collective-permute-start | bytes 786440 | tf_op jit(solution)/shard_map/ppermute | solution.py:113
  69.1 2.7 %collective-permute-done.6 = bf16[128,1024]{1,0:T(8,128)(2,1)S(1)} collective-permute-done((bf16[128,1024]{1,0:T(8,128)(2,1)S(1)}, bf16[128,1024]{1,0:T(8,128)(2,1)S(1)}, u32[]{:S(2)}, u32[]{:S(2)}) %collective-permute-start.6) | collective-permute-done | bytes 262176 | tf_op jit(solution)/shard_map/ppermute | solution.py:116
  71.8 3.4 %collective-permute-done.7 = bf16[128,1024]{1,0:T(8,128)(2,1)S(1)} collective-permute-done((bf16[128,1024]{1,0:T(8,128)(2,1)S(1)}, bf16[128,1024]{1,0:T(8,128)(2,1)S(1)}, u32[]{:S(2)}, u32[]{:S(2)}) %collective-permute-start.7) | collective-permute-done | bytes 262176 | tf_op jit(solution)/shard_map/ppermute | solution.py:113
  76.7 3.3 %fusion.6 = bf16[16,96,1024]{2,1,0:T(8,128)(2,1)S(1)} fusion(bf16[16,136,1024]{2,1,0:T(8,128)(2,1)} %bitcast.142, s32[16,128]{1,0:T(8,128)S(1)} %convolution_convert_fusion.5, pred[16,128]{1,0:T(8,128)(4,1)S(1)} %fusion.65), kind=kOutput, calls=%fused_computation.16 | convolution fusion | flops 404619264 | bytes 7350272 | tf_op jit(solution)/shard_map/sjt,std->sjd/dot_general | solution.py:186
  80.1 1.8 %fusion.28 = f32[1536,512]{1,0:T(8,128)S(1)} fusion(bf16[1536,1024]{1,0:T(8,128)(2,1)S(1)} %bitcast.143, bf16[1,512,1024]{2,1,0:T(8,128)(2,1)S(1)} %copy-done.11), kind=kOutput, calls=%fused_computation.43 | convolution fusion | flops 1610612736 | bytes 7340032 | tf_op jit(solution)/shard_map/dot_general | solution.py:16
  82.2 3.8 %multiply_convert_fusion.2 = (bf16[1536,512]{1,0:T(8,128)(2,1)S(1)}, f32[1536,512]{1,0:T(8,128)}) fusion(f32[1536,512]{1,0:T(8,128)S(1)} %fusion.28, bf16[1536,1024]{1,0:T(8,128)(2,1)S(1)} %bitcast.144, bf16[1,512,1024]{2,1,0:T(8,128)(2,1)S(1)} %copy-done.12), kind=kOutput, calls=%fused_computation.13 | convolution fusion | flops 1615331328 | bytes 12058624 | tf_op jit(solution)/shard_map/dot_general | solution.py:16
  86.0 1.8 %convolution_convert_fusion = bf16[1536,1024]{1,0:T(8,128)(2,1)S(1)} fusion(bf16[1536,512]{1,0:T(8,128)(2,1)S(1)} %get-tuple-element.21, bf16[1,512,1024]{2,1,0:T(8,128)(2,1)S(1)} %copy-done), kind=kOutput, calls=%fused_computation.8 | convolution fusion | flops 1612185600 | bytes 5767168 | tf_op jit(solution)/shard_map/dot_general | solution.py:198
  87.8 1.6 copy-done.4
  89.5 2.1 %convolution_convert_fusion.1 = bf16[8,128,1024]{2,1,0:T(8,128)(2,1)} fusion(bf16[8,2,96,1024]{3,2,1,0:T(8,128)(2,1)S(1)} %bitcast.149, s32[]{:T(128)S(6)} %select_n.146, pred[8,2,96,128]{3,2,1,0:T(32,128)(4,1)S(1)} %fusion.36), kind=kOutput, calls=%fused_computation.22 | convolution fusion | flops 202375168 | bytes 3769344 | tf_op jit(solution)/shard_map/sjt,sjd->std/dot_general | solution.py:205
  93.3 2.8 %add_convert_fusion = bf16[8,2,96,1024]{3,2,1,0:T(8,128)(2,1)S(1)} fusion(f32[8,2,96,1024]{3,2,1,0:T(8,128)S(1)} %fusion.10, bf16[8,128,1024]{2,1,0:T(8,128)(2,1)} %bitcast.63, f32[8,128]{1,0:T(8,128)S(1)} %bitcast.166, pred[2]{0:T(512)(128)(4,1)S(1)} %iota_compare_fusion.4, s32[8,2,128]{2,1,0:T(2,128)S(1)} %bitcast.163, pred[8,2,128]{2,1,0:T(4,128)(4,1)S(1)} %and.48), kind=kOutput, calls=%fused_computation | convolution fusion | flops 409731072 | bytes 11548674 | tf_op jit(solution)/shard_map/ikjt,itd->ikjd/dot_general | solution.py:237
  97.8 1.9 %fusion.22 = bf16[256,1,1024]{2,0,1:T(8,128)(2,1)} fusion(bf16[1536,1024]{1,0:T(8,128)(2,1)S(1)} %bitcast.151, bf16[1536,512]{1,0:T(8,128)(2,1)S(1)} %copy-done.14, s32[]{:T(128)S(6)} %select_n.174), kind=kOutput, calls=%fused_computation.36 | convolution fusion | flops 805568512 | bytes 4456452 | tf_op jit(solution)/shard_map/dot_general | solution.py:10
  99.7 4.0 %add_convert_fusion.1 = bf16[8,128,1024]{2,1,0:T(8,128)(2,1)} fusion(bf16[8,128,1024]{2,1,0:T(8,128)(2,1)} %collective-permute-done, f32[8,128]{1,0:T(8,128)S(1)} %get-tuple-element.7, f32[8,128]{1,0:T(8,128)S(1)} %get-tuple-element.6, bf16[8,2,96,1024]{3,2,1,0:T(8,128)(2,1)S(1)} %bitcast.150, s32[]{:T(128)S(6)} %select_n.144, ...), kind=kOutput, calls=%fused_computation.7 | convolution fusion | flops 208666624 | bytes 5874688 | tf_op jit(solution)/shard_map/sjt,sjd->std/dot_general | solution.py:205
  103.6 9.5 %all-to-all-start = ((bf16[8,128,1024]{2,1,0:T(8,128)(2,1)}), bf16[8,128,1024]{2,1,0:T(8,128)(2,1)S(1)}, u32[]{:S(2)}, u32[]{:S(2)}) async-start(bf16[8,128,1024]{2,1,0:T(8,128)(2,1)} %add_convert_fusion.1), calls=%async_computation | async-start | bytes 4194304 | tf_op jit(solution)/shard_map/all_to_all | solution.py:224
  113.2 5.9 %multiply_convert_fusion.1 = (bf16[1536,512]{1,0:T(8,128)(2,1)S(1)}, bf16[1536,512]{1,0:T(8,128)(2,1)S(1)}) fusion(f32[1536,512]{1,0:T(8,128)} %copy-done.19, f32[1536,512]{1,0:T(8,128)} %get-tuple-element.22, bf16[1536,1024]{1,0:T(8,128)(2,1)} %bitcast.152, bf16[1,512,1024]{2,1,0:T(8,128)(2,1)S(1)} %copy-done), kind=kOutput, calls=%fused_computation.12 | convolution fusion | flops 1620836352 | bytes 13631488 | tf_op jit(solution)/shard_map/dot_general | solution.py:16
  124.1 3.3 %convolution_bitcast_fusion = f32[256,1,1024]{2,0,1:T(8,128)S(1)} fusion(bf16[1536,1024]{1,0:T(8,128)(2,1)} %bitcast.153, bf16[1536,512]{1,0:T(8,128)(2,1)} %copy-done.13, s32[]{:T(128)S(6)} %select_n.173), kind=kOutput, calls=%fused_computation.28 | convolution fusion | flops 805306368 | bytes 4980740 | tf_op jit(solution)/shard_map/dot_general | solution.py:10
  130.1 29.1 %collective-permute-done.9 = bf16[256,3,1024]{2,0,1:T(8,128)(2,1)} collective-permute-done((bf16[256,3,1024]{2,0,1:T(8,128)(2,1)}, bf16[256,3,1024]{2,0,1:T(8,128)(2,1)}, u32[]{:S(2)}, u32[]{:S(2)}) %collective-permute-start.9) | collective-permute-done | bytes 1572896 | tf_op jit(solution)/shard_map/ppermute | solution.py:140
  159.2 3.6 %fusion.4 = f32[1,256,3,1024]{3,1,2,0:T(8,128)} fusion(f32[256,1,1024]{2,0,1:T(8,128)S(1)} %convolution_bitcast_fusion, f32[256,1,1024]{2,0,1:T(8,128)S(1)} %convolution_bitcast_fusion.1, f32[256,1,1024]{2,0,1:T(8,128)S(1)} %convolution_bitcast_fusion.2, bf16[256,3,1024]{2,0,1:T(8,128)(2,1)} %collective-permute-done.9), kind=kLoop, calls=%fused_computation.10 | loop fusion | flops 3145728 | bytes 7864320 | tf_op jit(solution)/shard_map/reshape | solution.py:142
  (95 shorter events, 24.8 us)
Async XLA Ops:
  7.2 78.8 %copy-start = (bf16[1,512,1024]{2,1,0:T(8,128)(2,1)S(1)}, bf16[1,512,1024]{2,1,0:T(8,128)(2,1)}, u32[]{:S(2)}) copy-start(bf16[1,512,1024]{2,1,0:T(8,128)(2,1)} %param.19) | copy-start | bytes 3145732
  7.2 31.5 %copy-start.10 = (bf16[128,1024]{1,0:T(8,128)(2,1)S(1)}, bf16[128,1024]{1,0:T(8,128)(2,1)}, u32[]{:S(2)}) copy-start(bf16[128,1024]{1,0:T(8,128)(2,1)} %param.16) | copy-start | bytes 786436
  7.2 68.1 %all-gather.2.cloned.1.call-start = ((), (), s32[]{:S(2)}) async-start(), calls=%async_computation.1 | async-start | bytes 4734976 | tf_op jit(solution)/shard_map/all_gather | solution.py:164
  14.6 24.1 %collective-permute-start.1 = (bf16[128,1024]{1,0:T(8,128)(2,1)}, bf16[128,1024]{1,0:T(8,128)(2,1)}, u32[]{:S(2)}, u32[]{:S(2)}) collective-permute-start(bf16[128,1024]{1,0:T(8,128)(2,1)} %param.16), channel_id=1, source_target_pairs={{0,4},{4,8},{8,12},{12,14},{14,10},{10,6},{6,2},{2,0},{1,5},{5,9},... | collective-permute-start | bytes 786440 | tf_op jit(solution)/shard_map/ppermute | solution.py:113
  17.7 23.1 %collective-permute-start.2 = (bf16[128,1024]{1,0:T(8,128)(2,1)}, bf16[128,1024]{1,0:T(8,128)(2,1)}, u32[]{:S(2)}, u32[]{:S(2)}) collective-permute-start(bf16[128,1024]{1,0:T(8,128)(2,1)} %param.16), channel_id=1, source_target_pairs={{0,2},{4,0},{8,4},{12,8},{14,12},{10,14},{6,10},{2,6},{1,3},{5,1},... | collective-permute-start | bytes 786440 | tf_op jit(solution)/shard_map/ppermute | solution.py:116
  38.7 11.2 %collective-permute-start.3 = (bf16[128,1024]{1,0:T(8,128)(2,1)}, bf16[128,1024]{1,0:T(8,128)(2,1)S(1)}, u32[]{:S(2)}, u32[]{:S(2)}) collective-permute-start(bf16[128,1024]{1,0:T(8,128)(2,1)} %collective-permute-done.1), channel_id=1, source_target_pairs={{0,4},{4,8},{8,12},{12,14},{14,10},{10,6},{6,2},{2,0},{1,5},{5,9},... | collective-permute-start | bytes 786440 | tf_op jit(solution)/shard_map/ppermute | solution.py:113
  40.8 14.7 %collective-permute-start.4 = (bf16[128,1024]{1,0:T(8,128)(2,1)}, bf16[128,1024]{1,0:T(8,128)(2,1)S(1)}, u32[]{:S(2)}, u32[]{:S(2)}) collective-permute-start(bf16[128,1024]{1,0:T(8,128)(2,1)} %collective-permute-done.2), channel_id=1, source_target_pairs={{0,2},{4,0},{8,4},{12,8},{14,12},{10,14},{6,10},{2,6},{1,3},{5,1},... | collective-permute-start | bytes 786440 | tf_op jit(solution)/shard_map/ppermute | solution.py:116
  49.9 13.1 %collective-permute-start.5 = (bf16[128,1024]{1,0:T(8,128)(2,1)S(1)}, bf16[128,1024]{1,0:T(8,128)(2,1)S(1)}, u32[]{:S(2)}, u32[]{:S(2)}) collective-permute-start(bf16[128,1024]{1,0:T(8,128)(2,1)S(1)} %collective-permute-done.3), channel_id=1, source_target_pairs={{0,4},{4,8},{8,12},{12,14},{14,10},{10,6},{6,2},{2,0},{1,5},{5,9},... | collective-permute-start | bytes 786440 | tf_op jit(solution)/shard_map/ppermute | solution.py:113
  55.5 16.2 %collective-permute-start.6 = (bf16[128,1024]{1,0:T(8,128)(2,1)S(1)}, bf16[128,1024]{1,0:T(8,128)(2,1)S(1)}, u32[]{:S(2)}, u32[]{:S(2)}) collective-permute-start(bf16[128,1024]{1,0:T(8,128)(2,1)S(1)} %collective-permute-done.4), channel_id=1, source_target_pairs={{0,2},{4,0},{8,4},{12,8},{14,12},{10,14},{6,10},{2,6},{1,3},{5,1},... | collective-permute-start | bytes 786440 | tf_op jit(solution)/shard_map/ppermute | solution.py:116
  63.1 12.1 %collective-permute-start.7 = (bf16[128,1024]{1,0:T(8,128)(2,1)S(1)}, bf16[128,1024]{1,0:T(8,128)(2,1)S(1)}, u32[]{:S(2)}, u32[]{:S(2)}) collective-permute-start(bf16[128,1024]{1,0:T(8,128)(2,1)S(1)} %collective-permute-done.5), channel_id=1, source_target_pairs={{0,4},{4,8},{8,12},{12,14},{14,10},{10,6},{6,2},{2,0},{1,5},{5,9},... | collective-permute-start | bytes 786440 | tf_op jit(solution)/shard_map/ppermute | solution.py:113
  75.2 16.9 %collective-permute-start.8 = (bf16[1024,1024]{1,0:T(8,128)(2,1)S(1)}, bf16[1024,1024]{1,0:T(8,128)(2,1)}, u32[]{:S(2)}, u32[]{:S(2)}) collective-permute-start(bf16[1024,1024]{1,0:T(8,128)(2,1)S(1)} %bitcast.140), channel_id=1, source_target_pairs={{0,1},{1,0},{2,3},{3,2},{4,5},{5,4},{6,7},{7,6},{8,9},{9,8},{10,11... | collective-permute-start | bytes 6291464 | tf_op jit(solution)/shard_map/ppermute | solution.py:119
  76.7 3.4 %copy-start.11 = (bf16[1,512,1024]{2,1,0:T(8,128)(2,1)S(1)}, bf16[1,512,1024]{2,1,0:T(8,128)(2,1)}, u32[]{:S(2)}) copy-start(bf16[1,512,1024]{2,1,0:T(8,128)(2,1)} %param.17) | copy-start | bytes 3145732
  80.1 7.7 %copy-start.7 = (pred[8,2,96,128]{3,2,1,0:T(32,128)(4,1)}, pred[8,2,96,128]{3,2,1,0:T(32,128)(4,1)S(1)}, u32[]{:S(2)}) copy-start(pred[8,2,96,128]{3,2,1,0:T(32,128)(4,1)S(1)} %fusion.36) | copy-start | bytes 589828
  82.2 3.8 %copy-start.19 = (f32[1536,512]{1,0:T(8,128)}, f32[1536,512]{1,0:T(8,128)S(1)}, u32[]{:S(2)}) copy-start(f32[1536,512]{1,0:T(8,128)S(1)} %fusion.28) | copy-start | bytes 9437188
  91.6 8.1 %collective-permute-start = (bf16[8,128,1024]{2,1,0:T(8,128)(2,1)}, bf16[8,128,1024]{2,1,0:T(8,128)(2,1)}, u32[]{:S(2)}, u32[]{:S(2)}) collective-permute-start(bf16[8,128,1024]{2,1,0:T(8,128)(2,1)} %convolution_convert_fusion.1), channel_id=1, source_target_pairs={{0,1},{1,0},{2,3},{3,2},{4,5},{5,4},{6,7},{7,6},{8,9},{9,8},{10,11... | collective-permute-start | bytes 6291464 | tf_op jit(solution)/shard_map/ppermute | solution.py:212
  93.3 4.5 %copy-start.14 = (bf16[1536,512]{1,0:T(8,128)(2,1)S(1)}, bf16[1536,512]{1,0:T(8,128)(2,1)}, u32[]{:S(2)}) copy-start(bf16[1536,512]{1,0:T(8,128)(2,1)} %copy-done.13) | copy-start | bytes 4718596
  96.1 3.5 %copy-start.5 = (bf16[1536,1024]{1,0:T(8,128)(2,1)S(1)}, bf16[1536,1024]{1,0:T(8,128)(2,1)}, u32[]{:S(2)}) copy-start(bf16[1536,1024]{1,0:T(8,128)(2,1)} %copy-done.4) | copy-start | bytes 9437188
  96.1 3.5 %copy-start.8 = (pred[8,2,96,128]{3,2,1,0:T(32,128)(4,1)S(1)}, pred[8,2,96,128]{3,2,1,0:T(32,128)(4,1)}, u32[]{:S(2)}) copy-start(pred[8,2,96,128]{3,2,1,0:T(32,128)(4,1)} %copy-done.7) | copy-start | bytes 589828
  103.6 59.1 %all-to-all-start = ((bf16[8,128,1024]{2,1,0:T(8,128)(2,1)}), bf16[8,128,1024]{2,1,0:T(8,128)(2,1)S(1)}, u32[]{:S(2)}, u32[]{:S(2)}) async-start(bf16[8,128,1024]{2,1,0:T(8,128)(2,1)} %add_convert_fusion.1), calls=%async_computation | async-start | bytes 4194304 | tf_op jit(solution)/shard_map/all_to_all | solution.py:224
  113.1 5.9 %copy-start.2 = (bf16[16,96,1024]{2,1,0:T(8,128)(2,1)S(1)}, bf16[16,96,1024]{2,1,0:T(8,128)(2,1)}, u32[]{:S(2)}) copy-start(bf16[16,96,1024]{2,1,0:T(8,128)(2,1)} %copy-done.1) | copy-start | bytes 9437188
  119.0 2.1 %copy-start.15 = (bf16[1536,512]{1,0:T(8,128)(2,1)}, bf16[1536,512]{1,0:T(8,128)(2,1)S(1)}, u32[]{:S(2)}) copy-start(bf16[1536,512]{1,0:T(8,128)(2,1)S(1)} %get-tuple-element.8) | copy-start | bytes 4718596
  122.6 36.6 %collective-permute-start.9 = (bf16[256,3,1024]{2,0,1:T(8,128)(2,1)}, bf16[256,3,1024]{2,0,1:T(8,128)(2,1)}, u32[]{:S(2)}, u32[]{:S(2)}) collective-permute-start(bf16[256,3,1024]{2,0,1:T(8,128)(2,1)} %pad_maximum_fusion), channel_id=1, source_target_pairs={{0,16},{16,0},{1,17},{17,1},{2,18},{18,2},{3,19},{19,3},{4,20},{20... | collective-permute-start | bytes 4718600 | tf_op jit(solution)/shard_map/ppermute | solution.py:140
  124.1 3.3 %copy-start.3 = (bf16[16,96,1024]{2,1,0:T(8,128)(2,1)S(1)}, bf16[16,96,1024]{2,1,0:T(8,128)(2,1)}, u32[]{:S(2)}) copy-start(bf16[16,96,1024]{2,1,0:T(8,128)(2,1)} %copy-done.1) | copy-start | bytes 9437188
  124.1 3.5 %copy-start.18 = (bf16[1536,512]{1,0:T(8,128)(2,1)S(1)}, bf16[1536,512]{1,0:T(8,128)(2,1)}, u32[]{:S(2)}) copy-start(bf16[1536,512]{1,0:T(8,128)(2,1)} %copy-done.17) | copy-start | bytes 4718596
  (8 other events, 13.8 us)
Sparse Core Ops, SparseCore 0:
  14.7 58.8 all-gather.1

commit v18 on v17

--- a/solution.py
+++ b/solution.py
@@ -223,7 +223,7 @@
     ).astype(jnp.bfloat16)
     returned = lax.all_to_all(combined, "ez", 0, 0, tiled=True)
 
-    cot_halves, _ = lax.optimization_barrier((cot_halves, expert_out))
+    cot_halves, _ = lax.optimization_barrier((cot_halves, combined))
     pick_by_core = pick.reshape(nchip, ncore, capacity, tok_rows)
     fac_by_core = fac.reshape(nchip, ncore, tok_rows)
     core_ids = lax.broadcasted_iota(jnp.int32, (1, ncore, 1, 1), 1)

time: 172 us -> 172 us (level)
  local copies, waits for them, and re-layouts: 10.6 us -> 19.7 us
  waiting for transfers between devices: 51.7 us -> 44.3 us
  matrix products: 35.9 us -> 33.9 us
    ppermute x4, waiting for transfers between devices: 18 us -> 11.1 us  [ring_gather(): up = lax.ppermute(up, 'ez', ahead)]
    dynamic_update_slice x4, local copies, waits for them, and re-layouts: 1.06 us -> 4.81 us  [ring_gather(): out = lax.dynamic_update_index_in_dim(out, up, ring[(at - step) % n], 0)]
    dynamic_update_slice x3, local copies, waits for them, and re-layouts: 1.02 us -> 4.04 us  [ring_gather(): out = lax.dynamic_update_index_in_dim(out, down, ring[(at + step) % n], 0)]
    dot_general x3, matrix products: 11.5 us -> 8.93 us  [contract_cols(): lax.dot_general(left, right, (((1,), (1,)), ((), ())), preferred_element_...]
    ppermute x4, starting transfers between devices: 14.9 us -> 16.7 us  [ring_gather(): up = lax.ppermute(up, 'ez', ahead)]
    unnamed x43 -> x41, local copies, waits for them, and re-layouts: 4.37 us -> 4.65 us
  transfers between devices with their start and end apart: 12 -> 12, of which waited for: 6 -> 6; matrix products, arithmetic and copies ran while one was open for 26% -> 32% of each run, Pallas kernels for 0% -> 0%
where the time goes in v18:
time: 172 us; the launch traced here: 171 us
  waiting for transfers between devices  44.3 us (26%)
  matrix products  33.9 us (20%)
  between operations  32.1 us (19%)
  starting transfers between devices  26.9 us (16%)
  local copies, waits for them, and re-layouts  19.7 us (11%)
  other arithmetic  13.7 us (8%)
    ppermute x1, waiting for transfers between devices, reduce_grads_dp(): lax.ppermute(grad_half(1 - d).astype(jnp.bfloat16), 'dp', [(0, 1), (1, 0)])  29.3 us
    ppermute x4, starting transfers between devices, ring_gather(): up = lax.ppermute(up, 'ez', ahead)  16.7 us
    ppermute x4, waiting for transfers between devices, ring_gather(): up = lax.ppermute(up, 'ez', ahead)  11.1 us
    dot_general x3, matrix products, contract_cols(): lax.dot_general(left, right, (((1,), (1,)), ((), ())), preferred_element_...  8.93 us
    dot_general x6, matrix products, contract_rows(): lax.dot_general(left, right, (((0,), (0,)), ((), ())), preferred_element_...  8.37 us
    all_to_all x1, starting transfers between devices, local_gather(): returned = lax.all_to_all(combined, 'ez', 0, 0, tiled=True)  8.26 us
    dot_general x2, matrix products, dense_for(): jnp.einsum('sjt,sjd->std', lax.dynamic_index_in_dim(pick_k, k, 1, keepdim...  5.83 us
    dot_general x2, matrix products, local_gather(): jnp.einsum('ikjt,itd->ikjd', masked_pick, scaled.astype(jnp.bfloat16), pr...  5.52 us
  transfers between devices with their start and end apart: 12, of which 6 were waited for; matrix products, arithmetic and copies ran while one was open for 32% of the time, Pallas kernels for 0%

profile of v18, /device:TPU:0, one launch (start us, length us, event | category | flops | bytes accessed | tf_op | source)
XLA Modules:
  0.0 170.6 jit_solution(11628062032771477930)
XLA Ops:
  12.9 1.7 pad_maximum_fusion.1
  14.6 3.1 %collective-permute-start.1 = (bf16[128,1024]{1,0:T(8,128)(2,1)}, bf16[128,1024]{1,0:T(8,128)(2,1)S(1)}, u32[]{:S(2)}, u32[]{:S(2)}) collective-permute-start(bf16[128,1024]{1,0:T(8,128)(2,1)} %param.16), channel_id=1, source_target_pairs={{0,4},{4,8},{8,12},{12,14},{14,10},{10,6},{6,2},{2,0},{1,5},{5,9},... | collective-permute-start | bytes 786440 | tf_op jit(solution)/shard_map/ppermute | solution.py:113
  40.6 2.0 %collective-permute-start.3 = (bf16[128,1024]{1,0:T(8,128)(2,1)S(1)}, bf16[128,1024]{1,0:T(8,128)(2,1)S(1)}, u32[]{:S(2)}, u32[]{:S(2)}) collective-permute-start(bf16[128,1024]{1,0:T(8,128)(2,1)S(1)} %collective-permute-done.1), channel_id=1, source_target_pairs={{0,4},{4,8},{8,12},{12,14},{14,10},{10,6},{6,2},{2,0},{1,5},{5,9},... | collective-permute-start | bytes 786440 | tf_op jit(solution)/shard_map/ppermute | solution.py:113
  44.1 9.4 %collective-permute-done.3 = bf16[128,1024]{1,0:T(8,128)(2,1)S(1)} collective-permute-done((bf16[128,1024]{1,0:T(8,128)(2,1)S(1)}, bf16[128,1024]{1,0:T(8,128)(2,1)S(1)}, u32[]{:S(2)}, u32[]{:S(2)}) %collective-permute-start.3) | collective-permute-done | bytes 262176 | tf_op jit(solution)/shard_map/ppermute | solution.py:113
  53.5 5.4 %collective-permute-start.5 = (bf16[128,1024]{1,0:T(8,128)(2,1)S(1)}, bf16[128,1024]{1,0:T(8,128)(2,1)}, u32[]{:S(2)}, u32[]{:S(2)}) collective-permute-start(bf16[128,1024]{1,0:T(8,128)(2,1)S(1)} %collective-permute-done.3), channel_id=1, source_target_pairs={{0,4},{4,8},{8,12},{12,14},{14,10},{10,6},{6,2},{2,0},{1,5},{5,9},... | collective-permute-start | bytes 786440 | tf_op jit(solution)/shard_map/ppermute | solution.py:113
  58.9 3.2 %collective-permute-done.4 = bf16[128,1024]{1,0:T(8,128)(2,1)} collective-permute-done((bf16[128,1024]{1,0:T(8,128)(2,1)S(1)}, bf16[128,1024]{1,0:T(8,128)(2,1)}, u32[]{:S(2)}, u32[]{:S(2)}) %collective-permute-start.4) | collective-permute-done | bytes 262176 | tf_op jit(solution)/shard_map/ppermute | solution.py:116
  66.1 6.3 %collective-permute-start.7 = (bf16[128,1024]{1,0:T(8,128)(2,1)}, bf16[128,1024]{1,0:T(8,128)(2,1)}, u32[]{:S(2)}, u32[]{:S(2)}) collective-permute-start(bf16[128,1024]{1,0:T(8,128)(2,1)} %collective-permute-done.5), channel_id=1, source_target_pairs={{0,4},{4,8},{8,12},{12,14},{14,10},{10,6},{6,2},{2,0},{1,5},{5,9},... | collective-permute-start | bytes 786440 | tf_op jit(solution)/shard_map/ppermute | solution.py:113
  72.4 1.7 bitcast_dynamic-update-slice_fusion.2
  75.8 3.3 %fusion.6 = bf16[16,96,1024]{2,1,0:T(8,128)(2,1)S(1)} fusion(bf16[16,136,1024]{2,1,0:T(8,128)(2,1)} %bitcast.141, s32[16,128]{1,0:T(8,128)S(1)} %convolution_convert_fusion.5, pred[16,128]{1,0:T(8,128)(4,1)S(1)} %fusion.65), kind=kOutput, calls=%fused_computation.16 | convolution fusion | flops 404619264 | bytes 7350272 | tf_op jit(solution)/shard_map/sjt,std->sjd/dot_general | solution.py:186
  79.1 1.8 %fusion.28 = f32[1536,512]{1,0:T(8,128)S(1)} fusion(bf16[1536,1024]{1,0:T(8,128)(2,1)S(1)} %bitcast.142, bf16[1,512,1024]{2,1,0:T(8,128)(2,1)S(1)} %copy-done.8), kind=kOutput, calls=%fused_computation.43 | convolution fusion | flops 1610612736 | bytes 7340032 | tf_op jit(solution)/shard_map/dot_general | solution.py:16
  81.2 3.8 %multiply_convert_fusion.2 = (bf16[1536,512]{1,0:T(8,128)(2,1)S(1)}, f32[1536,512]{1,0:T(8,128)}) fusion(f32[1536,512]{1,0:T(8,128)S(1)} %fusion.28, bf16[1536,1024]{1,0:T(8,128)(2,1)S(1)} %bitcast.143, bf16[1,512,1024]{2,1,0:T(8,128)(2,1)S(1)} %copy-done.9), kind=kOutput, calls=%fused_computation.13 | convolution fusion | flops 1615331328 | bytes 12058624 | tf_op jit(solution)/shard_map/dot_general | solution.py:16
  85.0 1.8 %convolution_convert_fusion = bf16[1536,1024]{1,0:T(8,128)(2,1)S(1)} fusion(bf16[1536,512]{1,0:T(8,128)(2,1)S(1)} %get-tuple-element.21, bf16[1,512,1024]{2,1,0:T(8,128)(2,1)S(1)} %copy-done), kind=kOutput, calls=%fused_computation.8 | convolution fusion | flops 1612185600 | bytes 5767168 | tf_op jit(solution)/shard_map/dot_general | solution.py:198
  88.6 2.1 %convolution_convert_fusion.1 = bf16[8,128,1024]{2,1,0:T(8,128)(2,1)} fusion(bf16[8,2,96,1024]{3,2,1,0:T(8,128)(2,1)S(1)} %bitcast.148, s32[]{:T(128)S(6)} %select_n.146, pred[8,2,96,128]{3,2,1,0:T(32,128)(4,1)S(1)} %fusion.36), kind=kOutput, calls=%fused_computation.22 | convolution fusion | flops 202375168 | bytes 3769344 | tf_op jit(solution)/shard_map/sjt,sjd->std/dot_general | solution.py:205
  90.7 1.7 bitcast_dynamic-update-slice_fusion.1
  92.3 1.7 bitcast_dynamic-update-slice_fusion
  95.0 3.8 %add_convert_fusion.1 = bf16[8,128,1024]{2,1,0:T(8,128)(2,1)} fusion(bf16[8,128,1024]{2,1,0:T(8,128)(2,1)S(1)} %collective-permute-done, f32[8,128]{1,0:T(8,128)S(1)} %get-tuple-element.7, f32[8,128]{1,0:T(8,128)S(1)} %get-tuple-element.6, bf16[8,2,96,1024]{3,2,1,0:T(8,128)(2,1)} %bitcast.149, s32[]{:T(128)S(6)} %select_n.144, ...), kind=kOutput, calls=%fused_computation.7 | convolution fusion | flops 208666624 | bytes 5874688 | tf_op jit(solution)/shard_map/sjt,sjd->std/dot_general | solution.py:205
  98.8 8.3 %all-to-all-start = ((bf16[8,128,1024]{2,1,0:T(8,128)(2,1)}), bf16[8,128,1024]{2,1,0:T(8,128)(2,1)S(1)}, u32[]{:S(2)}, u32[]{:S(2)}) async-start(bf16[8,128,1024]{2,1,0:T(8,128)(2,1)} %add_convert_fusion.1), calls=%async_computation | async-start | bytes 4194304 | tf_op jit(solution)/shard_map/all_to_all | solution.py:224
  107.1 2.6 %fusion.10 = f32[8,2,96,1024]{3,2,1,0:T(8,128)S(1)} fusion(bf16[8,128,1024]{2,1,0:T(8,128)(2,1)} %bitcast.61, f32[8,128]{1,0:T(8,128)S(1)} %bitcast.166, pred[2]{0:T(512)(128)(4,1)S(1)} %iota_compare_fusion.5, s32[8,2,128]{2,1,0:T(2,128)S(1)} %bitcast.161, pred[8,2,128]{2,1,0:T(4,128)(4,1)S(1)} %and.48), kind=kOutput, calls=%fused_computation.18 | convolution fusion | flops 406585344 | bytes 8402946 | tf_op jit(solution)/shard_map/ikjt,itd->ikjd/dot_general | solution.py:237
  109.7 2.9 %add_convert_fusion = bf16[8,2,96,1024]{3,2,1,0:T(8,128)(2,1)S(1)} fusion(f32[8,2,96,1024]{3,2,1,0:T(8,128)S(1)} %fusion.10, bf16[8,128,1024]{2,1,0:T(8,128)(2,1)} %bitcast.63, f32[8,128]{1,0:T(8,128)S(1)} %bitcast.165, pred[2]{0:T(512)(128)(4,1)S(1)} %iota_compare_fusion.4, s32[8,2,128]{2,1,0:T(2,128)S(1)} %bitcast.162, pred[8,2,128]{2,1,0:T(4,128)(4,1)S(1)} %and.48), kind=kOutput, calls=%fused_computation | convolution fusion | flops 409731072 | bytes 11548674 | tf_op jit(solution)/shard_map/ikjt,itd->ikjd/dot_general | solution.py:237
  113.7 2.0 %copy-done.17 = f32[1536,512]{1,0:T(8,128)S(1)} copy-done((f32[1536,512]{1,0:T(8,128)S(1)}, f32[1536,512]{1,0:T(8,128)}, u32[]{:S(2)}) %copy-start.17) | copy-done | bytes 3145752
  115.7 3.3 %multiply_convert_fusion.1 = (bf16[1536,512]{1,0:T(8,128)(2,1)S(1)}, bf16[1536,512]{1,0:T(8,128)(2,1)S(1)}) fusion(f32[1536,512]{1,0:T(8,128)S(1)} %copy-done.17, f32[1536,512]{1,0:T(8,128)S(1)} %copy-done.18, bf16[1536,1024]{1,0:T(8,128)(2,1)S(1)} %bitcast.151, bf16[1,512,1024]{2,1,0:T(8,128)(2,1)S(1)} %copy-done), kind=kOutput, calls=%fused_computation.12 | convolution fusion | flops 1620836352 | bytes 13631488 | tf_op jit(solution)/shard_map/dot_general | solution.py:16
  123.8 3.3 %convolution_bitcast_fusion = f32[256,1,1024]{2,0,1:T(8,128)S(1)} fusion(bf16[1536,1024]{1,0:T(8,128)(2,1)} %bitcast.152, bf16[1536,512]{1,0:T(8,128)(2,1)} %copy-done.10, s32[]{:T(128)S(6)} %select_n.173), kind=kOutput, calls=%fused_computation.28 | convolution fusion | flops 805306368 | bytes 4980740 | tf_op jit(solution)/shard_map/dot_general | solution.py:10
  129.8 29.3 %collective-permute-done.9 = bf16[256,3,1024]{2,0,1:T(8,128)(2,1)} collective-permute-done((bf16[256,3,1024]{2,0,1:T(8,128)(2,1)}, bf16[256,3,1024]{2,0,1:T(8,128)(2,1)}, u32[]{:S(2)}, u32[]{:S(2)}) %collective-permute-start.9) | collective-permute-done | bytes 1572896 | tf_op jit(solution)/shard_map/ppermute | solution.py:140
  159.0 3.6 %fusion.4 = f32[1,256,3,1024]{3,1,2,0:T(8,128)} fusion(f32[256,1,1024]{2,0,1:T(8,128)S(1)} %convolution_bitcast_fusion, f32[256,1,1024]{2,0,1:T(8,128)S(1)} %convolution_bitcast_fusion.1, f32[256,1,1024]{2,0,1:T(8,128)S(1)} %convolution_bitcast_fusion.2, bf16[256,3,1024]{2,0,1:T(8,128)(2,1)} %collective-permute-done.9), kind=kLoop, calls=%fused_computation.10 | loop fusion | flops 3145728 | bytes 7864320 | tf_op jit(solution)/shard_map/reshape | solution.py:142
  (93 shorter events, 30.6 us)
Async XLA Ops:
  7.2 77.8 %copy-start = (bf16[1,512,1024]{2,1,0:T(8,128)(2,1)S(1)}, bf16[1,512,1024]{2,1,0:T(8,128)(2,1)}, u32[]{:S(2)}) copy-start(bf16[1,512,1024]{2,1,0:T(8,128)(2,1)} %param.19) | copy-start | bytes 3145732
  7.2 32.7 %copy-start.7 = (bf16[128,1024]{1,0:T(8,128)(2,1)S(1)}, bf16[128,1024]{1,0:T(8,128)(2,1)}, u32[]{:S(2)}) copy-start(bf16[128,1024]{1,0:T(8,128)(2,1)} %param.16) | copy-start | bytes 786436
  7.2 67.2 %all-gather.2.cloned.1.call-start = ((), (), s32[]{:S(2)}) async-start(), calls=%async_computation.1 | async-start | bytes 4734976 | tf_op jit(solution)/shard_map/all_gather | solution.py:164
  14.6 26.0 %collective-permute-start.1 = (bf16[128,1024]{1,0:T(8,128)(2,1)}, bf16[128,1024]{1,0:T(8,128)(2,1)S(1)}, u32[]{:S(2)}, u32[]{:S(2)}) collective-permute-start(bf16[128,1024]{1,0:T(8,128)(2,1)} %param.16), channel_id=1, source_target_pairs={{0,4},{4,8},{8,12},{12,14},{14,10},{10,6},{6,2},{2,0},{1,5},{5,9},... | collective-permute-start | bytes 786440 | tf_op jit(solution)/shard_map/ppermute | solution.py:113
  17.7 24.9 %collective-permute-start.2 = (bf16[128,1024]{1,0:T(8,128)(2,1)}, bf16[128,1024]{1,0:T(8,128)(2,1)S(1)}, u32[]{:S(2)}, u32[]{:S(2)}) collective-permute-start(bf16[128,1024]{1,0:T(8,128)(2,1)} %param.16), channel_id=1, source_target_pairs={{0,2},{4,0},{8,4},{12,8},{14,12},{10,14},{6,10},{2,6},{1,3},{5,1},... | collective-permute-start | bytes 786440 | tf_op jit(solution)/shard_map/ppermute | solution.py:116
  40.6 12.8 %collective-permute-start.3 = (bf16[128,1024]{1,0:T(8,128)(2,1)S(1)}, bf16[128,1024]{1,0:T(8,128)(2,1)S(1)}, u32[]{:S(2)}, u32[]{:S(2)}) collective-permute-start(bf16[128,1024]{1,0:T(8,128)(2,1)S(1)} %collective-permute-done.1), channel_id=1, source_target_pairs={{0,4},{4,8},{8,12},{12,14},{14,10},{10,6},{6,2},{2,0},{1,5},{5,9},... | collective-permute-start | bytes 786440 | tf_op jit(solution)/shard_map/ppermute | solution.py:113
  42.6 19.4 %collective-permute-start.4 = (bf16[128,1024]{1,0:T(8,128)(2,1)S(1)}, bf16[128,1024]{1,0:T(8,128)(2,1)}, u32[]{:S(2)}, u32[]{:S(2)}) collective-permute-start(bf16[128,1024]{1,0:T(8,128)(2,1)S(1)} %collective-permute-done.2), channel_id=1, source_target_pairs={{0,2},{4,0},{8,4},{12,8},{14,12},{10,14},{6,10},{2,6},{1,3},{5,1},... | collective-permute-start | bytes 786440 | tf_op jit(solution)/shard_map/ppermute | solution.py:116
  53.5 12.6 %collective-permute-start.5 = (bf16[128,1024]{1,0:T(8,128)(2,1)S(1)}, bf16[128,1024]{1,0:T(8,128)(2,1)}, u32[]{:S(2)}, u32[]{:S(2)}) collective-permute-start(bf16[128,1024]{1,0:T(8,128)(2,1)S(1)} %collective-permute-done.3), channel_id=1, source_target_pairs={{0,4},{4,8},{8,12},{12,14},{14,10},{10,6},{6,2},{2,0},{1,5},{5,9},... | collective-permute-start | bytes 786440 | tf_op jit(solution)/shard_map/ppermute | solution.py:113
  62.0 28.6 %collective-permute-start.6 = (bf16[128,1024]{1,0:T(8,128)(2,1)}, bf16[128,1024]{1,0:T(8,128)(2,1)}, u32[]{:S(2)}, u32[]{:S(2)}) collective-permute-start(bf16[128,1024]{1,0:T(8,128)(2,1)} %collective-permute-done.4), channel_id=1, source_target_pairs={{0,2},{4,0},{8,4},{12,8},{14,12},{10,14},{6,10},{2,6},{1,3},{5,1},... | collective-permute-start | bytes 786440 | tf_op jit(solution)/shard_map/ppermute | solution.py:116
  66.1 26.3 %collective-permute-start.7 = (bf16[128,1024]{1,0:T(8,128)(2,1)}, bf16[128,1024]{1,0:T(8,128)(2,1)}, u32[]{:S(2)}, u32[]{:S(2)}) collective-permute-start(bf16[128,1024]{1,0:T(8,128)(2,1)} %collective-permute-done.5), channel_id=1, source_target_pairs={{0,4},{4,8},{8,12},{12,14},{14,10},{10,6},{6,2},{2,0},{1,5},{5,9},... | collective-permute-start | bytes 786440 | tf_op jit(solution)/shard_map/ppermute | solution.py:113
  75.8 3.3 %copy-start.8 = (bf16[1,512,1024]{2,1,0:T(8,128)(2,1)S(1)}, bf16[1,512,1024]{2,1,0:T(8,128)(2,1)}, u32[]{:S(2)}) copy-start(bf16[1,512,1024]{2,1,0:T(8,128)(2,1)} %param.17) | copy-start | bytes 3145732
  81.2 3.8 %copy-start.16 = (f32[1536,512]{1,0:T(8,128)}, f32[1536,512]{1,0:T(8,128)S(1)}, u32[]{:S(2)}) copy-start(f32[1536,512]{1,0:T(8,128)S(1)} %fusion.28) | copy-start | bytes 9437188
  87.0 3.7 %copy-start.6 = (pred[8,2,96,128]{3,2,1,0:T(32,128)(4,1)}, pred[8,2,96,128]{3,2,1,0:T(32,128)(4,1)S(1)}, u32[]{:S(2)}) copy-start(pred[8,2,96,128]{3,2,1,0:T(32,128)(4,1)S(1)} %fusion.36) | copy-start | bytes 589828
  90.7 4.4 %collective-permute-start = (bf16[8,128,1024]{2,1,0:T(8,128)(2,1)}, bf16[8,128,1024]{2,1,0:T(8,128)(2,1)S(1)}, u32[]{:S(2)}, u32[]{:S(2)}) collective-permute-start(bf16[8,128,1024]{2,1,0:T(8,128)(2,1)} %convolution_convert_fusion.1), channel_id=1, source_target_pairs={{0,1},{1,0},{2,3},{3,2},{4,5},{5,4},{6,7},{7,6},{8,9},{9,8},{10,11... | collective-permute-start | bytes 6291464 | tf_op jit(solution)/shard_map/ppermute | solution.py:212
  94.0 13.0 %collective-permute-start.8 = (bf16[1024,1024]{1,0:T(8,128)(2,1)}, bf16[1024,1024]{1,0:T(8,128)(2,1)}, u32[]{:S(2)}, u32[]{:S(2)}) collective-permute-start(bf16[1024,1024]{1,0:T(8,128)(2,1)} %bitcast.45), channel_id=1, source_target_pairs={{0,1},{1,0},{2,3},{3,2},{4,5},{5,4},{6,7},{7,6},{8,9},{9,8},{10,11... | collective-permute-start | bytes 6291464 | tf_op jit(solution)/shard_map/ppermute | solution.py:119
  98.8 63.9 %all-to-all-start = ((bf16[8,128,1024]{2,1,0:T(8,128)(2,1)}), bf16[8,128,1024]{2,1,0:T(8,128)(2,1)S(1)}, u32[]{:S(2)}, u32[]{:S(2)}) async-start(bf16[8,128,1024]{2,1,0:T(8,128)(2,1)} %add_convert_fusion.1), calls=%async_computation | async-start | bytes 4194304 | tf_op jit(solution)/shard_map/all_to_all | solution.py:224
  109.7 2.9 %copy-start.11 = (bf16[1536,512]{1,0:T(8,128)(2,1)S(1)}, bf16[1536,512]{1,0:T(8,128)(2,1)}, u32[]{:S(2)}) copy-start(bf16[1536,512]{1,0:T(8,128)(2,1)} %copy-done.10) | copy-start | bytes 4718596
  109.7 3.9 %copy-start.18 = (f32[1536,512]{1,0:T(8,128)S(1)}, f32[1536,512]{1,0:T(8,128)}, u32[]{:S(2)}) copy-start(f32[1536,512]{1,0:T(8,128)} %get-tuple-element.22) | copy-start | bytes 9437188
  112.6 6.3 %copy-start.5 = (bf16[8,2,96,1024]{3,2,1,0:T(8,128)(2,1)}, bf16[8,2,96,1024]{3,2,1,0:T(8,128)(2,1)S(1)}, u32[]{:S(2)}) copy-start(bf16[8,2,96,1024]{3,2,1,0:T(8,128)(2,1)S(1)} %add_convert_fusion) | copy-start | bytes 9437188
  112.6 3.0 %copy-start.17 = (f32[1536,512]{1,0:T(8,128)S(1)}, f32[1536,512]{1,0:T(8,128)}, u32[]{:S(2)}) copy-start(f32[1536,512]{1,0:T(8,128)} %copy-done.16) | copy-start | bytes 9437188
  115.7 3.3 %copy-start.2 = (bf16[16,96,1024]{2,1,0:T(8,128)(2,1)S(1)}, bf16[16,96,1024]{2,1,0:T(8,128)(2,1)}, u32[]{:S(2)}) copy-start(bf16[16,96,1024]{2,1,0:T(8,128)(2,1)} %copy-done.1) | copy-start | bytes 9437188
  122.5 36.6 %collective-permute-start.9 = (bf16[256,3,1024]{2,0,1:T(8,128)(2,1)}, bf16[256,3,1024]{2,0,1:T(8,128)(2,1)}, u32[]{:S(2)}, u32[]{:S(2)}) collective-permute-start(bf16[256,3,1024]{2,0,1:T(8,128)(2,1)} %pad_maximum_fusion), channel_id=1, source_target_pairs={{0,16},{16,0},{1,17},{17,1},{2,18},{18,2},{3,19},{19,3},{4,20},{20... | collective-permute-start | bytes 4718600 | tf_op jit(solution)/shard_map/ppermute | solution.py:140
  123.8 3.3 %copy-start.3 = (bf16[16,96,1024]{2,1,0:T(8,128)(2,1)S(1)}, bf16[16,96,1024]{2,1,0:T(8,128)(2,1)}, u32[]{:S(2)}) copy-start(bf16[16,96,1024]{2,1,0:T(8,128)(2,1)} %copy-done.1) | copy-start | bytes 9437188
  123.8 3.5 %copy-start.15 = (bf16[1536,512]{1,0:T(8,128)(2,1)S(1)}, bf16[1536,512]{1,0:T(8,128)(2,1)}, u32[]{:S(2)}) copy-start(bf16[1536,512]{1,0:T(8,128)(2,1)} %copy-done.14) | copy-start | bytes 4718596
  (7 other events, 13.1 us)
Sparse Core Ops, SparseCore 0:
  14.7 59.6 all-gather.1

commit v19 on v17

--- a/solution.py
+++ b/solution.py
@@ -137,8 +137,12 @@
         grads = jnp.concatenate([grad_half(h) for h in range(ndp)], axis=0)
         return reduce_grads(grads, width)
     d = lax.axis_index("dp")
-    sent = lax.ppermute(grad_half(1 - d).astype(jnp.bfloat16), "dp", [(0, 1), (1, 0)])
-    summed = grad_half(d) + sent.astype(jnp.float32)
+    theirs = grad_half(1 - d)
+    sent = [
+        lax.ppermute(theirs[:, :2].astype(jnp.bfloat16), "dp", [(0, 1), (1, 0)]),
+        lax.ppermute(theirs[:, 2:].astype(jnp.bfloat16), "dp", [(0, 1), (1, 0)]),
+    ]
+    summed = grad_half(d) + jnp.concatenate(sent, axis=1).astype(jnp.float32)
     return summed.reshape(1, summed.shape[0], 3, width)
 
 

time: 172 us -> 168 us (0.977)
  other arithmetic: 13.8 us -> 11 us
  starting transfers between devices: 26.5 us -> 28.9 us
  local copies, waits for them, and re-layouts: 10.6 us -> 8.71 us
    dot_general x2, matrix products: 3.91 us -> 8.35 us  [local_gather(): jnp.einsum('ikjt,itd->ikjd', masked_pick, scaled.astype(jnp.bfloat16), pr...]
    reshape x1 -> x0, other arithmetic: 3.61 us -> none  [reduce_grads_dp(): return summed.reshape(1, summed.shape[0], 3, width)]
    dot_general x6, matrix products: 9.21 us -> 6.12 us  [contract_rows(): lax.dot_general(left, right, (((0,), (0,)), ((), ())), preferred_element_...]
    dot_general x3, matrix products: 11.5 us -> 8.94 us  [contract_cols(): lax.dot_general(left, right, (((1,), (1,)), ((), ())), preferred_element_...]
    add x0 -> x1, other arithmetic: none -> 2.17 us  [reduce_grads_dp(): summed = grad_half(d) + jnp.concatenate(sent, axis=1).astype(jnp.float32)]
    unnamed x43 -> x33, local copies, waits for them, and re-layouts: 4.37 us -> 2.49 us
    ppermute x1 -> x2, waiting for transfers between devices: 29.1 us -> 30.1 us  [the longest x1 30.1 us: reduce_grads_dp(): lax.ppermute(theirs[:, 2:].astype(jnp.bfloat16), 'dp', [(0, 1), (1, 0)])]
  transfers between devices with their start and end apart: 12 -> 13, of which waited for: 6 -> 7; matrix products, arithmetic and copies ran while one was open for 26% -> 24% of each run, Pallas kernels for 0% -> 0%
where the time goes in v19:
time: 168 us; the launch traced here: 167 us
  waiting for transfers between devices  51.3 us (31%)
  matrix products  34.7 us (21%)
  between operations  32.6 us (19%)
  starting transfers between devices  28.9 us (17%)
  other arithmetic  11 us (7%)
  local copies, waits for them, and re-layouts  8.71 us (5%)
    ppermute x1, waiting for transfers between devices, reduce_grads_dp(): lax.ppermute(theirs[:, 2:].astype(jnp.bfloat16), 'dp', [(0, 1), (1, 0)])  30.1 us
    ppermute x4, waiting for transfers between devices, ring_gather(): up = lax.ppermute(up, 'ez', ahead)  17.8 us
    ppermute x4, starting transfers between devices, ring_gather(): up = lax.ppermute(up, 'ez', ahead)  16.5 us
    all_to_all x1, starting transfers between devices, local_gather(): returned = lax.all_to_all(combined, 'ez', 0, 0, tiled=True)  9.73 us
    dot_general x3, matrix products, contract_cols(): lax.dot_general(left, right, (((1,), (1,)), ((), ())), preferred_element_...  8.94 us
    dot_general x2, matrix products, local_gather(): jnp.einsum('ikjt,itd->ikjd', masked_pick, scaled.astype(jnp.bfloat16), pr...  8.35 us
    dot_general x6, matrix products, contract_rows(): lax.dot_general(left, right, (((0,), (0,)), ((), ())), preferred_element_...  6.12 us
    dot_general x2, matrix products, dense_for(): jnp.einsum('sjt,sjd->std', lax.dynamic_index_in_dim(pick_k, k, 1, keepdim...  6.09 us
  transfers between devices with their start and end apart: 13, of which 7 were waited for; matrix products, arithmetic and copies ran while one was open for 24% of the time, Pallas kernels for 0%

profile of v19, /device:TPU:0, one launch (start us, length us, event | category | flops | bytes accessed | tf_op | source)
XLA Modules:
  0.0 167.2 jit_solution(15376037386491243775)
XLA Ops:
  12.9 1.7 %pad_maximum_fusion.1 = bf16[136,1024]{1,0:T(8,128)(2,1)} fusion(bf16[8,1024]{1,0:T(8,128)(2,1)S(1)} %reshape.195, bf16[128,1024]{1,0:T(8,128)(2,1)} %param.11), kind=kLoop, calls=%fused_computation.64 | loop fusion | flops 557056 | bytes 557056 | tf_op jit(solution)/shard_map/concatenate | solution.py:166
  14.6 3.1 %collective-permute-start.1 = (bf16[128,1024]{1,0:T(8,128)(2,1)}, bf16[128,1024]{1,0:T(8,128)(2,1)}, u32[]{:S(2)}, u32[]{:S(2)}) collective-permute-start(bf16[128,1024]{1,0:T(8,128)(2,1)} %param.16), channel_id=1, source_target_pairs={{0,4},{4,8},{8,12},{12,14},{14,10},{10,6},{6,2},{2,0},{1,5},{5,9},... | collective-permute-start | bytes 786440 | tf_op jit(solution)/shard_map/ppermute | solution.py:113
  23.6 1.6 fusion.69
  39.0 2.1 %collective-permute-start.3 = (bf16[128,1024]{1,0:T(8,128)(2,1)}, bf16[128,1024]{1,0:T(8,128)(2,1)S(1)}, u32[]{:S(2)}, u32[]{:S(2)}) collective-permute-start(bf16[128,1024]{1,0:T(8,128)(2,1)} %collective-permute-done.1), channel_id=1, source_target_pairs={{0,4},{4,8},{8,12},{12,14},{14,10},{10,6},{6,2},{2,0},{1,5},{5,9},... | collective-permute-start | bytes 786440 | tf_op jit(solution)/shard_map/ppermute | solution.py:113
  43.0 7.7 %collective-permute-done.3 = bf16[128,1024]{1,0:T(8,128)(2,1)S(1)} collective-permute-done((bf16[128,1024]{1,0:T(8,128)(2,1)}, bf16[128,1024]{1,0:T(8,128)(2,1)S(1)}, u32[]{:S(2)}, u32[]{:S(2)}) %collective-permute-start.3) | collective-permute-done | bytes 262176 | tf_op jit(solution)/shard_map/ppermute | solution.py:113
  50.8 4.3 %collective-permute-start.5 = (bf16[128,1024]{1,0:T(8,128)(2,1)S(1)}, bf16[128,1024]{1,0:T(8,128)(2,1)S(1)}, u32[]{:S(2)}, u32[]{:S(2)}) collective-permute-start(bf16[128,1024]{1,0:T(8,128)(2,1)S(1)} %collective-permute-done.3), channel_id=1, source_target_pairs={{0,4},{4,8},{8,12},{12,14},{14,10},{10,6},{6,2},{2,0},{1,5},{5,9},... | collective-permute-start | bytes 786440 | tf_op jit(solution)/shard_map/ppermute | solution.py:113
  55.1 2.0 %collective-permute-done.4 = bf16[128,1024]{1,0:T(8,128)(2,1)S(1)} collective-permute-done((bf16[128,1024]{1,0:T(8,128)(2,1)}, bf16[128,1024]{1,0:T(8,128)(2,1)S(1)}, u32[]{:S(2)}, u32[]{:S(2)}) %collective-permute-start.4) | collective-permute-done | bytes 262176 | tf_op jit(solution)/shard_map/ppermute | solution.py:116
  57.1 6.7 %collective-permute-done.5 = bf16[128,1024]{1,0:T(8,128)(2,1)S(1)} collective-permute-done((bf16[128,1024]{1,0:T(8,128)(2,1)S(1)}, bf16[128,1024]{1,0:T(8,128)(2,1)S(1)}, u32[]{:S(2)}, u32[]{:S(2)}) %collective-permute-start.5) | collective-permute-done | bytes 262176 | tf_op jit(solution)/shard_map/ppermute | solution.py:113
  63.8 7.0 %collective-permute-start.7 = (bf16[128,1024]{1,0:T(8,128)(2,1)S(1)}, bf16[128,1024]{1,0:T(8,128)(2,1)S(1)}, u32[]{:S(2)}, u32[]{:S(2)}) collective-permute-start(bf16[128,1024]{1,0:T(8,128)(2,1)S(1)} %collective-permute-done.5), channel_id=1, source_target_pairs={{0,4},{4,8},{8,12},{12,14},{14,10},{10,6},{6,2},{2,0},{1,5},{5,9},... | collective-permute-start | bytes 786440 | tf_op jit(solution)/shard_map/ppermute | solution.py:113
  72.0 3.4 %collective-permute-done.7 = bf16[128,1024]{1,0:T(8,128)(2,1)S(1)} collective-permute-done((bf16[128,1024]{1,0:T(8,128)(2,1)S(1)}, bf16[128,1024]{1,0:T(8,128)(2,1)S(1)}, u32[]{:S(2)}, u32[]{:S(2)}) %collective-permute-start.7) | collective-permute-done | bytes 262176 | tf_op jit(solution)/shard_map/ppermute | solution.py:113
  77.0 3.2 %fusion.5 = bf16[16,96,1024]{2,1,0:T(8,128)(2,1)S(1)} fusion(bf16[16,136,1024]{2,1,0:T(8,128)(2,1)} %bitcast.142, s32[16,128]{1,0:T(8,128)S(1)} %convolution_convert_fusion.5, pred[16,128]{1,0:T(8,128)(4,1)S(1)} %fusion.64), kind=kOutput, calls=%fused_computation.15 | convolution fusion | flops 404619264 | bytes 7350272 | tf_op jit(solution)/shard_map/sjt,std->sjd/dot_general | solution.py:190
  80.2 1.8 %fusion.27 = f32[1536,512]{1,0:T(8,128)S(1)} fusion(bf16[1536,1024]{1,0:T(8,128)(2,1)S(1)} %bitcast.143, bf16[1,512,1024]{2,1,0:T(8,128)(2,1)S(1)} %copy-done.8), kind=kOutput, calls=%fused_computation.42 | convolution fusion | flops 1610612736 | bytes 7340032 | tf_op jit(solution)/shard_map/dot_general | solution.py:16
  82.3 3.8 %multiply_convert_fusion.2 = (bf16[1536,512]{1,0:T(8,128)(2,1)S(1)}, f32[1536,512]{1,0:T(8,128)}) fusion(f32[1536,512]{1,0:T(8,128)S(1)} %fusion.27, bf16[1536,1024]{1,0:T(8,128)(2,1)S(1)} %bitcast.144, bf16[1,512,1024]{2,1,0:T(8,128)(2,1)S(1)} %copy-done.9), kind=kOutput, calls=%fused_computation.12 | convolution fusion | flops 1615331328 | bytes 12058624 | tf_op jit(solution)/shard_map/dot_general | solution.py:16
  86.1 1.8 %convolution_convert_fusion = bf16[1536,1024]{1,0:T(8,128)(2,1)S(1)} fusion(bf16[1536,512]{1,0:T(8,128)(2,1)S(1)} %get-tuple-element.21, bf16[1,512,1024]{2,1,0:T(8,128)(2,1)S(1)} %copy-done), kind=kOutput, calls=%fused_computation.8 | convolution fusion | flops 1612185600 | bytes 5767168 | tf_op jit(solution)/shard_map/dot_general | solution.py:202
  87.9 1.6 copy-done.3
  89.6 2.1 %convolution_convert_fusion.1 = bf16[8,128,1024]{2,1,0:T(8,128)(2,1)} fusion(bf16[8,2,96,1024]{3,2,1,0:T(8,128)(2,1)S(1)} %bitcast.149, s32[]{:T(128)S(6)} %select_n.146, pred[8,2,96,128]{3,2,1,0:T(32,128)(4,1)S(1)} %fusion.35), kind=kOutput, calls=%fused_computation.21 | convolution fusion | flops 202375168 | bytes 3769344 | tf_op jit(solution)/shard_map/sjt,sjd->std/dot_general | solution.py:209
  92.3 3.7 %fusion.9 = f32[8,2,96,1024]{3,2,1,0:T(8,128)} fusion(bf16[8,128,1024]{2,1,0:T(8,128)(2,1)S(1)} %bitcast_dynamic-update-slice_fusion, f32[8,128]{1,0:T(8,128)S(1)} %bitcast.169, pred[2]{0:T(512)(128)(4,1)S(1)} %iota_compare_fusion.5, s32[8,2,128]{2,1,0:T(2,128)S(1)} %bitcast.164, pred[8,2,128]{2,1,0:T(4,128)(4,1)S(1)} %and.48), kind=kOutput, calls=%fused_computation.17 | convolution fusion | flops 406585344 | bytes 8402946 | tf_op jit(solution)/shard_map/ikjt,itd->ikjd/dot_general | solution.py:241
  96.3 4.0 %add_convert_fusion.1 = bf16[8,128,1024]{2,1,0:T(8,128)(2,1)} fusion(bf16[8,128,1024]{2,1,0:T(8,128)(2,1)} %collective-permute-done, f32[8,128]{1,0:T(8,128)S(1)} %get-tuple-element.7, f32[8,128]{1,0:T(8,128)S(1)} %get-tuple-element.6, bf16[8,2,96,1024]{3,2,1,0:T(8,128)(2,1)S(1)} %bitcast.150, s32[]{:T(128)S(6)} %select_n.144, ...), kind=kOutput, calls=%fused_computation.7 | convolution fusion | flops 208666624 | bytes 5874688 | tf_op jit(solution)/shard_map/sjt,sjd->std/dot_general | solution.py:209
  100.3 9.7 %all-to-all-start = ((bf16[8,128,1024]{2,1,0:T(8,128)(2,1)}), bf16[8,128,1024]{2,1,0:T(8,128)(2,1)S(1)}, u32[]{:S(2)}, u32[]{:S(2)}) async-start(bf16[8,128,1024]{2,1,0:T(8,128)(2,1)} %add_convert_fusion.1), calls=%async_computation | async-start | bytes 4194304 | tf_op jit(solution)/shard_map/all_to_all | solution.py:228
  110.0 4.6 %add_convert_fusion = bf16[8,2,96,1024]{3,2,1,0:T(8,128)(2,1)S(1)} fusion(f32[8,2,96,1024]{3,2,1,0:T(8,128)} %fusion.9, bf16[8,128,1024]{2,1,0:T(8,128)(2,1)} %bitcast.64, f32[8,128]{1,0:T(8,128)S(1)} %bitcast.168, pred[2]{0:T(512)(128)(4,1)S(1)} %iota_compare_fusion.4, s32[8,2,128]{2,1,0:T(2,128)S(1)} %bitcast.165, pred[8,2,128]{2,1,0:T(4,128)(4,1)S(1)} %and.48), kind=kOutput, calls=%fused_computation | convolution fusion | flops 409731072 | bytes 11548674 | tf_op jit(solution)/shard_map/ikjt,itd->ikjd/dot_general | solution.py:241
  115.3 3.3 %multiply_convert_fusion.1 = (bf16[1536,512]{1,0:T(8,128)(2,1)S(1)}, bf16[1536,512]{1,0:T(8,128)(2,1)S(1)}) fusion(f32[1536,512]{1,0:T(8,128)S(1)} %copy-done.13, f32[1536,512]{1,0:T(8,128)S(1)} %copy-done.14, bf16[1536,1024]{1,0:T(8,128)(2,1)S(1)} %bitcast.151, bf16[1,512,1024]{2,1,0:T(8,128)(2,1)S(1)} %copy-done), kind=kOutput, calls=%fused_computation.11 | convolution fusion | flops 1620836352 | bytes 13631488 | tf_op jit(solution)/shard_map/dot_general | solution.py:16
  120.7 1.6 collective-permute-start.9
  126.9 30.1 %collective-permute-done.10 = bf16[256,1,1024]{2,0,1:T(8,128)(2,1)S(1)} collective-permute-done((bf16[256,1,1024]{2,0,1:T(8,128)(2,1)S(1)}, bf16[256,1,1024]{2,0,1:T(8,128)(2,1)S(1)}, u32[]{:S(2)}, u32[]{:S(2)}) %collective-permute-start.10) | collective-permute-done | bytes 524320 | tf_op jit(solution)/shard_map/ppermute | solution.py:143
  157.1 2.2 %maximum_add_fusion = f32[1,256,3,1024]{3,1,2,0:T(8,128)} fusion(f32[1,256,1,1024]{3,1,2,0:T(8,128)S(1)} %convolution_bitcast_fusion, f32[1,256,1,1024]{3,1,2,0:T(8,128)S(1)} %convolution_bitcast_fusion.1, f32[1,256,1,1024]{3,1,2,0:T(8,128)S(1)} %convolution_bitcast_fusion.2, bf16[1,256,1,1024]{3,1,2,0:T(8,128)(2,1)S(1)} %bitcast.160, ...), kind=kLoop, calls=%fused_computation.9 | loop fusion | flops 3932160 | bytes 7864320 | tf_op jit(solution)/shard_map/add | solution.py:145
  (87 shorter events, 21.4 us)
Async XLA Ops:
  7.2 78.9 %copy-start = (bf16[1,512,1024]{2,1,0:T(8,128)(2,1)S(1)}, bf16[1,512,1024]{2,1,0:T(8,128)(2,1)}, u32[]{:S(2)}) copy-start(bf16[1,512,1024]{2,1,0:T(8,128)(2,1)} %param.19) | copy-start | bytes 3145732
  7.2 31.8 %copy-start.7 = (bf16[128,1024]{1,0:T(8,128)(2,1)S(1)}, bf16[128,1024]{1,0:T(8,128)(2,1)}, u32[]{:S(2)}) copy-start(bf16[128,1024]{1,0:T(8,128)(2,1)} %param.16) | copy-start | bytes 786436
  7.2 68.4 %all-gather.2.cloned.1.call-start = ((), (), s32[]{:S(2)}) async-start(), calls=%async_computation.1 | async-start | bytes 4734976 | tf_op jit(solution)/shard_map/all_gather | solution.py:168
  14.6 24.3 %collective-permute-start.1 = (bf16[128,1024]{1,0:T(8,128)(2,1)}, bf16[128,1024]{1,0:T(8,128)(2,1)}, u32[]{:S(2)}, u32[]{:S(2)}) collective-permute-start(bf16[128,1024]{1,0:T(8,128)(2,1)} %param.16), channel_id=1, source_target_pairs={{0,4},{4,8},{8,12},{12,14},{14,10},{10,6},{6,2},{2,0},{1,5},{5,9},... | collective-permute-start | bytes 786440 | tf_op jit(solution)/shard_map/ppermute | solution.py:113
  17.7 23.4 %collective-permute-start.2 = (bf16[128,1024]{1,0:T(8,128)(2,1)}, bf16[128,1024]{1,0:T(8,128)(2,1)}, u32[]{:S(2)}, u32[]{:S(2)}) collective-permute-start(bf16[128,1024]{1,0:T(8,128)(2,1)} %param.16), channel_id=1, source_target_pairs={{0,2},{4,0},{8,4},{12,8},{14,12},{10,14},{6,10},{2,6},{1,3},{5,1},... | collective-permute-start | bytes 786440 | tf_op jit(solution)/shard_map/ppermute | solution.py:116
  39.0 11.8 %collective-permute-start.3 = (bf16[128,1024]{1,0:T(8,128)(2,1)}, bf16[128,1024]{1,0:T(8,128)(2,1)S(1)}, u32[]{:S(2)}, u32[]{:S(2)}) collective-permute-start(bf16[128,1024]{1,0:T(8,128)(2,1)} %collective-permute-done.1), channel_id=1, source_target_pairs={{0,4},{4,8},{8,12},{12,14},{14,10},{10,6},{6,2},{2,0},{1,5},{5,9},... | collective-permute-start | bytes 786440 | tf_op jit(solution)/shard_map/ppermute | solution.py:113
  41.1 16.0 %collective-permute-start.4 = (bf16[128,1024]{1,0:T(8,128)(2,1)}, bf16[128,1024]{1,0:T(8,128)(2,1)S(1)}, u32[]{:S(2)}, u32[]{:S(2)}) collective-permute-start(bf16[128,1024]{1,0:T(8,128)(2,1)} %collective-permute-done.2), channel_id=1, source_target_pairs={{0,2},{4,0},{8,4},{12,8},{14,12},{10,14},{6,10},{2,6},{1,3},{5,1},... | collective-permute-start | bytes 786440 | tf_op jit(solution)/shard_map/ppermute | solution.py:116
  50.8 13.0 %collective-permute-start.5 = (bf16[128,1024]{1,0:T(8,128)(2,1)S(1)}, bf16[128,1024]{1,0:T(8,128)(2,1)S(1)}, u32[]{:S(2)}, u32[]{:S(2)}) collective-permute-start(bf16[128,1024]{1,0:T(8,128)(2,1)S(1)} %collective-permute-done.3), channel_id=1, source_target_pairs={{0,4},{4,8},{8,12},{12,14},{14,10},{10,6},{6,2},{2,0},{1,5},{5,9},... | collective-permute-start | bytes 786440 | tf_op jit(solution)/shard_map/ppermute | solution.py:113
  57.0 15.0 %collective-permute-start.6 = (bf16[128,1024]{1,0:T(8,128)(2,1)S(1)}, bf16[128,1024]{1,0:T(8,128)(2,1)S(1)}, u32[]{:S(2)}, u32[]{:S(2)}) collective-permute-start(bf16[128,1024]{1,0:T(8,128)(2,1)S(1)} %collective-permute-done.4), channel_id=1, source_target_pairs={{0,2},{4,0},{8,4},{12,8},{14,12},{10,14},{6,10},{2,6},{1,3},{5,1},... | collective-permute-start | bytes 786440 | tf_op jit(solution)/shard_map/ppermute | solution.py:116
  63.8 11.6 %collective-permute-start.7 = (bf16[128,1024]{1,0:T(8,128)(2,1)S(1)}, bf16[128,1024]{1,0:T(8,128)(2,1)S(1)}, u32[]{:S(2)}, u32[]{:S(2)}) collective-permute-start(bf16[128,1024]{1,0:T(8,128)(2,1)S(1)} %collective-permute-done.5), channel_id=1, source_target_pairs={{0,4},{4,8},{8,12},{12,14},{14,10},{10,6},{6,2},{2,0},{1,5},{5,9},... | collective-permute-start | bytes 786440 | tf_op jit(solution)/shard_map/ppermute | solution.py:113
  75.4 16.7 %collective-permute-start.8 = (bf16[1024,1024]{1,0:T(8,128)(2,1)S(1)}, bf16[1024,1024]{1,0:T(8,128)(2,1)}, u32[]{:S(2)}, u32[]{:S(2)}) collective-permute-start(bf16[1024,1024]{1,0:T(8,128)(2,1)S(1)} %bitcast.140), channel_id=1, source_target_pairs={{0,1},{1,0},{2,3},{3,2},{4,5},{5,4},{6,7},{7,6},{8,9},{9,8},{10,11... | collective-permute-start | bytes 6291464 | tf_op jit(solution)/shard_map/ppermute | solution.py:119
  76.9 3.3 %copy-start.8 = (bf16[1,512,1024]{2,1,0:T(8,128)(2,1)S(1)}, bf16[1,512,1024]{2,1,0:T(8,128)(2,1)}, u32[]{:S(2)}) copy-start(bf16[1,512,1024]{2,1,0:T(8,128)(2,1)} %param.17) | copy-start | bytes 3145732
  82.1 4.0 %copy-start.12 = (f32[1536,512]{1,0:T(8,128)}, f32[1536,512]{1,0:T(8,128)S(1)}, u32[]{:S(2)}) copy-start(f32[1536,512]{1,0:T(8,128)S(1)} %fusion.27) | copy-start | bytes 9437188
  82.3 5.7 %copy-start.5 = (pred[8,2,96,128]{3,2,1,0:T(32,128)(4,1)}, pred[8,2,96,128]{3,2,1,0:T(32,128)(4,1)S(1)}, u32[]{:S(2)}) copy-start(pred[8,2,96,128]{3,2,1,0:T(32,128)(4,1)S(1)} %fusion.35) | copy-start | bytes 589828
  91.7 4.6 %collective-permute-start = (bf16[8,128,1024]{2,1,0:T(8,128)(2,1)}, bf16[8,128,1024]{2,1,0:T(8,128)(2,1)}, u32[]{:S(2)}, u32[]{:S(2)}) collective-permute-start(bf16[8,128,1024]{2,1,0:T(8,128)(2,1)} %convolution_convert_fusion.1), channel_id=1, source_target_pairs={{0,1},{1,0},{2,3},{3,2},{4,5},{5,4},{6,7},{7,6},{8,9},{9,8},{10,11... | collective-permute-start | bytes 6291464 | tf_op jit(solution)/shard_map/ppermute | solution.py:216
  92.3 4.0 %copy-start.4 = (bf16[1536,1024]{1,0:T(8,128)(2,1)S(1)}, bf16[1536,1024]{1,0:T(8,128)(2,1)}, u32[]{:S(2)}) copy-start(bf16[1536,1024]{1,0:T(8,128)(2,1)} %copy-done.3) | copy-start | bytes 9437188
  92.3 4.0 %copy-start.6 = (pred[8,2,96,128]{3,2,1,0:T(32,128)(4,1)S(1)}, pred[8,2,96,128]{3,2,1,0:T(32,128)(4,1)}, u32[]{:S(2)}) copy-start(pred[8,2,96,128]{3,2,1,0:T(32,128)(4,1)} %copy-done.5) | copy-start | bytes 589828
  100.3 59.0 %all-to-all-start = ((bf16[8,128,1024]{2,1,0:T(8,128)(2,1)}), bf16[8,128,1024]{2,1,0:T(8,128)(2,1)S(1)}, u32[]{:S(2)}, u32[]{:S(2)}) async-start(bf16[8,128,1024]{2,1,0:T(8,128)(2,1)} %add_convert_fusion.1), calls=%async_computation | async-start | bytes 4194304 | tf_op jit(solution)/shard_map/all_to_all | solution.py:228
  110.0 4.7 %copy-start.13 = (f32[1536,512]{1,0:T(8,128)S(1)}, f32[1536,512]{1,0:T(8,128)}, u32[]{:S(2)}) copy-start(f32[1536,512]{1,0:T(8,128)} %copy-done.12) | copy-start | bytes 9437188
  110.0 5.3 %copy-start.14 = (f32[1536,512]{1,0:T(8,128)S(1)}, f32[1536,512]{1,0:T(8,128)}, u32[]{:S(2)}) copy-start(f32[1536,512]{1,0:T(8,128)} %get-tuple-element.22) | copy-start | bytes 9437188
  115.2 3.3 %copy-start.2 = (bf16[16,96,1024]{2,1,0:T(8,128)(2,1)S(1)}, bf16[16,96,1024]{2,1,0:T(8,128)(2,1)}, u32[]{:S(2)}) copy-start(bf16[16,96,1024]{2,1,0:T(8,128)(2,1)} %copy-done.1) | copy-start | bytes 9437188
  119.6 2.8 %copy-start.11 = (bf16[1536,512]{1,0:T(8,128)(2,1)S(1)}, bf16[1536,512]{1,0:T(8,128)(2,1)}, u32[]{:S(2)}) copy-start(bf16[1536,512]{1,0:T(8,128)(2,1)} %copy-done.10) | copy-start | bytes 4718596
  120.7 36.3 %collective-permute-start.9 = (bf16[256,2,1024]{2,0,1:T(8,128)(2,1)S(1)}, bf16[256,2,1024]{2,0,1:T(8,128)(2,1)S(1)}, u32[]{:S(2)}, u32[]{:S(2)}) collective-permute-start(bf16[256,2,1024]{2,0,1:T(8,128)(2,1)S(1)} %pad_maximum_fusion), channel_id=1, source_target_pairs={{0,16},{16,0},{1,17},{17,1},{2,18},{18,2},{3,19},{19,3},{4,20},{20... | collective-permute-start | bytes 3145736 | tf_op jit(solution)/shard_map/ppermute | solution.py:142
  123.4 33.7 %collective-permute-start.10 = (bf16[256,1,1024]{2,0,1:T(8,128)(2,1)S(1)}, bf16[256,1,1024]{2,0,1:T(8,128)(2,1)S(1)}, u32[]{:S(2)}, u32[]{:S(2)}) collective-permute-start(bf16[256,1,1024]{2,0,1:T(8,128)(2,1)S(1)} %fusion.21), channel_id=1, source_target_pairs={{0,16},{16,0},{1,17},{17,1},{2,18},{18,2},{3,19},{19,3},{4,20},{20... | collective-permute-start | bytes 1572872 | tf_op jit(solution)/shard_map/ppermute | solution.py:143
  (4 other events, 7.5 us)
Sparse Core Ops, SparseCore 0:
  14.7 58.3 all-gather.1

commit v20 on v19

--- a/solution.py
+++ b/solution.py
@@ -139,8 +139,8 @@
     d = lax.axis_index("dp")
     theirs = grad_half(1 - d)
     sent = [
-        lax.ppermute(theirs[:, :2].astype(jnp.bfloat16), "dp", [(0, 1), (1, 0)]),
-        lax.ppermute(theirs[:, 2:].astype(jnp.bfloat16), "dp", [(0, 1), (1, 0)]),
+        lax.ppermute(theirs[:, i:i + 1].astype(jnp.bfloat16), "dp", [(0, 1), (1, 0)])
+        for i in range(theirs.shape[1])
     ]
     summed = grad_half(d) + jnp.concatenate(sent, axis=1).astype(jnp.float32)
     return summed.reshape(1, summed.shape[0], 3, width)

time: 168 us -> 167 us (level)
    ppermute x2 -> x3, waiting for transfers between devices: 30.1 us -> 24.2 us  [reduce_grads_dp(): lax.ppermute(theirs[:, i:i + 1].astype(jnp.bfloat16), 'dp', [(0, 1), (1,...]
    all_to_all x1, waiting for transfers between devices: 0.01 us -> 4.41 us  [local_gather(): returned = lax.all_to_all(combined, 'ez', 0, 0, tiled=True)]
    ppermute x2 -> x3, starting transfers between devices: 2.13 us -> 3.77 us  [reduce_grads_dp(): lax.ppermute(theirs[:, i:i + 1].astype(jnp.bfloat16), 'dp', [(0, 1), (1,...]
  transfers between devices with their start and end apart: 13 -> 14, of which waited for: 7 -> 10; matrix products, arithmetic and copies ran while one was open for 24% -> 24% of each run, Pallas kernels for 0% -> 0%
where the time goes in v20:
time: 167 us
  waiting for transfers between devices  50.2 us (30%)
  matrix products  34.6 us (21%)
  between operations  32.4 us (19%)
  starting transfers between devices  30.3 us (18%)
  other arithmetic  10.9 us (7%)
  local copies, waits for them, and re-layouts  8.12 us (5%)
    ppermute x3, waiting for transfers between devices, reduce_grads_dp(): lax.ppermute(theirs[:, i:i + 1].astype(jnp.bfloat16), 'dp', [(0, 1), (1,...  24.2 us
    ppermute x4, waiting for transfers between devices, ring_gather(): up = lax.ppermute(up, 'ez', ahead)  17.8 us
    ppermute x4, starting transfers between devices, ring_gather(): up = lax.ppermute(up, 'ez', ahead)  16.1 us
    all_to_all x1, starting transfers between devices, local_gather(): returned = lax.all_to_all(combined, 'ez', 0, 0, tiled=True)  9.8 us
    dot_general x3, matrix products, contract_cols(): lax.dot_general(left, right, (((1,), (1,)), ((), ())), preferred_element_...  8.93 us
    dot_general x2, matrix products, local_gather(): jnp.einsum('ikjt,itd->ikjd', masked_pick, scaled.astype(jnp.bfloat16), pr...  8.34 us
    dot_general x6, matrix products, contract_rows(): lax.dot_general(left, right, (((0,), (0,)), ((), ())), preferred_element_...  6.08 us
    dot_general x2, matrix products, dense_for(): jnp.einsum('sjt,sjd->std', lax.dynamic_index_in_dim(pick_k, k, 1, keepdim...  6.08 us
  transfers between devices with their start and end apart: 14, of which 10 were waited for; matrix products, arithmetic and copies ran while one was open for 24% of the time, Pallas kernels for 0%

profile of v20, /device:TPU:0, one launch (start us, length us, event | category | flops | bytes accessed | tf_op | source)
XLA Modules:
  0.0 166.5 jit_solution(8722408739812350418)
XLA Ops:
  12.9 1.7 %pad_maximum_fusion = bf16[136,1024]{1,0:T(8,128)(2,1)} fusion(bf16[8,1024]{1,0:T(8,128)(2,1)S(1)} %reshape.210, bf16[128,1024]{1,0:T(8,128)(2,1)} %param.11), kind=kLoop, calls=%fused_computation.63 | loop fusion | flops 557056 | bytes 557056 | tf_op jit(solution)/shard_map/concatenate | solution.py:166
  14.6 3.1 %collective-permute-start.1 = (bf16[128,1024]{1,0:T(8,128)(2,1)}, bf16[128,1024]{1,0:T(8,128)(2,1)}, u32[]{:S(2)}, u32[]{:S(2)}) collective-permute-start(bf16[128,1024]{1,0:T(8,128)(2,1)} %param.16), channel_id=1, source_target_pairs={{0,4},{4,8},{8,12},{12,14},{14,10},{10,6},{6,2},{2,0},{1,5},{5,9},... | collective-permute-start | bytes 786440 | tf_op jit(solution)/shard_map/ppermute | solution.py:113
  38.8 2.1 %collective-permute-start.3 = (bf16[128,1024]{1,0:T(8,128)(2,1)}, bf16[128,1024]{1,0:T(8,128)(2,1)S(1)}, u32[]{:S(2)}, u32[]{:S(2)}) collective-permute-start(bf16[128,1024]{1,0:T(8,128)(2,1)} %collective-permute-done.1), channel_id=1, source_target_pairs={{0,4},{4,8},{8,12},{12,14},{14,10},{10,6},{6,2},{2,0},{1,5},{5,9},... | collective-permute-start | bytes 786440 | tf_op jit(solution)/shard_map/ppermute | solution.py:113
  42.9 7.5 %collective-permute-done.3 = bf16[128,1024]{1,0:T(8,128)(2,1)S(1)} collective-permute-done((bf16[128,1024]{1,0:T(8,128)(2,1)}, bf16[128,1024]{1,0:T(8,128)(2,1)S(1)}, u32[]{:S(2)}, u32[]{:S(2)}) %collective-permute-start.3) | collective-permute-done | bytes 262176 | tf_op jit(solution)/shard_map/ppermute | solution.py:113
  50.4 3.8 %collective-permute-start.5 = (bf16[128,1024]{1,0:T(8,128)(2,1)S(1)}, bf16[128,1024]{1,0:T(8,128)(2,1)S(1)}, u32[]{:S(2)}, u32[]{:S(2)}) collective-permute-start(bf16[128,1024]{1,0:T(8,128)(2,1)S(1)} %collective-permute-done.3), channel_id=1, source_target_pairs={{0,4},{4,8},{8,12},{12,14},{14,10},{10,6},{6,2},{2,0},{1,5},{5,9},... | collective-permute-start | bytes 786440 | tf_op jit(solution)/shard_map/ppermute | solution.py:113
  54.1 2.2 %collective-permute-done.4 = bf16[128,1024]{1,0:T(8,128)(2,1)S(1)} collective-permute-done((bf16[128,1024]{1,0:T(8,128)(2,1)}, bf16[128,1024]{1,0:T(8,128)(2,1)S(1)}, u32[]{:S(2)}, u32[]{:S(2)}) %collective-permute-start.4) | collective-permute-done | bytes 262176 | tf_op jit(solution)/shard_map/ppermute | solution.py:116
  56.4 7.0 %collective-permute-done.5 = bf16[128,1024]{1,0:T(8,128)(2,1)S(1)} collective-permute-done((bf16[128,1024]{1,0:T(8,128)(2,1)S(1)}, bf16[128,1024]{1,0:T(8,128)(2,1)S(1)}, u32[]{:S(2)}, u32[]{:S(2)}) %collective-permute-start.5) | collective-permute-done | bytes 262176 | tf_op jit(solution)/shard_map/ppermute | solution.py:113
  63.4 7.2 %collective-permute-start.7 = (bf16[128,1024]{1,0:T(8,128)(2,1)S(1)}, bf16[128,1024]{1,0:T(8,128)(2,1)S(1)}, u32[]{:S(2)}, u32[]{:S(2)}) collective-permute-start(bf16[128,1024]{1,0:T(8,128)(2,1)S(1)} %collective-permute-done.5), channel_id=1, source_target_pairs={{0,4},{4,8},{8,12},{12,14},{14,10},{10,6},{6,2},{2,0},{1,5},{5,9},... | collective-permute-start | bytes 786440 | tf_op jit(solution)/shard_map/ppermute | solution.py:113
  71.9 3.4 %collective-permute-done.7 = bf16[128,1024]{1,0:T(8,128)(2,1)S(1)} collective-permute-done((bf16[128,1024]{1,0:T(8,128)(2,1)S(1)}, bf16[128,1024]{1,0:T(8,128)(2,1)S(1)}, u32[]{:S(2)}, u32[]{:S(2)}) %collective-permute-start.7) | collective-permute-done | bytes 262176 | tf_op jit(solution)/shard_map/ppermute | solution.py:113
  76.8 3.2 %fusion.5 = bf16[16,96,1024]{2,1,0:T(8,128)(2,1)S(1)} fusion(bf16[16,136,1024]{2,1,0:T(8,128)(2,1)} %bitcast.143, s32[16,128]{1,0:T(8,128)S(1)} %convolution_convert_fusion.5, pred[16,128]{1,0:T(8,128)(4,1)S(1)} %fusion.64), kind=kOutput, calls=%fused_computation.15 | convolution fusion | flops 404619264 | bytes 7350272 | tf_op jit(solution)/shard_map/sjt,std->sjd/dot_general | solution.py:190
  80.1 1.8 %fusion.27 = f32[1536,512]{1,0:T(8,128)S(1)} fusion(bf16[1536,1024]{1,0:T(8,128)(2,1)S(1)} %bitcast.144, bf16[1,512,1024]{2,1,0:T(8,128)(2,1)S(1)} %copy-done.8), kind=kOutput, calls=%fused_computation.41 | convolution fusion | flops 1610612736 | bytes 7340032 | tf_op jit(solution)/shard_map/dot_general | solution.py:16
  82.1 3.8 %multiply_convert_fusion.2 = (bf16[1536,512]{1,0:T(8,128)(2,1)S(1)}, f32[1536,512]{1,0:T(8,128)}) fusion(f32[1536,512]{1,0:T(8,128)S(1)} %fusion.27, bf16[1536,1024]{1,0:T(8,128)(2,1)S(1)} %bitcast.145, bf16[1,512,1024]{2,1,0:T(8,128)(2,1)S(1)} %copy-done.9), kind=kOutput, calls=%fused_computation.12 | convolution fusion | flops 1615331328 | bytes 12058624 | tf_op jit(solution)/shard_map/dot_general | solution.py:16
  86.0 1.8 %convolution_convert_fusion = bf16[1536,1024]{1,0:T(8,128)(2,1)S(1)} fusion(bf16[1536,512]{1,0:T(8,128)(2,1)S(1)} %get-tuple-element.21, bf16[1,512,1024]{2,1,0:T(8,128)(2,1)S(1)} %copy-done), kind=kOutput, calls=%fused_computation.8 | convolution fusion | flops 1612185600 | bytes 5767168 | tf_op jit(solution)/shard_map/dot_general | solution.py:202
  89.4 2.1 %convolution_convert_fusion.1 = bf16[8,128,1024]{2,1,0:T(8,128)(2,1)} fusion(bf16[8,2,96,1024]{3,2,1,0:T(8,128)(2,1)S(1)} %bitcast.150, s32[]{:T(128)S(6)} %select_n.146, pred[8,2,96,128]{3,2,1,0:T(32,128)(4,1)S(1)} %fusion.35), kind=kOutput, calls=%fused_computation.21 | convolution fusion | flops 202375168 | bytes 3769344 | tf_op jit(solution)/shard_map/sjt,sjd->std/dot_general | solution.py:209
  92.2 3.7 %fusion.9 = f32[8,2,96,1024]{3,2,1,0:T(8,128)} fusion(bf16[8,128,1024]{2,1,0:T(8,128)(2,1)S(1)} %bitcast_dynamic-update-slice_fusion, f32[8,128]{1,0:T(8,128)S(1)} %bitcast.171, pred[2]{0:T(512)(128)(4,1)S(1)} %iota_compare_fusion.5, s32[8,2,128]{2,1,0:T(2,128)S(1)} %bitcast.166, pred[8,2,128]{2,1,0:T(4,128)(4,1)S(1)} %and.48), kind=kOutput, calls=%fused_computation.17 | convolution fusion | flops 406585344 | bytes 8402946 | tf_op jit(solution)/shard_map/ikjt,itd->ikjd/dot_general | solution.py:241
  96.1 4.0 %add_convert_fusion.1 = bf16[8,128,1024]{2,1,0:T(8,128)(2,1)} fusion(bf16[8,128,1024]{2,1,0:T(8,128)(2,1)} %collective-permute-done, f32[8,128]{1,0:T(8,128)S(1)} %get-tuple-element.7, f32[8,128]{1,0:T(8,128)S(1)} %get-tuple-element.6, bf16[8,2,96,1024]{3,2,1,0:T(8,128)(2,1)S(1)} %bitcast.151, s32[]{:T(128)S(6)} %select_n.144, ...), kind=kOutput, calls=%fused_computation.7 | convolution fusion | flops 208666624 | bytes 5874688 | tf_op jit(solution)/shard_map/sjt,sjd->std/dot_general | solution.py:209
  100.1 9.8 %all-to-all-start = ((bf16[8,128,1024]{2,1,0:T(8,128)(2,1)}), bf16[8,128,1024]{2,1,0:T(8,128)(2,1)S(1)}, u32[]{:S(2)}, u32[]{:S(2)}) async-start(bf16[8,128,1024]{2,1,0:T(8,128)(2,1)} %add_convert_fusion.1), calls=%async_computation | async-start | bytes 4194304 | tf_op jit(solution)/shard_map/all_to_all | solution.py:228
  109.9 4.6 %add_convert_fusion = bf16[8,2,96,1024]{3,2,1,0:T(8,128)(2,1)S(1)} fusion(f32[8,2,96,1024]{3,2,1,0:T(8,128)} %fusion.9, bf16[8,128,1024]{2,1,0:T(8,128)(2,1)} %bitcast.65, f32[8,128]{1,0:T(8,128)S(1)} %bitcast.170, pred[2]{0:T(512)(128)(4,1)S(1)} %iota_compare_fusion.4, s32[8,2,128]{2,1,0:T(2,128)S(1)} %bitcast.167, pred[8,2,128]{2,1,0:T(4,128)(4,1)S(1)} %and.48), kind=kOutput, calls=%fused_computation | convolution fusion | flops 409731072 | bytes 11548674 | tf_op jit(solution)/shard_map/ikjt,itd->ikjd/dot_general | solution.py:241
  117.2 3.3 %multiply_convert_fusion.1 = (bf16[1536,512]{1,0:T(8,128)(2,1)S(1)}, bf16[1536,512]{1,0:T(8,128)(2,1)S(1)}) fusion(f32[1536,512]{1,0:T(8,128)S(1)} %copy-done.13, f32[1536,512]{1,0:T(8,128)S(1)} %copy-done.14, bf16[1536,1024]{1,0:T(8,128)(2,1)S(1)} %bitcast.153, bf16[1,512,1024]{2,1,0:T(8,128)(2,1)S(1)} %copy-done), kind=kOutput, calls=%fused_computation.11 | convolution fusion | flops 1620836352 | bytes 13631488 | tf_op jit(solution)/shard_map/dot_general | solution.py:16
  127.8 2.7 %collective-permute-done.11 = bf16[256,1,1024]{2,0,1:T(8,128)(2,1)S(1)} collective-permute-done((bf16[256,1,1024]{2,0,1:T(8,128)(2,1)S(1)}, bf16[256,1,1024]{2,0,1:T(8,128)(2,1)S(1)}, u32[]{:S(2)}, u32[]{:S(2)}) %collective-permute-start.11) | collective-permute-done | bytes 524320 | tf_op jit(solution)/shard_map/ppermute | solution.py:142
  130.5 11.2 %collective-permute-done.10 = bf16[256,1,1024]{2,0,1:T(8,128)(2,1)S(1)} collective-permute-done((bf16[256,1,1024]{2,0,1:T(8,128)(2,1)S(1)}, bf16[256,1,1024]{2,0,1:T(8,128)(2,1)S(1)}, u32[]{:S(2)}, u32[]{:S(2)}) %collective-permute-start.10) | collective-permute-done | bytes 524320 | tf_op jit(solution)/shard_map/ppermute | solution.py:142
  141.7 10.3 %collective-permute-done.9 = bf16[256,1,1024]{2,0,1:T(8,128)(2,1)S(1)} collective-permute-done((bf16[256,1,1024]{2,0,1:T(8,128)(2,1)S(1)}, bf16[256,1,1024]{2,0,1:T(8,128)(2,1)S(1)}, u32[]{:S(2)}, u32[]{:S(2)}) %collective-permute-start.9) | collective-permute-done | bytes 524320 | tf_op jit(solution)/shard_map/ppermute | solution.py:142
  152.0 2.2 %maximum_add_fusion = f32[1,256,3,1024]{3,1,2,0:T(8,128)} fusion(f32[1,256,1,1024]{3,1,2,0:T(8,128)S(1)} %convolution_bitcast_fusion, f32[1,256,1,1024]{3,1,2,0:T(8,128)S(1)} %convolution_bitcast_fusion.1, f32[1,256,1,1024]{3,1,2,0:T(8,128)S(1)} %convolution_bitcast_fusion.2, bf16[1,256,1,1024]{3,1,2,0:T(8,128)(2,1)S(1)} %bitcast.160, ...), kind=kLoop, calls=%fused_computation.9 | loop fusion | flops 4718592 | bytes 7864320 | tf_op jit(solution)/shard_map/add | solution.py:145
  154.2 4.4 %all-to-all-done = bf16[8,128,1024]{2,1,0:T(8,128)(2,1)S(1)} async-done(((bf16[8,128,1024]{2,1,0:T(8,128)(2,1)}), bf16[8,128,1024]{2,1,0:T(8,128)(2,1)S(1)}, u32[]{:S(2)}, u32[]{:S(2)}) %all-to-all-start) | async-done | bytes 2097184 | tf_op jit(solution)/shard_map/all_to_all | solution.py:228
  (88 shorter events, 27.2 us)
Async XLA Ops:
  7.2 78.8 %copy-start = (bf16[1,512,1024]{2,1,0:T(8,128)(2,1)S(1)}, bf16[1,512,1024]{2,1,0:T(8,128)(2,1)}, u32[]{:S(2)}) copy-start(bf16[1,512,1024]{2,1,0:T(8,128)(2,1)} %param.19) | copy-start | bytes 3145732
  7.2 31.6 %copy-start.7 = (bf16[128,1024]{1,0:T(8,128)(2,1)S(1)}, bf16[128,1024]{1,0:T(8,128)(2,1)}, u32[]{:S(2)}) copy-start(bf16[128,1024]{1,0:T(8,128)(2,1)} %param.16) | copy-start | bytes 786436
  7.2 68.2 %all-gather.2.cloned.1.call-start = ((), (), s32[]{:S(2)}) async-start(), calls=%async_computation.1 | async-start | bytes 4734976 | tf_op jit(solution)/shard_map/all_gather | solution.py:168
  14.6 24.2 %collective-permute-start.1 = (bf16[128,1024]{1,0:T(8,128)(2,1)}, bf16[128,1024]{1,0:T(8,128)(2,1)}, u32[]{:S(2)}, u32[]{:S(2)}) collective-permute-start(bf16[128,1024]{1,0:T(8,128)(2,1)} %param.16), channel_id=1, source_target_pairs={{0,4},{4,8},{8,12},{12,14},{14,10},{10,6},{6,2},{2,0},{1,5},{5,9},... | collective-permute-start | bytes 786440 | tf_op jit(solution)/shard_map/ppermute | solution.py:113
  17.7 23.2 %collective-permute-start.2 = (bf16[128,1024]{1,0:T(8,128)(2,1)}, bf16[128,1024]{1,0:T(8,128)(2,1)}, u32[]{:S(2)}, u32[]{:S(2)}) collective-permute-start(bf16[128,1024]{1,0:T(8,128)(2,1)} %param.16), channel_id=1, source_target_pairs={{0,2},{4,0},{8,4},{12,8},{14,12},{10,14},{6,10},{2,6},{1,3},{5,1},... | collective-permute-start | bytes 786440 | tf_op jit(solution)/shard_map/ppermute | solution.py:116
  38.8 11.5 %collective-permute-start.3 = (bf16[128,1024]{1,0:T(8,128)(2,1)}, bf16[128,1024]{1,0:T(8,128)(2,1)S(1)}, u32[]{:S(2)}, u32[]{:S(2)}) collective-permute-start(bf16[128,1024]{1,0:T(8,128)(2,1)} %collective-permute-done.1), channel_id=1, source_target_pairs={{0,4},{4,8},{8,12},{12,14},{14,10},{10,6},{6,2},{2,0},{1,5},{5,9},... | collective-permute-start | bytes 786440 | tf_op jit(solution)/shard_map/ppermute | solution.py:113
  40.9 15.4 %collective-permute-start.4 = (bf16[128,1024]{1,0:T(8,128)(2,1)}, bf16[128,1024]{1,0:T(8,128)(2,1)S(1)}, u32[]{:S(2)}, u32[]{:S(2)}) collective-permute-start(bf16[128,1024]{1,0:T(8,128)(2,1)} %collective-permute-done.2), channel_id=1, source_target_pairs={{0,2},{4,0},{8,4},{12,8},{14,12},{10,14},{6,10},{2,6},{1,3},{5,1},... | collective-permute-start | bytes 786440 | tf_op jit(solution)/shard_map/ppermute | solution.py:116
  50.4 13.0 %collective-permute-start.5 = (bf16[128,1024]{1,0:T(8,128)(2,1)S(1)}, bf16[128,1024]{1,0:T(8,128)(2,1)S(1)}, u32[]{:S(2)}, u32[]{:S(2)}) collective-permute-start(bf16[128,1024]{1,0:T(8,128)(2,1)S(1)} %collective-permute-done.3), channel_id=1, source_target_pairs={{0,4},{4,8},{8,12},{12,14},{14,10},{10,6},{6,2},{2,0},{1,5},{5,9},... | collective-permute-start | bytes 786440 | tf_op jit(solution)/shard_map/ppermute | solution.py:113
  56.3 15.5 %collective-permute-start.6 = (bf16[128,1024]{1,0:T(8,128)(2,1)S(1)}, bf16[128,1024]{1,0:T(8,128)(2,1)S(1)}, u32[]{:S(2)}, u32[]{:S(2)}) collective-permute-start(bf16[128,1024]{1,0:T(8,128)(2,1)S(1)} %collective-permute-done.4), channel_id=1, source_target_pairs={{0,2},{4,0},{8,4},{12,8},{14,12},{10,14},{6,10},{2,6},{1,3},{5,1},... | collective-permute-start | bytes 786440 | tf_op jit(solution)/shard_map/ppermute | solution.py:116
  63.4 11.9 %collective-permute-start.7 = (bf16[128,1024]{1,0:T(8,128)(2,1)S(1)}, bf16[128,1024]{1,0:T(8,128)(2,1)S(1)}, u32[]{:S(2)}, u32[]{:S(2)}) collective-permute-start(bf16[128,1024]{1,0:T(8,128)(2,1)S(1)} %collective-permute-done.5), channel_id=1, source_target_pairs={{0,4},{4,8},{8,12},{12,14},{14,10},{10,6},{6,2},{2,0},{1,5},{5,9},... | collective-permute-start | bytes 786440 | tf_op jit(solution)/shard_map/ppermute | solution.py:113
  75.3 16.7 %collective-permute-start.8 = (bf16[1024,1024]{1,0:T(8,128)(2,1)S(1)}, bf16[1024,1024]{1,0:T(8,128)(2,1)}, u32[]{:S(2)}, u32[]{:S(2)}) collective-permute-start(bf16[1024,1024]{1,0:T(8,128)(2,1)S(1)} %bitcast.141), channel_id=1, source_target_pairs={{0,1},{1,0},{2,3},{3,2},{4,5},{5,4},{6,7},{7,6},{8,9},{9,8},{10,11... | collective-permute-start | bytes 6291464 | tf_op jit(solution)/shard_map/ppermute | solution.py:119
  76.8 3.3 %copy-start.8 = (bf16[1,512,1024]{2,1,0:T(8,128)(2,1)S(1)}, bf16[1,512,1024]{2,1,0:T(8,128)(2,1)}, u32[]{:S(2)}) copy-start(bf16[1,512,1024]{2,1,0:T(8,128)(2,1)} %param.17) | copy-start | bytes 3145732
  81.9 4.0 %copy-start.12 = (f32[1536,512]{1,0:T(8,128)}, f32[1536,512]{1,0:T(8,128)S(1)}, u32[]{:S(2)}) copy-start(f32[1536,512]{1,0:T(8,128)S(1)} %fusion.27) | copy-start | bytes 9437188
  82.1 5.7 %copy-start.5 = (pred[8,2,96,128]{3,2,1,0:T(32,128)(4,1)}, pred[8,2,96,128]{3,2,1,0:T(32,128)(4,1)S(1)}, u32[]{:S(2)}) copy-start(pred[8,2,96,128]{3,2,1,0:T(32,128)(4,1)S(1)} %fusion.35) | copy-start | bytes 589828
  91.5 4.6 %collective-permute-start = (bf16[8,128,1024]{2,1,0:T(8,128)(2,1)}, bf16[8,128,1024]{2,1,0:T(8,128)(2,1)}, u32[]{:S(2)}, u32[]{:S(2)}) collective-permute-start(bf16[8,128,1024]{2,1,0:T(8,128)(2,1)} %convolution_convert_fusion.1), channel_id=1, source_target_pairs={{0,1},{1,0},{2,3},{3,2},{4,5},{5,4},{6,7},{7,6},{8,9},{9,8},{10,11... | collective-permute-start | bytes 6291464 | tf_op jit(solution)/shard_map/ppermute | solution.py:216
  92.2 4.0 %copy-start.4 = (bf16[1536,1024]{1,0:T(8,128)(2,1)S(1)}, bf16[1536,1024]{1,0:T(8,128)(2,1)}, u32[]{:S(2)}) copy-start(bf16[1536,1024]{1,0:T(8,128)(2,1)} %copy-done.3) | copy-start | bytes 9437188
  92.2 4.0 %copy-start.6 = (pred[8,2,96,128]{3,2,1,0:T(32,128)(4,1)S(1)}, pred[8,2,96,128]{3,2,1,0:T(32,128)(4,1)}, u32[]{:S(2)}) copy-start(pred[8,2,96,128]{3,2,1,0:T(32,128)(4,1)} %copy-done.5) | copy-start | bytes 589828
  100.1 58.5 %all-to-all-start = ((bf16[8,128,1024]{2,1,0:T(8,128)(2,1)}), bf16[8,128,1024]{2,1,0:T(8,128)(2,1)S(1)}, u32[]{:S(2)}, u32[]{:S(2)}) async-start(bf16[8,128,1024]{2,1,0:T(8,128)(2,1)} %add_convert_fusion.1), calls=%async_computation | async-start | bytes 4194304 | tf_op jit(solution)/shard_map/all_to_all | solution.py:228
  109.9 4.7 %copy-start.11 = (bf16[1536,512]{1,0:T(8,128)(2,1)S(1)}, bf16[1536,512]{1,0:T(8,128)(2,1)}, u32[]{:S(2)}) copy-start(bf16[1536,512]{1,0:T(8,128)(2,1)} %copy-done.10) | copy-start | bytes 4718596
  109.9 7.3 %copy-start.14 = (f32[1536,512]{1,0:T(8,128)S(1)}, f32[1536,512]{1,0:T(8,128)}, u32[]{:S(2)}) copy-start(f32[1536,512]{1,0:T(8,128)} %get-tuple-element.22) | copy-start | bytes 9437188
  115.6 14.9 %collective-permute-start.11 = (bf16[256,1,1024]{2,0,1:T(8,128)(2,1)S(1)}, bf16[256,1,1024]{2,0,1:T(8,128)(2,1)S(1)}, u32[]{:S(2)}, u32[]{:S(2)}) collective-permute-start(bf16[256,1,1024]{2,0,1:T(8,128)(2,1)S(1)} %fusion.21), channel_id=1, source_target_pairs={{0,16},{16,0},{1,17},{17,1},{2,18},{18,2},{3,19},{19,3},{4,20},{20... | collective-permute-start | bytes 1572872 | tf_op jit(solution)/shard_map/ppermute | solution.py:142
  117.2 3.3 %copy-start.2 = (bf16[16,96,1024]{2,1,0:T(8,128)(2,1)S(1)}, bf16[16,96,1024]{2,1,0:T(8,128)(2,1)}, u32[]{:S(2)}) copy-start(bf16[16,96,1024]{2,1,0:T(8,128)(2,1)} %copy-done.1) | copy-start | bytes 9437188
  121.6 20.1 %collective-permute-start.10 = (bf16[256,1,1024]{2,0,1:T(8,128)(2,1)S(1)}, bf16[256,1,1024]{2,0,1:T(8,128)(2,1)S(1)}, u32[]{:S(2)}, u32[]{:S(2)}) collective-permute-start(bf16[256,1,1024]{2,0,1:T(8,128)(2,1)S(1)} %fusion.20), channel_id=1, source_target_pairs={{0,16},{16,0},{1,17},{17,1},{2,18},{18,2},{3,19},{19,3},{4,20},{20... | collective-permute-start | bytes 1572872 | tf_op jit(solution)/shard_map/ppermute | solution.py:142
  123.4 28.5 %collective-permute-start.9 = (bf16[256,1,1024]{2,0,1:T(8,128)(2,1)S(1)}, bf16[256,1,1024]{2,0,1:T(8,128)(2,1)S(1)}, u32[]{:S(2)}, u32[]{:S(2)}) collective-permute-start(bf16[256,1,1024]{2,0,1:T(8,128)(2,1)S(1)} %fusion.19), channel_id=1, source_target_pairs={{0,16},{16,0},{1,17},{17,1},{2,18},{18,2},{3,19},{19,3},{4,20},{20... | collective-permute-start | bytes 1572872 | tf_op jit(solution)/shard_map/ppermute | solution.py:142
  (5 other events, 10.2 us)
Sparse Core Ops, SparseCore 0:
  14.7 58.2 all-gather.1

commit v21 on v20

--- a/solution.py
+++ b/solution.py
@@ -137,12 +137,11 @@
         grads = jnp.concatenate([grad_half(h) for h in range(ndp)], axis=0)
         return reduce_grads(grads, width)
     d = lax.axis_index("dp")
-    theirs = grad_half(1 - d)
     sent = [
-        lax.ppermute(theirs[:, i:i + 1].astype(jnp.bfloat16), "dp", [(0, 1), (1, 0)])
-        for i in range(theirs.shape[1])
+        lax.ppermute(g.astype(jnp.bfloat16), "dp", [(0, 1), (1, 0)])
+        for g in grad_half(1 - d, False)
     ]
-    summed = grad_half(d) + jnp.concatenate(sent, axis=1).astype(jnp.float32)
+    summed = grad_half(d) + jnp.stack(sent, axis=1).astype(jnp.float32)
     return summed.reshape(1, summed.shape[0], 3, width)
 
 
@@ -250,18 +249,16 @@
     d_up = (back * act).astype(jnp.bfloat16)
     share = d_gate.shape[1] // lax.axis_size("dp")
 
-    def grad_half(h):
+    def grad_half(h, stacked=True):
         def part(v):
             return lax.dynamic_slice_in_dim(v, h * share, share, axis=1)
 
-        return jnp.stack(
-            [
-                contract_rows(part(d_gate), rows_x),
-                contract_rows(part(d_up), rows_x),
-                contract_rows(part(hidden), rows_q),
-            ],
-            axis=1,
-        )
+        kinds = [
+            contract_rows(part(d_gate), rows_x),
+            contract_rows(part(d_up), rows_x),
+            contract_rows(part(hidden), rows_q),
+        ]
+        return jnp.stack(kinds, axis=1) if stacked else kinds
 
     weight_grads = reduce_grads_dp(grad_half, width)
 

time: 167 us -> 167 us (level)
  no operation moved by 1% of the time
where the time goes in v21:
time: 167 us
  waiting for transfers between devices  50.2 us (30%)
  matrix products  34.6 us (21%)
  between operations  32.4 us (19%)
  starting transfers between devices  30.3 us (18%)
  other arithmetic  10.9 us (7%)
  local copies, waits for them, and re-layouts  8.12 us (5%)
    ppermute x3, waiting for transfers between devices, reduce_grads_dp(): lax.ppermute(g.astype(jnp.bfloat16), 'dp', [(0, 1), (1, 0)])  24.2 us
    ppermute x4, waiting for transfers between devices, ring_gather(): up = lax.ppermute(up, 'ez', ahead)  17.8 us
    ppermute x4, starting transfers between devices, ring_gather(): up = lax.ppermute(up, 'ez', ahead)  16.1 us
    all_to_all x1, starting transfers between devices, local_gather(): returned = lax.all_to_all(combined, 'ez', 0, 0, tiled=True)  9.8 us
    dot_general x3, matrix products, contract_cols(): lax.dot_general(left, right, (((1,), (1,)), ((), ())), preferred_element_...  8.93 us
    dot_general x2, matrix products, local_gather(): jnp.einsum('ikjt,itd->ikjd', masked_pick, scaled.astype(jnp.bfloat16), pr...  8.34 us
    dot_general x6, matrix products, contract_rows(): lax.dot_general(left, right, (((0,), (0,)), ((), ())), preferred_element_...  6.08 us
    dot_general x2, matrix products, dense_for(): jnp.einsum('sjt,sjd->std', lax.dynamic_index_in_dim(pick_k, k, 1, keepdim...  6.08 us
  transfers between devices with their start and end apart: 14, of which 10 were waited for; matrix products, arithmetic and copies ran while one was open for 24% of the time, Pallas kernels for 0%

profile of v21, /device:TPU:0, one launch (start us, length us, event | category | flops | bytes accessed | tf_op | source)
XLA Modules:
  0.0 166.5 jit_solution(8722408739812350418)
XLA Ops:
  12.9 1.7 %pad_maximum_fusion = bf16[136,1024]{1,0:T(8,128)(2,1)} fusion(bf16[8,1024]{1,0:T(8,128)(2,1)S(1)} %reshape.210, bf16[128,1024]{1,0:T(8,128)(2,1)} %param.11), kind=kLoop, calls=%fused_computation.60 | loop fusion | flops 557056 | bytes 557056 | tf_op jit(solution)/shard_map/concatenate | solution.py:165
  14.6 3.1 %collective-permute-start.1 = (bf16[128,1024]{1,0:T(8,128)(2,1)}, bf16[128,1024]{1,0:T(8,128)(2,1)}, u32[]{:S(2)}, u32[]{:S(2)}) collective-permute-start(bf16[128,1024]{1,0:T(8,128)(2,1)} %param.16), channel_id=1, source_target_pairs={{0,4},{4,8},{8,12},{12,14},{14,10},{10,6},{6,2},{2,0},{1,5},{5,9},... | collective-permute-start | bytes 786440 | tf_op jit(solution)/shard_map/ppermute | solution.py:113
  38.8 2.1 %collective-permute-start.3 = (bf16[128,1024]{1,0:T(8,128)(2,1)}, bf16[128,1024]{1,0:T(8,128)(2,1)S(1)}, u32[]{:S(2)}, u32[]{:S(2)}) collective-permute-start(bf16[128,1024]{1,0:T(8,128)(2,1)} %collective-permute-done.1), channel_id=1, source_target_pairs={{0,4},{4,8},{8,12},{12,14},{14,10},{10,6},{6,2},{2,0},{1,5},{5,9},... | collective-permute-start | bytes 786440 | tf_op jit(solution)/shard_map/ppermute | solution.py:113
  42.9 7.5 %collective-permute-done.3 = bf16[128,1024]{1,0:T(8,128)(2,1)S(1)} collective-permute-done((bf16[128,1024]{1,0:T(8,128)(2,1)}, bf16[128,1024]{1,0:T(8,128)(2,1)S(1)}, u32[]{:S(2)}, u32[]{:S(2)}) %collective-permute-start.3) | collective-permute-done | bytes 262176 | tf_op jit(solution)/shard_map/ppermute | solution.py:113
  50.4 3.8 %collective-permute-start.5 = (bf16[128,1024]{1,0:T(8,128)(2,1)S(1)}, bf16[128,1024]{1,0:T(8,128)(2,1)S(1)}, u32[]{:S(2)}, u32[]{:S(2)}) collective-permute-start(bf16[128,1024]{1,0:T(8,128)(2,1)S(1)} %collective-permute-done.3), channel_id=1, source_target_pairs={{0,4},{4,8},{8,12},{12,14},{14,10},{10,6},{6,2},{2,0},{1,5},{5,9},... | collective-permute-start | bytes 786440 | tf_op jit(solution)/shard_map/ppermute | solution.py:113
  54.1 2.2 %collective-permute-done.4 = bf16[128,1024]{1,0:T(8,128)(2,1)S(1)} collective-permute-done((bf16[128,1024]{1,0:T(8,128)(2,1)}, bf16[128,1024]{1,0:T(8,128)(2,1)S(1)}, u32[]{:S(2)}, u32[]{:S(2)}) %collective-permute-start.4) | collective-permute-done | bytes 262176 | tf_op jit(solution)/shard_map/ppermute | solution.py:116
  56.4 7.0 %collective-permute-done.5 = bf16[128,1024]{1,0:T(8,128)(2,1)S(1)} collective-permute-done((bf16[128,1024]{1,0:T(8,128)(2,1)S(1)}, bf16[128,1024]{1,0:T(8,128)(2,1)S(1)}, u32[]{:S(2)}, u32[]{:S(2)}) %collective-permute-start.5) | collective-permute-done | bytes 262176 | tf_op jit(solution)/shard_map/ppermute | solution.py:113
  63.4 7.2 %collective-permute-start.7 = (bf16[128,1024]{1,0:T(8,128)(2,1)S(1)}, bf16[128,1024]{1,0:T(8,128)(2,1)S(1)}, u32[]{:S(2)}, u32[]{:S(2)}) collective-permute-start(bf16[128,1024]{1,0:T(8,128)(2,1)S(1)} %collective-permute-done.5), channel_id=1, source_target_pairs={{0,4},{4,8},{8,12},{12,14},{14,10},{10,6},{6,2},{2,0},{1,5},{5,9},... | collective-permute-start | bytes 786440 | tf_op jit(solution)/shard_map/ppermute | solution.py:113
  71.9 3.4 %collective-permute-done.7 = bf16[128,1024]{1,0:T(8,128)(2,1)S(1)} collective-permute-done((bf16[128,1024]{1,0:T(8,128)(2,1)S(1)}, bf16[128,1024]{1,0:T(8,128)(2,1)S(1)}, u32[]{:S(2)}, u32[]{:S(2)}) %collective-permute-start.7) | collective-permute-done | bytes 262176 | tf_op jit(solution)/shard_map/ppermute | solution.py:113
  76.8 3.2 %fusion.5 = bf16[16,96,1024]{2,1,0:T(8,128)(2,1)S(1)} fusion(bf16[16,136,1024]{2,1,0:T(8,128)(2,1)} %bitcast.137, s32[16,128]{1,0:T(8,128)S(1)} %convolution_convert_fusion.5, pred[16,128]{1,0:T(8,128)(4,1)S(1)} %fusion.61), kind=kOutput, calls=%fused_computation.15 | convolution fusion | flops 404619264 | bytes 7350272 | tf_op jit(solution)/shard_map/sjt,std->sjd/dot_general | solution.py:189
  80.1 1.8 %fusion.24 = f32[1536,512]{1,0:T(8,128)S(1)} fusion(bf16[1536,1024]{1,0:T(8,128)(2,1)S(1)} %bitcast.138, bf16[1,512,1024]{2,1,0:T(8,128)(2,1)S(1)} %copy-done.8), kind=kOutput, calls=%fused_computation.38 | convolution fusion | flops 1610612736 | bytes 7340032 | tf_op jit(solution)/shard_map/dot_general | solution.py:16
  82.1 3.8 %multiply_convert_fusion.2 = (bf16[1536,512]{1,0:T(8,128)(2,1)S(1)}, f32[1536,512]{1,0:T(8,128)}) fusion(f32[1536,512]{1,0:T(8,128)S(1)} %fusion.24, bf16[1536,1024]{1,0:T(8,128)(2,1)S(1)} %bitcast.139, bf16[1,512,1024]{2,1,0:T(8,128)(2,1)S(1)} %copy-done.9), kind=kOutput, calls=%fused_computation.12 | convolution fusion | flops 1615331328 | bytes 12058624 | tf_op jit(solution)/shard_map/dot_general | solution.py:16
  86.0 1.8 %convolution_convert_fusion = bf16[1536,1024]{1,0:T(8,128)(2,1)S(1)} fusion(bf16[1536,512]{1,0:T(8,128)(2,1)S(1)} %get-tuple-element.21, bf16[1,512,1024]{2,1,0:T(8,128)(2,1)S(1)} %copy-done), kind=kOutput, calls=%fused_computation.8 | convolution fusion | flops 1612185600 | bytes 5767168 | tf_op jit(solution)/shard_map/dot_general | solution.py:201
  89.4 2.1 %convolution_convert_fusion.1 = bf16[8,128,1024]{2,1,0:T(8,128)(2,1)} fusion(bf16[8,2,96,1024]{3,2,1,0:T(8,128)(2,1)S(1)} %bitcast.144, s32[]{:T(128)S(6)} %select_n.146, pred[8,2,96,128]{3,2,1,0:T(32,128)(4,1)S(1)} %fusion.32), kind=kOutput, calls=%fused_computation.21 | convolution fusion | flops 202375168 | bytes 3769344 | tf_op jit(solution)/shard_map/sjt,sjd->std/dot_general | solution.py:208
  92.2 3.7 %fusion.9 = f32[8,2,96,1024]{3,2,1,0:T(8,128)} fusion(bf16[8,128,1024]{2,1,0:T(8,128)(2,1)S(1)} %bitcast_dynamic-update-slice_fusion, f32[8,128]{1,0:T(8,128)S(1)} %bitcast.165, pred[2]{0:T(512)(128)(4,1)S(1)} %iota_compare_fusion.5, s32[8,2,128]{2,1,0:T(2,128)S(1)} %bitcast.160, pred[8,2,128]{2,1,0:T(4,128)(4,1)S(1)} %and.48), kind=kOutput, calls=%fused_computation.17 | convolution fusion | flops 406585344 | bytes 8402946 | tf_op jit(solution)/shard_map/ikjt,itd->ikjd/dot_general | solution.py:240
  96.1 4.0 %add_convert_fusion.1 = bf16[8,128,1024]{2,1,0:T(8,128)(2,1)} fusion(bf16[8,128,1024]{2,1,0:T(8,128)(2,1)} %collective-permute-done, f32[8,128]{1,0:T(8,128)S(1)} %get-tuple-element.7, f32[8,128]{1,0:T(8,128)S(1)} %get-tuple-element.6, bf16[8,2,96,1024]{3,2,1,0:T(8,128)(2,1)S(1)} %bitcast.145, s32[]{:T(128)S(6)} %select_n.144, ...), kind=kOutput, calls=%fused_computation.7 | convolution fusion | flops 208666624 | bytes 5874688 | tf_op jit(solution)/shard_map/sjt,sjd->std/dot_general | solution.py:208
  100.1 9.8 %all-to-all-start = ((bf16[8,128,1024]{2,1,0:T(8,128)(2,1)}), bf16[8,128,1024]{2,1,0:T(8,128)(2,1)S(1)}, u32[]{:S(2)}, u32[]{:S(2)}) async-start(bf16[8,128,1024]{2,1,0:T(8,128)(2,1)} %add_convert_fusion.1), calls=%async_computation | async-start | bytes 4194304 | tf_op jit(solution)/shard_map/all_to_all | solution.py:227
  109.9 4.6 %add_convert_fusion = bf16[8,2,96,1024]{3,2,1,0:T(8,128)(2,1)S(1)} fusion(f32[8,2,96,1024]{3,2,1,0:T(8,128)} %fusion.9, bf16[8,128,1024]{2,1,0:T(8,128)(2,1)} %bitcast.62, f32[8,128]{1,0:T(8,128)S(1)} %bitcast.164, pred[2]{0:T(512)(128)(4,1)S(1)} %iota_compare_fusion.4, s32[8,2,128]{2,1,0:T(2,128)S(1)} %bitcast.161, pred[8,2,128]{2,1,0:T(4,128)(4,1)S(1)} %and.48), kind=kOutput, calls=%fused_computation | convolution fusion | flops 409731072 | bytes 11548674 | tf_op jit(solution)/shard_map/ikjt,itd->ikjd/dot_general | solution.py:240
  117.2 3.3 %multiply_convert_fusion.1 = (bf16[1536,512]{1,0:T(8,128)(2,1)S(1)}, bf16[1536,512]{1,0:T(8,128)(2,1)S(1)}) fusion(f32[1536,512]{1,0:T(8,128)S(1)} %copy-done.13, f32[1536,512]{1,0:T(8,128)S(1)} %copy-done.14, bf16[1536,1024]{1,0:T(8,128)(2,1)S(1)} %bitcast.147, bf16[1,512,1024]{2,1,0:T(8,128)(2,1)S(1)} %copy-done), kind=kOutput, calls=%fused_computation.11 | convolution fusion | flops 1620836352 | bytes 13631488 | tf_op jit(solution)/shard_map/dot_general | solution.py:16
  127.8 2.7 %collective-permute-done.11 = bf16[256,1024]{1,0:T(8,128)(2,1)S(1)} collective-permute-done((bf16[256,1024]{1,0:T(8,128)(2,1)S(1)}, bf16[256,1024]{1,0:T(8,128)(2,1)S(1)}, u32[]{:S(2)}, u32[]{:S(2)}) %collective-permute-start.11) | collective-permute-done | bytes 524320 | tf_op jit(solution)/shard_map/ppermute | solution.py:141
  130.5 11.2 %collective-permute-done.10 = bf16[256,1024]{1,0:T(8,128)(2,1)S(1)} collective-permute-done((bf16[256,1024]{1,0:T(8,128)(2,1)S(1)}, bf16[256,1024]{1,0:T(8,128)(2,1)S(1)}, u32[]{:S(2)}, u32[]{:S(2)}) %collective-permute-start.10) | collective-permute-done | bytes 524320 | tf_op jit(solution)/shard_map/ppermute | solution.py:141
  141.7 10.3 %collective-permute-done.9 = bf16[256,1024]{1,0:T(8,128)(2,1)S(1)} collective-permute-done((bf16[256,1024]{1,0:T(8,128)(2,1)S(1)}, bf16[256,1024]{1,0:T(8,128)(2,1)S(1)}, u32[]{:S(2)}, u32[]{:S(2)}) %collective-permute-start.9) | collective-permute-done | bytes 524320 | tf_op jit(solution)/shard_map/ppermute | solution.py:141
  152.0 2.2 %maximum_add_fusion = f32[1,256,3,1024]{3,1,2,0:T(8,128)} fusion(f32[1,256,1,1024]{3,1,2,0:T(8,128)S(1)} %convolution_bitcast_fusion, f32[1,256,1,1024]{3,1,2,0:T(8,128)S(1)} %convolution_bitcast_fusion.1, f32[1,256,1,1024]{3,1,2,0:T(8,128)S(1)} %convolution_bitcast_fusion.2, bf16[1,256,1,1024]{3,1,2,0:T(8,128)(2,1)S(1)} %bitcast.154, ...), kind=kLoop, calls=%fused_computation.9 | loop fusion | flops 4718592 | bytes 7864320 | tf_op jit(solution)/shard_map/add | solution.py:144
  154.2 4.4 %all-to-all-done = bf16[8,128,1024]{2,1,0:T(8,128)(2,1)S(1)} async-done(((bf16[8,128,1024]{2,1,0:T(8,128)(2,1)}), bf16[8,128,1024]{2,1,0:T(8,128)(2,1)S(1)}, u32[]{:S(2)}, u32[]{:S(2)}) %all-to-all-start) | async-done | bytes 2097184 | tf_op jit(solution)/shard_map/all_to_all | solution.py:227
  (88 shorter events, 27.2 us)
Async XLA Ops:
  7.2 78.8 %copy-start = (bf16[1,512,1024]{2,1,0:T(8,128)(2,1)S(1)}, bf16[1,512,1024]{2,1,0:T(8,128)(2,1)}, u32[]{:S(2)}) copy-start(bf16[1,512,1024]{2,1,0:T(8,128)(2,1)} %param.19) | copy-start | bytes 3145732
  7.2 31.6 %copy-start.7 = (bf16[128,1024]{1,0:T(8,128)(2,1)S(1)}, bf16[128,1024]{1,0:T(8,128)(2,1)}, u32[]{:S(2)}) copy-start(bf16[128,1024]{1,0:T(8,128)(2,1)} %param.16) | copy-start | bytes 786436
  7.2 68.2 %all-gather.2.cloned.1.call-start = ((), (), s32[]{:S(2)}) async-start(), calls=%async_computation.1 | async-start | bytes 4734976 | tf_op jit(solution)/shard_map/all_gather | solution.py:167
  14.6 24.2 %collective-permute-start.1 = (bf16[128,1024]{1,0:T(8,128)(2,1)}, bf16[128,1024]{1,0:T(8,128)(2,1)}, u32[]{:S(2)}, u32[]{:S(2)}) collective-permute-start(bf16[128,1024]{1,0:T(8,128)(2,1)} %param.16), channel_id=1, source_target_pairs={{0,4},{4,8},{8,12},{12,14},{14,10},{10,6},{6,2},{2,0},{1,5},{5,9},... | collective-permute-start | bytes 786440 | tf_op jit(solution)/shard_map/ppermute | solution.py:113
  17.7 23.2 %collective-permute-start.2 = (bf16[128,1024]{1,0:T(8,128)(2,1)}, bf16[128,1024]{1,0:T(8,128)(2,1)}, u32[]{:S(2)}, u32[]{:S(2)}) collective-permute-start(bf16[128,1024]{1,0:T(8,128)(2,1)} %param.16), channel_id=1, source_target_pairs={{0,2},{4,0},{8,4},{12,8},{14,12},{10,14},{6,10},{2,6},{1,3},{5,1},... | collective-permute-start | bytes 786440 | tf_op jit(solution)/shard_map/ppermute | solution.py:116
  38.8 11.5 %collective-permute-start.3 = (bf16[128,1024]{1,0:T(8,128)(2,1)}, bf16[128,1024]{1,0:T(8,128)(2,1)S(1)}, u32[]{:S(2)}, u32[]{:S(2)}) collective-permute-start(bf16[128,1024]{1,0:T(8,128)(2,1)} %collective-permute-done.1), channel_id=1, source_target_pairs={{0,4},{4,8},{8,12},{12,14},{14,10},{10,6},{6,2},{2,0},{1,5},{5,9},... | collective-permute-start | bytes 786440 | tf_op jit(solution)/shard_map/ppermute | solution.py:113
  40.9 15.4 %collective-permute-start.4 = (bf16[128,1024]{1,0:T(8,128)(2,1)}, bf16[128,1024]{1,0:T(8,128)(2,1)S(1)}, u32[]{:S(2)}, u32[]{:S(2)}) collective-permute-start(bf16[128,1024]{1,0:T(8,128)(2,1)} %collective-permute-done.2), channel_id=1, source_target_pairs={{0,2},{4,0},{8,4},{12,8},{14,12},{10,14},{6,10},{2,6},{1,3},{5,1},... | collective-permute-start | bytes 786440 | tf_op jit(solution)/shard_map/ppermute | solution.py:116
  50.4 13.0 %collective-permute-start.5 = (bf16[128,1024]{1,0:T(8,128)(2,1)S(1)}, bf16[128,1024]{1,0:T(8,128)(2,1)S(1)}, u32[]{:S(2)}, u32[]{:S(2)}) collective-permute-start(bf16[128,1024]{1,0:T(8,128)(2,1)S(1)} %collective-permute-done.3), channel_id=1, source_target_pairs={{0,4},{4,8},{8,12},{12,14},{14,10},{10,6},{6,2},{2,0},{1,5},{5,9},... | collective-permute-start | bytes 786440 | tf_op jit(solution)/shard_map/ppermute | solution.py:113
  56.3 15.5 %collective-permute-start.6 = (bf16[128,1024]{1,0:T(8,128)(2,1)S(1)}, bf16[128,1024]{1,0:T(8,128)(2,1)S(1)}, u32[]{:S(2)}, u32[]{:S(2)}) collective-permute-start(bf16[128,1024]{1,0:T(8,128)(2,1)S(1)} %collective-permute-done.4), channel_id=1, source_target_pairs={{0,2},{4,0},{8,4},{12,8},{14,12},{10,14},{6,10},{2,6},{1,3},{5,1},... | collective-permute-start | bytes 786440 | tf_op jit(solution)/shard_map/ppermute | solution.py:116
  63.4 11.9 %collective-permute-start.7 = (bf16[128,1024]{1,0:T(8,128)(2,1)S(1)}, bf16[128,1024]{1,0:T(8,128)(2,1)S(1)}, u32[]{:S(2)}, u32[]{:S(2)}) collective-permute-start(bf16[128,1024]{1,0:T(8,128)(2,1)S(1)} %collective-permute-done.5), channel_id=1, source_target_pairs={{0,4},{4,8},{8,12},{12,14},{14,10},{10,6},{6,2},{2,0},{1,5},{5,9},... | collective-permute-start | bytes 786440 | tf_op jit(solution)/shard_map/ppermute | solution.py:113
  75.3 16.7 %collective-permute-start.8 = (bf16[1024,1024]{1,0:T(8,128)(2,1)S(1)}, bf16[1024,1024]{1,0:T(8,128)(2,1)}, u32[]{:S(2)}, u32[]{:S(2)}) collective-permute-start(bf16[1024,1024]{1,0:T(8,128)(2,1)S(1)} %bitcast.135), channel_id=1, source_target_pairs={{0,1},{1,0},{2,3},{3,2},{4,5},{5,4},{6,7},{7,6},{8,9},{9,8},{10,11... | collective-permute-start | bytes 6291464 | tf_op jit(solution)/shard_map/ppermute | solution.py:119
  76.8 3.3 %copy-start.8 = (bf16[1,512,1024]{2,1,0:T(8,128)(2,1)S(1)}, bf16[1,512,1024]{2,1,0:T(8,128)(2,1)}, u32[]{:S(2)}) copy-start(bf16[1,512,1024]{2,1,0:T(8,128)(2,1)} %param.17) | copy-start | bytes 3145732
  81.9 4.0 %copy-start.12 = (f32[1536,512]{1,0:T(8,128)}, f32[1536,512]{1,0:T(8,128)S(1)}, u32[]{:S(2)}) copy-start(f32[1536,512]{1,0:T(8,128)S(1)} %fusion.24) | copy-start | bytes 9437188
  82.1 5.7 %copy-start.5 = (pred[8,2,96,128]{3,2,1,0:T(32,128)(4,1)}, pred[8,2,96,128]{3,2,1,0:T(32,128)(4,1)S(1)}, u32[]{:S(2)}) copy-start(pred[8,2,96,128]{3,2,1,0:T(32,128)(4,1)S(1)} %fusion.32) | copy-start | bytes 589828
  91.5 4.6 %collective-permute-start = (bf16[8,128,1024]{2,1,0:T(8,128)(2,1)}, bf16[8,128,1024]{2,1,0:T(8,128)(2,1)}, u32[]{:S(2)}, u32[]{:S(2)}) collective-permute-start(bf16[8,128,1024]{2,1,0:T(8,128)(2,1)} %convolution_convert_fusion.1), channel_id=1, source_target_pairs={{0,1},{1,0},{2,3},{3,2},{4,5},{5,4},{6,7},{7,6},{8,9},{9,8},{10,11... | collective-permute-start | bytes 6291464 | tf_op jit(solution)/shard_map/ppermute | solution.py:215
  92.2 4.0 %copy-start.4 = (bf16[1536,1024]{1,0:T(8,128)(2,1)S(1)}, bf16[1536,1024]{1,0:T(8,128)(2,1)}, u32[]{:S(2)}) copy-start(bf16[1536,1024]{1,0:T(8,128)(2,1)} %copy-done.3) | copy-start | bytes 9437188
  92.2 4.0 %copy-start.6 = (pred[8,2,96,128]{3,2,1,0:T(32,128)(4,1)S(1)}, pred[8,2,96,128]{3,2,1,0:T(32,128)(4,1)}, u32[]{:S(2)}) copy-start(pred[8,2,96,128]{3,2,1,0:T(32,128)(4,1)} %copy-done.5) | copy-start | bytes 589828
  100.1 58.5 %all-to-all-start = ((bf16[8,128,1024]{2,1,0:T(8,128)(2,1)}), bf16[8,128,1024]{2,1,0:T(8,128)(2,1)S(1)}, u32[]{:S(2)}, u32[]{:S(2)}) async-start(bf16[8,128,1024]{2,1,0:T(8,128)(2,1)} %add_convert_fusion.1), calls=%async_computation | async-start | bytes 4194304 | tf_op jit(solution)/shard_map/all_to_all | solution.py:227
  109.9 4.7 %copy-start.11 = (bf16[1536,512]{1,0:T(8,128)(2,1)S(1)}, bf16[1536,512]{1,0:T(8,128)(2,1)}, u32[]{:S(2)}) copy-start(bf16[1536,512]{1,0:T(8,128)(2,1)} %copy-done.10) | copy-start | bytes 4718596
  109.9 7.3 %copy-start.14 = (f32[1536,512]{1,0:T(8,128)S(1)}, f32[1536,512]{1,0:T(8,128)}, u32[]{:S(2)}) copy-start(f32[1536,512]{1,0:T(8,128)} %get-tuple-element.22) | copy-start | bytes 9437188
  115.6 14.9 %collective-permute-start.11 = (bf16[256,1024]{1,0:T(8,128)(2,1)S(1)}, bf16[256,1024]{1,0:T(8,128)(2,1)S(1)}, u32[]{:S(2)}, u32[]{:S(2)}) collective-permute-start(bf16[256,1024]{1,0:T(8,128)(2,1)S(1)} %convolution_convert_fusion.2), channel_id=1, source_target_pairs={{0,16},{16,0},{1,17},{17,1},{2,18},{18,2},{3,19},{19,3},{4,20},{20... | collective-permute-start | bytes 1572872 | tf_op jit(solution)/shard_map/ppermute | solution.py:141
  117.2 3.3 %copy-start.2 = (bf16[16,96,1024]{2,1,0:T(8,128)(2,1)S(1)}, bf16[16,96,1024]{2,1,0:T(8,128)(2,1)}, u32[]{:S(2)}) copy-start(bf16[16,96,1024]{2,1,0:T(8,128)(2,1)} %copy-done.1) | copy-start | bytes 9437188
  121.6 20.1 %collective-permute-start.10 = (bf16[256,1024]{1,0:T(8,128)(2,1)S(1)}, bf16[256,1024]{1,0:T(8,128)(2,1)S(1)}, u32[]{:S(2)}, u32[]{:S(2)}) collective-permute-start(bf16[256,1024]{1,0:T(8,128)(2,1)S(1)} %convolution_convert_fusion.3), channel_id=1, source_target_pairs={{0,16},{16,0},{1,17},{17,1},{2,18},{18,2},{3,19},{19,3},{4,20},{20... | collective-permute-start | bytes 1572872 | tf_op jit(solution)/shard_map/ppermute | solution.py:141
  123.4 28.5 %collective-permute-start.9 = (bf16[256,1024]{1,0:T(8,128)(2,1)S(1)}, bf16[256,1024]{1,0:T(8,128)(2,1)S(1)}, u32[]{:S(2)}, u32[]{:S(2)}) collective-permute-start(bf16[256,1024]{1,0:T(8,128)(2,1)S(1)} %convolution_convert_fusion.4), channel_id=1, source_target_pairs={{0,16},{16,0},{1,17},{17,1},{2,18},{18,2},{3,19},{19,3},{4,20},{20... | collective-permute-start | bytes 1572872 | tf_op jit(solution)/shard_map/ppermute | solution.py:141
  (5 other events, 10.2 us)
Sparse Core Ops, SparseCore 0:
  14.7 58.2 all-gather.1
